TPU v7x, 256 devices: a whole 4x4x8 slice. The times are simulated.
256 devices in a mesh: gx: 16 (over y, x_hi, core), gy: 16 (over z, x_lo).
Axes of the slice: x: 4 (x_hi: 2, x_lo: 2; x = x_hi * 2 + x_lo), y: 4, z: 8, core: 2. Of those that a mesh axis runs over, the one named last changes fastest.
Arguments:
- features: bfloat16 [16, 16, 2, 512, 128], P('gx', 'gy'), may hold values from -6 to 6
- occupancy: int32 [16, 16, 2, 512], P('gx', 'gy'), may hold values 0 or 1
- brick_pos: int32 [16, 16, 2], P('gx', 'gy'), may hold values from 0 to 15, as said below
- brick_count: int32 [16, 16], P('gx', 'gy'), may hold values from 1 to 2, as said below
- weight: bfloat16 [27, 128, 128], replicated, may hold values from -0.109375 to 0.109375
- cotangent: bfloat16 [16, 16, 2, 512, 128], P('gx', 'gy'), may hold values from -6 to 6
Outputs:
- output: bfloat16 [16, 16, 2, 512, 128], P('gx', 'gy')
- input_grad: bfloat16 [16, 16, 2, 512, 128], P('gx', 'gy')
- weight_grad: float32 [27, 128, 128], replicated
Inputs may be any that keep to these rules, and one draw needn't show every extreme that they name: `brick_pos`: within a tile the 2 slots hold distinct positions. `brick_count`: some tile holds exactly 2 live slots.
All inputs are finite; a program needn't handle non-finite values. No bound on the sum of `occupancy` on one device may be relied on, other than what follows from the above.
Results may differ from a plain program's by a relative error of at most 0.001.
Values may be sent and summed in bfloat16 or wider, within the bound.
No kernel may reach another device: no remote copies, remote signals or barrier semaphores. Data moves between devices by JAX's collectives and lax.ppermute only.
A program may use at most 64 MiB of HBM per device.

v0:
```python
import jax
import jax.numpy as jnp
from jax import lax
from jax.sharding import PartitionSpec as P

BRICK = 8
TBX = 2
TBY = 2
ZL = 4
OFFS = 27


def with_halo(value, sides, width):
    for axis, dim in sides:
        size, length = (lax.axis_size(axis), value.shape[dim])
        up = [(i, (i + 1) % size) for i in range(size - 1)]
        down = [(j, i) for i, j in up]
        last = lax.slice_in_dim(value, length - width, length, axis=dim)
        leading = lax.slice_in_dim(value, 0, width, axis=dim)
        before = lax.ppermute(last, axis, up)
        after = lax.ppermute(leading, axis, down)
        value = jnp.concatenate([before, value, after], axis=dim)
    return value


def place_bricks(bricks, places, alive):
    spots = jnp.arange(TBX * TBY * ZL, dtype=jnp.int32)
    picker = ((places[None, :] == spots[:, None]) & alive[None, :]).astype(jnp.bfloat16)
    dense = jnp.einsum("ps,svc->pvc", picker, bricks, preferred_element_type=jnp.float32).astype(
        jnp.bfloat16
    )
    chans = bricks.shape[-1]
    dense = dense.reshape(TBX, TBY, ZL, BRICK, BRICK, BRICK, chans)
    dense = dense.transpose(0, 3, 1, 4, 2, 5, 6)
    return dense.reshape(TBX * BRICK, TBY * BRICK, ZL * BRICK, chans)


def cut_windows(padded, places):
    padded = jnp.pad(padded, ((0, 0), (0, 0), (1, 1), (0, 0)))
    chans = padded.shape[-1]
    along_x = places // (TBY * ZL)
    along_y = places // ZL % TBY
    along_z = places % ZL
    zero_index = jnp.zeros_like(along_x)

    def one_window(start_x, start_y, start_z, start_c):
        return lax.dynamic_slice(
            padded, (start_x, start_y, start_z, start_c), (BRICK + 2, BRICK + 2, BRICK + 2, chans)
        )

    return jax.vmap(one_window)(along_x * BRICK, along_y * BRICK, along_z * BRICK, zero_index)


def offset_rows(windows, offset):
    first = offset // 9
    second = offset // 3 % 3
    third = offset % 3
    piece = windows[:, first : first + BRICK, second : second + BRICK, third : third + BRICK, :]
    return piece.reshape(-1, windows.shape[-1])


def forward_pass(feat_padded, places, weight, keeper_rows):
    feat_windows = cut_windows(feat_padded, places)
    output_sum = jnp.zeros((keeper_rows.shape[0], weight.shape[-1]), jnp.float32)
    for offset in range(OFFS):
        output_sum = output_sum + jnp.dot(
            offset_rows(feat_windows, offset), weight[offset], preferred_element_type=jnp.float32
        )
    return ((output_sum * keeper_rows).astype(jnp.bfloat16), feat_windows)


def local(features, occupancy, brick_pos, brick_count, weight, cotangent):
    slots = features.shape[2]
    chans = features.shape[-1]
    places = brick_pos[0, 0]
    alive = jnp.arange(slots, dtype=jnp.int32) < brick_count[0, 0]
    keeper = (occupancy[0, 0] * alive[:, None].astype(jnp.int32)).astype(jnp.bfloat16)
    keeper_rows = keeper.reshape(-1, 1).astype(jnp.float32)
    feat_masked = features[0, 0] * keeper[:, :, None]
    grad_masked = cotangent[0, 0] * keeper[:, :, None]
    feat_dense = place_bricks(feat_masked, places, alive)
    grad_dense = place_bricks(grad_masked, places, alive)
    feat_padded = with_halo(feat_dense, (("gx", 0), ("gy", 1)), 1)
    output_rows, feat_windows = forward_pass(feat_padded, places, weight, keeper_rows)
    grad_padded = with_halo(grad_dense, (("gx", 0), ("gy", 1)), 1)
    grad_windows = cut_windows(grad_padded, places)
    grad_rows = grad_masked.reshape(-1, chans)
    input_sum = jnp.zeros((grad_rows.shape[0], chans), jnp.float32)
    blocks = []
    for offset in range(OFFS):
        input_sum = input_sum + lax.dot_general(
            offset_rows(grad_windows, offset),
            weight[OFFS - 1 - offset],
            (((1,), (1,)), ((), ())),
            preferred_element_type=jnp.float32,
        )
        blocks.append(
            lax.dot_general(
                offset_rows(feat_windows, offset),
                grad_rows,
                (((0,), (0,)), ((), ())),
                preferred_element_type=jnp.float32,
            )
        )
    weight_local = jnp.stack(blocks)
    input_rows = (input_sum * keeper_rows).astype(jnp.bfloat16)
    tiles = lax.axis_size("gx") * lax.axis_size("gy")
    weight_total = lax.psum(weight_local, ("gx", "gy"))
    weight_grad = weight_total / jnp.float32(tiles)
    output = output_rows.reshape(1, 1, slots, -1, chans)
    input_grad = input_rows.reshape(1, 1, slots, -1, chans)
    return (output, input_grad, weight_grad)


def solution(mesh):
    return jax.shard_map(
        local,
        mesh=mesh,
        in_specs=(
            P("gx", "gy", None, None, None),
            P("gx", "gy", None, None),
            P("gx", "gy", None),
            P("gx", "gy"),
            P(),
            P("gx", "gy", None, None, None),
        ),
        out_specs=(P("gx", "gy", None, None, None), P("gx", "gy", None, None, None), P()),
        check_vma=False,
    )
```

profile of v0, /device:TPU:1, one launch (start us, length us, event | category | flops | bytes accessed | tf_op | source)
XLA Modules:
  0.0 400.6 jit_solution(5784793127298901972)
XLA Ops:
  8.6 1.2 bitcast_multiply_fusion
  9.9 1.5 convolution_convert_fusion
  12.3 6.0 %collective-permute-start.4 = (bf16[1,16,32,128]{3,2,1,0:T(8,128)(2,1)S(1)}, bf16[1,16,32,128]{3,2,1,0:T(8,128)(2,1)S(1)}, u32[]{:S(2)}, u32[]{:S(2)}) collective-permute-start(bf16[1,16,32,128]{3,2,1,0:T(8,128)(2,1)S(1)} %get-tuple-element.53), channel_id=1, source_target_pairs={{0,16},{16,32},{32,48},{48,64},{64,80},{80,96},{96,112},{112,128},... | collective-permute-start | bytes 393224 | tf_op jit(solution)/shard_map/ppermute | solution.py:20
  18.3 1.9 collective-permute-start.5
  22.7 5.1 %collective-permute-start = (bf16[1,16,32,128]{3,2,1,0:T(8,128)(2,1)}, bf16[1,16,32,128]{3,2,1,0:T(8,128)(2,1)S(1)}, u32[]{:S(2)}, u32[]{:S(2)}) collective-permute-start(bf16[1,16,32,128]{3,2,1,0:T(8,128)(2,1)} %get-tuple-element.55), channel_id=1, source_target_pairs={{0,16},{16,32},{32,48},{48,64},{64,80},{80,96},{96,112},{112,128},... | collective-permute-start | bytes 393224 | tf_op jit(solution)/shard_map/ppermute | solution.py:20
  27.8 1.9 collective-permute-start.1
  30.8 2.2 collective-permute-start.6
  33.0 1.3 collective-permute-start.7
  34.4 1.4 collective-permute-done.1
  36.6 4.3 %collective-permute-start.2 = (bf16[18,1,32,128]{3,2,1,0:T(8,128)(2,1)}, bf16[18,1,32,128]{3,2,1,0:T(8,128)(2,1)}, u32[]{:S(2)}, u32[]{:S(2)}) collective-permute-start(bf16[18,1,32,128]{3,2,1,0:T(8,128)(2,1)} %get-tuple-element.51), channel_id=1, source_target_pairs={{0,1},{1,2},{2,3},{3,4},{4,5},{5,6},{6,7},{7,8},{8,9},{9,10},{10,1... | collective-permute-start | bytes 442376 | tf_op jit(solution)/shard_map/ppermute | solution.py:20
  40.9 1.3 collective-permute-start.3
  42.2 4.2 %select_maximum_fusion = bf16[18,18,34,128]{3,2,1,0:T(8,128)(2,1)} fusion(bf16[18,1,32,128]{3,2,1,0:T(8,128)(2,1)S(1)} %collective-permute-done.7, bf16[18,1,32,128]{3,2,1,0:T(8,128)(2,1)S(1)} %collective-permute-done.6, bf16[1,16,32,128]{3,2,1,0:T(8,128)(2,1)S(1)} %collective-permute-done.5, bf16[16,16,32,128]{3,2,1,0:T(8,128)(2,1)S(1)} %bitcast.521, ...), kind=kLoop, calls=%fused_computation.7 | loop fusion | flops 25380864 | bytes 5474304 | tf_op jit(solution)/shard_map/concatenate | solution.py:22
  46.5 7.6 %while.3 = (s32[]{:T(128)}, bf16[18,18,34,128]{3,2,1,0:T(8,128)(2,1)}, s32[2,4]{1,0:T(2,128)S(1)}, bf16[2,10,10,10,128]{4,3,2,1,0:T(8,128)(2,1)S(1)}, s32[]{:T(128)}) while((s32[]{:T(128)}, bf16[18,18,34,128]{3,2,1,0:T(8,128)(2,1)}, s32[2,4]{1,0:T(2,128)S(1)}, bf16[2,10,10,10,128]{4,3,2,1,0:T(8,128)(2,1)S(1)}, s32[]{:T(128)}) %tuple.103), condition=%wide.while_cond.1, body=%wide.while_body.1.sunk | while | flops 2 | bytes 665745 | solution.py:47
  47.1 3.2 bitcast_dynamic-update-slice_fusion.5
  51.0 3.1 bitcast_dynamic-update-slice_fusion.5
  54.1 2.7 fusion.165
  56.8 1.4 fusion.166
  58.2 5.1 %select_maximum_fusion.4 = bf16[18,18,34,128]{3,2,1,0:T(8,128)(2,1)} fusion(bf16[18,1,32,128]{3,2,1,0:T(8,128)(2,1)} %collective-permute-done.3, bf16[18,1,32,128]{3,2,1,0:T(8,128)(2,1)} %collective-permute-done.2, bf16[1,16,32,128]{3,2,1,0:T(8,128)(2,1)S(1)} %collective-permute-done.1, bf16[16,16,32,128]{3,2,1,0:T(8,128)(2,1)S(1)} %bitcast.518, ...), kind=kLoop, calls=%fused_computation.11 | loop fusion | flops 25380864 | bytes 5474304 | tf_op jit(solution)/shard_map/concatenate | solution.py:22
  63.5 8.0 %while.2 = (s32[]{:T(128)}, bf16[18,18,34,128]{3,2,1,0:T(8,128)(2,1)}, s32[2,4]{1,0:T(2,128)S(1)}, bf16[2,10,10,10,128]{4,3,2,1,0:T(8,128)(2,1)S(1)}, s32[]{:T(128)}) while((s32[]{:T(128)}, bf16[18,18,34,128]{3,2,1,0:T(8,128)(2,1)}, s32[2,4]{1,0:T(2,128)S(1)}, bf16[2,10,10,10,128]{4,3,2,1,0:T(8,128)(2,1)S(1)}, s32[]{:T(128)}) %tuple.108), condition=%wide.while_cond, body=%wide.while_body.sunk | while | flops 2 | bytes 665745 | solution.py:47
  64.2 3.3 bitcast_dynamic-update-slice_fusion.4
  68.1 3.2 bitcast_dynamic-update-slice_fusion.4
  72.0 1.0 fusion.167
  74.5 0.9 fusion.35
  75.4 1.0 convolution_add_fusion.50
  76.3 0.9 fusion.34
  77.3 1.0 convolution_add_fusion.49
  78.2 0.9 fusion.33
  79.1 1.0 convolution_add_fusion.48
  80.1 0.9 fusion.32
  81.0 1.0 convolution_add_fusion.47
  82.0 0.9 fusion.31
  82.9 1.0 convolution_add_fusion.46
  84.8 1.0 convolution_add_fusion.45
  86.9 0.9 fusion.28
  88.0 0.9 fusion.27
  89.0 1.0 convolution_add_fusion.43
  89.9 0.9 fusion.26
  90.8 1.0 convolution_add_fusion.42
  92.7 1.0 convolution_add_fusion.41
  94.6 1.0 convolution_add_fusion.40
  95.6 0.9 fusion.23
  96.5 1.0 convolution_add_fusion.39
  97.4 0.9 fusion.22
  98.3 1.0 convolution_add_fusion.38
  99.3 0.9 fusion.21
  100.2 1.0 convolution_add_fusion.37
  101.2 0.9 fusion.20
  102.1 1.0 convolution_add_fusion.36
  103.1 0.9 fusion.19
  104.0 1.0 convolution_add_fusion.35
  104.9 0.9 fusion.18
  105.9 1.0 convolution_add_fusion.34
  106.8 0.9 fusion.17
  107.7 1.0 convolution_add_fusion.33
  109.6 1.0 convolution_add_fusion.32
  111.5 1.0 convolution_add_fusion.31
  113.4 1.0 convolution_add_fusion.30
  115.2 1.0 convolution_add_fusion.29
  117.1 1.0 convolution_add_fusion.28
  119.0 1.0 convolution_add_fusion.27
  128.6 0.9 fusion.9
  130.0 0.9 fusion.8
  131.0 259.9 %all-reduce.4.cloned.1.call-done = f32[27,128,128]{2,1,0:T(8,128)} async-done(((f32[27,128,128]{2,1,0:T(8,128)}), f32[27,128,128]{2,1,0:T(8,128)}) %all-reduce.4.cloned.1.call-update) | async-done | bytes 1769488 | tf_op jit(solution)/shard_map/psum | solution.py:108
  390.8 2.9 broadcast_multiply_fusion
  (144 shorter events, 28.8 us)
Async XLA Ops:
  7.2 383.7 %all-reduce.4.cloned.1.call-start = ((), (), s32[]{:S(2)}) async-start(), calls=%async_computation | async-start | bytes 3538944 | tf_op jit(solution)/shard_map/psum | solution.py:108
  11.4 8.8 %copy-start.32 = (s32[1,1,2]{2,1,0:T(1,128)S(1)}, s32[1,1,2]{2,1,0:T(1,128)}, u32[]{:S(2)}) copy-start(s32[1,1,2]{2,1,0:T(1,128)} %param.8) | copy-start | bytes 28
  12.2 17.8 %copy-start = (bf16[2,8,2,8,4,8,128]{6,5,4,3,2,1,0:T(8,128)(2,1)}, bf16[2,8,2,8,4,8,128]{6,5,4,3,2,1,0:T(8,128)(2,1)S(1)}, u32[]{:S(2)}) copy-start(bf16[2,8,2,8,4,8,128]{6,5,4,3,2,1,0:T(8,128)(2,1)S(1)} %copy.13) | copy-start | bytes 6291460
  12.3 17.8 %collective-permute-start.4 = (bf16[1,16,32,128]{3,2,1,0:T(8,128)(2,1)S(1)}, bf16[1,16,32,128]{3,2,1,0:T(8,128)(2,1)S(1)}, u32[]{:S(2)}, u32[]{:S(2)}) collective-permute-start(bf16[1,16,32,128]{3,2,1,0:T(8,128)(2,1)S(1)} %get-tuple-element.53), channel_id=1, source_target_pairs={{0,16},{16,32},{32,48},{48,64},{64,80},{80,96},{96,112},{112,128},... | collective-permute-start | bytes 393224 | tf_op jit(solution)/shard_map/ppermute | solution.py:20
  18.3 11.7 %collective-permute-start.5 = (bf16[1,16,32,128]{3,2,1,0:T(8,128)(2,1)S(1)}, bf16[1,16,32,128]{3,2,1,0:T(8,128)(2,1)S(1)}, u32[]{:S(2)}, u32[]{:S(2)}) collective-permute-start(bf16[1,16,32,128]{3,2,1,0:T(8,128)(2,1)S(1)} %get-tuple-element.54), channel_id=1, source_target_pairs={{16,0},{32,16},{48,32},{64,48},{80,64},{96,80},{112,96},{128,112},... | collective-permute-start | bytes 393224 | tf_op jit(solution)/shard_map/ppermute | solution.py:21
  21.1 8.6 %copy-start.30 = (bf16[1,1,2,512,128]{4,3,2,1,0:T(8,128)(2,1)S(1)}, bf16[1,1,2,512,128]{4,3,2,1,0:T(8,128)(2,1)}, u32[]{:S(2)}) copy-start(bf16[1,1,2,512,128]{4,3,2,1,0:T(8,128)(2,1)} %param.11) | copy-start | bytes 786436
  21.1 8.8 %copy-start.31 = (s32[1,1,2,512]{3,2,1,0:T(2,128)S(1)}, s32[1,1,2,512]{3,2,1,0:T(2,128)}, u32[]{:S(2)}) copy-start(s32[1,1,2,512]{3,2,1,0:T(2,128)} %param.7) | copy-start | bytes 12292
  22.7 11.7 %collective-permute-start = (bf16[1,16,32,128]{3,2,1,0:T(8,128)(2,1)}, bf16[1,16,32,128]{3,2,1,0:T(8,128)(2,1)S(1)}, u32[]{:S(2)}, u32[]{:S(2)}) collective-permute-start(bf16[1,16,32,128]{3,2,1,0:T(8,128)(2,1)} %get-tuple-element.55), channel_id=1, source_target_pairs={{0,16},{16,32},{32,48},{48,64},{64,80},{80,96},{96,112},{112,128},... | collective-permute-start | bytes 393224 | tf_op jit(solution)/shard_map/ppermute | solution.py:20
  27.8 8.0 %collective-permute-start.1 = (bf16[1,16,32,128]{3,2,1,0:T(8,128)(2,1)}, bf16[1,16,32,128]{3,2,1,0:T(8,128)(2,1)S(1)}, u32[]{:S(2)}, u32[]{:S(2)}) collective-permute-start(bf16[1,16,32,128]{3,2,1,0:T(8,128)(2,1)} %get-tuple-element.56), channel_id=1, source_target_pairs={{16,0},{32,16},{48,32},{64,48},{80,64},{96,80},{112,96},{128,112},... | collective-permute-start | bytes 393224 | tf_op jit(solution)/shard_map/ppermute | solution.py:21
  30.8 11.4 %collective-permute-start.6 = (bf16[18,1,32,128]{3,2,1,0:T(8,128)(2,1)}, bf16[18,1,32,128]{3,2,1,0:T(8,128)(2,1)S(1)}, u32[]{:S(2)}, u32[]{:S(2)}) collective-permute-start(bf16[18,1,32,128]{3,2,1,0:T(8,128)(2,1)} %get-tuple-element.49), channel_id=1, source_target_pairs={{0,1},{1,2},{2,3},{3,4},{4,5},{5,6},{6,7},{7,8},{8,9},{9,10},{10,1... | collective-permute-start | bytes 442376 | tf_op jit(solution)/shard_map/ppermute | solution.py:20
  33.0 9.2 %collective-permute-start.7 = (bf16[18,1,32,128]{3,2,1,0:T(8,128)(2,1)S(1)}, bf16[18,1,32,128]{3,2,1,0:T(8,128)(2,1)S(1)}, u32[]{:S(2)}, u32[]{:S(2)}) collective-permute-start(bf16[18,1,32,128]{3,2,1,0:T(8,128)(2,1)S(1)} %get-tuple-element.50), channel_id=1, source_target_pairs={{1,0},{2,1},{3,2},{4,3},{5,4},{6,5},{7,6},{8,7},{9,8},{10,9},{11,1... | collective-permute-start | bytes 442376 | tf_op jit(solution)/shard_map/ppermute | solution.py:21
  34.4 7.8 %copy-start.1 = (bf16[2,8,2,8,4,8,128]{6,5,4,3,2,1,0:T(8,128)(2,1)S(1)}, bf16[2,8,2,8,4,8,128]{6,5,4,3,2,1,0:T(8,128)(2,1)}, u32[]{:S(2)}) copy-start(bf16[2,8,2,8,4,8,128]{6,5,4,3,2,1,0:T(8,128)(2,1)} %copy-done) | copy-start | bytes 6291460
  36.6 21.7 %collective-permute-start.2 = (bf16[18,1,32,128]{3,2,1,0:T(8,128)(2,1)}, bf16[18,1,32,128]{3,2,1,0:T(8,128)(2,1)}, u32[]{:S(2)}, u32[]{:S(2)}) collective-permute-start(bf16[18,1,32,128]{3,2,1,0:T(8,128)(2,1)} %get-tuple-element.51), channel_id=1, source_target_pairs={{0,1},{1,2},{2,3},{3,4},{4,5},{5,6},{6,7},{7,8},{8,9},{9,10},{10,1... | collective-permute-start | bytes 442376 | tf_op jit(solution)/shard_map/ppermute | solution.py:20
  40.9 17.4 %collective-permute-start.3 = (bf16[18,1,32,128]{3,2,1,0:T(8,128)(2,1)}, bf16[18,1,32,128]{3,2,1,0:T(8,128)(2,1)}, u32[]{:S(2)}, u32[]{:S(2)}) collective-permute-start(bf16[18,1,32,128]{3,2,1,0:T(8,128)(2,1)} %get-tuple-element.52), channel_id=1, source_target_pairs={{1,0},{2,1},{3,2},{4,3},{5,4},{6,5},{7,6},{8,7},{9,8},{10,9},{11,1... | collective-permute-start | bytes 442376 | tf_op jit(solution)/shard_map/ppermute | solution.py:21
  72.0 1.2 copy-start.2
  82.9 3.8 copy-start.3
  119.0 2.0 copy-start.29
  120.0 1.2 copy-start.28
  120.9 1.0 copy-start.27
  121.0 1.2 copy-start.26
  121.2 1.2 copy-start.25
  121.9 1.0 copy-start.24
  122.1 1.0 copy-start.23
  122.4 1.0 copy-start.22
  122.9 1.0 copy-start.21
  123.1 1.0 copy-start.20
  123.4 1.0 copy-start.19
  123.9 1.0 copy-start.18
  124.1 1.0 copy-start.17
  124.4 1.0 copy-start.16
  124.9 1.0 copy-start.15
  125.1 1.0 copy-start.14
  125.4 1.0 copy-start.13
  125.9 1.0 copy-start.12
  126.1 1.0 copy-start.11
  126.4 1.0 copy-start.10
  126.8 1.0 copy-start.9
  127.1 1.0 copy-start.8
  127.3 1.0 copy-start.7
  128.1 1.4 copy-start.6
  128.3 1.4 copy-start.5
  128.6 1.4 copy-start.4
Sparse Core Ops, SparseCore 0:
  121.1 269.7 all-reduce.3
where the time goes:
time: 404 us; the launch traced here: 401 us
  waiting for transfers between devices  261 us (65%)
  matrix products  57.5 us (14%)
  local copies, waits for them, and re-layouts  25.9 us (6%)
  starting transfers between devices  24.1 us (6%)
  other arithmetic  15.9 us (4%)
  between operations  15.5 us (4%)
    psum x1, waiting for transfers between devices, local(): weight_total = lax.psum(weight_local, ('gx', 'gy'))  260 us
    dot_general x27, matrix products, local(): lax.dot_general(offset_rows(feat_windows, offset), grad_rows, (((0,), (0,...  24.5 us
    dot_general x27, matrix products, forward_pass(): jnp.dot(offset_rows(feat_windows, offset), weight[offset], preferred_elem...  23.8 us
    ppermute x4, starting transfers between devices, with_halo(): before = lax.ppermute(last, axis, up)  17.7 us
    gather x12, local copies, waits for them, and re-layouts  15.3 us
    concatenate x2, other arithmetic, with_halo(): value = jnp.concatenate([before, value, after], axis=dim)  9.34 us
  transfers between devices with their start and end apart: 9, of which 2 were waited for; matrix products, arithmetic and copies ran while one was open for 7% of the time, Pallas kernels for 0%

commit v1 on v0

--- a/solution.py
+++ b/solution.py
@@ -21,6 +21,31 @@
         after = lax.ppermute(leading, axis, down)
         value = jnp.concatenate([before, value, after], axis=dim)
     return value
+
+
+STEPS = (("gx", 0), ("gy", 0), ("gx", 2), ("gy", 1), ("gx", 1), ("gx", 3), ("gy", 2), ("gy", 3))
+
+
+def butterfly_sum(value, steps=STEPS):
+    lanes = value.shape[-1]
+    flat = value.reshape(-1, lanes)
+    rows = flat.shape[0]
+    parts = 1 << len(steps)
+    padded_rows = -(-rows // parts) * parts
+    buf = jnp.pad(flat, ((0, padded_rows - rows), (0, 0)))
+    for axis, b in steps:
+        half = buf.shape[0] // 2
+        pairs = [(i, i ^ (1 << b)) for i in range(lax.axis_size(axis))]
+        bit = (lax.axis_index(axis) >> b) & 1
+        keep = lax.dynamic_slice_in_dim(buf, bit * half, half, 0)
+        send = lax.dynamic_slice_in_dim(buf, (1 - bit) * half, half, 0)
+        buf = keep + lax.ppermute(send, axis, pairs)
+    for axis, b in reversed(steps):
+        pairs = [(i, i ^ (1 << b)) for i in range(lax.axis_size(axis))]
+        bit = (lax.axis_index(axis) >> b) & 1
+        got = lax.ppermute(buf, axis, pairs)
+        buf = jnp.concatenate([jnp.where(bit == 0, buf, got), jnp.where(bit == 0, got, buf)], 0)
+    return buf[:rows].reshape(value.shape)
 
 
 def place_bricks(bricks, places, alive):
@@ -105,7 +130,7 @@
     weight_local = jnp.stack(blocks)
     input_rows = (input_sum * keeper_rows).astype(jnp.bfloat16)
     tiles = lax.axis_size("gx") * lax.axis_size("gy")
-    weight_total = lax.psum(weight_local, ("gx", "gy"))
+    weight_total = butterfly_sum(weight_local)
     weight_grad = weight_total / jnp.float32(tiles)
     output = output_rows.reshape(1, 1, slots, -1, chans)
     input_grad = input_rows.reshape(1, 1, slots, -1, chans)

time: 404 us -> 209 us (0.52)
  waiting for transfers between devices: 261 us -> 45 us
  starting transfers between devices: 24.1 us -> 80.2 us
  matrix products: 57.5 us -> 41.1 us
  between operations: 15.5 us -> 2.86 us
    psum x1 -> x0, waiting for transfers between devices: 260 us -> none  [local(): weight_total = lax.psum(weight_local, ('gx', 'gy'))]
    ppermute x0 -> x16, starting transfers between devices: none -> 54.6 us  [the longest x8 29.7 us: butterfly_sum(): got = lax.ppermute(buf, axis, pairs)]
    ppermute x0 -> x16, waiting for transfers between devices: none -> 39.4 us  [the longest x8 20.6 us: butterfly_sum(): buf = keep + lax.ppermute(send, axis, pairs)]
    dot_general x27, matrix products: 24.5 us -> 7.24 us  [local(): lax.dot_general(offset_rows(feat_windows, offset), grad_rows, (((0,), (0,...]
    ppermute x4, waiting for transfers between devices: 1.42 us -> 5.58 us  [with_halo(): after = lax.ppermute(leading, axis, down)]
  transfers between devices with their start and end apart: 9 -> 24, of which waited for: 2 -> 15; matrix products, arithmetic and copies ran while one was open for 7% -> 13% of each run, Pallas kernels for 0% -> 0%
where the time goes in v1:
time: 209 us; the launch traced here: 208 us
  starting transfers between devices  80.2 us (38%)
  waiting for transfers between devices  45 us (22%)
  matrix products  41.1 us (20%)
  local copies, waits for them, and re-layouts  23.9 us (11%)
  other arithmetic  14.3 us (7%)
  between operations  2.86 us (1%)
    ppermute x8, starting transfers between devices, butterfly_sum(): got = lax.ppermute(buf, axis, pairs)  29.7 us
    ppermute x8, starting transfers between devices, butterfly_sum(): buf = keep + lax.ppermute(send, axis, pairs)  24.9 us
    dot_general x27, matrix products, forward_pass(): jnp.dot(offset_rows(feat_windows, offset), weight[offset], preferred_elem...  24.6 us
    ppermute x8, waiting for transfers between devices, butterfly_sum(): buf = keep + lax.ppermute(send, axis, pairs)  20.6 us
    ppermute x4, starting transfers between devices, with_halo(): before = lax.ppermute(last, axis, up)  19.2 us
    ppermute x8, waiting for transfers between devices, butterfly_sum(): got = lax.ppermute(buf, axis, pairs)  18.8 us
    gather x12, local copies, waits for them, and re-layouts  15.1 us
    concatenate x2, other arithmetic, with_halo(): value = jnp.concatenate([before, value, after], axis=dim)  9.34 us
  transfers between devices with their start and end apart: 24, of which 15 were waited for; matrix products, arithmetic and copies ran while one was open for 13% of the time, Pallas kernels for 0%

profile of v1, /device:TPU:1, one launch (start us, length us, event | category | flops | bytes accessed | tf_op | source)
XLA Modules:
  0.0 207.7 jit_solution(15571714313214118097)
XLA Ops:
  2.1 1.2 bitcast_multiply_fusion
  3.3 1.5 convolution_convert_fusion
  6.4 6.0 %collective-permute-start.4 = (bf16[1,16,32,128]{3,2,1,0:T(8,128)(2,1)}, bf16[1,16,32,128]{3,2,1,0:T(8,128)(2,1)S(1)}, u32[]{:S(2)}, u32[]{:S(2)}) collective-permute-start(bf16[1,16,32,128]{3,2,1,0:T(8,128)(2,1)} %get-tuple-element.53), channel_id=1, source_target_pairs={{0,16},{16,32},{32,48},{48,64},{64,80},{80,96},{96,112},{112,128},... | collective-permute-start | bytes 393224 | tf_op jit(solution)/shard_map/ppermute | solution.py:20
  12.4 1.9 collective-permute-start.5
  16.1 5.1 %collective-permute-start = (bf16[1,16,32,128]{3,2,1,0:T(8,128)(2,1)S(1)}, bf16[1,16,32,128]{3,2,1,0:T(8,128)(2,1)S(1)}, u32[]{:S(2)}, u32[]{:S(2)}) collective-permute-start(bf16[1,16,32,128]{3,2,1,0:T(8,128)(2,1)S(1)} %get-tuple-element.55), channel_id=1, source_target_pairs={{0,16},{16,32},{32,48},{48,64},{64,80},{80,96},{96,112},{112,128},... | collective-permute-start | bytes 393224 | tf_op jit(solution)/shard_map/ppermute | solution.py:20
  21.2 1.9 collective-permute-start.1
  23.5 5.6 %collective-permute-done.1 = bf16[1,16,32,128]{3,2,1,0:T(8,128)(2,1)S(1)} collective-permute-done((bf16[1,16,32,128]{3,2,1,0:T(8,128)(2,1)S(1)}, bf16[1,16,32,128]{3,2,1,0:T(8,128)(2,1)S(1)}, u32[]{:S(2)}, u32[]{:S(2)}) %collective-permute-start.1) | collective-permute-done | bytes 131104 | tf_op jit(solution)/shard_map/ppermute | solution.py:21
  29.1 2.2 %collective-permute-start.2 = (bf16[18,1,32,128]{3,2,1,0:T(8,128)(2,1)S(1)}, bf16[18,1,32,128]{3,2,1,0:T(8,128)(2,1)S(1)}, u32[]{:S(2)}, u32[]{:S(2)}) collective-permute-start(bf16[18,1,32,128]{3,2,1,0:T(8,128)(2,1)S(1)} %get-tuple-element.51), channel_id=1, source_target_pairs={{0,1},{1,2},{2,3},{3,4},{4,5},{5,6},{6,7},{7,8},{8,9},{9,10},{10,1... | collective-permute-start | bytes 442376 | tf_op jit(solution)/shard_map/ppermute | solution.py:20
  31.3 1.3 collective-permute-start.3
  33.6 5.8 %collective-permute-start.6 = (bf16[18,1,32,128]{3,2,1,0:T(8,128)(2,1)}, bf16[18,1,32,128]{3,2,1,0:T(8,128)(2,1)}, u32[]{:S(2)}, u32[]{:S(2)}) collective-permute-start(bf16[18,1,32,128]{3,2,1,0:T(8,128)(2,1)} %get-tuple-element.49), channel_id=1, source_target_pairs={{0,1},{1,2},{2,3},{3,4},{4,5},{5,6},{6,7},{7,8},{8,9},{9,10},{10,1... | collective-permute-start | bytes 442376 | tf_op jit(solution)/shard_map/ppermute | solution.py:20
  39.4 1.3 collective-permute-start.7
  40.7 4.2 %select_maximum_fusion.4 = bf16[18,18,34,128]{3,2,1,0:T(8,128)(2,1)} fusion(bf16[18,1,32,128]{3,2,1,0:T(8,128)(2,1)S(1)} %collective-permute-done.3, bf16[18,1,32,128]{3,2,1,0:T(8,128)(2,1)S(1)} %collective-permute-done.2, bf16[1,16,32,128]{3,2,1,0:T(8,128)(2,1)S(1)} %collective-permute-done.1, bf16[16,16,32,128]{3,2,1,0:T(8,128)(2,1)S(1)} %bitcast.523, ...), kind=kLoop, calls=%fused_computation.11 | loop fusion | flops 25380864 | bytes 5474304 | tf_op jit(solution)/shard_map/concatenate | solution.py:22
  45.1 7.5 %while.2 = (s32[]{:T(128)}, bf16[18,18,34,128]{3,2,1,0:T(8,128)(2,1)}, s32[2,4]{1,0:T(2,128)S(1)}, bf16[2,10,10,10,128]{4,3,2,1,0:T(8,128)(2,1)S(1)}, s32[]{:T(128)}) while((s32[]{:T(128)}, bf16[18,18,34,128]{3,2,1,0:T(8,128)(2,1)}, s32[2,4]{1,0:T(2,128)S(1)}, bf16[2,10,10,10,128]{4,3,2,1,0:T(8,128)(2,1)S(1)}, s32[]{:T(128)}) %tuple.108), condition=%wide.while_cond, body=%wide.while_body.sunk | while | flops 2 | bytes 665745 | solution.py:72
  45.7 3.1 %bitcast_dynamic-update-slice_fusion.4 = bf16[2,10,10,10,128]{4,3,2,1,0:T(8,128)(2,1)S(1)} fusion(bf16[2,10,10,10,128]{4,3,2,1,0:T(8,128)(2,1)S(1)} %get-tuple-element.206, s32[]{:T(128)S(6)} %copy.25, bf16[18,18,34,128]{3,2,1,0:T(8,128)(2,1)} %get-tuple-element.209, s32[]{:T(128)} %bitcast.483, s32[]{:T(128)} %bitcast.484, s32[]{:T(128)} %bitcast.485), kind=kLoop, calls=%fused_computation.clone.1 | loop fusion | bytes 665616 | tf_op jit(solution)/shard_map/vmap()/gather
  49.4 3.1 %bitcast_dynamic-update-slice_fusion.4 = bf16[2,10,10,10,128]{4,3,2,1,0:T(8,128)(2,1)S(1)} fusion(bf16[2,10,10,10,128]{4,3,2,1,0:T(8,128)(2,1)S(1)} %get-tuple-element.206, s32[]{:T(128)S(6)} %copy.25, bf16[18,18,34,128]{3,2,1,0:T(8,128)(2,1)} %get-tuple-element.209, s32[]{:T(128)} %bitcast.483, s32[]{:T(128)} %bitcast.484, s32[]{:T(128)} %bitcast.485), kind=kLoop, calls=%fused_computation.clone.1 | loop fusion | bytes 665616 | tf_op jit(solution)/shard_map/vmap()/gather
  52.5 2.7 %fusion.169 = (bf16[2,8,8,8,128]{4,3,2,1,0:T(8,128)(2,1)}, bf16[2,8,8,8,128]{4,3,2,1,0:T(8,128)(2,1)}, bf16[2,8,8,8,128]{4,3,2,1,0:T(8,128)(2,1)}, bf16[2,8,8,8,...) fusion(bf16[2,10,10,10,128]{4,3,2,1,0:T(8,128)(2,1)S(1)} %get-t, ...), kind=kLoop, calls=%fused_computation.333 | loop fusion | bytes 9961472 | tf_op jit(solution)/shard_map/slice | solution.py:83
  55.2 1.4 fusion.170
  56.6 5.1 %select_maximum_fusion = bf16[18,18,34,128]{3,2,1,0:T(8,128)(2,1)} fusion(bf16[18,1,32,128]{3,2,1,0:T(8,128)(2,1)} %collective-permute-done.7, bf16[18,1,32,128]{3,2,1,0:T(8,128)(2,1)} %collective-permute-done.6, bf16[1,16,32,128]{3,2,1,0:T(8,128)(2,1)S(1)} %copy-done.33, bf16[16,16,32,128]{3,2,1,0:T(8,128)(2,1)S(1)} %bitcast.520, ...), kind=kLoop, calls=%fused_computation.7 | loop fusion | flops 25380864 | bytes 5474304 | tf_op jit(solution)/shard_map/concatenate | solution.py:22
  61.9 7.9 %while.3 = (s32[]{:T(128)}, bf16[18,18,34,128]{3,2,1,0:T(8,128)(2,1)}, s32[2,4]{1,0:T(2,128)S(1)}, bf16[2,10,10,10,128]{4,3,2,1,0:T(8,128)(2,1)S(1)}, s32[]{:T(128)}) while((s32[]{:T(128)}, bf16[18,18,34,128]{3,2,1,0:T(8,128)(2,1)}, s32[2,4]{1,0:T(2,128)S(1)}, bf16[2,10,10,10,128]{4,3,2,1,0:T(8,128)(2,1)S(1)}, s32[]{:T(128)}) %tuple.114), condition=%wide.while_cond.1, body=%wide.while_body.1.sunk | while | flops 2 | bytes 665745 | solution.py:72
  62.6 3.2 %bitcast_dynamic-update-slice_fusion.5 = bf16[2,10,10,10,128]{4,3,2,1,0:T(8,128)(2,1)S(1)} fusion(bf16[2,10,10,10,128]{4,3,2,1,0:T(8,128)(2,1)S(1)} %get-tuple-element.221, s32[]{:T(128)S(6)} %copy.31, bf16[18,18,34,128]{3,2,1,0:T(8,128)(2,1)} %get-tuple-element.224, s32[]{:T(128)} %bitcast.487, s32[]{:T(128)} %bitcast.488, s32[]{:T(128)} %bitcast.489), kind=kLoop, calls=%fused_computation.2.clone.1 | loop fusion | bytes 665616 | tf_op jit(solution)/shard_map/vmap()/gather
  66.4 3.2 %bitcast_dynamic-update-slice_fusion.5 = bf16[2,10,10,10,128]{4,3,2,1,0:T(8,128)(2,1)S(1)} fusion(bf16[2,10,10,10,128]{4,3,2,1,0:T(8,128)(2,1)S(1)} %get-tuple-element.221, s32[]{:T(128)S(6)} %copy.31, bf16[18,18,34,128]{3,2,1,0:T(8,128)(2,1)} %get-tuple-element.224, s32[]{:T(128)} %bitcast.487, s32[]{:T(128)} %bitcast.488, s32[]{:T(128)} %bitcast.489), kind=kLoop, calls=%fused_computation.2.clone.1 | loop fusion | bytes 665616 | tf_op jit(solution)/shard_map/vmap()/gather
  72.2 1.0 convolution_add_fusion.49
  73.5 1.0 convolution_add_fusion.48
  74.8 1.0 convolution_add_fusion.47
  81.7 1.0 convolution_add_fusion.42
  83.0 1.0 convolution_add_fusion.41
  84.3 1.0 convolution_add_fusion.40
  85.6 1.0 convolution_add_fusion.39
  86.9 1.0 convolution_add_fusion.38
  88.2 1.0 convolution_add_fusion.37
  89.5 1.0 convolution_add_fusion.36
  90.9 1.0 convolution_add_fusion.35
  92.2 1.0 convolution_add_fusion.34
  93.5 1.0 convolution_add_fusion.33
  94.8 1.0 convolution_add_fusion.32
  96.1 1.0 convolution_add_fusion.31
  98.7 1.0 convolution_add_fusion.29
  104.5 1.0 fusion.167
  105.6 2.4 %collective-permute-start.9 = (f32[896,128]{1,0:T(8,128)S(1)}, f32[896,128]{1,0:T(8,128)S(1)}, u32[]{:S(2)}, u32[]{:S(2)}) collective-permute-start(f32[896,128]{1,0:T(8,128)S(1)} %constant_dynamic-slice_fusion.8), channel_id=1, source_target_pairs={{0,1},{1,0},{2,3},{3,2},{4,5},{5,4},{6,7},{7,6},{8,9},{9,8},{10,11... | collective-permute-start | bytes 1376264 | tf_op jit(solution)/shard_map/ppermute | solution.py:42
  108.5 10.0 %collective-permute-done.9 = f32[896,128]{1,0:T(8,128)S(1)} collective-permute-done((f32[896,128]{1,0:T(8,128)S(1)}, f32[896,128]{1,0:T(8,128)S(1)}, u32[]{:S(2)}, u32[]{:S(2)}) %collective-permute-start.9) | collective-permute-done | bytes 458784 | tf_op jit(solution)/shard_map/ppermute | solution.py:42
  118.6 1.4 collective-permute-start.10
  120.2 4.6 %collective-permute-done.10 = f32[448,128]{1,0:T(8,128)S(1)} collective-permute-done((f32[448,128]{1,0:T(8,128)S(1)}, f32[448,128]{1,0:T(8,128)S(1)}, u32[]{:S(2)}, u32[]{:S(2)}) %collective-permute-start.10) | collective-permute-done | bytes 229408 | tf_op jit(solution)/shard_map/ppermute | solution.py:42
  124.8 2.5 %collective-permute-start.11 = (f32[224,128]{1,0:T(8,128)S(1)}, f32[224,128]{1,0:T(8,128)S(1)}, u32[]{:S(2)}, u32[]{:S(2)}) collective-permute-start(f32[224,128]{1,0:T(8,128)S(1)} %constant_dynamic-slice_fusion.6), channel_id=1, source_target_pairs={{0,2},{1,3},{2,0},{3,1},{4,6},{5,7},{6,4},{7,5},{8,10},{9,11},{10,... | collective-permute-start | bytes 344072 | tf_op jit(solution)/shard_map/ppermute | solution.py:42
  127.6 1.9 collective-permute-done.11
  129.6 3.1 %collective-permute-start.12 = (f32[112,128]{1,0:T(8,128)S(1)}, f32[112,128]{1,0:T(8,128)S(1)}, u32[]{:S(2)}, u32[]{:S(2)}) collective-permute-start(f32[112,128]{1,0:T(8,128)S(1)} %constant_dynamic-slice_fusion.5), channel_id=1, source_target_pairs={{0,32},{16,48},{32,0},{48,16},{64,96},{80,112},{96,64},{112,80},{1... | collective-permute-start | bytes 172040 | tf_op jit(solution)/shard_map/ppermute | solution.py:42
  132.9 1.3 collective-permute-done.12
  134.3 3.7 %collective-permute-start.13 = (f32[56,128]{1,0:T(8,128)S(1)}, f32[56,128]{1,0:T(8,128)S(1)}, u32[]{:S(2)}, u32[]{:S(2)}) collective-permute-start(f32[56,128]{1,0:T(8,128)S(1)} %constant_dynamic-slice_fusion.4), channel_id=1, source_target_pairs={{0,128},{16,144},{32,160},{48,176},{64,192},{80,208},{96,224},{112... | collective-permute-start | bytes 86024 | tf_op jit(solution)/shard_map/ppermute | solution.py:42
  138.3 1.0 collective-permute-done.13
  139.3 5.0 %collective-permute-start.14 = (f32[28,128]{1,0:T(8,128)S(1)}, f32[28,128]{1,0:T(8,128)S(1)}, u32[]{:S(2)}, u32[]{:S(2)}) collective-permute-start(f32[28,128]{1,0:T(8,128)S(1)} %constant_dynamic-slice_fusion.3), channel_id=1, source_target_pairs={{0,4},{1,5},{2,6},{3,7},{4,0},{5,1},{6,2},{7,3},{8,12},{9,13},{10,... | collective-permute-start | bytes 43016 | tf_op jit(solution)/shard_map/ppermute | solution.py:42
  145.5 6.6 %collective-permute-start.15 = (f32[14,128]{1,0:T(8,128)S(1)}, f32[14,128]{1,0:T(8,128)S(1)}, u32[]{:S(2)}, u32[]{:S(2)}) collective-permute-start(f32[14,128]{1,0:T(8,128)S(1)} %constant_dynamic-slice_fusion.2), channel_id=1, source_target_pairs={{0,8},{1,9},{2,10},{3,11},{4,12},{5,13},{6,14},{7,15},{8,0},{9,1},... | collective-permute-start | bytes 21512 | tf_op jit(solution)/shard_map/ppermute | solution.py:42
  153.1 5.4 %collective-permute-start.16 = (f32[14,128]{1,0:T(8,128)S(1)}, f32[14,128]{1,0:T(8,128)S(1)}, u32[]{:S(2)}, u32[]{:S(2)}) collective-permute-start(f32[14,128]{1,0:T(8,128)S(1)} %dynamic-slice_add_fusion.6), channel_id=1, source_target_pairs={{0,8},{1,9},{2,10},{3,11},{4,12},{5,13},{6,14},{7,15},{8,0},{9,1},... | collective-permute-start | bytes 21512 | tf_op jit(solution)/shard_map/ppermute | solution.py:46
  158.8 1.1 collective-permute-done.16
  159.9 1.4 collective-permute-start.17
  161.5 2.0 collective-permute-done.17
  163.5 2.8 %collective-permute-start.18 = (f32[56,128]{1,0:T(8,128)S(1)}, f32[56,128]{1,0:T(8,128)S(1)}, u32[]{:S(2)}, u32[]{:S(2)}) collective-permute-start(f32[56,128]{1,0:T(8,128)S(1)} %pad_maximum_fusion.12), channel_id=1, source_target_pairs={{0,128},{16,144},{32,160},{48,176},{64,192},{80,208},{96,224},{112... | collective-permute-start | bytes 86024 | tf_op jit(solution)/shard_map/ppermute | solution.py:46
  166.5 1.3 collective-permute-done.18
  167.8 2.5 %collective-permute-start.19 = (f32[112,128]{1,0:T(8,128)S(1)}, f32[112,128]{1,0:T(8,128)S(1)}, u32[]{:S(2)}, u32[]{:S(2)}) collective-permute-start(f32[112,128]{1,0:T(8,128)S(1)} %pad_maximum_fusion.11), channel_id=1, source_target_pairs={{0,32},{16,48},{32,0},{48,16},{64,96},{80,112},{96,64},{112,80},{1... | collective-permute-start | bytes 172040 | tf_op jit(solution)/shard_map/ppermute | solution.py:46
  170.6 1.9 collective-permute-done.19
  173.3 3.0 %collective-permute-done.20 = f32[224,128]{1,0:T(8,128)S(1)} collective-permute-done((f32[224,128]{1,0:T(8,128)S(1)}, f32[224,128]{1,0:T(8,128)S(1)}, u32[]{:S(2)}, u32[]{:S(2)}) %collective-permute-start.20) | collective-permute-done | bytes 114720 | tf_op jit(solution)/shard_map/ppermute | solution.py:46
  176.3 1.0 collective-permute-start.21
  177.5 3.7 %collective-permute-done.21 = f32[448,128]{1,0:T(8,128)S(1)} collective-permute-done((f32[448,128]{1,0:T(8,128)S(1)}, f32[448,128]{1,0:T(8,128)S(1)}, u32[]{:S(2)}, u32[]{:S(2)}) %collective-permute-start.21) | collective-permute-done | bytes 229408 | tf_op jit(solution)/shard_map/ppermute | solution.py:46
  182.7 6.0 %collective-permute-done.22 = f32[896,128]{1,0:T(8,128)S(1)} collective-permute-done((f32[896,128]{1,0:T(8,128)S(1)}, f32[896,128]{1,0:T(8,128)S(1)}, u32[]{:S(2)}, u32[]{:S(2)}) %collective-permute-start.22) | collective-permute-done | bytes 458784 | tf_op jit(solution)/shard_map/ppermute | solution.py:46
  188.9 15.0 %collective-permute-start.23 = (f32[1792,128]{1,0:T(8,128)S(1)}, f32[1792,128]{1,0:T(8,128)S(1)}, u32[]{:S(2)}, u32[]{:S(2)}) collective-permute-start(f32[1792,128]{1,0:T(8,128)S(1)} %pad_maximum_fusion.1), channel_id=1, source_target_pairs={{0,16},{16,0},{32,48},{48,32},{64,80},{80,64},{96,112},{112,96},{1... | collective-permute-start | bytes 2752520 | tf_op jit(solution)/shard_map/ppermute | solution.py:46
  206.3 1.3 fusion.6
  (210 shorter events, 35.4 us)
Async XLA Ops:
  4.8 9.5 %copy-start.35 = (s32[1,1,2]{2,1,0:T(1,128)S(1)}, s32[1,1,2]{2,1,0:T(1,128)}, u32[]{:S(2)}) copy-start(s32[1,1,2]{2,1,0:T(1,128)} %param.8) | copy-start | bytes 28
  6.4 26.4 %collective-permute-start.4 = (bf16[1,16,32,128]{3,2,1,0:T(8,128)(2,1)}, bf16[1,16,32,128]{3,2,1,0:T(8,128)(2,1)S(1)}, u32[]{:S(2)}, u32[]{:S(2)}) collective-permute-start(bf16[1,16,32,128]{3,2,1,0:T(8,128)(2,1)} %get-tuple-element.53), channel_id=1, source_target_pairs={{0,16},{16,32},{32,48},{48,64},{64,80},{80,96},{96,112},{112,128},... | collective-permute-start | bytes 393224 | tf_op jit(solution)/shard_map/ppermute | solution.py:20
  12.4 20.4 %collective-permute-start.5 = (bf16[1,16,32,128]{3,2,1,0:T(8,128)(2,1)}, bf16[1,16,32,128]{3,2,1,0:T(8,128)(2,1)S(1)}, u32[]{:S(2)}, u32[]{:S(2)}) collective-permute-start(bf16[1,16,32,128]{3,2,1,0:T(8,128)(2,1)} %get-tuple-element.54), channel_id=1, source_target_pairs={{16,0},{32,16},{48,32},{64,48},{80,64},{96,80},{112,96},{128,112},... | collective-permute-start | bytes 393224 | tf_op jit(solution)/shard_map/ppermute | solution.py:21
  15.2 8.0 %copy-start.29 = (bf16[1,1,2,512,128]{4,3,2,1,0:T(8,128)(2,1)S(1)}, bf16[1,1,2,512,128]{4,3,2,1,0:T(8,128)(2,1)}, u32[]{:S(2)}) copy-start(bf16[1,1,2,512,128]{4,3,2,1,0:T(8,128)(2,1)} %param.11) | copy-start | bytes 786436
  15.2 8.2 %copy-start.34 = (s32[1,1,2,512]{3,2,1,0:T(2,128)S(1)}, s32[1,1,2,512]{3,2,1,0:T(2,128)}, u32[]{:S(2)}) copy-start(s32[1,1,2,512]{3,2,1,0:T(2,128)} %param.7) | copy-start | bytes 12292
  16.1 13.0 %copy-start = (bf16[2,8,2,8,4,8,128]{6,5,4,3,2,1,0:T(8,128)(2,1)}, bf16[2,8,2,8,4,8,128]{6,5,4,3,2,1,0:T(8,128)(2,1)S(1)}, u32[]{:S(2)}) copy-start(bf16[2,8,2,8,4,8,128]{6,5,4,3,2,1,0:T(8,128)(2,1)S(1)} %copy.10) | copy-start | bytes 6291460
  16.1 7.4 %collective-permute-start = (bf16[1,16,32,128]{3,2,1,0:T(8,128)(2,1)S(1)}, bf16[1,16,32,128]{3,2,1,0:T(8,128)(2,1)S(1)}, u32[]{:S(2)}, u32[]{:S(2)}) collective-permute-start(bf16[1,16,32,128]{3,2,1,0:T(8,128)(2,1)S(1)} %get-tuple-element.55), channel_id=1, source_target_pairs={{0,16},{16,32},{32,48},{48,64},{64,80},{80,96},{96,112},{112,128},... | collective-permute-start | bytes 393224 | tf_op jit(solution)/shard_map/ppermute | solution.py:20
  21.2 7.8 %collective-permute-start.1 = (bf16[1,16,32,128]{3,2,1,0:T(8,128)(2,1)S(1)}, bf16[1,16,32,128]{3,2,1,0:T(8,128)(2,1)S(1)}, u32[]{:S(2)}, u32[]{:S(2)}) collective-permute-start(bf16[1,16,32,128]{3,2,1,0:T(8,128)(2,1)S(1)} %get-tuple-element.56), channel_id=1, source_target_pairs={{16,0},{32,16},{48,32},{64,48},{80,64},{96,80},{112,96},{128,112},... | collective-permute-start | bytes 393224 | tf_op jit(solution)/shard_map/ppermute | solution.py:21
  29.1 11.6 %collective-permute-start.2 = (bf16[18,1,32,128]{3,2,1,0:T(8,128)(2,1)S(1)}, bf16[18,1,32,128]{3,2,1,0:T(8,128)(2,1)S(1)}, u32[]{:S(2)}, u32[]{:S(2)}) collective-permute-start(bf16[18,1,32,128]{3,2,1,0:T(8,128)(2,1)S(1)} %get-tuple-element.51), channel_id=1, source_target_pairs={{0,1},{1,2},{2,3},{3,4},{4,5},{5,6},{6,7},{7,8},{8,9},{9,10},{10,1... | collective-permute-start | bytes 442376 | tf_op jit(solution)/shard_map/ppermute | solution.py:20
  31.3 9.4 %collective-permute-start.3 = (bf16[18,1,32,128]{3,2,1,0:T(8,128)(2,1)S(1)}, bf16[18,1,32,128]{3,2,1,0:T(8,128)(2,1)S(1)}, u32[]{:S(2)}, u32[]{:S(2)}) collective-permute-start(bf16[18,1,32,128]{3,2,1,0:T(8,128)(2,1)S(1)} %get-tuple-element.52), channel_id=1, source_target_pairs={{1,0},{2,1},{3,2},{4,3},{5,4},{6,5},{7,6},{8,7},{9,8},{10,9},{11,1... | collective-permute-start | bytes 442376 | tf_op jit(solution)/shard_map/ppermute | solution.py:21
  32.8 7.9 %copy-start.1 = (bf16[2,8,2,8,4,8,128]{6,5,4,3,2,1,0:T(8,128)(2,1)S(1)}, bf16[2,8,2,8,4,8,128]{6,5,4,3,2,1,0:T(8,128)(2,1)}, u32[]{:S(2)}) copy-start(bf16[2,8,2,8,4,8,128]{6,5,4,3,2,1,0:T(8,128)(2,1)} %copy-done) | copy-start | bytes 6291460
  32.8 7.9 %copy-start.30 = (bf16[1,16,32,128]{3,2,1,0:T(8,128)(2,1)}, bf16[1,16,32,128]{3,2,1,0:T(8,128)(2,1)S(1)}, u32[]{:S(2)}) copy-start(bf16[1,16,32,128]{3,2,1,0:T(8,128)(2,1)S(1)} %collective-permute-done.4) | copy-start | bytes 393220
  32.8 7.9 %copy-start.32 = (bf16[1,16,32,128]{3,2,1,0:T(8,128)(2,1)}, bf16[1,16,32,128]{3,2,1,0:T(8,128)(2,1)S(1)}, u32[]{:S(2)}) copy-start(bf16[1,16,32,128]{3,2,1,0:T(8,128)(2,1)S(1)} %collective-permute-done.5) | copy-start | bytes 393220
  33.6 23.0 %collective-permute-start.6 = (bf16[18,1,32,128]{3,2,1,0:T(8,128)(2,1)}, bf16[18,1,32,128]{3,2,1,0:T(8,128)(2,1)}, u32[]{:S(2)}, u32[]{:S(2)}) collective-permute-start(bf16[18,1,32,128]{3,2,1,0:T(8,128)(2,1)} %get-tuple-element.49), channel_id=1, source_target_pairs={{0,1},{1,2},{2,3},{3,4},{4,5},{5,6},{6,7},{7,8},{8,9},{9,10},{10,1... | collective-permute-start | bytes 442376 | tf_op jit(solution)/shard_map/ppermute | solution.py:20
  39.4 17.2 %collective-permute-start.7 = (bf16[18,1,32,128]{3,2,1,0:T(8,128)(2,1)}, bf16[18,1,32,128]{3,2,1,0:T(8,128)(2,1)}, u32[]{:S(2)}, u32[]{:S(2)}) collective-permute-start(bf16[18,1,32,128]{3,2,1,0:T(8,128)(2,1)} %get-tuple-element.50), channel_id=1, source_target_pairs={{1,0},{2,1},{3,2},{4,3},{5,4},{6,5},{7,6},{8,7},{9,8},{10,9},{11,1... | collective-permute-start | bytes 442376 | tf_op jit(solution)/shard_map/ppermute | solution.py:21
  55.2 1.4 copy-start.31
  55.2 1.4 copy-start.33
  61.8 8.1 %copy-start.2 = (bf16[27,128,128]{2,1,0:T(8,128)(2,1)S(1)}, bf16[27,128,128]{2,1,0:T(8,128)(2,1)}, u32[]{:S(2)}) copy-start(bf16[27,128,128]{2,1,0:T(8,128)(2,1)} %param.10) | copy-start | bytes 2654212
  61.9 8.5 %copy-start.28 = (bf16[2,8,8,8,128]{4,3,2,1,0:T(8,128)(2,1)S(1)}, bf16[2,8,8,8,128]{4,3,2,1,0:T(8,128)(2,1)}, u32[]{:S(2)}) copy-start(bf16[2,8,8,8,128]{4,3,2,1,0:T(8,128)(2,1)} %get-tuple-element.113) | copy-start | bytes 786436
  69.8 1.0 copy-start.27
  70.3 1.8 copy-start.26
  70.8 2.6 %copy-start.25 = (bf16[2,8,8,8,128]{4,3,2,1,0:T(8,128)(2,1)S(1)}, bf16[2,8,8,8,128]{4,3,2,1,0:T(8,128)(2,1)}, u32[]{:S(2)}) copy-start(bf16[2,8,8,8,128]{4,3,2,1,0:T(8,128)(2,1)} %get-tuple-element.110) | copy-start | bytes 786436
  72.1 2.6 %copy-start.24 = (bf16[2,8,8,8,128]{4,3,2,1,0:T(8,128)(2,1)S(1)}, bf16[2,8,8,8,128]{4,3,2,1,0:T(8,128)(2,1)}, u32[]{:S(2)}) copy-start(bf16[2,8,8,8,128]{4,3,2,1,0:T(8,128)(2,1)} %get-tuple-element.109) | copy-start | bytes 786436
  73.5 2.6 %copy-start.23 = (bf16[2,8,8,8,128]{4,3,2,1,0:T(8,128)(2,1)S(1)}, bf16[2,8,8,8,128]{4,3,2,1,0:T(8,128)(2,1)}, u32[]{:S(2)}) copy-start(bf16[2,8,8,8,128]{4,3,2,1,0:T(8,128)(2,1)} %get-tuple-element.108) | copy-start | bytes 786436
  74.8 2.6 %copy-start.22 = (bf16[2,8,8,8,128]{4,3,2,1,0:T(8,128)(2,1)S(1)}, bf16[2,8,8,8,128]{4,3,2,1,0:T(8,128)(2,1)}, u32[]{:S(2)}) copy-start(bf16[2,8,8,8,128]{4,3,2,1,0:T(8,128)(2,1)} %get-tuple-element.107) | copy-start | bytes 786436
  78.6 1.0 copy-start.21
  79.1 1.0 copy-start.20
  79.8 1.5 copy-start.19
  80.3 2.3 %copy-start.18 = (bf16[2,8,8,8,128]{4,3,2,1,0:T(8,128)(2,1)S(1)}, bf16[2,8,8,8,128]{4,3,2,1,0:T(8,128)(2,1)}, u32[]{:S(2)}) copy-start(bf16[2,8,8,8,128]{4,3,2,1,0:T(8,128)(2,1)} %get-tuple-element.103) | copy-start | bytes 786436
  81.7 2.3 %copy-start.17 = (bf16[2,8,8,8,128]{4,3,2,1,0:T(8,128)(2,1)S(1)}, bf16[2,8,8,8,128]{4,3,2,1,0:T(8,128)(2,1)}, u32[]{:S(2)}) copy-start(bf16[2,8,8,8,128]{4,3,2,1,0:T(8,128)(2,1)} %get-tuple-element.102) | copy-start | bytes 786436
  83.0 2.3 %copy-start.16 = (bf16[2,8,8,8,128]{4,3,2,1,0:T(8,128)(2,1)S(1)}, bf16[2,8,8,8,128]{4,3,2,1,0:T(8,128)(2,1)}, u32[]{:S(2)}) copy-start(bf16[2,8,8,8,128]{4,3,2,1,0:T(8,128)(2,1)} %get-tuple-element.101) | copy-start | bytes 786436
  84.3 2.3 %copy-start.15 = (bf16[2,8,8,8,128]{4,3,2,1,0:T(8,128)(2,1)S(1)}, bf16[2,8,8,8,128]{4,3,2,1,0:T(8,128)(2,1)}, u32[]{:S(2)}) copy-start(bf16[2,8,8,8,128]{4,3,2,1,0:T(8,128)(2,1)} %get-tuple-element.100) | copy-start | bytes 786436
  85.6 2.3 %copy-start.14 = (bf16[2,8,8,8,128]{4,3,2,1,0:T(8,128)(2,1)S(1)}, bf16[2,8,8,8,128]{4,3,2,1,0:T(8,128)(2,1)}, u32[]{:S(2)}) copy-start(bf16[2,8,8,8,128]{4,3,2,1,0:T(8,128)(2,1)} %get-tuple-element.99) | copy-start | bytes 786436
  86.9 2.3 %copy-start.13 = (bf16[2,8,8,8,128]{4,3,2,1,0:T(8,128)(2,1)S(1)}, bf16[2,8,8,8,128]{4,3,2,1,0:T(8,128)(2,1)}, u32[]{:S(2)}) copy-start(bf16[2,8,8,8,128]{4,3,2,1,0:T(8,128)(2,1)} %get-tuple-element.98) | copy-start | bytes 786436
  88.2 2.3 %copy-start.12 = (bf16[2,8,8,8,128]{4,3,2,1,0:T(8,128)(2,1)S(1)}, bf16[2,8,8,8,128]{4,3,2,1,0:T(8,128)(2,1)}, u32[]{:S(2)}) copy-start(bf16[2,8,8,8,128]{4,3,2,1,0:T(8,128)(2,1)} %get-tuple-element.97) | copy-start | bytes 786436
  89.5 2.3 %copy-start.11 = (bf16[2,8,8,8,128]{4,3,2,1,0:T(8,128)(2,1)S(1)}, bf16[2,8,8,8,128]{4,3,2,1,0:T(8,128)(2,1)}, u32[]{:S(2)}) copy-start(bf16[2,8,8,8,128]{4,3,2,1,0:T(8,128)(2,1)} %get-tuple-element.96) | copy-start | bytes 786436
  90.8 2.3 %copy-start.10 = (bf16[2,8,8,8,128]{4,3,2,1,0:T(8,128)(2,1)S(1)}, bf16[2,8,8,8,128]{4,3,2,1,0:T(8,128)(2,1)}, u32[]{:S(2)}) copy-start(bf16[2,8,8,8,128]{4,3,2,1,0:T(8,128)(2,1)} %get-tuple-element.95) | copy-start | bytes 786436
  92.2 2.3 %copy-start.9 = (bf16[2,8,8,8,128]{4,3,2,1,0:T(8,128)(2,1)S(1)}, bf16[2,8,8,8,128]{4,3,2,1,0:T(8,128)(2,1)}, u32[]{:S(2)}) copy-start(bf16[2,8,8,8,128]{4,3,2,1,0:T(8,128)(2,1)} %get-tuple-element.94) | copy-start | bytes 786436
  93.5 2.3 %copy-start.8 = (bf16[2,8,8,8,128]{4,3,2,1,0:T(8,128)(2,1)S(1)}, bf16[2,8,8,8,128]{4,3,2,1,0:T(8,128)(2,1)}, u32[]{:S(2)}) copy-start(bf16[2,8,8,8,128]{4,3,2,1,0:T(8,128)(2,1)} %get-tuple-element.93) | copy-start | bytes 786436
  94.8 2.3 %copy-start.7 = (bf16[2,8,8,8,128]{4,3,2,1,0:T(8,128)(2,1)S(1)}, bf16[2,8,8,8,128]{4,3,2,1,0:T(8,128)(2,1)}, u32[]{:S(2)}) copy-start(bf16[2,8,8,8,128]{4,3,2,1,0:T(8,128)(2,1)} %get-tuple-element.92) | copy-start | bytes 786436
  96.1 2.3 %copy-start.6 = (bf16[2,8,8,8,128]{4,3,2,1,0:T(8,128)(2,1)S(1)}, bf16[2,8,8,8,128]{4,3,2,1,0:T(8,128)(2,1)}, u32[]{:S(2)}) copy-start(bf16[2,8,8,8,128]{4,3,2,1,0:T(8,128)(2,1)} %get-tuple-element.91) | copy-start | bytes 786436
  97.4 2.3 %copy-start.5 = (bf16[2,8,8,8,128]{4,3,2,1,0:T(8,128)(2,1)S(1)}, bf16[2,8,8,8,128]{4,3,2,1,0:T(8,128)(2,1)}, u32[]{:S(2)}) copy-start(bf16[2,8,8,8,128]{4,3,2,1,0:T(8,128)(2,1)} %get-tuple-element.90) | copy-start | bytes 786436
  98.7 2.3 %copy-start.4 = (bf16[2,8,8,8,128]{4,3,2,1,0:T(8,128)(2,1)S(1)}, bf16[2,8,8,8,128]{4,3,2,1,0:T(8,128)(2,1)}, u32[]{:S(2)}) copy-start(bf16[2,8,8,8,128]{4,3,2,1,0:T(8,128)(2,1)} %get-tuple-element.89) | copy-start | bytes 786436
  100.0 2.3 %copy-start.3 = (bf16[2,8,8,8,128]{4,3,2,1,0:T(8,128)(2,1)S(1)}, bf16[2,8,8,8,128]{4,3,2,1,0:T(8,128)(2,1)}, u32[]{:S(2)}) copy-start(bf16[2,8,8,8,128]{4,3,2,1,0:T(8,128)(2,1)} %get-tuple-element.88) | copy-start | bytes 786436
  102.7 2.8 %collective-permute-start.8 = (f32[1792,128]{1,0:T(8,128)S(1)}, f32[1792,128]{1,0:T(8,128)S(1)}, u32[]{:S(2)}, u32[]{:S(2)}) collective-permute-start(f32[1792,128]{1,0:T(8,128)S(1)} %pad_dynamic-slice_fusion), channel_id=1, source_target_pairs={{0,16},{16,0},{32,48},{48,32},{64,80},{80,64},{96,112},{112,96},{1... | collective-permute-start | bytes 2752520 | tf_op jit(solution)/shard_map/ppermute | solution.py:42
  105.6 12.8 %collective-permute-start.9 = (f32[896,128]{1,0:T(8,128)S(1)}, f32[896,128]{1,0:T(8,128)S(1)}, u32[]{:S(2)}, u32[]{:S(2)}) collective-permute-start(f32[896,128]{1,0:T(8,128)S(1)} %constant_dynamic-slice_fusion.8), channel_id=1, source_target_pairs={{0,1},{1,0},{2,3},{3,2},{4,5},{5,4},{6,7},{7,6},{8,9},{9,8},{10,11... | collective-permute-start | bytes 1376264 | tf_op jit(solution)/shard_map/ppermute | solution.py:42
  118.6 6.2 %collective-permute-start.10 = (f32[448,128]{1,0:T(8,128)S(1)}, f32[448,128]{1,0:T(8,128)S(1)}, u32[]{:S(2)}, u32[]{:S(2)}) collective-permute-start(f32[448,128]{1,0:T(8,128)S(1)} %constant_dynamic-slice_fusion.7), channel_id=1, source_target_pairs={{0,64},{16,80},{32,96},{48,112},{64,0},{80,16},{96,32},{112,48},{1... | collective-permute-start | bytes 688136 | tf_op jit(solution)/shard_map/ppermute | solution.py:42
  124.8 4.7 %collective-permute-start.11 = (f32[224,128]{1,0:T(8,128)S(1)}, f32[224,128]{1,0:T(8,128)S(1)}, u32[]{:S(2)}, u32[]{:S(2)}) collective-permute-start(f32[224,128]{1,0:T(8,128)S(1)} %constant_dynamic-slice_fusion.6), channel_id=1, source_target_pairs={{0,2},{1,3},{2,0},{3,1},{4,6},{5,7},{6,4},{7,5},{8,10},{9,11},{10,... | collective-permute-start | bytes 344072 | tf_op jit(solution)/shard_map/ppermute | solution.py:42
  129.6 4.7 %collective-permute-start.12 = (f32[112,128]{1,0:T(8,128)S(1)}, f32[112,128]{1,0:T(8,128)S(1)}, u32[]{:S(2)}, u32[]{:S(2)}) collective-permute-start(f32[112,128]{1,0:T(8,128)S(1)} %constant_dynamic-slice_fusion.5), channel_id=1, source_target_pairs={{0,32},{16,48},{32,0},{48,16},{64,96},{80,112},{96,64},{112,80},{1... | collective-permute-start | bytes 172040 | tf_op jit(solution)/shard_map/ppermute | solution.py:42
  134.3 5.0 %collective-permute-start.13 = (f32[56,128]{1,0:T(8,128)S(1)}, f32[56,128]{1,0:T(8,128)S(1)}, u32[]{:S(2)}, u32[]{:S(2)}) collective-permute-start(f32[56,128]{1,0:T(8,128)S(1)} %constant_dynamic-slice_fusion.4), channel_id=1, source_target_pairs={{0,128},{16,144},{32,160},{48,176},{64,192},{80,208},{96,224},{112... | collective-permute-start | bytes 86024 | tf_op jit(solution)/shard_map/ppermute | solution.py:42
  139.3 6.2 %collective-permute-start.14 = (f32[28,128]{1,0:T(8,128)S(1)}, f32[28,128]{1,0:T(8,128)S(1)}, u32[]{:S(2)}, u32[]{:S(2)}) collective-permute-start(f32[28,128]{1,0:T(8,128)S(1)} %constant_dynamic-slice_fusion.3), channel_id=1, source_target_pairs={{0,4},{1,5},{2,6},{3,7},{4,0},{5,1},{6,2},{7,3},{8,12},{9,13},{10,... | collective-permute-start | bytes 43016 | tf_op jit(solution)/shard_map/ppermute | solution.py:42
  145.5 7.6 %collective-permute-start.15 = (f32[14,128]{1,0:T(8,128)S(1)}, f32[14,128]{1,0:T(8,128)S(1)}, u32[]{:S(2)}, u32[]{:S(2)}) collective-permute-start(f32[14,128]{1,0:T(8,128)S(1)} %constant_dynamic-slice_fusion.2), channel_id=1, source_target_pairs={{0,8},{1,9},{2,10},{3,11},{4,12},{5,13},{6,14},{7,15},{8,0},{9,1},... | collective-permute-start | bytes 21512 | tf_op jit(solution)/shard_map/ppermute | solution.py:42
  153.1 6.7 %collective-permute-start.16 = (f32[14,128]{1,0:T(8,128)S(1)}, f32[14,128]{1,0:T(8,128)S(1)}, u32[]{:S(2)}, u32[]{:S(2)}) collective-permute-start(f32[14,128]{1,0:T(8,128)S(1)} %dynamic-slice_add_fusion.6), channel_id=1, source_target_pairs={{0,8},{1,9},{2,10},{3,11},{4,12},{5,13},{6,14},{7,15},{8,0},{9,1},... | collective-permute-start | bytes 21512 | tf_op jit(solution)/shard_map/ppermute | solution.py:46
  159.9 3.6 %collective-permute-start.17 = (f32[28,128]{1,0:T(8,128)S(1)}, f32[28,128]{1,0:T(8,128)S(1)}, u32[]{:S(2)}, u32[]{:S(2)}) collective-permute-start(f32[28,128]{1,0:T(8,128)S(1)} %pad_maximum_fusion.13), channel_id=1, source_target_pairs={{0,4},{1,5},{2,6},{3,7},{4,0},{5,1},{6,2},{7,3},{8,12},{9,13},{10,... | collective-permute-start | bytes 43016 | tf_op jit(solution)/shard_map/ppermute | solution.py:46
  163.5 4.3 %collective-permute-start.18 = (f32[56,128]{1,0:T(8,128)S(1)}, f32[56,128]{1,0:T(8,128)S(1)}, u32[]{:S(2)}, u32[]{:S(2)}) collective-permute-start(f32[56,128]{1,0:T(8,128)S(1)} %pad_maximum_fusion.12), channel_id=1, source_target_pairs={{0,128},{16,144},{32,160},{48,176},{64,192},{80,208},{96,224},{112... | collective-permute-start | bytes 86024 | tf_op jit(solution)/shard_map/ppermute | solution.py:46
  167.8 4.6 %collective-permute-start.19 = (f32[112,128]{1,0:T(8,128)S(1)}, f32[112,128]{1,0:T(8,128)S(1)}, u32[]{:S(2)}, u32[]{:S(2)}) collective-permute-start(f32[112,128]{1,0:T(8,128)S(1)} %pad_maximum_fusion.11), channel_id=1, source_target_pairs={{0,32},{16,48},{32,0},{48,16},{64,96},{80,112},{96,64},{112,80},{1... | collective-permute-start | bytes 172040 | tf_op jit(solution)/shard_map/ppermute | solution.py:46
  172.5 3.7 %collective-permute-start.20 = (f32[224,128]{1,0:T(8,128)S(1)}, f32[224,128]{1,0:T(8,128)S(1)}, u32[]{:S(2)}, u32[]{:S(2)}) collective-permute-start(f32[224,128]{1,0:T(8,128)S(1)} %pad_maximum_fusion.10), channel_id=1, source_target_pairs={{0,2},{1,3},{2,0},{3,1},{4,6},{5,7},{6,4},{7,5},{8,10},{9,11},{10,... | collective-permute-start | bytes 344072 | tf_op jit(solution)/shard_map/ppermute | solution.py:46
  176.3 5.0 %collective-permute-start.21 = (f32[448,128]{1,0:T(8,128)S(1)}, f32[448,128]{1,0:T(8,128)S(1)}, u32[]{:S(2)}, u32[]{:S(2)}) collective-permute-start(f32[448,128]{1,0:T(8,128)S(1)} %pad_maximum_fusion.3), channel_id=1, source_target_pairs={{0,64},{16,80},{32,96},{48,112},{64,0},{80,16},{96,32},{112,48},{1... | collective-permute-start | bytes 688136 | tf_op jit(solution)/shard_map/ppermute | solution.py:46
  181.3 7.4 %collective-permute-start.22 = (f32[896,128]{1,0:T(8,128)S(1)}, f32[896,128]{1,0:T(8,128)S(1)}, u32[]{:S(2)}, u32[]{:S(2)}) collective-permute-start(f32[896,128]{1,0:T(8,128)S(1)} %pad_maximum_fusion.2), channel_id=1, source_target_pairs={{0,1},{1,0},{2,3},{3,2},{4,5},{5,4},{6,7},{7,6},{8,9},{9,8},{10,11... | collective-permute-start | bytes 1376264 | tf_op jit(solution)/shard_map/ppermute | solution.py:46
  188.9 17.4 %collective-permute-start.23 = (f32[1792,128]{1,0:T(8,128)S(1)}, f32[1792,128]{1,0:T(8,128)S(1)}, u32[]{:S(2)}, u32[]{:S(2)}) collective-permute-start(f32[1792,128]{1,0:T(8,128)S(1)} %pad_maximum_fusion.1), channel_id=1, source_target_pairs={{0,16},{16,0},{32,48},{48,32},{64,80},{80,64},{96,112},{112,96},{1... | collective-permute-start | bytes 2752520 | tf_op jit(solution)/shard_map/ppermute | solution.py:46

commit v2 on v1

--- a/solution.py
+++ b/solution.py
@@ -63,35 +63,21 @@
 def cut_windows(padded, places):
     padded = jnp.pad(padded, ((0, 0), (0, 0), (1, 1), (0, 0)))
     chans = padded.shape[-1]
-    along_x = places // (TBY * ZL)
-    along_y = places // ZL % TBY
-    along_z = places % ZL
-    zero_index = jnp.zeros_like(along_x)
-
-    def one_window(start_x, start_y, start_z, start_c):
-        return lax.dynamic_slice(
-            padded, (start_x, start_y, start_z, start_c), (BRICK + 2, BRICK + 2, BRICK + 2, chans)
-        )
-
-    return jax.vmap(one_window)(along_x * BRICK, along_y * BRICK, along_z * BRICK, zero_index)
+    windows = []
+    for slot in range(places.shape[0]):
+        place = places[slot]
+        starts = (place // (TBY * ZL) * BRICK, place // ZL % TBY * BRICK, place % ZL * BRICK, 0)
+        windows.append(lax.dynamic_slice(padded, starts, (BRICK + 2, BRICK + 2, BRICK + 2, chans)))
+    return jnp.stack(windows)
 
 
-def offset_rows(windows, offset):
-    first = offset // 9
-    second = offset // 3 % 3
-    third = offset % 3
-    piece = windows[:, first : first + BRICK, second : second + BRICK, third : third + BRICK, :]
-    return piece.reshape(-1, windows.shape[-1])
-
-
-def forward_pass(feat_padded, places, weight, keeper_rows):
-    feat_windows = cut_windows(feat_padded, places)
-    output_sum = jnp.zeros((keeper_rows.shape[0], weight.shape[-1]), jnp.float32)
+def stack_offsets(windows):
+    pieces = []
     for offset in range(OFFS):
-        output_sum = output_sum + jnp.dot(
-            offset_rows(feat_windows, offset), weight[offset], preferred_element_type=jnp.float32
-        )
-    return ((output_sum * keeper_rows).astype(jnp.bfloat16), feat_windows)
+        first, second, third = offset // 9, offset // 3 % 3, offset % 3
+        piece = windows[:, first : first + BRICK, second : second + BRICK, third : third + BRICK, :]
+        pieces.append(piece.reshape(-1, windows.shape[-1]))
+    return jnp.stack(pieces)
 
 
 def local(features, occupancy, brick_pos, brick_count, weight, cotangent):
@@ -103,35 +89,21 @@
     keeper_rows = keeper.reshape(-1, 1).astype(jnp.float32)
     feat_masked = features[0, 0] * keeper[:, :, None]
     grad_masked = cotangent[0, 0] * keeper[:, :, None]
+    grad_rows = grad_masked.reshape(-1, chans)
     feat_dense = place_bricks(feat_masked, places, alive)
-    grad_dense = place_bricks(grad_masked, places, alive)
     feat_padded = with_halo(feat_dense, (("gx", 0), ("gy", 1)), 1)
-    output_rows, feat_windows = forward_pass(feat_padded, places, weight, keeper_rows)
-    grad_padded = with_halo(grad_dense, (("gx", 0), ("gy", 1)), 1)
-    grad_windows = cut_windows(grad_padded, places)
-    grad_rows = grad_masked.reshape(-1, chans)
-    input_sum = jnp.zeros((grad_rows.shape[0], chans), jnp.float32)
-    blocks = []
-    for offset in range(OFFS):
-        input_sum = input_sum + lax.dot_general(
-            offset_rows(grad_windows, offset),
-            weight[OFFS - 1 - offset],
-            (((1,), (1,)), ((), ())),
-            preferred_element_type=jnp.float32,
-        )
-        blocks.append(
-            lax.dot_general(
-                offset_rows(feat_windows, offset),
-                grad_rows,
-                (((0,), (0,)), ((), ())),
-                preferred_element_type=jnp.float32,
-            )
-        )
-    weight_local = jnp.stack(blocks)
-    input_rows = (input_sum * keeper_rows).astype(jnp.bfloat16)
+    feat_stack = stack_offsets(cut_windows(feat_padded, places))
+    weight_local = jnp.einsum("dvc,ve->dce", feat_stack, grad_rows, preferred_element_type=jnp.float32)
     tiles = lax.axis_size("gx") * lax.axis_size("gy")
     weight_total = butterfly_sum(weight_local)
     weight_grad = weight_total / jnp.float32(tiles)
+    output_sum = jnp.einsum("dvc,dce->ve", feat_stack, weight, preferred_element_type=jnp.float32)
+    output_rows = (output_sum * keeper_rows).astype(jnp.bfloat16)
+    grad_dense = place_bricks(grad_masked, places, alive)
+    grad_padded = with_halo(grad_dense, (("gx", 0), ("gy", 1)), 1)
+    grad_stack = stack_offsets(cut_windows(grad_padded, places))
+    input_sum = jnp.einsum("dvc,dec->ve", grad_stack, weight[::-1], preferred_element_type=jnp.float32)
+    input_rows = (input_sum * keeper_rows).astype(jnp.bfloat16)
     output = output_rows.reshape(1, 1, slots, -1, chans)
     input_grad = input_rows.reshape(1, 1, slots, -1, chans)
     return (output, input_grad, weight_grad)

time: 209 us -> 198 us (0.947)
  matrix products: 41.1 us -> 15.9 us
  local copies, waits for them, and re-layouts: 23.9 us -> 34.5 us
  between operations: 2.86 us -> 7.56 us
    dot_general x81 -> x3, matrix products: 38.7 us -> 13.5 us  [the longest x1 5.7 us: local(): jnp.einsum('dvc,dce->ve', feat_stack, weight, preferred_element_type=jnp....]
    unnamed x77 -> x68, local copies, waits for them, and re-layouts: 0.71 us -> 19.7 us
    gather x12 -> x0, local copies, waits for them, and re-layouts: 15.1 us -> none
    dot_general x0 -> x1, local copies, waits for them, and re-layouts: none -> 10 us  [local(): jnp.einsum('dvc,ve->dce', feat_stack, grad_rows, preferred_element_type=j...]
    ppermute x4, waiting for transfers between devices: 5.58 us -> 0.01 us  [with_halo(): after = lax.ppermute(leading, axis, down)]
    slice x4 -> x1, local copies, waits for them, and re-layouts: 5.53 us -> 0.66 us  [cut_windows(): place = places[slot]]
    ppermute x8, waiting for transfers between devices: 20.6 us -> 25.2 us  [butterfly_sum(): buf = keep + lax.ppermute(send, axis, pairs)]
    ppermute x4, starting transfers between devices: 6.41 us -> 9.59 us  [with_halo(): after = lax.ppermute(leading, axis, down)]
  transfers between devices with their start and end apart: 24 -> 24, of which waited for: 15 -> 15; matrix products, arithmetic and copies ran while one was open for 13% -> 11% of each run, Pallas kernels for 0% -> 0%
where the time goes in v2:
time: 198 us; the launch traced here: 197 us
  starting transfers between devices  78.7 us (40%)
  waiting for transfers between devices  44.7 us (23%)
  local copies, waits for them, and re-layouts  34.5 us (17%)
  matrix products  15.9 us (8%)
  other arithmetic  15.2 us (8%)
  between operations  7.56 us (4%)
    ppermute x8, starting transfers between devices, butterfly_sum(): got = lax.ppermute(buf, axis, pairs)  29.7 us
    ppermute x8, waiting for transfers between devices, butterfly_sum(): buf = keep + lax.ppermute(send, axis, pairs)  25.2 us
    ppermute x8, starting transfers between devices, butterfly_sum(): buf = keep + lax.ppermute(send, axis, pairs)  22.6 us
    unnamed x68, local copies, waits for them, and re-layouts  19.7 us
    ppermute x8, waiting for transfers between devices, butterfly_sum(): got = lax.ppermute(buf, axis, pairs)  19.6 us
    ppermute x4, starting transfers between devices, with_halo(): before = lax.ppermute(last, axis, up)  16.8 us
    dot_general x1, local copies, waits for them, and re-layouts, local(): jnp.einsum('dvc,ve->dce', feat_stack, grad_rows, preferred_element_type=j...  10 us
    ppermute x4, starting transfers between devices, with_halo(): after = lax.ppermute(leading, axis, down)  9.59 us
  transfers between devices with their start and end apart: 24, of which 15 were waited for; matrix products, arithmetic and copies ran while one was open for 11% of the time, Pallas kernels for 0%

profile of v2, /device:TPU:1, one launch (start us, length us, event | category | flops | bytes accessed | tf_op | source)
XLA Modules:
  0.0 196.6 jit_solution(10686984544054928453)
XLA Ops:
  1.4 0.8 broadcast_bitcast_fusion
  2.2 1.2 bitcast_multiply_fusion
  3.4 1.6 convolution_convert_fusion.1
  5.0 0.8 copy.12
  5.9 5.1 %collective-permute-start.1 = (bf16[1,16,32,128]{3,2,1,0:T(8,128)(2,1)S(1)}, bf16[1,16,32,128]{3,2,1,0:T(8,128)(2,1)S(1)}, u32[]{:S(2)}, u32[]{:S(2)}) collective-permute-start(bf16[1,16,32,128]{3,2,1,0:T(8,128)(2,1)S(1)} %get-tuple-element.14), channel_id=1, source_target_pairs={{16,0},{32,16},{48,32},{64,48},{80,64},{96,80},{112,96},{128,112},... | collective-permute-start | bytes 393224 | tf_op jit(solution)/shard_map/ppermute | solution.py:21
  11.0 2.8 %collective-permute-start = (bf16[1,16,32,128]{3,2,1,0:T(8,128)(2,1)S(1)}, bf16[1,16,32,128]{3,2,1,0:T(8,128)(2,1)S(1)}, u32[]{:S(2)}, u32[]{:S(2)}) collective-permute-start(bf16[1,16,32,128]{3,2,1,0:T(8,128)(2,1)S(1)} %get-tuple-element.13), channel_id=1, source_target_pairs={{0,16},{16,32},{32,48},{48,64},{64,80},{80,96},{96,112},{112,128},... | collective-permute-start | bytes 393224 | tf_op jit(solution)/shard_map/ppermute | solution.py:20
  13.8 0.9 convolution_convert_fusion
  14.7 0.8 copy.14
  15.5 0.7 fusion.75
  16.3 1.9 collective-permute-start.5
  18.2 5.1 %collective-permute-start.4 = (bf16[1,16,32,128]{3,2,1,0:T(8,128)(2,1)}, bf16[1,16,32,128]{3,2,1,0:T(8,128)(2,1)S(1)}, u32[]{:S(2)}, u32[]{:S(2)}) collective-permute-start(bf16[1,16,32,128]{3,2,1,0:T(8,128)(2,1)} %get-tuple-element.11), channel_id=1, source_target_pairs={{0,16},{16,32},{32,48},{48,64},{64,80},{80,96},{96,112},{112,128},... | collective-permute-start | bytes 393224 | tf_op jit(solution)/shard_map/ppermute | solution.py:20
  23.6 0.8 pad_maximum_fusion.11
  24.4 1.3 collective-permute-start.3
  25.7 4.7 %collective-permute-start.2 = (bf16[18,1,32,128]{3,2,1,0:T(8,128)(2,1)}, bf16[18,1,32,128]{3,2,1,0:T(8,128)(2,1)}, u32[]{:S(2)}, u32[]{:S(2)}) collective-permute-start(bf16[18,1,32,128]{3,2,1,0:T(8,128)(2,1)} %get-tuple-element.9), channel_id=1, source_target_pairs={{0,1},{1,2},{2,3},{3,4},{4,5},{5,6},{6,7},{7,8},{8,9},{9,10},{10,1... | collective-permute-start | bytes 442376 | tf_op jit(solution)/shard_map/ppermute | solution.py:20
  36.6 1.3 collective-permute-start.7
  37.9 4.2 %collective-permute-start.6 = (bf16[18,1,32,128]{3,2,1,0:T(8,128)(2,1)S(1)}, bf16[18,1,32,128]{3,2,1,0:T(8,128)(2,1)S(1)}, u32[]{:S(2)}, u32[]{:S(2)}) collective-permute-start(bf16[18,1,32,128]{3,2,1,0:T(8,128)(2,1)S(1)} %get-tuple-element.7), channel_id=1, source_target_pairs={{0,1},{1,2},{2,3},{3,4},{4,5},{5,6},{6,7},{7,8},{8,9},{9,10},{10,1... | collective-permute-start | bytes 442376 | tf_op jit(solution)/shard_map/ppermute | solution.py:20
  42.1 4.6 %select_maximum_fusion.4 = bf16[18,18,34,128]{3,2,1,0:T(8,128)(2,1)S(1)} fusion(bf16[18,1,32,128]{3,2,1,0:T(8,128)(2,1)} %collective-permute-done.3, bf16[18,1,32,128]{3,2,1,0:T(8,128)(2,1)} %collective-permute-done.2, bf16[1,16,32,128]{3,2,1,0:T(8,128)(2,1)} %copy-done.3, bf16[16,16,32,128]{3,2,1,0:T(8,128)(2,1)} %bitcast.123, ...), kind=kLoop, calls=%fused_computation.111 | loop fusion | flops 25380864 | bytes 5474304 | tf_op jit(solution)/shard_map/concatenate | solution.py:22
  49.2 3.0 %select_maximum_fusion = bf16[18,18,34,128]{3,2,1,0:T(8,128)(2,1)S(1)} fusion(bf16[18,1,32,128]{3,2,1,0:T(8,128)(2,1)S(1)} %collective-permute-done.7, bf16[18,1,32,128]{3,2,1,0:T(8,128)(2,1)S(1)} %collective-permute-done.6, bf16[1,16,32,128]{3,2,1,0:T(8,128)(2,1)S(1)} %collective-permute-done.5, bf16[16,16,32,128]{3,2,1,0:T(8,128)(2,1)S(1)} %bitcast.120, ...), kind=kLoop, calls=%fused_computation.107 | loop fusion | flops 25380864 | bytes 5474304 | tf_op jit(solution)/shard_map/concatenate | solution.py:22
  52.6 0.7 constant_dynamic-update-slice_fusion.25
  54.7 0.7 constant_dynamic-update-slice_fusion.22
  56.2 0.7 constant_dynamic-update-slice_fusion.20
  57.6 0.7 constant_dynamic-update-slice_fusion.18
  61.2 0.7 constant_dynamic-update-slice_fusion.13
  61.9 0.7 constant_dynamic-update-slice_fusion.12
  62.7 0.7 constant_dynamic-update-slice_fusion.11
  63.4 0.7 constant_dynamic-update-slice_fusion.10
  64.1 0.7 constant_dynamic-update-slice_fusion.9
  64.9 0.7 constant_dynamic-update-slice_fusion.8
  67.7 0.7 constant_dynamic-update-slice_fusion.4
  69.2 0.7 constant_dynamic-update-slice_fusion.2
  71.3 10.0 %copy.15 = bf16[27,128,1024]{2,1,0:T(8,128)(2,1)} copy(bf16[27,128,1024]{1,2,0:T(8,128)(2,1)} %bitcast.78) | data formatting | bytes 14155776 | tf_op jit(solution)/shard_map/dvc,ve->dce/dot_general | solution.py:96
  81.3 5.1 %fusion.78 = f32[3456,128]{1,0:T(8,128)S(1)} fusion(bf16[3456,1024]{1,0:T(8,128)(2,1)} %bitcast.117, bf16[1024,128]{1,0:T(8,128)(2,1)S(1)} %bitcast.127), kind=kOutput, calls=%fused_computation.308 | convolution fusion | flops 905969664 | bytes 9109504 | tf_op jit(solution)/shard_map/dvc,ve->dce/dot_general | solution.py:96
  87.4 1.6 collective-permute-done.8
  89.2 2.4 %collective-permute-start.9 = (f32[896,128]{1,0:T(8,128)S(1)}, f32[896,128]{1,0:T(8,128)S(1)}, u32[]{:S(2)}, u32[]{:S(2)}) collective-permute-start(f32[896,128]{1,0:T(8,128)S(1)} %constant_dynamic-slice_fusion.6), channel_id=1, source_target_pairs={{0,1},{1,0},{2,3},{3,2},{4,5},{5,4},{6,7},{7,6},{8,9},{9,8},{10,11... | collective-permute-start | bytes 1376264 | tf_op jit(solution)/shard_map/ppermute | solution.py:42
  92.1 10.2 %collective-permute-done.9 = f32[896,128]{1,0:T(8,128)S(1)} collective-permute-done((f32[896,128]{1,0:T(8,128)S(1)}, f32[896,128]{1,0:T(8,128)S(1)}, u32[]{:S(2)}, u32[]{:S(2)}) %collective-permute-start.9) | collective-permute-done | bytes 458784 | tf_op jit(solution)/shard_map/ppermute | solution.py:42
  102.4 1.4 collective-permute-start.10
  104.2 4.6 %collective-permute-done.10 = f32[448,128]{1,0:T(8,128)S(1)} collective-permute-done((f32[448,128]{1,0:T(8,128)S(1)}, f32[448,128]{1,0:T(8,128)S(1)}, u32[]{:S(2)}, u32[]{:S(2)}) %collective-permute-start.10) | collective-permute-done | bytes 229408 | tf_op jit(solution)/shard_map/ppermute | solution.py:42
  108.9 2.0 %collective-permute-start.11 = (f32[224,128]{1,0:T(8,128)S(1)}, f32[224,128]{1,0:T(8,128)S(1)}, u32[]{:S(2)}, u32[]{:S(2)}) collective-permute-start(f32[224,128]{1,0:T(8,128)S(1)} %constant_dynamic-slice_fusion.4), channel_id=1, source_target_pairs={{0,2},{1,3},{2,0},{3,1},{4,6},{5,7},{6,4},{7,5},{8,10},{9,11},{10,... | collective-permute-start | bytes 344072 | tf_op jit(solution)/shard_map/ppermute | solution.py:42
  110.9 2.1 %collective-permute-done.11 = f32[224,128]{1,0:T(8,128)S(1)} collective-permute-done((f32[224,128]{1,0:T(8,128)S(1)}, f32[224,128]{1,0:T(8,128)S(1)}, u32[]{:S(2)}, u32[]{:S(2)}) %collective-permute-start.11) | collective-permute-done | bytes 114720 | tf_op jit(solution)/shard_map/ppermute | solution.py:42
  113.1 4.4 %collective-permute-start.12 = (f32[112,128]{1,0:T(8,128)S(1)}, f32[112,128]{1,0:T(8,128)S(1)}, u32[]{:S(2)}, u32[]{:S(2)}) collective-permute-start(f32[112,128]{1,0:T(8,128)S(1)} %constant_dynamic-slice_fusion.3), channel_id=1, source_target_pairs={{0,32},{16,48},{32,0},{48,16},{64,96},{80,112},{96,64},{112,80},{1... | collective-permute-start | bytes 172040 | tf_op jit(solution)/shard_map/ppermute | solution.py:42
  117.5 1.5 collective-permute-done.12
  119.1 3.0 %collective-permute-start.13 = (f32[56,128]{1,0:T(8,128)S(1)}, f32[56,128]{1,0:T(8,128)S(1)}, u32[]{:S(2)}, u32[]{:S(2)}) collective-permute-start(f32[56,128]{1,0:T(8,128)S(1)} %constant_dynamic-slice_fusion.2), channel_id=1, source_target_pairs={{0,128},{16,144},{32,160},{48,176},{64,192},{80,208},{96,224},{112... | collective-permute-start | bytes 86024 | tf_op jit(solution)/shard_map/ppermute | solution.py:42
  122.2 1.3 collective-permute-done.13
  123.4 5.5 %collective-permute-start.14 = (f32[28,128]{1,0:T(8,128)S(1)}, f32[28,128]{1,0:T(8,128)S(1)}, u32[]{:S(2)}, u32[]{:S(2)}) collective-permute-start(f32[28,128]{1,0:T(8,128)S(1)} %constant_dynamic-slice_fusion.1), channel_id=1, source_target_pairs={{0,4},{1,5},{2,6},{3,7},{4,0},{5,1},{6,2},{7,3},{8,12},{9,13},{10,... | collective-permute-start | bytes 43016 | tf_op jit(solution)/shard_map/ppermute | solution.py:42
  129.0 1.1 collective-permute-done.14
  130.1 3.8 %collective-permute-start.15 = (f32[14,128]{1,0:T(8,128)S(1)}, f32[14,128]{1,0:T(8,128)S(1)}, u32[]{:S(2)}, u32[]{:S(2)}) collective-permute-start(f32[14,128]{1,0:T(8,128)S(1)} %constant_dynamic-slice_fusion), channel_id=1, source_target_pairs={{0,8},{1,9},{2,10},{3,11},{4,12},{5,13},{6,14},{7,15},{8,0},{9,1},... | collective-permute-start | bytes 21512 | tf_op jit(solution)/shard_map/ppermute | solution.py:42
  134.0 2.7 %collective-permute-done.15 = f32[14,128]{1,0:T(8,128)S(1)} collective-permute-done((f32[14,128]{1,0:T(8,128)S(1)}, f32[14,128]{1,0:T(8,128)S(1)}, u32[]{:S(2)}, u32[]{:S(2)}) %collective-permute-start.15) | collective-permute-done | bytes 7200 | tf_op jit(solution)/shard_map/ppermute | solution.py:42
  136.7 3.8 %collective-permute-start.16 = (f32[14,128]{1,0:T(8,128)S(1)}, f32[14,128]{1,0:T(8,128)S(1)}, u32[]{:S(2)}, u32[]{:S(2)}) collective-permute-start(f32[14,128]{1,0:T(8,128)S(1)} %dynamic-slice_add_fusion.6), channel_id=1, source_target_pairs={{0,8},{1,9},{2,10},{3,11},{4,12},{5,13},{6,14},{7,15},{8,0},{9,1},... | collective-permute-start | bytes 21512 | tf_op jit(solution)/shard_map/ppermute | solution.py:46
  140.5 2.6 %collective-permute-done.16 = f32[14,128]{1,0:T(8,128)S(1)} collective-permute-done((f32[14,128]{1,0:T(8,128)S(1)}, f32[14,128]{1,0:T(8,128)S(1)}, u32[]{:S(2)}, u32[]{:S(2)}) %collective-permute-start.16) | collective-permute-done | bytes 7200 | tf_op jit(solution)/shard_map/ppermute | solution.py:46
  143.2 2.7 %collective-permute-start.17 = (f32[28,128]{1,0:T(8,128)S(1)}, f32[28,128]{1,0:T(8,128)S(1)}, u32[]{:S(2)}, u32[]{:S(2)}) collective-permute-start(f32[28,128]{1,0:T(8,128)S(1)} %pad_maximum_fusion.15), channel_id=1, source_target_pairs={{0,4},{1,5},{2,6},{3,7},{4,0},{5,1},{6,2},{7,3},{8,12},{9,13},{10,... | collective-permute-start | bytes 43016 | tf_op jit(solution)/shard_map/ppermute | solution.py:46
  145.9 1.1 collective-permute-done.17
  147.0 3.0 %collective-permute-start.18 = (f32[56,128]{1,0:T(8,128)S(1)}, f32[56,128]{1,0:T(8,128)S(1)}, u32[]{:S(2)}, u32[]{:S(2)}) collective-permute-start(f32[56,128]{1,0:T(8,128)S(1)} %pad_maximum_fusion.14), channel_id=1, source_target_pairs={{0,128},{16,144},{32,160},{48,176},{64,192},{80,208},{96,224},{112... | collective-permute-start | bytes 86024 | tf_op jit(solution)/shard_map/ppermute | solution.py:46
  150.0 1.3 collective-permute-done.18
  151.4 3.1 %collective-permute-start.19 = (f32[112,128]{1,0:T(8,128)S(1)}, f32[112,128]{1,0:T(8,128)S(1)}, u32[]{:S(2)}, u32[]{:S(2)}) collective-permute-start(f32[112,128]{1,0:T(8,128)S(1)} %pad_maximum_fusion.13), channel_id=1, source_target_pairs={{0,32},{16,48},{32,0},{48,16},{64,96},{80,112},{96,64},{112,80},{1... | collective-permute-start | bytes 172040 | tf_op jit(solution)/shard_map/ppermute | solution.py:46
  154.4 1.5 collective-permute-done.19
  156.0 1.5 collective-permute-start.20
  157.6 2.4 %collective-permute-done.20 = f32[224,128]{1,0:T(8,128)S(1)} collective-permute-done((f32[224,128]{1,0:T(8,128)S(1)}, f32[224,128]{1,0:T(8,128)S(1)}, u32[]{:S(2)}, u32[]{:S(2)}) %collective-permute-start.20) | collective-permute-done | bytes 114720 | tf_op jit(solution)/shard_map/ppermute | solution.py:46
  160.1 1.1 collective-permute-start.21
  161.2 3.8 %collective-permute-done.21 = f32[448,128]{1,0:T(8,128)S(1)} collective-permute-done((f32[448,128]{1,0:T(8,128)S(1)}, f32[448,128]{1,0:T(8,128)S(1)}, u32[]{:S(2)}, u32[]{:S(2)}) %collective-permute-start.21) | collective-permute-done | bytes 229408 | tf_op jit(solution)/shard_map/ppermute | solution.py:46
  165.8 6.8 %collective-permute-done.22 = f32[896,128]{1,0:T(8,128)S(1)} collective-permute-done((f32[896,128]{1,0:T(8,128)S(1)}, f32[896,128]{1,0:T(8,128)S(1)}, u32[]{:S(2)}, u32[]{:S(2)}) %collective-permute-start.22) | collective-permute-done | bytes 458784 | tf_op jit(solution)/shard_map/ppermute | solution.py:46
  172.7 14.1 %collective-permute-start.23 = (f32[1792,128]{1,0:T(8,128)S(1)}, f32[1792,128]{1,0:T(8,128)S(1)}, u32[]{:S(2)}, u32[]{:S(2)}) collective-permute-start(f32[1792,128]{1,0:T(8,128)S(1)} %pad_maximum_fusion.1), channel_id=1, source_target_pairs={{0,16},{16,0},{32,48},{48,32},{64,80},{80,64},{96,112},{112,96},{1... | collective-permute-start | bytes 2752520 | tf_op jit(solution)/shard_map/ppermute | solution.py:46
  186.8 5.7 %fusion.9 = bf16[1024,128]{1,0:T(8,128)(2,1)} fusion(bf16[27,1024,128]{2,1,0:T(8,128)(2,1)} %constant_dynamic-update-slice_fusion, bf16[27,128,128]{2,1,0:T(8,128)(2,1)S(1)} %copy-done, f32[1024]{0:T(1024)S(1)} %fusion.67), kind=kOutput, calls=%fused_computation.128 | convolution fusion | flops 906231808 | bytes 8228864 | tf_op jit(solution)/shard_map/dvc,dce->ve/dot_general | solution.py:100
  192.5 2.7 %fusion.10 = bf16[1024,128]{1,0:T(8,128)(2,1)} fusion(bf16[27,1024,128]{2,1,0:T(8,128)(2,1)S(1)} %constant_dynamic-update-slice_fusion.27, bf16[27,128,128]{2,1,0:T(8,128)(2,1)S(1)} %copy-done, f32[1024]{0:T(1024)S(1)} %fusion.67), kind=kOutput, calls=%fused_computation.129 | convolution fusion | flops 906231808 | bytes 8228864 | tf_op jit(solution)/shard_map/dvc,dec->ve/dot_general | solution.py:105
  195.3 1.3 fusion.6
  (114 shorter events, 17.5 us)
Async XLA Ops:
  0.6 186.2 %copy-start = (bf16[27,128,128]{2,1,0:T(8,128)(2,1)S(1)}, bf16[27,128,128]{2,1,0:T(8,128)(2,1)}, u32[]{:S(2)}) copy-start(bf16[27,128,128]{2,1,0:T(8,128)(2,1)} %param.10) | copy-start | bytes 2654212
  0.6 13.2 %copy-start.6 = (s32[1,1,2]{2,1,0:T(1,128)S(1)}, s32[1,1,2]{2,1,0:T(1,128)}, u32[]{:S(2)}) copy-start(s32[1,1,2]{2,1,0:T(1,128)} %param.8) | copy-start | bytes 28
  3.4 19.9 %copy-start.2 = (bf16[1,1,2,512,128]{4,3,2,1,0:T(8,128)(2,1)S(1)}, bf16[1,1,2,512,128]{4,3,2,1,0:T(8,128)(2,1)}, u32[]{:S(2)}) copy-start(bf16[1,1,2,512,128]{4,3,2,1,0:T(8,128)(2,1)} %param.11) | copy-start | bytes 786436
  3.4 20.1 %copy-start.5 = (s32[1,1,2,512]{3,2,1,0:T(2,128)S(1)}, s32[1,1,2,512]{3,2,1,0:T(2,128)}, u32[]{:S(2)}) copy-start(s32[1,1,2,512]{3,2,1,0:T(2,128)} %param.7) | copy-start | bytes 12292
  5.8 17.8 %copy-start.1 = (bf16[2,2,4,8,8,8,128]{6,5,2,4,1,3,0:T(8,128)(2,1)}, bf16[2,2,4,8,8,8,128]{6,5,2,4,1,3,0:T(8,128)(2,1)S(1)}, u32[]{:S(2)}) copy-start(bf16[2,2,4,8,8,8,128]{6,5,2,4,1,3,0:T(8,128)(2,1)S(1)} %copy.12) | copy-start | bytes 6291460
  5.9 17.7 %collective-permute-start.1 = (bf16[1,16,32,128]{3,2,1,0:T(8,128)(2,1)S(1)}, bf16[1,16,32,128]{3,2,1,0:T(8,128)(2,1)S(1)}, u32[]{:S(2)}, u32[]{:S(2)}) collective-permute-start(bf16[1,16,32,128]{3,2,1,0:T(8,128)(2,1)S(1)} %get-tuple-element.14), channel_id=1, source_target_pairs={{16,0},{32,16},{48,32},{64,48},{80,64},{96,80},{112,96},{128,112},... | collective-permute-start | bytes 393224 | tf_op jit(solution)/shard_map/ppermute | solution.py:21
  11.0 12.6 %collective-permute-start = (bf16[1,16,32,128]{3,2,1,0:T(8,128)(2,1)S(1)}, bf16[1,16,32,128]{3,2,1,0:T(8,128)(2,1)S(1)}, u32[]{:S(2)}, u32[]{:S(2)}) collective-permute-start(bf16[1,16,32,128]{3,2,1,0:T(8,128)(2,1)S(1)} %get-tuple-element.13), channel_id=1, source_target_pairs={{0,16},{16,32},{32,48},{48,64},{64,80},{80,96},{96,112},{112,128},... | collective-permute-start | bytes 393224 | tf_op jit(solution)/shard_map/ppermute | solution.py:20
  16.3 20.2 %collective-permute-start.5 = (bf16[1,16,32,128]{3,2,1,0:T(8,128)(2,1)}, bf16[1,16,32,128]{3,2,1,0:T(8,128)(2,1)S(1)}, u32[]{:S(2)}, u32[]{:S(2)}) collective-permute-start(bf16[1,16,32,128]{3,2,1,0:T(8,128)(2,1)} %get-tuple-element.12), channel_id=1, source_target_pairs={{16,0},{32,16},{48,32},{64,48},{80,64},{96,80},{112,96},{128,112},... | collective-permute-start | bytes 393224 | tf_op jit(solution)/shard_map/ppermute | solution.py:21
  18.2 18.3 %collective-permute-start.4 = (bf16[1,16,32,128]{3,2,1,0:T(8,128)(2,1)}, bf16[1,16,32,128]{3,2,1,0:T(8,128)(2,1)S(1)}, u32[]{:S(2)}, u32[]{:S(2)}) collective-permute-start(bf16[1,16,32,128]{3,2,1,0:T(8,128)(2,1)} %get-tuple-element.11), channel_id=1, source_target_pairs={{0,16},{16,32},{32,48},{48,64},{64,80},{80,96},{96,112},{112,128},... | collective-permute-start | bytes 393224 | tf_op jit(solution)/shard_map/ppermute | solution.py:20
  23.6 0.8 copy-start.3
  23.6 0.8 copy-start.4
  24.4 17.6 %collective-permute-start.3 = (bf16[18,1,32,128]{3,2,1,0:T(8,128)(2,1)}, bf16[18,1,32,128]{3,2,1,0:T(8,128)(2,1)}, u32[]{:S(2)}, u32[]{:S(2)}) collective-permute-start(bf16[18,1,32,128]{3,2,1,0:T(8,128)(2,1)} %get-tuple-element.10), channel_id=1, source_target_pairs={{1,0},{2,1},{3,2},{4,3},{5,4},{6,5},{7,6},{8,7},{9,8},{10,9},{11,1... | collective-permute-start | bytes 442376 | tf_op jit(solution)/shard_map/ppermute | solution.py:21
  25.7 16.4 %collective-permute-start.2 = (bf16[18,1,32,128]{3,2,1,0:T(8,128)(2,1)}, bf16[18,1,32,128]{3,2,1,0:T(8,128)(2,1)}, u32[]{:S(2)}, u32[]{:S(2)}) collective-permute-start(bf16[18,1,32,128]{3,2,1,0:T(8,128)(2,1)} %get-tuple-element.9), channel_id=1, source_target_pairs={{0,1},{1,2},{2,3},{3,4},{4,5},{5,6},{6,7},{7,8},{8,9},{9,10},{10,1... | collective-permute-start | bytes 442376 | tf_op jit(solution)/shard_map/ppermute | solution.py:20
  36.6 12.6 %collective-permute-start.7 = (bf16[18,1,32,128]{3,2,1,0:T(8,128)(2,1)S(1)}, bf16[18,1,32,128]{3,2,1,0:T(8,128)(2,1)S(1)}, u32[]{:S(2)}, u32[]{:S(2)}) collective-permute-start(bf16[18,1,32,128]{3,2,1,0:T(8,128)(2,1)S(1)} %get-tuple-element.8), channel_id=1, source_target_pairs={{1,0},{2,1},{3,2},{4,3},{5,4},{6,5},{7,6},{8,7},{9,8},{10,9},{11,1... | collective-permute-start | bytes 442376 | tf_op jit(solution)/shard_map/ppermute | solution.py:21
  37.9 11.3 %collective-permute-start.6 = (bf16[18,1,32,128]{3,2,1,0:T(8,128)(2,1)S(1)}, bf16[18,1,32,128]{3,2,1,0:T(8,128)(2,1)S(1)}, u32[]{:S(2)}, u32[]{:S(2)}) collective-permute-start(bf16[18,1,32,128]{3,2,1,0:T(8,128)(2,1)S(1)} %get-tuple-element.7), channel_id=1, source_target_pairs={{0,1},{1,2},{2,3},{3,4},{4,5},{5,6},{6,7},{7,8},{8,9},{9,10},{10,1... | collective-permute-start | bytes 442376 | tf_op jit(solution)/shard_map/ppermute | solution.py:20
  86.5 2.6 %collective-permute-start.8 = (f32[1792,128]{1,0:T(8,128)S(1)}, f32[1792,128]{1,0:T(8,128)S(1)}, u32[]{:S(2)}, u32[]{:S(2)}) collective-permute-start(f32[1792,128]{1,0:T(8,128)S(1)} %pad_dynamic-slice_fusion), channel_id=1, source_target_pairs={{0,16},{16,0},{32,48},{48,32},{64,80},{80,64},{96,112},{112,96},{1... | collective-permute-start | bytes 2752520 | tf_op jit(solution)/shard_map/ppermute | solution.py:42
  89.2 13.1 %collective-permute-start.9 = (f32[896,128]{1,0:T(8,128)S(1)}, f32[896,128]{1,0:T(8,128)S(1)}, u32[]{:S(2)}, u32[]{:S(2)}) collective-permute-start(f32[896,128]{1,0:T(8,128)S(1)} %constant_dynamic-slice_fusion.6), channel_id=1, source_target_pairs={{0,1},{1,0},{2,3},{3,2},{4,5},{5,4},{6,7},{7,6},{8,9},{9,8},{10,11... | collective-permute-start | bytes 1376264 | tf_op jit(solution)/shard_map/ppermute | solution.py:42
  102.4 6.4 %collective-permute-start.10 = (f32[448,128]{1,0:T(8,128)S(1)}, f32[448,128]{1,0:T(8,128)S(1)}, u32[]{:S(2)}, u32[]{:S(2)}) collective-permute-start(f32[448,128]{1,0:T(8,128)S(1)} %constant_dynamic-slice_fusion.5), channel_id=1, source_target_pairs={{0,64},{16,80},{32,96},{48,112},{64,0},{80,16},{96,32},{112,48},{1... | collective-permute-start | bytes 688136 | tf_op jit(solution)/shard_map/ppermute | solution.py:42
  108.9 4.2 %collective-permute-start.11 = (f32[224,128]{1,0:T(8,128)S(1)}, f32[224,128]{1,0:T(8,128)S(1)}, u32[]{:S(2)}, u32[]{:S(2)}) collective-permute-start(f32[224,128]{1,0:T(8,128)S(1)} %constant_dynamic-slice_fusion.4), channel_id=1, source_target_pairs={{0,2},{1,3},{2,0},{3,1},{4,6},{5,7},{6,4},{7,5},{8,10},{9,11},{10,... | collective-permute-start | bytes 344072 | tf_op jit(solution)/shard_map/ppermute | solution.py:42
  113.1 5.9 %collective-permute-start.12 = (f32[112,128]{1,0:T(8,128)S(1)}, f32[112,128]{1,0:T(8,128)S(1)}, u32[]{:S(2)}, u32[]{:S(2)}) collective-permute-start(f32[112,128]{1,0:T(8,128)S(1)} %constant_dynamic-slice_fusion.3), channel_id=1, source_target_pairs={{0,32},{16,48},{32,0},{48,16},{64,96},{80,112},{96,64},{112,80},{1... | collective-permute-start | bytes 172040 | tf_op jit(solution)/shard_map/ppermute | solution.py:42
  119.1 4.3 %collective-permute-start.13 = (f32[56,128]{1,0:T(8,128)S(1)}, f32[56,128]{1,0:T(8,128)S(1)}, u32[]{:S(2)}, u32[]{:S(2)}) collective-permute-start(f32[56,128]{1,0:T(8,128)S(1)} %constant_dynamic-slice_fusion.2), channel_id=1, source_target_pairs={{0,128},{16,144},{32,160},{48,176},{64,192},{80,208},{96,224},{112... | collective-permute-start | bytes 86024 | tf_op jit(solution)/shard_map/ppermute | solution.py:42
  123.4 6.6 %collective-permute-start.14 = (f32[28,128]{1,0:T(8,128)S(1)}, f32[28,128]{1,0:T(8,128)S(1)}, u32[]{:S(2)}, u32[]{:S(2)}) collective-permute-start(f32[28,128]{1,0:T(8,128)S(1)} %constant_dynamic-slice_fusion.1), channel_id=1, source_target_pairs={{0,4},{1,5},{2,6},{3,7},{4,0},{5,1},{6,2},{7,3},{8,12},{9,13},{10,... | collective-permute-start | bytes 43016 | tf_op jit(solution)/shard_map/ppermute | solution.py:42
  130.1 6.6 %collective-permute-start.15 = (f32[14,128]{1,0:T(8,128)S(1)}, f32[14,128]{1,0:T(8,128)S(1)}, u32[]{:S(2)}, u32[]{:S(2)}) collective-permute-start(f32[14,128]{1,0:T(8,128)S(1)} %constant_dynamic-slice_fusion), channel_id=1, source_target_pairs={{0,8},{1,9},{2,10},{3,11},{4,12},{5,13},{6,14},{7,15},{8,0},{9,1},... | collective-permute-start | bytes 21512 | tf_op jit(solution)/shard_map/ppermute | solution.py:42
  136.7 6.5 %collective-permute-start.16 = (f32[14,128]{1,0:T(8,128)S(1)}, f32[14,128]{1,0:T(8,128)S(1)}, u32[]{:S(2)}, u32[]{:S(2)}) collective-permute-start(f32[14,128]{1,0:T(8,128)S(1)} %dynamic-slice_add_fusion.6), channel_id=1, source_target_pairs={{0,8},{1,9},{2,10},{3,11},{4,12},{5,13},{6,14},{7,15},{8,0},{9,1},... | collective-permute-start | bytes 21512 | tf_op jit(solution)/shard_map/ppermute | solution.py:46
  143.2 3.8 %collective-permute-start.17 = (f32[28,128]{1,0:T(8,128)S(1)}, f32[28,128]{1,0:T(8,128)S(1)}, u32[]{:S(2)}, u32[]{:S(2)}) collective-permute-start(f32[28,128]{1,0:T(8,128)S(1)} %pad_maximum_fusion.15), channel_id=1, source_target_pairs={{0,4},{1,5},{2,6},{3,7},{4,0},{5,1},{6,2},{7,3},{8,12},{9,13},{10,... | collective-permute-start | bytes 43016 | tf_op jit(solution)/shard_map/ppermute | solution.py:46
  147.0 4.3 %collective-permute-start.18 = (f32[56,128]{1,0:T(8,128)S(1)}, f32[56,128]{1,0:T(8,128)S(1)}, u32[]{:S(2)}, u32[]{:S(2)}) collective-permute-start(f32[56,128]{1,0:T(8,128)S(1)} %pad_maximum_fusion.14), channel_id=1, source_target_pairs={{0,128},{16,144},{32,160},{48,176},{64,192},{80,208},{96,224},{112... | collective-permute-start | bytes 86024 | tf_op jit(solution)/shard_map/ppermute | solution.py:46
  151.4 4.6 %collective-permute-start.19 = (f32[112,128]{1,0:T(8,128)S(1)}, f32[112,128]{1,0:T(8,128)S(1)}, u32[]{:S(2)}, u32[]{:S(2)}) collective-permute-start(f32[112,128]{1,0:T(8,128)S(1)} %pad_maximum_fusion.13), channel_id=1, source_target_pairs={{0,32},{16,48},{32,0},{48,16},{64,96},{80,112},{96,64},{112,80},{1... | collective-permute-start | bytes 172040 | tf_op jit(solution)/shard_map/ppermute | solution.py:46
  156.0 4.0 %collective-permute-start.20 = (f32[224,128]{1,0:T(8,128)S(1)}, f32[224,128]{1,0:T(8,128)S(1)}, u32[]{:S(2)}, u32[]{:S(2)}) collective-permute-start(f32[224,128]{1,0:T(8,128)S(1)} %pad_maximum_fusion.12), channel_id=1, source_target_pairs={{0,2},{1,3},{2,0},{3,1},{4,6},{5,7},{6,4},{7,5},{8,10},{9,11},{10,... | collective-permute-start | bytes 344072 | tf_op jit(solution)/shard_map/ppermute | solution.py:46
  160.1 5.0 %collective-permute-start.21 = (f32[448,128]{1,0:T(8,128)S(1)}, f32[448,128]{1,0:T(8,128)S(1)}, u32[]{:S(2)}, u32[]{:S(2)}) collective-permute-start(f32[448,128]{1,0:T(8,128)S(1)} %pad_maximum_fusion.5), channel_id=1, source_target_pairs={{0,64},{16,80},{32,96},{48,112},{64,0},{80,16},{96,32},{112,48},{1... | collective-permute-start | bytes 688136 | tf_op jit(solution)/shard_map/ppermute | solution.py:46
  165.1 7.4 %collective-permute-start.22 = (f32[896,128]{1,0:T(8,128)S(1)}, f32[896,128]{1,0:T(8,128)S(1)}, u32[]{:S(2)}, u32[]{:S(2)}) collective-permute-start(f32[896,128]{1,0:T(8,128)S(1)} %pad_maximum_fusion.2), channel_id=1, source_target_pairs={{0,1},{1,0},{2,3},{3,2},{4,5},{5,4},{6,7},{7,6},{8,9},{9,8},{10,11... | collective-permute-start | bytes 1376264 | tf_op jit(solution)/shard_map/ppermute | solution.py:46
  172.7 22.5 %collective-permute-start.23 = (f32[1792,128]{1,0:T(8,128)S(1)}, f32[1792,128]{1,0:T(8,128)S(1)}, u32[]{:S(2)}, u32[]{:S(2)}) collective-permute-start(f32[1792,128]{1,0:T(8,128)S(1)} %pad_maximum_fusion.1), channel_id=1, source_target_pairs={{0,16},{16,0},{32,48},{48,32},{64,80},{80,64},{96,112},{112,96},{1... | collective-permute-start | bytes 2752520 | tf_op jit(solution)/shard_map/ppermute | solution.py:46

commit v3 on v2

--- a/solution.py
+++ b/solution.py
@@ -26,7 +26,7 @@
 STEPS = (("gx", 0), ("gy", 0), ("gx", 2), ("gy", 1), ("gx", 1), ("gx", 3), ("gy", 2), ("gy", 3))
 
 
-def butterfly_sum(value, steps=STEPS):
+def butterfly_scatter(value, steps=STEPS):
     lanes = value.shape[-1]
     flat = value.reshape(-1, lanes)
     rows = flat.shape[0]
@@ -40,35 +40,41 @@
         keep = lax.dynamic_slice_in_dim(buf, bit * half, half, 0)
         send = lax.dynamic_slice_in_dim(buf, (1 - bit) * half, half, 0)
         buf = keep + lax.ppermute(send, axis, pairs)
+    return buf
+
+
+def butterfly_gather(buf, like, steps=STEPS):
     for axis, b in reversed(steps):
         pairs = [(i, i ^ (1 << b)) for i in range(lax.axis_size(axis))]
         bit = (lax.axis_index(axis) >> b) & 1
         got = lax.ppermute(buf, axis, pairs)
         buf = jnp.concatenate([jnp.where(bit == 0, buf, got), jnp.where(bit == 0, got, buf)], 0)
-    return buf[:rows].reshape(value.shape)
+    return buf[: like.size // like.shape[-1]].reshape(like.shape)
 
 
 def place_bricks(bricks, places, alive):
     spots = jnp.arange(TBX * TBY * ZL, dtype=jnp.int32)
     picker = ((places[None, :] == spots[:, None]) & alive[None, :]).astype(jnp.bfloat16)
-    dense = jnp.einsum("ps,svc->pvc", picker, bricks, preferred_element_type=jnp.float32).astype(
+    dense = jnp.einsum("ps,tsvc->tpvc", picker, bricks, preferred_element_type=jnp.float32).astype(
         jnp.bfloat16
     )
-    chans = bricks.shape[-1]
-    dense = dense.reshape(TBX, TBY, ZL, BRICK, BRICK, BRICK, chans)
-    dense = dense.transpose(0, 3, 1, 4, 2, 5, 6)
-    return dense.reshape(TBX * BRICK, TBY * BRICK, ZL * BRICK, chans)
+    kinds, chans = bricks.shape[0], bricks.shape[-1]
+    dense = dense.reshape(kinds, TBX, TBY, ZL, BRICK, BRICK, BRICK, chans)
+    dense = dense.transpose(0, 1, 4, 2, 5, 3, 6, 7)
+    return dense.reshape(kinds, TBX * BRICK, TBY * BRICK, ZL * BRICK, chans)
 
 
 def cut_windows(padded, places):
-    padded = jnp.pad(padded, ((0, 0), (0, 0), (1, 1), (0, 0)))
-    chans = padded.shape[-1]
+    padded = jnp.pad(padded, ((0, 0), (0, 0), (0, 0), (1, 1), (0, 0)))
+    kinds, chans = padded.shape[0], padded.shape[-1]
     windows = []
     for slot in range(places.shape[0]):
         place = places[slot]
-        starts = (place // (TBY * ZL) * BRICK, place // ZL % TBY * BRICK, place % ZL * BRICK, 0)
-        windows.append(lax.dynamic_slice(padded, starts, (BRICK + 2, BRICK + 2, BRICK + 2, chans)))
-    return jnp.stack(windows)
+        starts = (0, place // (TBY * ZL) * BRICK, place // ZL % TBY * BRICK, place % ZL * BRICK, 0)
+        windows.append(
+            lax.dynamic_slice(padded, starts, (kinds, BRICK + 2, BRICK + 2, BRICK + 2, chans))
+        )
+    return jnp.stack(windows, 1)
 
 
 def stack_offsets(windows):
@@ -87,23 +93,23 @@
     alive = jnp.arange(slots, dtype=jnp.int32) < brick_count[0, 0]
     keeper = (occupancy[0, 0] * alive[:, None].astype(jnp.int32)).astype(jnp.bfloat16)
     keeper_rows = keeper.reshape(-1, 1).astype(jnp.float32)
-    feat_masked = features[0, 0] * keeper[:, :, None]
-    grad_masked = cotangent[0, 0] * keeper[:, :, None]
-    grad_rows = grad_masked.reshape(-1, chans)
-    feat_dense = place_bricks(feat_masked, places, alive)
-    feat_padded = with_halo(feat_dense, (("gx", 0), ("gy", 1)), 1)
-    feat_stack = stack_offsets(cut_windows(feat_padded, places))
-    weight_local = jnp.einsum("dvc,ve->dce", feat_stack, grad_rows, preferred_element_type=jnp.float32)
+    both = jnp.stack([features[0, 0], cotangent[0, 0]]) * keeper[None, :, :, None]
+    grad_rows = both[1].reshape(-1, chans)
+    dense = place_bricks(both, places, alive)
+    padded = with_halo(dense, (("gx", 1), ("gy", 2)), 1)
+    windows = cut_windows(padded, places)
+    feat_stack = stack_offsets(windows[0])
+    weight_local = jnp.einsum("ve,dvc->edc", grad_rows, feat_stack, preferred_element_type=jnp.float32)
     tiles = lax.axis_size("gx") * lax.axis_size("gy")
-    weight_total = butterfly_sum(weight_local)
-    weight_grad = weight_total / jnp.float32(tiles)
+    half_done = butterfly_scatter(weight_local)
     output_sum = jnp.einsum("dvc,dce->ve", feat_stack, weight, preferred_element_type=jnp.float32)
     output_rows = (output_sum * keeper_rows).astype(jnp.bfloat16)
-    grad_dense = place_bricks(grad_masked, places, alive)
-    grad_padded = with_halo(grad_dense, (("gx", 0), ("gy", 1)), 1)
-    grad_stack = stack_offsets(cut_windows(grad_padded, places))
+    grad_stack = stack_offsets(windows[1])
     input_sum = jnp.einsum("dvc,dec->ve", grad_stack, weight[::-1], preferred_element_type=jnp.float32)
     input_rows = (input_sum * keeper_rows).astype(jnp.bfloat16)
+    half_done, output_rows, input_rows = lax.optimization_barrier((half_done, output_rows, input_rows))
+    weight_total = butterfly_gather(half_done, weight_local)
+    weight_grad = weight_total.transpose(1, 2, 0) / jnp.float32(tiles)
     output = output_rows.reshape(1, 1, slots, -1, chans)
     input_grad = input_rows.reshape(1, 1, slots, -1, chans)
     return (output, input_grad, weight_grad)

time: 198 us -> 173 us (0.87)
  starting transfers between devices: 78.7 us -> 65.5 us
  matrix products: 15.9 us -> 8.6 us
  local copies, waits for them, and re-layouts: 34.5 us -> 27.7 us
  waiting for transfers between devices: 44.7 us -> 49.7 us
  other arithmetic: 15.2 us -> 13 us
    ppermute x4 -> x2, starting transfers between devices: 16.8 us -> 7.03 us  [with_halo(): before = lax.ppermute(last, axis, up)]
    dot_general x1, local copies, waits for them, and re-layouts: 10 us -> 2.44 us  [local(): jnp.einsum('ve,dvc->edc', grad_rows, feat_stack, preferred_element_type=j...]
    unnamed x68 -> x103, local copies, waits for them, and re-layouts: 19.7 us -> 13.5 us
    slice x0 -> x6, local copies, waits for them, and re-layouts: none -> 5.37 us  [the longest x4 5.37 us: stack_offsets(): windows[:, first:first + BRICK, second:second + BRICK, third:third + BRIC...]
    dot_general x3 -> x2, matrix products: 7.49 us -> 3.19 us  [the longest x1 2.04 us: place_bricks(): jnp.einsum('ps,tsvc->tpvc', picker, bricks, preferred_element_type=jnp.fl...]
    ppermute x4 -> x2, starting transfers between devices: 9.59 us -> 6.4 us  [with_halo(): after = lax.ppermute(leading, axis, down)]
    ppermute x4 -> x2, waiting for transfers between devices: 0.01 us -> 3.1 us  [with_halo(): before = lax.ppermute(last, axis, up)]
    dot_general x1, matrix products: 5.7 us -> 2.71 us  [local(): jnp.einsum('dvc,dce->ve', feat_stack, weight, preferred_element_type=jnp....]
  transfers between devices with their start and end apart: 24 -> 20, of which waited for: 15 -> 17; matrix products, arithmetic and copies ran while one was open for 11% -> 9% of each run, Pallas kernels for 0% -> 0%
where the time goes in v3:
time: 173 us; the launch traced here: 172 us
  starting transfers between devices  65.5 us (38%)
  waiting for transfers between devices  49.7 us (29%)
  local copies, waits for them, and re-layouts  27.7 us (16%)
  other arithmetic  13 us (8%)
  matrix products  8.6 us (5%)
  between operations  7.78 us (4%)
    ppermute x8, starting transfers between devices, butterfly_scatter(): buf = keep + lax.ppermute(send, axis, pairs)  26.2 us
    ppermute x8, starting transfers between devices, butterfly_gather(): got = lax.ppermute(buf, axis, pairs)  25.9 us
    ppermute x8, waiting for transfers between devices, butterfly_gather(): got = lax.ppermute(buf, axis, pairs)  25.4 us
    ppermute x8, waiting for transfers between devices, butterfly_scatter(): buf = keep + lax.ppermute(send, axis, pairs)  19.2 us
    unnamed x103, local copies, waits for them, and re-layouts  13.5 us
    concatenate x1, other arithmetic, with_halo(): value = jnp.concatenate([before, value, after], axis=dim)  7.54 us
    ppermute x2, starting transfers between devices, with_halo(): before = lax.ppermute(last, axis, up)  7.03 us
    ppermute x2, starting transfers between devices, with_halo(): after = lax.ppermute(leading, axis, down)  6.4 us
  transfers between devices with their start and end apart: 20, of which 17 were waited for; matrix products, arithmetic and copies ran while one was open for 9% of the time, Pallas kernels for 0%

profile of v3, /device:TPU:1, one launch (start us, length us, event | category | flops | bytes accessed | tf_op | source)
XLA Modules:
  0.0 172.3 jit_solution(10898999899901553348)
XLA Ops:
  1.4 0.8 broadcast_bitcast_fusion
  2.1 1.2 maximum_multiply_fusion
  3.4 2.0 %convolution_convert_fusion = bf16[2,512,128,16]{2,3,1,0:T(8,128)(2,1)S(1)} fusion(bf16[2,2,512,128]{3,2,1,0:T(8,128)(2,1)S(1)} %maximum_multiply_fusion, pred[2]{0:T(512)(128)(4,1)S(1)} %get-tuple-element.94, s32[2]{0:T(128)} %bitcast.181), kind=kOutput, calls=%fused_computation.10 | convolution fusion | flops 10485824 | bytes 4718602 | tf_op jit(solution)/shard_map/ps,tsvc->tpvc/dot_general | solution.py:58
  5.5 1.6 copy.13
  7.1 5.1 %collective-permute-start.1 = (bf16[2,1,16,32,128]{4,3,2,1,0:T(8,128)(2,1)S(1)}, bf16[2,1,16,32,128]{4,3,2,1,0:T(8,128)(2,1)S(1)}, u32[]{:S(2)}, u32[]{:S(2)}) collective-permute-start(bf16[2,1,16,32,128]{4,3,2,1,0:T(8,128)(2,1)S(1)} %get-tuple-element.17), channel_id=1, source_target_pairs={{16,0},{32,16},{48,32},{64,48},{80,64},{96,80},{112,96},{128,112},... | collective-permute-start | bytes 786440 | tf_op jit(solution)/shard_map/ppermute | solution.py:21
  12.3 2.8 %collective-permute-start = (bf16[2,1,16,32,128]{4,3,2,1,0:T(8,128)(2,1)S(1)}, bf16[2,1,16,32,128]{4,3,2,1,0:T(8,128)(2,1)S(1)}, u32[]{:S(2)}, u32[]{:S(2)}) collective-permute-start(bf16[2,1,16,32,128]{4,3,2,1,0:T(8,128)(2,1)S(1)} %get-tuple-element.16), channel_id=1, source_target_pairs={{0,16},{16,32},{32,48},{48,64},{64,80},{80,96},{96,112},{112,128},... | collective-permute-start | bytes 786440 | tf_op jit(solution)/shard_map/ppermute | solution.py:20
  15.1 2.1 %collective-permute-done.1 = bf16[2,1,16,32,128]{4,3,2,1,0:T(8,128)(2,1)S(1)} collective-permute-done((bf16[2,1,16,32,128]{4,3,2,1,0:T(8,128)(2,1)S(1)}, bf16[2,1,16,32,128]{4,3,2,1,0:T(8,128)(2,1)S(1)}, u32[]{:S(2)}, u32[]{:S(2)}) %collective-permute-start.1) | collective-permute-done | bytes 262176 | tf_op jit(solution)/shard_map/ppermute | solution.py:21
  17.2 1.2 collective-permute-done
  18.5 1.3 collective-permute-start.3
  19.8 4.2 %collective-permute-start.2 = (bf16[2,18,1,32,128]{4,3,2,1,0:T(8,128)(2,1)S(1)}, bf16[2,18,1,32,128]{4,3,2,1,0:T(8,128)(2,1)S(1)}, u32[]{:S(2)}, u32[]{:S(2)}) collective-permute-start(bf16[2,18,1,32,128]{4,3,2,1,0:T(8,128)(2,1)S(1)} %get-tuple-element.14), channel_id=1, source_target_pairs={{0,1},{1,2},{2,3},{3,4},{4,5},{5,6},{6,7},{7,8},{8,9},{9,10},{10,1... | collective-permute-start | bytes 884744 | tf_op jit(solution)/shard_map/ppermute | solution.py:20
  24.0 0.6 fusion.30
  30.0 1.9 %collective-permute-done.2 = bf16[2,18,1,32,128]{4,3,2,1,0:T(8,128)(2,1)S(1)} collective-permute-done((bf16[2,18,1,32,128]{4,3,2,1,0:T(8,128)(2,1)S(1)}, bf16[2,18,1,32,128]{4,3,2,1,0:T(8,128)(2,1)S(1)}, u32[]{:S(2)}, u32[]{:S(2)}) %collective-permute-start.2) | collective-permute-done | bytes 294944 | tf_op jit(solution)/shard_map/ppermute | solution.py:20
  31.9 7.5 %select_maximum_fusion = bf16[2,18,18,34,128]{4,3,2,1,0:T(8,128)(2,1)S(1)} fusion(bf16[2,18,1,32,128]{4,3,2,1,0:T(8,128)(2,1)S(1)} %collective-permute-done.3, bf16[2,18,1,32,128]{4,3,2,1,0:T(8,128)(2,1)S(1)} %collective-permute-done.2, bf16[2,1,16,32,128]{4,3,2,1,0:T(8,128)(2,1)S(1)} %collective-permute-done.1, bf16[2,16,16,32,128]{4,3,2,1,0:T(8,128)(2,1)} %bitcast.116, ...), kind=kLoop, calls=%fused_computation.3 | loop fusion | flops 50761728 | bytes 10948608 | tf_op jit(solution)/shard_map/concatenate | solution.py:22
  39.5 0.8 dynamic-slice_bitcast_fusion
  40.6 0.4 fusion.29
  41.0 1.0 fusion.28
  42.1 1.4 fusion.27
  43.5 2.4 %fusion.26 = (bf16[2,8,8,8,128]{4,3,2,1,0:T(8,128)(2,1)S(1)}, bf16[2,8,8,8,128]{4,3,2,1,0:T(8,128)(2,1)S(1)}, bf16[2,8,8,8,128]{4,3,2,1,0:T(8,128)(2,1)S(1)}, bf...) fusion(bf16[2,10,10,10,128]{4,3,2,1,0:T(8,128)(2,1)S(1)} %get-t, ...), kind=kLoop, calls=%fused_computation.140 | loop fusion | bytes 9961472 | tf_op jit(solution)/shard_map/slice | solution.py:84
  47.2 1.1 fusion.31
  48.3 1.6 copy-done.2
  49.9 2.4 %copy.14 = f32[128,27,128]{2,1,0:T(8,128)} copy(f32[128,27,128]{2,0,1:T(8,128)S(1)} %fusion.31) | data formatting | bytes 3538944 | tf_op jit(solution)/shard_map/ve,dvc->edc/dot_general | solution.py:102
  52.4 1.6 reshape.78
  54.3 1.1 constant_dynamic-update-slice_fusion.53
  55.4 1.0 constant_dynamic-update-slice_fusion.52
  56.4 1.1 constant_dynamic-update-slice_fusion.51
  57.6 1.2 constant_dynamic-update-slice_fusion.50
  58.8 1.0 constant_dynamic-update-slice_fusion.49
  59.7 1.0 constant_dynamic-update-slice_fusion.48
  60.7 1.0 constant_dynamic-update-slice_fusion.47
  61.7 1.0 constant_dynamic-update-slice_fusion.46
  63.6 2.3 %collective-permute-start.5 = (f32[896,128]{1,0:T(8,128)S(1)}, f32[896,128]{1,0:T(8,128)S(1)}, u32[]{:S(2)}, u32[]{:S(2)}) collective-permute-start(f32[896,128]{1,0:T(8,128)S(1)} %constant_dynamic-slice_fusion.6), channel_id=1, source_target_pairs={{0,1},{1,0},{2,3},{3,2},{4,5},{5,4},{6,7},{7,6},{8,9},{9,8},{10,11... | collective-permute-start | bytes 1376264 | tf_op jit(solution)/shard_map/ppermute | solution.py:42
  66.0 2.7 %fusion.9 = bf16[1024,128]{1,0:T(8,128)(2,1)} fusion(bf16[27,1024,128]{2,1,0:T(8,128)(2,1)S(1)} %bitcast.118, bf16[27,128,128]{2,1,0:T(8,128)(2,1)S(1)} %copy-done, f32[1024]{0:T(1024)S(1)} %fusion.17), kind=kOutput, calls=%fused_computation.21 | convolution fusion | flops 906231808 | bytes 8228864 | tf_op jit(solution)/shard_map/dvc,dce->ve/dot_general | solution.py:105
  68.7 7.6 %collective-permute-done.5 = f32[896,128]{1,0:T(8,128)S(1)} collective-permute-done((f32[896,128]{1,0:T(8,128)S(1)}, f32[896,128]{1,0:T(8,128)S(1)}, u32[]{:S(2)}, u32[]{:S(2)}) %collective-permute-start.5) | collective-permute-done | bytes 458784 | tf_op jit(solution)/shard_map/ppermute | solution.py:42
  76.4 5.9 %collective-permute-start.6 = (f32[448,128]{1,0:T(8,128)S(1)}, f32[448,128]{1,0:T(8,128)S(1)}, u32[]{:S(2)}, u32[]{:S(2)}) collective-permute-start(f32[448,128]{1,0:T(8,128)S(1)} %constant_dynamic-slice_fusion.5), channel_id=1, source_target_pairs={{0,64},{16,80},{32,96},{48,112},{64,0},{80,16},{96,32},{112,48},{1... | collective-permute-start | bytes 688136 | tf_op jit(solution)/shard_map/ppermute | solution.py:42
  82.4 5.1 %collective-permute-done.6 = f32[448,128]{1,0:T(8,128)S(1)} collective-permute-done((f32[448,128]{1,0:T(8,128)S(1)}, f32[448,128]{1,0:T(8,128)S(1)}, u32[]{:S(2)}, u32[]{:S(2)}) %collective-permute-start.6) | collective-permute-done | bytes 229408 | tf_op jit(solution)/shard_map/ppermute | solution.py:42
  87.6 1.3 collective-permute-start.7
  88.9 2.4 %collective-permute-done.7 = f32[224,128]{1,0:T(8,128)S(1)} collective-permute-done((f32[224,128]{1,0:T(8,128)S(1)}, f32[224,128]{1,0:T(8,128)S(1)}, u32[]{:S(2)}, u32[]{:S(2)}) %collective-permute-start.7) | collective-permute-done | bytes 114720 | tf_op jit(solution)/shard_map/ppermute | solution.py:42
  91.4 4.0 %collective-permute-start.8 = (f32[112,128]{1,0:T(8,128)S(1)}, f32[112,128]{1,0:T(8,128)S(1)}, u32[]{:S(2)}, u32[]{:S(2)}) collective-permute-start(f32[112,128]{1,0:T(8,128)S(1)} %constant_dynamic-slice_fusion.3), channel_id=1, source_target_pairs={{0,32},{16,48},{32,0},{48,16},{64,96},{80,112},{96,64},{112,80},{1... | collective-permute-start | bytes 172040 | tf_op jit(solution)/shard_map/ppermute | solution.py:42
  95.5 1.5 collective-permute-done.8
  97.0 3.0 %collective-permute-start.9 = (f32[56,128]{1,0:T(8,128)S(1)}, f32[56,128]{1,0:T(8,128)S(1)}, u32[]{:S(2)}, u32[]{:S(2)}) collective-permute-start(f32[56,128]{1,0:T(8,128)S(1)} %constant_dynamic-slice_fusion.2), channel_id=1, source_target_pairs={{0,128},{16,144},{32,160},{48,176},{64,192},{80,208},{96,224},{112... | collective-permute-start | bytes 86024 | tf_op jit(solution)/shard_map/ppermute | solution.py:42
  100.0 1.3 collective-permute-done.9
  101.4 4.3 %collective-permute-start.10 = (f32[28,128]{1,0:T(8,128)S(1)}, f32[28,128]{1,0:T(8,128)S(1)}, u32[]{:S(2)}, u32[]{:S(2)}) collective-permute-start(f32[28,128]{1,0:T(8,128)S(1)} %constant_dynamic-slice_fusion.1), channel_id=1, source_target_pairs={{0,4},{1,5},{2,6},{3,7},{4,0},{5,1},{6,2},{7,3},{8,12},{9,13},{10,... | collective-permute-start | bytes 43016 | tf_op jit(solution)/shard_map/ppermute | solution.py:42
  105.7 1.1 collective-permute-done.10
  106.8 5.2 %collective-permute-start.11 = (f32[14,128]{1,0:T(8,128)S(1)}, f32[14,128]{1,0:T(8,128)S(1)}, u32[]{:S(2)}, u32[]{:S(2)}) collective-permute-start(f32[14,128]{1,0:T(8,128)S(1)} %constant_dynamic-slice_fusion), channel_id=1, source_target_pairs={{0,8},{1,9},{2,10},{3,11},{4,12},{5,13},{6,14},{7,15},{8,0},{9,1},... | collective-permute-start | bytes 21512 | tf_op jit(solution)/shard_map/ppermute | solution.py:42
  112.1 2.7 %fusion.10 = bf16[1024,128]{1,0:T(8,128)(2,1)} fusion(bf16[27,1024,128]{2,1,0:T(8,128)(2,1)S(1)} %constant_dynamic-update-slice_fusion.27, bf16[27,128,128]{2,1,0:T(8,128)(2,1)S(1)} %copy-done, f32[1024]{0:T(1024)S(1)} %fusion.17), kind=kOutput, calls=%fused_computation.22 | convolution fusion | flops 906231808 | bytes 8228864 | tf_op jit(solution)/shard_map/dvc,dec->ve/dot_general | solution.py:108
  114.8 3.8 %collective-permute-start.12 = (f32[14,128]{1,0:T(8,128)S(1)}, f32[14,128]{1,0:T(8,128)S(1)}, u32[]{:S(2)}, u32[]{:S(2)}) collective-permute-start(f32[14,128]{1,0:T(8,128)S(1)} %dynamic-slice_add_fusion.6), channel_id=1, source_target_pairs={{0,8},{1,9},{2,10},{3,11},{4,12},{5,13},{6,14},{7,15},{8,0},{9,1},... | collective-permute-start | bytes 21512 | tf_op jit(solution)/shard_map/ppermute | solution.py:50
  118.6 2.7 %collective-permute-done.12 = f32[14,128]{1,0:T(8,128)S(1)} collective-permute-done((f32[14,128]{1,0:T(8,128)S(1)}, f32[14,128]{1,0:T(8,128)S(1)}, u32[]{:S(2)}, u32[]{:S(2)}) %collective-permute-start.12) | collective-permute-done | bytes 7200 | tf_op jit(solution)/shard_map/ppermute | solution.py:50
  121.3 1.3 collective-permute-start.13
  122.6 2.3 %collective-permute-done.13 = f32[28,128]{1,0:T(8,128)S(1)} collective-permute-done((f32[28,128]{1,0:T(8,128)S(1)}, f32[28,128]{1,0:T(8,128)S(1)}, u32[]{:S(2)}, u32[]{:S(2)}) %collective-permute-start.13) | collective-permute-done | bytes 14368 | tf_op jit(solution)/shard_map/ppermute | solution.py:50
  124.9 2.7 %collective-permute-start.14 = (f32[56,128]{1,0:T(8,128)S(1)}, f32[56,128]{1,0:T(8,128)S(1)}, u32[]{:S(2)}, u32[]{:S(2)}) collective-permute-start(f32[56,128]{1,0:T(8,128)S(1)} %pad_maximum_fusion.10), channel_id=1, source_target_pairs={{0,128},{16,144},{32,160},{48,176},{64,192},{80,208},{96,224},{112... | collective-permute-start | bytes 86024 | tf_op jit(solution)/shard_map/ppermute | solution.py:50
  127.7 1.6 collective-permute-done.14
  129.3 3.0 %collective-permute-start.15 = (f32[112,128]{1,0:T(8,128)S(1)}, f32[112,128]{1,0:T(8,128)S(1)}, u32[]{:S(2)}, u32[]{:S(2)}) collective-permute-start(f32[112,128]{1,0:T(8,128)S(1)} %pad_maximum_fusion.9), channel_id=1, source_target_pairs={{0,32},{16,48},{32,0},{48,16},{64,96},{80,112},{96,64},{112,80},{1... | collective-permute-start | bytes 172040 | tf_op jit(solution)/shard_map/ppermute | solution.py:50
  132.3 1.6 collective-permute-done.15
  133.9 0.8 collective-permute-start.16
  134.7 3.2 %collective-permute-done.16 = f32[224,128]{1,0:T(8,128)S(1)} collective-permute-done((f32[224,128]{1,0:T(8,128)S(1)}, f32[224,128]{1,0:T(8,128)S(1)}, u32[]{:S(2)}, u32[]{:S(2)}) %collective-permute-start.16) | collective-permute-done | bytes 114720 | tf_op jit(solution)/shard_map/ppermute | solution.py:50
  138.0 0.8 collective-permute-start.17
  138.7 4.5 %collective-permute-done.17 = f32[448,128]{1,0:T(8,128)S(1)} collective-permute-done((f32[448,128]{1,0:T(8,128)S(1)}, f32[448,128]{1,0:T(8,128)S(1)}, u32[]{:S(2)}, u32[]{:S(2)}) %collective-permute-start.17) | collective-permute-done | bytes 229408 | tf_op jit(solution)/shard_map/ppermute | solution.py:50
  143.4 7.3 %collective-permute-done.18 = f32[896,128]{1,0:T(8,128)S(1)} collective-permute-done((f32[896,128]{1,0:T(8,128)S(1)}, f32[896,128]{1,0:T(8,128)S(1)}, u32[]{:S(2)}, u32[]{:S(2)}) %collective-permute-start.18) | collective-permute-done | bytes 458784 | tf_op jit(solution)/shard_map/ppermute | solution.py:50
  150.9 13.3 %collective-permute-start.19 = (f32[1792,128]{1,0:T(8,128)S(1)}, f32[1792,128]{1,0:T(8,128)}, u32[]{:S(2)}, u32[]{:S(2)}) collective-permute-start(f32[1792,128]{1,0:T(8,128)S(1)} %pad_maximum_fusion.1), channel_id=1, source_target_pairs={{0,16},{16,0},{32,48},{48,32},{64,80},{80,64},{96,112},{112,96},{1... | collective-permute-start | bytes 2752520 | tf_op jit(solution)/shard_map/ppermute | solution.py:50
  164.2 2.2 %collective-permute-done.19 = f32[1792,128]{1,0:T(8,128)} collective-permute-done((f32[1792,128]{1,0:T(8,128)S(1)}, f32[1792,128]{1,0:T(8,128)}, u32[]{:S(2)}, u32[]{:S(2)}) %collective-permute-start.19) | collective-permute-done | bytes 917536 | tf_op jit(solution)/shard_map/ppermute | solution.py:50
  166.4 1.3 broadcast_select_fusion.1
  167.7 1.3 fusion.6
  169.1 1.5 div.53
  170.6 1.8 %copy.15 = f32[27,128,128]{2,1,0:T(8,128)} copy(f32[27,128,128]{1,0,2:T(8,128)S(1)} %bitcast.120) | data formatting | bytes 3538944
  (138 shorter events, 3.1 us)
Async XLA Ops:
  0.6 65.3 %copy-start = (bf16[27,128,128]{2,1,0:T(8,128)(2,1)S(1)}, bf16[27,128,128]{2,1,0:T(8,128)(2,1)}, u32[]{:S(2)}) copy-start(bf16[27,128,128]{2,1,0:T(8,128)(2,1)} %param.10) | copy-start | bytes 2654212
  3.4 11.7 %copy-start.3 = (bf16[2,2,512,128]{3,2,1,0:T(8,128)(2,1)}, bf16[2,2,512,128]{3,2,1,0:T(8,128)(2,1)S(1)}, u32[]{:S(2)}) copy-start(bf16[2,2,512,128]{3,2,1,0:T(8,128)(2,1)S(1)} %maximum_multiply_fusion) | copy-start | bytes 1572868
  5.4 18.5 %copy-start.21 = (s32[1,1,2]{2,1,0:T(1,128)S(1)}, s32[1,1,2]{2,1,0:T(1,128)}, u32[]{:S(2)}) copy-start(s32[1,1,2]{2,1,0:T(1,128)} %param.8) | copy-start | bytes 28
  5.5 24.5 %copy-start.20 = (s32[1,1,2,512]{3,2,1,0:T(2,128)S(1)}, s32[1,1,2,512]{3,2,1,0:T(2,128)}, u32[]{:S(2)}) copy-start(s32[1,1,2,512]{3,2,1,0:T(2,128)} %param.7) | copy-start | bytes 12292
  7.1 11.3 %copy-start.1 = (bf16[2,2,2,4,8,8,8,128]{7,6,3,5,2,4,1,0:T(8,128)(2,1)}, bf16[2,2,2,4,8,8,8,128]{7,6,3,5,2,4,1,0:T(8,128)(2,1)S(1)}, u32[]{:S(2)}) copy-start(bf16[2,2,2,4,8,8,8,128]{7,6,3,5,2,4,1,0:T(8,128)(2,1)S(1)} %copy.13) | copy-start | bytes 12582916
  7.1 10.1 %collective-permute-start.1 = (bf16[2,1,16,32,128]{4,3,2,1,0:T(8,128)(2,1)S(1)}, bf16[2,1,16,32,128]{4,3,2,1,0:T(8,128)(2,1)S(1)}, u32[]{:S(2)}, u32[]{:S(2)}) collective-permute-start(bf16[2,1,16,32,128]{4,3,2,1,0:T(8,128)(2,1)S(1)} %get-tuple-element.17), channel_id=1, source_target_pairs={{16,0},{32,16},{48,32},{64,48},{80,64},{96,80},{112,96},{128,112},... | collective-permute-start | bytes 786440 | tf_op jit(solution)/shard_map/ppermute | solution.py:21
  12.3 6.1 %collective-permute-start = (bf16[2,1,16,32,128]{4,3,2,1,0:T(8,128)(2,1)S(1)}, bf16[2,1,16,32,128]{4,3,2,1,0:T(8,128)(2,1)S(1)}, u32[]{:S(2)}, u32[]{:S(2)}) collective-permute-start(bf16[2,1,16,32,128]{4,3,2,1,0:T(8,128)(2,1)S(1)} %get-tuple-element.16), channel_id=1, source_target_pairs={{0,16},{16,32},{32,48},{48,64},{64,80},{80,96},{96,112},{112,128},... | collective-permute-start | bytes 786440 | tf_op jit(solution)/shard_map/ppermute | solution.py:20
  18.5 11.5 %collective-permute-start.3 = (bf16[2,18,1,32,128]{4,3,2,1,0:T(8,128)(2,1)S(1)}, bf16[2,18,1,32,128]{4,3,2,1,0:T(8,128)(2,1)S(1)}, u32[]{:S(2)}, u32[]{:S(2)}) collective-permute-start(bf16[2,18,1,32,128]{4,3,2,1,0:T(8,128)(2,1)S(1)} %get-tuple-element.15), channel_id=1, source_target_pairs={{1,0},{2,1},{3,2},{4,3},{5,4},{6,5},{7,6},{8,7},{9,8},{10,9},{11,1... | collective-permute-start | bytes 884744 | tf_op jit(solution)/shard_map/ppermute | solution.py:21
  19.8 12.1 %collective-permute-start.2 = (bf16[2,18,1,32,128]{4,3,2,1,0:T(8,128)(2,1)S(1)}, bf16[2,18,1,32,128]{4,3,2,1,0:T(8,128)(2,1)S(1)}, u32[]{:S(2)}, u32[]{:S(2)}) collective-permute-start(bf16[2,18,1,32,128]{4,3,2,1,0:T(8,128)(2,1)S(1)} %get-tuple-element.14), channel_id=1, source_target_pairs={{0,1},{1,2},{2,3},{3,4},{4,5},{5,6},{6,7},{7,8},{8,9},{9,10},{10,1... | collective-permute-start | bytes 884744 | tf_op jit(solution)/shard_map/ppermute | solution.py:20
  46.0 1.2 slice-start.2
  47.1 2.8 %copy-start.2 = (bf16[27,1024,128]{2,1,0:T(8,128)(2,1)}, bf16[27,1024,128]{2,1,0:T(8,128)(2,1)S(1)}, u32[]{:S(2)}) copy-start(bf16[27,1024,128]{2,1,0:T(8,128)(2,1)S(1)} %constant_dynamic-update-slice_fusion) | copy-start | bytes 21233668
  54.0 8.7 %copy-start.19 = (bf16[2,8,8,8,128]{4,3,2,1,0:T(8,128)(2,1)S(1)}, bf16[2,8,8,8,128]{4,3,2,1,0:T(8,128)(2,1)}, u32[]{:S(2)}) copy-start(bf16[2,8,8,8,128]{4,3,2,1,0:T(8,128)(2,1)} %get-tuple-element.42) | copy-start | bytes 786436
  54.0 8.8 %copy-start.18 = (bf16[2,8,8,8,128]{4,3,2,1,0:T(8,128)(2,1)S(1)}, bf16[2,8,8,8,128]{4,3,2,1,0:T(8,128)(2,1)}, u32[]{:S(2)}) copy-start(bf16[2,8,8,8,128]{4,3,2,1,0:T(8,128)(2,1)} %get-tuple-element.41) | copy-start | bytes 786436
  54.0 8.8 %copy-start.17 = (bf16[2,8,8,8,128]{4,3,2,1,0:T(8,128)(2,1)S(1)}, bf16[2,8,8,8,128]{4,3,2,1,0:T(8,128)(2,1)}, u32[]{:S(2)}) copy-start(bf16[2,8,8,8,128]{4,3,2,1,0:T(8,128)(2,1)} %get-tuple-element.40) | copy-start | bytes 786436
  54.0 8.8 %copy-start.16 = (bf16[2,8,8,8,128]{4,3,2,1,0:T(8,128)(2,1)S(1)}, bf16[2,8,8,8,128]{4,3,2,1,0:T(8,128)(2,1)}, u32[]{:S(2)}) copy-start(bf16[2,8,8,8,128]{4,3,2,1,0:T(8,128)(2,1)} %get-tuple-element.39) | copy-start | bytes 786436
  54.0 8.9 %copy-start.15 = (bf16[2,8,8,8,128]{4,3,2,1,0:T(8,128)(2,1)S(1)}, bf16[2,8,8,8,128]{4,3,2,1,0:T(8,128)(2,1)}, u32[]{:S(2)}) copy-start(bf16[2,8,8,8,128]{4,3,2,1,0:T(8,128)(2,1)} %get-tuple-element.38) | copy-start | bytes 786436
  54.0 8.9 %copy-start.14 = (bf16[2,8,8,8,128]{4,3,2,1,0:T(8,128)(2,1)S(1)}, bf16[2,8,8,8,128]{4,3,2,1,0:T(8,128)(2,1)}, u32[]{:S(2)}) copy-start(bf16[2,8,8,8,128]{4,3,2,1,0:T(8,128)(2,1)} %get-tuple-element.37) | copy-start | bytes 786436
  54.1 9.0 %copy-start.13 = (bf16[2,8,8,8,128]{4,3,2,1,0:T(8,128)(2,1)S(1)}, bf16[2,8,8,8,128]{4,3,2,1,0:T(8,128)(2,1)}, u32[]{:S(2)}) copy-start(bf16[2,8,8,8,128]{4,3,2,1,0:T(8,128)(2,1)} %get-tuple-element.36) | copy-start | bytes 786436
  54.1 9.0 %copy-start.12 = (bf16[2,8,8,8,128]{4,3,2,1,0:T(8,128)(2,1)S(1)}, bf16[2,8,8,8,128]{4,3,2,1,0:T(8,128)(2,1)}, u32[]{:S(2)}) copy-start(bf16[2,8,8,8,128]{4,3,2,1,0:T(8,128)(2,1)} %get-tuple-element.35) | copy-start | bytes 786436
  54.1 9.1 %copy-start.11 = (bf16[2,8,8,8,128]{4,3,2,1,0:T(8,128)(2,1)S(1)}, bf16[2,8,8,8,128]{4,3,2,1,0:T(8,128)(2,1)}, u32[]{:S(2)}) copy-start(bf16[2,8,8,8,128]{4,3,2,1,0:T(8,128)(2,1)} %get-tuple-element.34) | copy-start | bytes 786436
  54.1 9.1 %copy-start.10 = (bf16[2,8,8,8,128]{4,3,2,1,0:T(8,128)(2,1)S(1)}, bf16[2,8,8,8,128]{4,3,2,1,0:T(8,128)(2,1)}, u32[]{:S(2)}) copy-start(bf16[2,8,8,8,128]{4,3,2,1,0:T(8,128)(2,1)} %get-tuple-element.33) | copy-start | bytes 786436
  54.1 9.2 %copy-start.9 = (bf16[2,8,8,8,128]{4,3,2,1,0:T(8,128)(2,1)S(1)}, bf16[2,8,8,8,128]{4,3,2,1,0:T(8,128)(2,1)}, u32[]{:S(2)}) copy-start(bf16[2,8,8,8,128]{4,3,2,1,0:T(8,128)(2,1)} %get-tuple-element.32) | copy-start | bytes 786436
  54.1 9.2 %copy-start.8 = (bf16[2,8,8,8,128]{4,3,2,1,0:T(8,128)(2,1)S(1)}, bf16[2,8,8,8,128]{4,3,2,1,0:T(8,128)(2,1)}, u32[]{:S(2)}) copy-start(bf16[2,8,8,8,128]{4,3,2,1,0:T(8,128)(2,1)} %get-tuple-element.31) | copy-start | bytes 786436
  54.1 9.3 %copy-start.7 = (bf16[2,8,8,8,128]{4,3,2,1,0:T(8,128)(2,1)S(1)}, bf16[2,8,8,8,128]{4,3,2,1,0:T(8,128)(2,1)}, u32[]{:S(2)}) copy-start(bf16[2,8,8,8,128]{4,3,2,1,0:T(8,128)(2,1)} %get-tuple-element.30) | copy-start | bytes 786436
  54.2 9.2 %collective-permute-start.4 = (f32[1792,128]{1,0:T(8,128)S(1)}, f32[1792,128]{1,0:T(8,128)S(1)}, u32[]{:S(2)}, u32[]{:S(2)}) collective-permute-start(f32[1792,128]{1,0:T(8,128)S(1)} %pad_dynamic-slice_fusion), channel_id=1, source_target_pairs={{0,16},{16,0},{32,48},{48,32},{64,80},{80,64},{96,112},{112,96},{1... | collective-permute-start | bytes 2752520 | tf_op jit(solution)/shard_map/ppermute | solution.py:42
  56.4 9.5 %slice-start = ((s8[7077888]{0:T(1024)(128)(4,1)}), s8[4194304]{0:T(1024)(128)(4,1)S(1)}, s32[]{:S(2)}) async-start(s8[7077888]{0:T(1024)(128)(4,1)} %bitcast.117), calls=%async_computation | async-start | bytes 8388608
  63.1 2.9 %slice-start.1 = ((s8[7077888]{0:T(1024)(128)(4,1)}), s8[2883584]{0:T(1024)(128)(4,1)S(1)}, s32[]{:S(2)}) async-start(s8[7077888]{0:T(1024)(128)(4,1)} %bitcast.117), calls=%async_computation.1 | async-start | bytes 5767168
  63.5 18.8 %copy-start.6 = (bf16[2,8,8,8,128]{4,3,2,1,0:T(8,128)(2,1)S(1)}, bf16[2,8,8,8,128]{4,3,2,1,0:T(8,128)(2,1)}, u32[]{:S(2)}) copy-start(bf16[2,8,8,8,128]{4,3,2,1,0:T(8,128)(2,1)} %get-tuple-element.29) | copy-start | bytes 786436
  63.6 18.8 %copy-start.5 = (bf16[2,8,8,8,128]{4,3,2,1,0:T(8,128)(2,1)S(1)}, bf16[2,8,8,8,128]{4,3,2,1,0:T(8,128)(2,1)}, u32[]{:S(2)}) copy-start(bf16[2,8,8,8,128]{4,3,2,1,0:T(8,128)(2,1)} %get-tuple-element.28) | copy-start | bytes 786436
  63.6 25.3 %copy-start.4 = (bf16[2,8,8,8,128]{4,3,2,1,0:T(8,128)(2,1)S(1)}, bf16[2,8,8,8,128]{4,3,2,1,0:T(8,128)(2,1)}, u32[]{:S(2)}) copy-start(bf16[2,8,8,8,128]{4,3,2,1,0:T(8,128)(2,1)} %get-tuple-element.27) | copy-start | bytes 786436
  63.6 12.7 %collective-permute-start.5 = (f32[896,128]{1,0:T(8,128)S(1)}, f32[896,128]{1,0:T(8,128)S(1)}, u32[]{:S(2)}, u32[]{:S(2)}) collective-permute-start(f32[896,128]{1,0:T(8,128)S(1)} %constant_dynamic-slice_fusion.6), channel_id=1, source_target_pairs={{0,1},{1,0},{2,3},{3,2},{4,5},{5,4},{6,7},{7,6},{8,9},{9,8},{10,11... | collective-permute-start | bytes 1376264 | tf_op jit(solution)/shard_map/ppermute | solution.py:42
  76.4 11.2 %collective-permute-start.6 = (f32[448,128]{1,0:T(8,128)S(1)}, f32[448,128]{1,0:T(8,128)S(1)}, u32[]{:S(2)}, u32[]{:S(2)}) collective-permute-start(f32[448,128]{1,0:T(8,128)S(1)} %constant_dynamic-slice_fusion.5), channel_id=1, source_target_pairs={{0,64},{16,80},{32,96},{48,112},{64,0},{80,16},{96,32},{112,48},{1... | collective-permute-start | bytes 688136 | tf_op jit(solution)/shard_map/ppermute | solution.py:42
  87.6 3.7 %collective-permute-start.7 = (f32[224,128]{1,0:T(8,128)S(1)}, f32[224,128]{1,0:T(8,128)S(1)}, u32[]{:S(2)}, u32[]{:S(2)}) collective-permute-start(f32[224,128]{1,0:T(8,128)S(1)} %constant_dynamic-slice_fusion.4), channel_id=1, source_target_pairs={{0,2},{1,3},{2,0},{3,1},{4,6},{5,7},{6,4},{7,5},{8,10},{9,11},{10,... | collective-permute-start | bytes 344072 | tf_op jit(solution)/shard_map/ppermute | solution.py:42
  91.4 5.6 %collective-permute-start.8 = (f32[112,128]{1,0:T(8,128)S(1)}, f32[112,128]{1,0:T(8,128)S(1)}, u32[]{:S(2)}, u32[]{:S(2)}) collective-permute-start(f32[112,128]{1,0:T(8,128)S(1)} %constant_dynamic-slice_fusion.3), channel_id=1, source_target_pairs={{0,32},{16,48},{32,0},{48,16},{64,96},{80,112},{96,64},{112,80},{1... | collective-permute-start | bytes 172040 | tf_op jit(solution)/shard_map/ppermute | solution.py:42
  97.0 4.3 %collective-permute-start.9 = (f32[56,128]{1,0:T(8,128)S(1)}, f32[56,128]{1,0:T(8,128)S(1)}, u32[]{:S(2)}, u32[]{:S(2)}) collective-permute-start(f32[56,128]{1,0:T(8,128)S(1)} %constant_dynamic-slice_fusion.2), channel_id=1, source_target_pairs={{0,128},{16,144},{32,160},{48,176},{64,192},{80,208},{96,224},{112... | collective-permute-start | bytes 86024 | tf_op jit(solution)/shard_map/ppermute | solution.py:42
  101.4 5.4 %collective-permute-start.10 = (f32[28,128]{1,0:T(8,128)S(1)}, f32[28,128]{1,0:T(8,128)S(1)}, u32[]{:S(2)}, u32[]{:S(2)}) collective-permute-start(f32[28,128]{1,0:T(8,128)S(1)} %constant_dynamic-slice_fusion.1), channel_id=1, source_target_pairs={{0,4},{1,5},{2,6},{3,7},{4,0},{5,1},{6,2},{7,3},{8,12},{9,13},{10,... | collective-permute-start | bytes 43016 | tf_op jit(solution)/shard_map/ppermute | solution.py:42
  106.8 7.9 %collective-permute-start.11 = (f32[14,128]{1,0:T(8,128)S(1)}, f32[14,128]{1,0:T(8,128)S(1)}, u32[]{:S(2)}, u32[]{:S(2)}) collective-permute-start(f32[14,128]{1,0:T(8,128)S(1)} %constant_dynamic-slice_fusion), channel_id=1, source_target_pairs={{0,8},{1,9},{2,10},{3,11},{4,12},{5,13},{6,14},{7,15},{8,0},{9,1},... | collective-permute-start | bytes 21512 | tf_op jit(solution)/shard_map/ppermute | solution.py:42
  114.8 6.5 %collective-permute-start.12 = (f32[14,128]{1,0:T(8,128)S(1)}, f32[14,128]{1,0:T(8,128)S(1)}, u32[]{:S(2)}, u32[]{:S(2)}) collective-permute-start(f32[14,128]{1,0:T(8,128)S(1)} %dynamic-slice_add_fusion.6), channel_id=1, source_target_pairs={{0,8},{1,9},{2,10},{3,11},{4,12},{5,13},{6,14},{7,15},{8,0},{9,1},... | collective-permute-start | bytes 21512 | tf_op jit(solution)/shard_map/ppermute | solution.py:50
  121.3 3.6 %collective-permute-start.13 = (f32[28,128]{1,0:T(8,128)S(1)}, f32[28,128]{1,0:T(8,128)S(1)}, u32[]{:S(2)}, u32[]{:S(2)}) collective-permute-start(f32[28,128]{1,0:T(8,128)S(1)} %pad_maximum_fusion.11), channel_id=1, source_target_pairs={{0,4},{1,5},{2,6},{3,7},{4,0},{5,1},{6,2},{7,3},{8,12},{9,13},{10,... | collective-permute-start | bytes 43016 | tf_op jit(solution)/shard_map/ppermute | solution.py:50
  124.9 4.3 %collective-permute-start.14 = (f32[56,128]{1,0:T(8,128)S(1)}, f32[56,128]{1,0:T(8,128)S(1)}, u32[]{:S(2)}, u32[]{:S(2)}) collective-permute-start(f32[56,128]{1,0:T(8,128)S(1)} %pad_maximum_fusion.10), channel_id=1, source_target_pairs={{0,128},{16,144},{32,160},{48,176},{64,192},{80,208},{96,224},{112... | collective-permute-start | bytes 86024 | tf_op jit(solution)/shard_map/ppermute | solution.py:50
  129.3 4.6 %collective-permute-start.15 = (f32[112,128]{1,0:T(8,128)S(1)}, f32[112,128]{1,0:T(8,128)S(1)}, u32[]{:S(2)}, u32[]{:S(2)}) collective-permute-start(f32[112,128]{1,0:T(8,128)S(1)} %pad_maximum_fusion.9), channel_id=1, source_target_pairs={{0,32},{16,48},{32,0},{48,16},{64,96},{80,112},{96,64},{112,80},{1... | collective-permute-start | bytes 172040 | tf_op jit(solution)/shard_map/ppermute | solution.py:50
  133.9 4.0 %collective-permute-start.16 = (f32[224,128]{1,0:T(8,128)S(1)}, f32[224,128]{1,0:T(8,128)S(1)}, u32[]{:S(2)}, u32[]{:S(2)}) collective-permute-start(f32[224,128]{1,0:T(8,128)S(1)} %pad_maximum_fusion.8), channel_id=1, source_target_pairs={{0,2},{1,3},{2,0},{3,1},{4,6},{5,7},{6,4},{7,5},{8,10},{9,11},{10,... | collective-permute-start | bytes 344072 | tf_op jit(solution)/shard_map/ppermute | solution.py:50
  138.0 5.3 %collective-permute-start.17 = (f32[448,128]{1,0:T(8,128)S(1)}, f32[448,128]{1,0:T(8,128)S(1)}, u32[]{:S(2)}, u32[]{:S(2)}) collective-permute-start(f32[448,128]{1,0:T(8,128)S(1)} %pad_maximum_fusion.7), channel_id=1, source_target_pairs={{0,64},{16,80},{32,96},{48,112},{64,0},{80,16},{96,32},{112,48},{1... | collective-permute-start | bytes 688136 | tf_op jit(solution)/shard_map/ppermute | solution.py:50
  143.3 7.4 %collective-permute-start.18 = (f32[896,128]{1,0:T(8,128)S(1)}, f32[896,128]{1,0:T(8,128)S(1)}, u32[]{:S(2)}, u32[]{:S(2)}) collective-permute-start(f32[896,128]{1,0:T(8,128)S(1)} %pad_maximum_fusion.3), channel_id=1, source_target_pairs={{0,1},{1,0},{2,3},{3,2},{4,5},{5,4},{6,7},{7,6},{8,9},{9,8},{10,11... | collective-permute-start | bytes 1376264 | tf_op jit(solution)/shard_map/ppermute | solution.py:50
  150.9 15.6 %collective-permute-start.19 = (f32[1792,128]{1,0:T(8,128)S(1)}, f32[1792,128]{1,0:T(8,128)}, u32[]{:S(2)}, u32[]{:S(2)}) collective-permute-start(f32[1792,128]{1,0:T(8,128)S(1)} %pad_maximum_fusion.1), channel_id=1, source_target_pairs={{0,16},{16,0},{32,48},{48,32},{64,80},{80,64},{96,112},{112,96},{1... | collective-permute-start | bytes 2752520 | tf_op jit(solution)/shard_map/ppermute | solution.py:50

commit v4 on v3

--- a/solution.py
+++ b/solution.py
@@ -10,17 +10,23 @@
 OFFS = 27
 
 
-def with_halo(value, sides, width):
+def with_halo(value, sides):
+    pads = [(0, 0)] * value.ndim
+    for _, dim in sides:
+        pads[dim] = (1, 1)
+    pads[-2] = (1, 1)
+    padded = jnp.pad(value, pads)
     for axis, dim in sides:
-        size, length = (lax.axis_size(axis), value.shape[dim])
+        size, length = lax.axis_size(axis), padded.shape[dim]
         up = [(i, (i + 1) % size) for i in range(size - 1)]
         down = [(j, i) for i, j in up]
-        last = lax.slice_in_dim(value, length - width, length, axis=dim)
-        leading = lax.slice_in_dim(value, 0, width, axis=dim)
-        before = lax.ppermute(last, axis, up)
-        after = lax.ppermute(leading, axis, down)
-        value = jnp.concatenate([before, value, after], axis=dim)
-    return value
+        last = lax.slice_in_dim(padded, length - 2, length - 1, axis=dim)
+        leading = lax.slice_in_dim(padded, 1, 2, axis=dim)
+        padded = lax.dynamic_update_slice_in_dim(padded, lax.ppermute(last, axis, up), 0, axis=dim)
+        padded = lax.dynamic_update_slice_in_dim(
+            padded, lax.ppermute(leading, axis, down), length - 1, axis=dim
+        )
+    return padded
 
 
 STEPS = (("gx", 0), ("gy", 0), ("gx", 2), ("gy", 1), ("gx", 1), ("gx", 3), ("gy", 2), ("gy", 3))
@@ -65,7 +71,6 @@
 
 
 def cut_windows(padded, places):
-    padded = jnp.pad(padded, ((0, 0), (0, 0), (0, 0), (1, 1), (0, 0)))
     kinds, chans = padded.shape[0], padded.shape[-1]
     windows = []
     for slot in range(places.shape[0]):
@@ -96,11 +101,12 @@
     both = jnp.stack([features[0, 0], cotangent[0, 0]]) * keeper[None, :, :, None]
     grad_rows = both[1].reshape(-1, chans)
     dense = place_bricks(both, places, alive)
-    padded = with_halo(dense, (("gx", 1), ("gy", 2)), 1)
+    padded = with_halo(dense, (("gx", 1), ("gy", 2)))
     windows = cut_windows(padded, places)
     feat_stack = stack_offsets(windows[0])
-    weight_local = jnp.einsum("ve,dvc->edc", grad_rows, feat_stack, preferred_element_type=jnp.float32)
     tiles = lax.axis_size("gx") * lax.axis_size("gy")
+    weight_local = jnp.einsum("ve,dvc->dec", grad_rows, feat_stack, preferred_element_type=jnp.float32)
+    weight_local = weight_local * jnp.float32(1.0 / tiles)
     half_done = butterfly_scatter(weight_local)
     output_sum = jnp.einsum("dvc,dce->ve", feat_stack, weight, preferred_element_type=jnp.float32)
     output_rows = (output_sum * keeper_rows).astype(jnp.bfloat16)
@@ -109,7 +115,7 @@
     input_rows = (input_sum * keeper_rows).astype(jnp.bfloat16)
     half_done, output_rows, input_rows = lax.optimization_barrier((half_done, output_rows, input_rows))
     weight_total = butterfly_gather(half_done, weight_local)
-    weight_grad = weight_total.transpose(1, 2, 0) / jnp.float32(tiles)
+    weight_grad = weight_total.transpose(0, 2, 1)
     output = output_rows.reshape(1, 1, slots, -1, chans)
     input_grad = input_rows.reshape(1, 1, slots, -1, chans)
     return (output, input_grad, weight_grad)

time: 173 us -> 166 us (0.960)
  other arithmetic: 13 us -> 4.23 us
  local copies, waits for them, and re-layouts: 27.7 us -> 22.6 us
  waiting for transfers between devices: 49.7 us -> 54.6 us
  starting transfers between devices: 65.5 us -> 68.4 us
    unnamed x103 -> x63, local copies, waits for them, and re-layouts: 13.5 us -> 3.83 us
    concatenate x1 -> x0, other arithmetic: 7.54 us -> none  [with_halo(): value = jnp.concatenate([before, value, after], axis=dim)]
    pad x0 -> x1, local copies, waits for them, and re-layouts: none -> 5.22 us  [with_halo(): padded = jnp.pad(value, pads)]
    slice x1 -> x3, local copies, waits for them, and re-layouts: 0.04 us -> 3.19 us  [the longest x2 2.16 us: with_halo(): leading = lax.slice_in_dim(padded, 1, 2, axis=dim)]
    ppermute x8, waiting for transfers between devices: 19.2 us -> 22.2 us  [butterfly_scatter(): buf = keep + lax.ppermute(send, axis, pairs)]
    ppermute x4, waiting for transfers between devices: 5.2 us -> 8.01 us  [the longest x2 4.41 us: with_halo(): lax.ppermute(last, axis, up)]
    dynamic_update_slice x0 -> x3, local copies, waits for them, and re-layouts: none -> 2.48 us  [the longest x2 1.67 us: with_halo(): lax.dynamic_update_slice_in_dim(padded, lax.ppermute(leading, axis, down)...]
    dot_general x1 -> x0, local copies, waits for them, and re-layouts: 2.44 us -> none  [local(): jnp.einsum('ve,dvc->edc', grad_rows, feat_stack, preferred_element_type=j...]
  transfers between devices with their start and end apart: 20 -> 20, of which waited for: 17 -> 18; matrix products, arithmetic and copies ran while one was open for 9% -> 8% of each run, Pallas kernels for 0% -> 0%
where the time goes in v4:
time: 166 us
  starting transfers between devices  68.4 us (41%)
  waiting for transfers between devices  54.6 us (33%)
  local copies, waits for them, and re-layouts  22.6 us (14%)
  matrix products  8.6 us (5%)
  between operations  7.51 us (5%)
  other arithmetic  4.23 us (3%)
    ppermute x8, starting transfers between devices, butterfly_scatter(): buf = keep + lax.ppermute(send, axis, pairs)  28.4 us
    ppermute x8, starting transfers between devices, butterfly_gather(): got = lax.ppermute(buf, axis, pairs)  27.8 us
    ppermute x8, waiting for transfers between devices, butterfly_gather(): got = lax.ppermute(buf, axis, pairs)  24.4 us
    ppermute x8, waiting for transfers between devices, butterfly_scatter(): buf = keep + lax.ppermute(send, axis, pairs)  22.2 us
    ppermute x2, starting transfers between devices, with_halo(): lax.ppermute(last, axis, up)  8.87 us
    pad x1, local copies, waits for them, and re-layouts, with_halo(): padded = jnp.pad(value, pads)  5.22 us
    ppermute x2, waiting for transfers between devices, with_halo(): lax.ppermute(last, axis, up)  4.41 us
    unnamed x63, local copies, waits for them, and re-layouts  3.83 us
  transfers between devices with their start and end apart: 20, of which 18 were waited for; matrix products, arithmetic and copies ran while one was open for 8% of the time, Pallas kernels for 0%

profile of v4, /device:TPU:1, one launch (start us, length us, event | category | flops | bytes accessed | tf_op | source)
XLA Modules:
  0.0 165.8 jit_solution(17669431996447814010)
XLA Ops:
  1.4 0.8 broadcast_bitcast_fusion
  2.1 1.2 maximum_multiply_fusion
  3.4 2.0 %convolution_convert_fusion = bf16[2,512,128,16]{2,3,1,0:T(8,128)(2,1)S(1)} fusion(bf16[2,2,512,128]{3,2,1,0:T(8,128)(2,1)S(1)} %maximum_multiply_fusion, pred[2]{0:T(512)(128)(4,1)S(1)} %get-tuple-element.94, s32[2]{0:T(128)} %bitcast.185), kind=kOutput, calls=%fused_computation | convolution fusion | flops 10485824 | bytes 4718602 | tf_op jit(solution)/shard_map/ps,tsvc->tpvc/dot_general | solution.py:64
  5.4 1.6 copy.12
  7.1 0.2 pad_slice_fusion.2
  7.3 6.0 %collective-permute-start = (bf16[2,1,18,34,128]{4,3,2,1,0:T(8,128)(2,1)S(1)}, bf16[2,1,18,34,128]{4,3,2,1,0:T(8,128)(2,1)S(1)}, u32[]{:S(2)}, u32[]{:S(2)}) collective-permute-start(bf16[2,1,18,34,128]{4,3,2,1,0:T(8,128)(2,1)S(1)} %get-tuple-element.17), channel_id=1, source_target_pairs={{0,16},{16,32},{32,48},{48,64},{64,80},{80,96},{96,112},{112,128},... | collective-permute-start | bytes 940040 | tf_op jit(solution)/shard_map/ppermute | solution.py:25
  13.4 1.9 %collective-permute-start.1 = (bf16[2,1,18,34,128]{4,3,2,1,0:T(8,128)(2,1)S(1)}, bf16[2,1,18,34,128]{4,3,2,1,0:T(8,128)(2,1)S(1)}, u32[]{:S(2)}, u32[]{:S(2)}) collective-permute-start(bf16[2,1,18,34,128]{4,3,2,1,0:T(8,128)(2,1)S(1)} %get-tuple-element.16), channel_id=1, source_target_pairs={{16,0},{32,16},{48,32},{64,48},{80,64},{96,80},{112,96},{128,112},... | collective-permute-start | bytes 940040 | tf_op jit(solution)/shard_map/ppermute | solution.py:27
  15.3 5.2 %pad.8 = bf16[2,18,18,34,128]{4,3,2,1,0:T(8,128)(2,1)} pad(bf16[2,16,16,32,128]{4,3,2,1,0:T(8,128)(2,1)S(1)} %bitcast.120, bf16[]{:T(256)} %constant.82.clone.1), padding=0_0x1_1x1_1x1_1x0_0 | pad | bytes 9834498 | tf_op jit(solution)/shard_map/jit(_pad)/pad | solution.py:18
  20.5 0.8 constant_dynamic-update-slice_fusion.57
  21.3 2.4 %collective-permute-done.1 = bf16[2,1,18,34,128]{4,3,2,1,0:T(8,128)(2,1)S(1)} collective-permute-done((bf16[2,1,18,34,128]{4,3,2,1,0:T(8,128)(2,1)S(1)}, bf16[2,1,18,34,128]{4,3,2,1,0:T(8,128)(2,1)S(1)}, u32[]{:S(2)}, u32[]{:S(2)}) %collective-permute-start.1) | collective-permute-done | bytes 313376 | tf_op jit(solution)/shard_map/ppermute | solution.py:27
  23.7 0.8 constant_dynamic-update-slice_fusion.56
  24.5 1.0 slice.259
  25.5 2.8 %collective-permute-start.2 = (bf16[2,18,1,34,128]{4,3,2,1,0:T(8,128)(2,1)S(1)}, bf16[2,18,1,34,128]{4,3,2,1,0:T(8,128)(2,1)S(1)}, u32[]{:S(2)}, u32[]{:S(2)}) collective-permute-start(bf16[2,18,1,34,128]{4,3,2,1,0:T(8,128)(2,1)S(1)} %slice.259), channel_id=1, source_target_pairs={{0,1},{1,2},{2,3},{3,4},{4,5},{5,6},{6,7},{7,8},{8,9},{9,10},{10,1... | collective-permute-start | bytes 940040 | tf_op jit(solution)/shard_map/ppermute | solution.py:25
  28.4 4.4 %collective-permute-done.2 = bf16[2,18,1,34,128]{4,3,2,1,0:T(8,128)(2,1)S(1)} collective-permute-done((bf16[2,18,1,34,128]{4,3,2,1,0:T(8,128)(2,1)S(1)}, bf16[2,18,1,34,128]{4,3,2,1,0:T(8,128)(2,1)S(1)}, u32[]{:S(2)}, u32[]{:S(2)}) %collective-permute-start.2) | collective-permute-done | bytes 313376 | tf_op jit(solution)/shard_map/ppermute | solution.py:25
  32.8 2.0 %fusion.18 = (bf16[2,18,1,34,128]{4,3,2,1,0:T(8,128)(2,1)S(1)}, bf16[2,18,18,34,128]{4,3,2,1,0:T(8,128)(2,1)}) fusion(bf16[2,18,18,34,128]{4,3,2,1,0:T(8,128)(2,1)} %constant_dynamic-update-slice_fusion.56, bf16[2,18,1,34,128]{4,3,2,1,0:T(8,128)(2,1)S(1)} %collective-permute-done.2), kind=kLoop, calls=%fused_computation.132 | loop fusion | bytes 1363968 | tf_op jit(solution)/shard_map/slice | solution.py:24
  34.8 1.5 collective-permute-start.3
  36.2 0.6 fusion.23
  42.2 1.2 collective-permute-done.3
  43.5 0.9 constant_dynamic-update-slice_fusion.54
  44.3 2.4 %dynamic-slice_bitcast_fusion = (bf16[2,1,10,10,10,128]{5,4,3,2,1,0:T(8,128)(2,1)S(1)}, bf16[2,1,10,10,10,128]{5,4,3,2,1,0:T(8,128)(2,1)S(1)}) fusion(bf16[2,18,18,34,128]{4,3,2,1,0:T(8,128)(2,1)} %constant_dynamic-update-slice_fusion.54, s32[]{:T(128)S(6)} %select_n.202, s32[]{:T(128)S(6)} %select_n.205, s32[]{:T(128)S(6)} %select_n.207, s32[]{:T(128)S(6)} %select_n.195, ...), kind=kLoop, calls=%fused_computation.21 | loop fusion | bytes 2048024 | tf_op jit(solution)/shard_map/stack | solution.py:82
  46.7 0.3 fusion.7
  47.0 0.4 fusion.22
  47.4 1.0 fusion.21
  48.5 0.5 fusion.20
  48.9 1.0 fusion.19
  51.2 1.1 convolution_multiply_fusion
  52.3 0.1 pad_dynamic-slice_fusion
  52.4 0.1 collective-permute-start.4
  53.4 1.5 collective-permute-done.4
  55.0 0.1 fusion.4
  55.2 2.8 %collective-permute-start.5 = (f32[896,128]{1,0:T(8,128)S(1)}, f32[896,128]{1,0:T(8,128)S(1)}, u32[]{:S(2)}, u32[]{:S(2)}) collective-permute-start(f32[896,128]{1,0:T(8,128)S(1)} %constant_dynamic-slice_fusion.6), channel_id=1, source_target_pairs={{0,1},{1,0},{2,3},{3,2},{4,5},{5,4},{6,7},{7,6},{8,9},{9,8},{10,11... | collective-permute-start | bytes 1376264 | tf_op jit(solution)/shard_map/ppermute | solution.py:48
  57.9 2.7 %fusion.2 = bf16[1024,128]{1,0:T(8,128)(2,1)} fusion(bf16[27,1024,128]{2,1,0:T(8,128)(2,1)S(1)} %constant_dynamic-update-slice_fusion, bf16[27,128,128]{2,1,0:T(8,128)(2,1)S(1)} %copy-done, f32[1024]{0:T(1024)S(1)} %fusion.10), kind=kOutput, calls=%fused_computation.11 | convolution fusion | flops 906231808 | bytes 8228864 | tf_op jit(solution)/shard_map/dvc,dce->ve/dot_general | solution.py:111
  60.6 8.0 %collective-permute-done.5 = f32[896,128]{1,0:T(8,128)S(1)} collective-permute-done((f32[896,128]{1,0:T(8,128)S(1)}, f32[896,128]{1,0:T(8,128)S(1)}, u32[]{:S(2)}, u32[]{:S(2)}) %collective-permute-start.5) | collective-permute-done | bytes 458784 | tf_op jit(solution)/shard_map/ppermute | solution.py:48
  68.8 9.1 %collective-permute-start.6 = (f32[448,128]{1,0:T(8,128)S(1)}, f32[448,128]{1,0:T(8,128)S(1)}, u32[]{:S(2)}, u32[]{:S(2)}) collective-permute-start(f32[448,128]{1,0:T(8,128)S(1)} %constant_dynamic-slice_fusion.5), channel_id=1, source_target_pairs={{0,64},{16,80},{32,96},{48,112},{64,0},{80,16},{96,32},{112,48},{1... | collective-permute-start | bytes 688136 | tf_op jit(solution)/shard_map/ppermute | solution.py:48
  78.0 5.0 %collective-permute-done.6 = f32[448,128]{1,0:T(8,128)S(1)} collective-permute-done((f32[448,128]{1,0:T(8,128)S(1)}, f32[448,128]{1,0:T(8,128)S(1)}, u32[]{:S(2)}, u32[]{:S(2)}) %collective-permute-start.6) | collective-permute-done | bytes 229408 | tf_op jit(solution)/shard_map/ppermute | solution.py:48
  83.0 1.5 collective-permute-start.7
  84.5 2.2 %collective-permute-done.7 = f32[224,128]{1,0:T(8,128)S(1)} collective-permute-done((f32[224,128]{1,0:T(8,128)S(1)}, f32[224,128]{1,0:T(8,128)S(1)}, u32[]{:S(2)}, u32[]{:S(2)}) %collective-permute-start.7) | collective-permute-done | bytes 114720 | tf_op jit(solution)/shard_map/ppermute | solution.py:48
  86.7 1.7 %collective-permute-start.8 = (f32[112,128]{1,0:T(8,128)S(1)}, f32[112,128]{1,0:T(8,128)S(1)}, u32[]{:S(2)}, u32[]{:S(2)}) collective-permute-start(f32[112,128]{1,0:T(8,128)S(1)} %constant_dynamic-slice_fusion.3), channel_id=1, source_target_pairs={{0,32},{16,48},{32,0},{48,16},{64,96},{80,112},{96,64},{112,80},{1... | collective-permute-start | bytes 172040 | tf_op jit(solution)/shard_map/ppermute | solution.py:48
  88.4 2.9 %collective-permute-done.8 = f32[112,128]{1,0:T(8,128)S(1)} collective-permute-done((f32[112,128]{1,0:T(8,128)S(1)}, f32[112,128]{1,0:T(8,128)S(1)}, u32[]{:S(2)}, u32[]{:S(2)}) %collective-permute-start.8) | collective-permute-done | bytes 57376 | tf_op jit(solution)/shard_map/ppermute | solution.py:48
  91.4 2.9 %collective-permute-start.9 = (f32[56,128]{1,0:T(8,128)S(1)}, f32[56,128]{1,0:T(8,128)S(1)}, u32[]{:S(2)}, u32[]{:S(2)}) collective-permute-start(f32[56,128]{1,0:T(8,128)S(1)} %constant_dynamic-slice_fusion.2), channel_id=1, source_target_pairs={{0,128},{16,144},{32,160},{48,176},{64,192},{80,208},{96,224},{112... | collective-permute-start | bytes 86024 | tf_op jit(solution)/shard_map/ppermute | solution.py:48
  94.3 1.4 collective-permute-done.9
  95.7 5.9 %collective-permute-start.10 = (f32[28,128]{1,0:T(8,128)S(1)}, f32[28,128]{1,0:T(8,128)S(1)}, u32[]{:S(2)}, u32[]{:S(2)}) collective-permute-start(f32[28,128]{1,0:T(8,128)S(1)} %constant_dynamic-slice_fusion.1), channel_id=1, source_target_pairs={{0,4},{1,5},{2,6},{3,7},{4,0},{5,1},{6,2},{7,3},{8,12},{9,13},{10,... | collective-permute-start | bytes 43016 | tf_op jit(solution)/shard_map/ppermute | solution.py:48
  101.6 1.1 collective-permute-done.10
  102.8 4.5 %collective-permute-start.11 = (f32[14,128]{1,0:T(8,128)S(1)}, f32[14,128]{1,0:T(8,128)S(1)}, u32[]{:S(2)}, u32[]{:S(2)}) collective-permute-start(f32[14,128]{1,0:T(8,128)S(1)} %constant_dynamic-slice_fusion), channel_id=1, source_target_pairs={{0,8},{1,9},{2,10},{3,11},{4,12},{5,13},{6,14},{7,15},{8,0},{9,1},... | collective-permute-start | bytes 21512 | tf_op jit(solution)/shard_map/ppermute | solution.py:48
  107.3 2.7 %fusion.3 = bf16[1024,128]{1,0:T(8,128)(2,1)} fusion(bf16[27,1024,128]{2,1,0:T(8,128)(2,1)S(1)} %constant_dynamic-update-slice_fusion.27, bf16[27,128,128]{2,1,0:T(8,128)(2,1)S(1)} %copy-done, f32[1024]{0:T(1024)S(1)} %fusion.10), kind=kOutput, calls=%fused_computation.12 | convolution fusion | flops 906231808 | bytes 8228864 | tf_op jit(solution)/shard_map/dvc,dec->ve/dot_general | solution.py:114
  110.0 3.8 %collective-permute-start.12 = (f32[14,128]{1,0:T(8,128)S(1)}, f32[14,128]{1,0:T(8,128)S(1)}, u32[]{:S(2)}, u32[]{:S(2)}) collective-permute-start(f32[14,128]{1,0:T(8,128)S(1)} %dynamic-slice_add_fusion.6), channel_id=1, source_target_pairs={{0,8},{1,9},{2,10},{3,11},{4,12},{5,13},{6,14},{7,15},{8,0},{9,1},... | collective-permute-start | bytes 21512 | tf_op jit(solution)/shard_map/ppermute | solution.py:56
  113.8 2.7 %collective-permute-done.12 = f32[14,128]{1,0:T(8,128)S(1)} collective-permute-done((f32[14,128]{1,0:T(8,128)S(1)}, f32[14,128]{1,0:T(8,128)S(1)}, u32[]{:S(2)}, u32[]{:S(2)}) %collective-permute-start.12) | collective-permute-done | bytes 7200 | tf_op jit(solution)/shard_map/ppermute | solution.py:56
  116.5 2.0 %collective-permute-start.13 = (f32[28,128]{1,0:T(8,128)S(1)}, f32[28,128]{1,0:T(8,128)S(1)}, u32[]{:S(2)}, u32[]{:S(2)}) collective-permute-start(f32[28,128]{1,0:T(8,128)S(1)} %pad_maximum_fusion.8), channel_id=1, source_target_pairs={{0,4},{1,5},{2,6},{3,7},{4,0},{5,1},{6,2},{7,3},{8,12},{9,13},{10,... | collective-permute-start | bytes 43016 | tf_op jit(solution)/shard_map/ppermute | solution.py:56
  118.5 1.6 collective-permute-done.13
  120.1 2.9 %collective-permute-start.14 = (f32[56,128]{1,0:T(8,128)S(1)}, f32[56,128]{1,0:T(8,128)S(1)}, u32[]{:S(2)}, u32[]{:S(2)}) collective-permute-start(f32[56,128]{1,0:T(8,128)S(1)} %pad_maximum_fusion.7), channel_id=1, source_target_pairs={{0,128},{16,144},{32,160},{48,176},{64,192},{80,208},{96,224},{112... | collective-permute-start | bytes 86024 | tf_op jit(solution)/shard_map/ppermute | solution.py:56
  123.0 1.4 collective-permute-done.14
  124.4 1.7 %collective-permute-start.15 = (f32[112,128]{1,0:T(8,128)S(1)}, f32[112,128]{1,0:T(8,128)S(1)}, u32[]{:S(2)}, u32[]{:S(2)}) collective-permute-start(f32[112,128]{1,0:T(8,128)S(1)} %pad_maximum_fusion.6), channel_id=1, source_target_pairs={{0,32},{16,48},{32,0},{48,16},{64,96},{80,112},{96,64},{112,80},{1... | collective-permute-start | bytes 172040 | tf_op jit(solution)/shard_map/ppermute | solution.py:56
  126.1 2.9 %collective-permute-done.15 = f32[112,128]{1,0:T(8,128)S(1)} collective-permute-done((f32[112,128]{1,0:T(8,128)S(1)}, f32[112,128]{1,0:T(8,128)S(1)}, u32[]{:S(2)}, u32[]{:S(2)}) %collective-permute-start.15) | collective-permute-done | bytes 57376 | tf_op jit(solution)/shard_map/ppermute | solution.py:56
  129.1 1.2 collective-permute-start.16
  130.3 2.8 %collective-permute-done.16 = f32[224,128]{1,0:T(8,128)S(1)} collective-permute-done((f32[224,128]{1,0:T(8,128)S(1)}, f32[224,128]{1,0:T(8,128)S(1)}, u32[]{:S(2)}, u32[]{:S(2)}) %collective-permute-start.16) | collective-permute-done | bytes 114720 | tf_op jit(solution)/shard_map/ppermute | solution.py:56
  133.2 1.0 collective-permute-start.17
  134.1 4.0 %collective-permute-done.17 = f32[448,128]{1,0:T(8,128)S(1)} collective-permute-done((f32[448,128]{1,0:T(8,128)S(1)}, f32[448,128]{1,0:T(8,128)S(1)}, u32[]{:S(2)}, u32[]{:S(2)}) %collective-permute-start.17) | collective-permute-done | bytes 229408 | tf_op jit(solution)/shard_map/ppermute | solution.py:56
  138.2 0.6 collective-permute-start.18
  138.8 6.8 %collective-permute-done.18 = f32[896,128]{1,0:T(8,128)S(1)} collective-permute-done((f32[896,128]{1,0:T(8,128)S(1)}, f32[896,128]{1,0:T(8,128)S(1)}, u32[]{:S(2)}, u32[]{:S(2)}) %collective-permute-start.18) | collective-permute-done | bytes 458784 | tf_op jit(solution)/shard_map/ppermute | solution.py:56
  145.7 14.5 %collective-permute-start.19 = (f32[1792,128]{1,0:T(8,128)S(1)}, f32[1792,128]{1,0:T(8,128)}, u32[]{:S(2)}, u32[]{:S(2)}) collective-permute-start(f32[1792,128]{1,0:T(8,128)S(1)} %pad_maximum_fusion.1), channel_id=1, source_target_pairs={{0,16},{16,0},{32,48},{48,32},{64,80},{80,64},{96,112},{112,96},{1... | collective-permute-start | bytes 2752520 | tf_op jit(solution)/shard_map/ppermute | solution.py:56
  160.3 2.2 %collective-permute-done.19 = f32[1792,128]{1,0:T(8,128)} collective-permute-done((f32[1792,128]{1,0:T(8,128)S(1)}, f32[1792,128]{1,0:T(8,128)}, u32[]{:S(2)}, u32[]{:S(2)}) %collective-permute-start.19) | collective-permute-done | bytes 917536 | tf_op jit(solution)/shard_map/ppermute | solution.py:56
  162.5 1.3 broadcast_select_fusion.1
  163.8 0.1 pad_maximum_fusion
  163.9 1.9 %copy.14 = f32[27,128,128]{2,1,0:T(8,128)} copy(f32[27,128,128]{1,2,0:T(8,128)S(1)} %bitcast.124) | data formatting | bytes 3538944
  (98 shorter events, 2.5 us)
Async XLA Ops:
  0.6 57.3 %copy-start = (bf16[27,128,128]{2,1,0:T(8,128)(2,1)S(1)}, bf16[27,128,128]{2,1,0:T(8,128)(2,1)}, u32[]{:S(2)}) copy-start(bf16[27,128,128]{2,1,0:T(8,128)(2,1)} %param.10) | copy-start | bytes 2654212
  3.4 25.0 %copy-start.1 = (bf16[2,2,512,128]{3,2,1,0:T(8,128)(2,1)}, bf16[2,2,512,128]{3,2,1,0:T(8,128)(2,1)S(1)}, u32[]{:S(2)}) copy-start(bf16[2,2,512,128]{3,2,1,0:T(8,128)(2,1)S(1)} %maximum_multiply_fusion) | copy-start | bytes 1572868
  7.3 13.2 %collective-permute-start = (bf16[2,1,18,34,128]{4,3,2,1,0:T(8,128)(2,1)S(1)}, bf16[2,1,18,34,128]{4,3,2,1,0:T(8,128)(2,1)S(1)}, u32[]{:S(2)}, u32[]{:S(2)}) collective-permute-start(bf16[2,1,18,34,128]{4,3,2,1,0:T(8,128)(2,1)S(1)} %get-tuple-element.17), channel_id=1, source_target_pairs={{0,16},{16,32},{32,48},{48,64},{64,80},{80,96},{96,112},{112,128},... | collective-permute-start | bytes 940040 | tf_op jit(solution)/shard_map/ppermute | solution.py:25
  13.3 22.9 %copy-start.3 = (s32[1,1,2]{2,1,0:T(1,128)S(1)}, s32[1,1,2]{2,1,0:T(1,128)}, u32[]{:S(2)}) copy-start(s32[1,1,2]{2,1,0:T(1,128)} %param.8) | copy-start | bytes 28
  13.3 28.8 %copy-start.2 = (s32[1,1,2,512]{3,2,1,0:T(2,128)S(1)}, s32[1,1,2,512]{3,2,1,0:T(2,128)}, u32[]{:S(2)}) copy-start(s32[1,1,2,512]{3,2,1,0:T(2,128)} %param.7) | copy-start | bytes 12292
  13.4 10.3 %collective-permute-start.1 = (bf16[2,1,18,34,128]{4,3,2,1,0:T(8,128)(2,1)S(1)}, bf16[2,1,18,34,128]{4,3,2,1,0:T(8,128)(2,1)S(1)}, u32[]{:S(2)}, u32[]{:S(2)}) collective-permute-start(bf16[2,1,18,34,128]{4,3,2,1,0:T(8,128)(2,1)S(1)} %get-tuple-element.16), channel_id=1, source_target_pairs={{16,0},{32,16},{48,32},{64,48},{80,64},{96,80},{112,96},{128,112},... | collective-permute-start | bytes 940040 | tf_op jit(solution)/shard_map/ppermute | solution.py:27
  25.5 7.3 %collective-permute-start.2 = (bf16[2,18,1,34,128]{4,3,2,1,0:T(8,128)(2,1)S(1)}, bf16[2,18,1,34,128]{4,3,2,1,0:T(8,128)(2,1)S(1)}, u32[]{:S(2)}, u32[]{:S(2)}) collective-permute-start(bf16[2,18,1,34,128]{4,3,2,1,0:T(8,128)(2,1)S(1)} %slice.259), channel_id=1, source_target_pairs={{0,1},{1,2},{2,3},{3,4},{4,5},{5,6},{6,7},{7,8},{8,9},{9,10},{10,1... | collective-permute-start | bytes 940040 | tf_op jit(solution)/shard_map/ppermute | solution.py:25
  34.8 8.7 %collective-permute-start.3 = (bf16[2,18,1,34,128]{4,3,2,1,0:T(8,128)(2,1)S(1)}, bf16[2,18,1,34,128]{4,3,2,1,0:T(8,128)(2,1)S(1)}, u32[]{:S(2)}, u32[]{:S(2)}) collective-permute-start(bf16[2,18,1,34,128]{4,3,2,1,0:T(8,128)(2,1)S(1)} %get-tuple-element.14), channel_id=1, source_target_pairs={{1,0},{2,1},{3,2},{4,3},{5,4},{6,5},{7,6},{8,7},{9,8},{10,9},{11,1... | collective-permute-start | bytes 940040 | tf_op jit(solution)/shard_map/ppermute | solution.py:27
  50.0 1.2 slice-start
  52.4 2.6 %collective-permute-start.4 = (f32[1792,128]{1,0:T(8,128)S(1)}, f32[1792,128]{1,0:T(8,128)S(1)}, u32[]{:S(2)}, u32[]{:S(2)}) collective-permute-start(f32[1792,128]{1,0:T(8,128)S(1)} %pad_dynamic-slice_fusion), channel_id=1, source_target_pairs={{0,16},{16,0},{32,48},{48,32},{64,80},{80,64},{96,112},{112,96},{1... | collective-permute-start | bytes 2752520 | tf_op jit(solution)/shard_map/ppermute | solution.py:48
  55.2 13.5 %collective-permute-start.5 = (f32[896,128]{1,0:T(8,128)S(1)}, f32[896,128]{1,0:T(8,128)S(1)}, u32[]{:S(2)}, u32[]{:S(2)}) collective-permute-start(f32[896,128]{1,0:T(8,128)S(1)} %constant_dynamic-slice_fusion.6), channel_id=1, source_target_pairs={{0,1},{1,0},{2,3},{3,2},{4,5},{5,4},{6,7},{7,6},{8,9},{9,8},{10,11... | collective-permute-start | bytes 1376264 | tf_op jit(solution)/shard_map/ppermute | solution.py:48
  68.8 14.1 %collective-permute-start.6 = (f32[448,128]{1,0:T(8,128)S(1)}, f32[448,128]{1,0:T(8,128)S(1)}, u32[]{:S(2)}, u32[]{:S(2)}) collective-permute-start(f32[448,128]{1,0:T(8,128)S(1)} %constant_dynamic-slice_fusion.5), channel_id=1, source_target_pairs={{0,64},{16,80},{32,96},{48,112},{64,0},{80,16},{96,32},{112,48},{1... | collective-permute-start | bytes 688136 | tf_op jit(solution)/shard_map/ppermute | solution.py:48
  83.0 3.7 %collective-permute-start.7 = (f32[224,128]{1,0:T(8,128)S(1)}, f32[224,128]{1,0:T(8,128)S(1)}, u32[]{:S(2)}, u32[]{:S(2)}) collective-permute-start(f32[224,128]{1,0:T(8,128)S(1)} %constant_dynamic-slice_fusion.4), channel_id=1, source_target_pairs={{0,2},{1,3},{2,0},{3,1},{4,6},{5,7},{6,4},{7,5},{8,10},{9,11},{10,... | collective-permute-start | bytes 344072 | tf_op jit(solution)/shard_map/ppermute | solution.py:48
  86.7 4.6 %collective-permute-start.8 = (f32[112,128]{1,0:T(8,128)S(1)}, f32[112,128]{1,0:T(8,128)S(1)}, u32[]{:S(2)}, u32[]{:S(2)}) collective-permute-start(f32[112,128]{1,0:T(8,128)S(1)} %constant_dynamic-slice_fusion.3), channel_id=1, source_target_pairs={{0,32},{16,48},{32,0},{48,16},{64,96},{80,112},{96,64},{112,80},{1... | collective-permute-start | bytes 172040 | tf_op jit(solution)/shard_map/ppermute | solution.py:48
  91.4 4.3 %collective-permute-start.9 = (f32[56,128]{1,0:T(8,128)S(1)}, f32[56,128]{1,0:T(8,128)S(1)}, u32[]{:S(2)}, u32[]{:S(2)}) collective-permute-start(f32[56,128]{1,0:T(8,128)S(1)} %constant_dynamic-slice_fusion.2), channel_id=1, source_target_pairs={{0,128},{16,144},{32,160},{48,176},{64,192},{80,208},{96,224},{112... | collective-permute-start | bytes 86024 | tf_op jit(solution)/shard_map/ppermute | solution.py:48
  95.7 7.0 %collective-permute-start.10 = (f32[28,128]{1,0:T(8,128)S(1)}, f32[28,128]{1,0:T(8,128)S(1)}, u32[]{:S(2)}, u32[]{:S(2)}) collective-permute-start(f32[28,128]{1,0:T(8,128)S(1)} %constant_dynamic-slice_fusion.1), channel_id=1, source_target_pairs={{0,4},{1,5},{2,6},{3,7},{4,0},{5,1},{6,2},{7,3},{8,12},{9,13},{10,... | collective-permute-start | bytes 43016 | tf_op jit(solution)/shard_map/ppermute | solution.py:48
  102.8 7.2 %collective-permute-start.11 = (f32[14,128]{1,0:T(8,128)S(1)}, f32[14,128]{1,0:T(8,128)S(1)}, u32[]{:S(2)}, u32[]{:S(2)}) collective-permute-start(f32[14,128]{1,0:T(8,128)S(1)} %constant_dynamic-slice_fusion), channel_id=1, source_target_pairs={{0,8},{1,9},{2,10},{3,11},{4,12},{5,13},{6,14},{7,15},{8,0},{9,1},... | collective-permute-start | bytes 21512 | tf_op jit(solution)/shard_map/ppermute | solution.py:48
  110.0 6.5 %collective-permute-start.12 = (f32[14,128]{1,0:T(8,128)S(1)}, f32[14,128]{1,0:T(8,128)S(1)}, u32[]{:S(2)}, u32[]{:S(2)}) collective-permute-start(f32[14,128]{1,0:T(8,128)S(1)} %dynamic-slice_add_fusion.6), channel_id=1, source_target_pairs={{0,8},{1,9},{2,10},{3,11},{4,12},{5,13},{6,14},{7,15},{8,0},{9,1},... | collective-permute-start | bytes 21512 | tf_op jit(solution)/shard_map/ppermute | solution.py:56
  116.5 3.6 %collective-permute-start.13 = (f32[28,128]{1,0:T(8,128)S(1)}, f32[28,128]{1,0:T(8,128)S(1)}, u32[]{:S(2)}, u32[]{:S(2)}) collective-permute-start(f32[28,128]{1,0:T(8,128)S(1)} %pad_maximum_fusion.8), channel_id=1, source_target_pairs={{0,4},{1,5},{2,6},{3,7},{4,0},{5,1},{6,2},{7,3},{8,12},{9,13},{10,... | collective-permute-start | bytes 43016 | tf_op jit(solution)/shard_map/ppermute | solution.py:56
  120.1 4.3 %collective-permute-start.14 = (f32[56,128]{1,0:T(8,128)S(1)}, f32[56,128]{1,0:T(8,128)S(1)}, u32[]{:S(2)}, u32[]{:S(2)}) collective-permute-start(f32[56,128]{1,0:T(8,128)S(1)} %pad_maximum_fusion.7), channel_id=1, source_target_pairs={{0,128},{16,144},{32,160},{48,176},{64,192},{80,208},{96,224},{112... | collective-permute-start | bytes 86024 | tf_op jit(solution)/shard_map/ppermute | solution.py:56
  124.4 4.6 %collective-permute-start.15 = (f32[112,128]{1,0:T(8,128)S(1)}, f32[112,128]{1,0:T(8,128)S(1)}, u32[]{:S(2)}, u32[]{:S(2)}) collective-permute-start(f32[112,128]{1,0:T(8,128)S(1)} %pad_maximum_fusion.6), channel_id=1, source_target_pairs={{0,32},{16,48},{32,0},{48,16},{64,96},{80,112},{96,64},{112,80},{1... | collective-permute-start | bytes 172040 | tf_op jit(solution)/shard_map/ppermute | solution.py:56
  129.1 4.0 %collective-permute-start.16 = (f32[224,128]{1,0:T(8,128)S(1)}, f32[224,128]{1,0:T(8,128)S(1)}, u32[]{:S(2)}, u32[]{:S(2)}) collective-permute-start(f32[224,128]{1,0:T(8,128)S(1)} %pad_maximum_fusion.5), channel_id=1, source_target_pairs={{0,2},{1,3},{2,0},{3,1},{4,6},{5,7},{6,4},{7,5},{8,10},{9,11},{10,... | collective-permute-start | bytes 344072 | tf_op jit(solution)/shard_map/ppermute | solution.py:56
  133.2 5.0 %collective-permute-start.17 = (f32[448,128]{1,0:T(8,128)S(1)}, f32[448,128]{1,0:T(8,128)S(1)}, u32[]{:S(2)}, u32[]{:S(2)}) collective-permute-start(f32[448,128]{1,0:T(8,128)S(1)} %pad_maximum_fusion.4), channel_id=1, source_target_pairs={{0,64},{16,80},{32,96},{48,112},{64,0},{80,16},{96,32},{112,48},{1... | collective-permute-start | bytes 688136 | tf_op jit(solution)/shard_map/ppermute | solution.py:56
  138.2 7.4 %collective-permute-start.18 = (f32[896,128]{1,0:T(8,128)S(1)}, f32[896,128]{1,0:T(8,128)S(1)}, u32[]{:S(2)}, u32[]{:S(2)}) collective-permute-start(f32[896,128]{1,0:T(8,128)S(1)} %pad_maximum_fusion.3), channel_id=1, source_target_pairs={{0,1},{1,0},{2,3},{3,2},{4,5},{5,4},{6,7},{7,6},{8,9},{9,8},{10,11... | collective-permute-start | bytes 1376264 | tf_op jit(solution)/shard_map/ppermute | solution.py:56
  145.7 16.8 %collective-permute-start.19 = (f32[1792,128]{1,0:T(8,128)S(1)}, f32[1792,128]{1,0:T(8,128)}, u32[]{:S(2)}, u32[]{:S(2)}) collective-permute-start(f32[1792,128]{1,0:T(8,128)S(1)} %pad_maximum_fusion.1), channel_id=1, source_target_pairs={{0,16},{16,0},{32,48},{48,32},{64,80},{80,64},{96,112},{112,96},{1... | collective-permute-start | bytes 2752520 | tf_op jit(solution)/shard_map/ppermute | solution.py:56

commit v5 on v4

--- a/solution.py
+++ b/solution.py
@@ -10,22 +10,34 @@
 OFFS = 27
 
 
-def with_halo(value, sides):
-    pads = [(0, 0)] * value.ndim
-    for _, dim in sides:
-        pads[dim] = (1, 1)
-    pads[-2] = (1, 1)
-    padded = jnp.pad(value, pads)
-    for axis, dim in sides:
-        size, length = lax.axis_size(axis), padded.shape[dim]
-        up = [(i, (i + 1) % size) for i in range(size - 1)]
-        down = [(j, i) for i, j in up]
-        last = lax.slice_in_dim(padded, length - 2, length - 1, axis=dim)
-        leading = lax.slice_in_dim(padded, 1, 2, axis=dim)
-        padded = lax.dynamic_update_slice_in_dim(padded, lax.ppermute(last, axis, up), 0, axis=dim)
-        padded = lax.dynamic_update_slice_in_dim(
-            padded, lax.ppermute(leading, axis, down), length - 1, axis=dim
-        )
+ZPAD = 8
+
+
+def shift_pairs(size_x, size_y, dx, dy):
+    pairs = []
+    for i in range(size_x):
+        for j in range(size_y):
+            if 0 <= i + dx < size_x and 0 <= j + dy < size_y:
+                pairs.append((i * size_y + j, (i + dx) * size_y + j + dy))
+    return pairs
+
+
+def with_halo(value):
+    kinds, nx, ny, nz, chans = value.shape
+    padded = jnp.pad(value, ((0, 0), (1, 1), (1, 1), (ZPAD, ZPAD), (0, 0)))
+    sx, sy = lax.axis_size("gx"), lax.axis_size("gy")
+    zs = slice(ZPAD, ZPAD + nz)
+    pieces = []
+    for dx, dy in ((1, 0), (-1, 0), (0, 1), (0, -1), (1, 1), (1, -1), (-1, 1), (-1, -1)):
+        xs = slice(nx, nx + 1) if dx > 0 else (slice(1, 2) if dx < 0 else slice(0, nx + 2))
+        ys = slice(ny, ny + 1) if dy > 0 else (slice(1, 2) if dy < 0 else slice(0, ny + 2))
+        face = padded[:, xs, ys, zs, :]
+        got = lax.ppermute(face, ("gx", "gy"), shift_pairs(sx, sy, dx, dy))
+        at_x = 0 if dx > 0 else (nx + 1 if dx < 0 else 0)
+        at_y = 0 if dy > 0 else (ny + 1 if dy < 0 else 0)
+        pieces.append((got, at_x, at_y))
+    for got, at_x, at_y in pieces:
+        padded = lax.dynamic_update_slice(padded, got, (0, at_x, at_y, ZPAD, 0))
     return padded
 
 
@@ -75,7 +87,7 @@
     windows = []
     for slot in range(places.shape[0]):
         place = places[slot]
-        starts = (0, place // (TBY * ZL) * BRICK, place // ZL % TBY * BRICK, place % ZL * BRICK, 0)
+        starts = (0, place // (TBY * ZL) * BRICK, place // ZL % TBY * BRICK, place % ZL * BRICK + ZPAD - 1, 0)
         windows.append(
             lax.dynamic_slice(padded, starts, (kinds, BRICK + 2, BRICK + 2, BRICK + 2, chans))
         )
@@ -101,7 +113,7 @@
     both = jnp.stack([features[0, 0], cotangent[0, 0]]) * keeper[None, :, :, None]
     grad_rows = both[1].reshape(-1, chans)
     dense = place_bricks(both, places, alive)
-    padded = with_halo(dense, (("gx", 1), ("gy", 2)))
+    padded = with_halo(dense)
     windows = cut_windows(padded, places)
     feat_stack = stack_offsets(windows[0])
     tiles = lax.axis_size("gx") * lax.axis_size("gy")

time: 166 us -> 173 us (1.042)
  starting transfers between devices: 68.4 us -> 82.1 us
  waiting for transfers between devices: 54.6 us -> 44.6 us
  local copies, waits for them, and re-layouts: 22.6 us -> 24.9 us
    ppermute x4 -> x8, starting transfers between devices: 12.3 us -> 25.7 us  [with_halo(): got = lax.ppermute(face, ('gx', 'gy'), shift_pairs(sx, sy, dx, dy))]
    ppermute x4 -> x8, waiting for transfers between devices: 8.01 us -> 1.58 us  [with_halo(): got = lax.ppermute(face, ('gx', 'gy'), shift_pairs(sx, sy, dx, dy))]
    dynamic_update_slice x3 -> x8, local copies, waits for them, and re-layouts: 2.48 us -> 6.51 us  [with_halo(): padded = lax.dynamic_update_slice(padded, got, (0, at_x, at_y, ZPAD, 0))]
    slice x3, local copies, waits for them, and re-layouts: 3.19 us -> 0.1 us  [with_halo(): face = padded[:, xs, ys, zs, :]]
    ppermute x8, starting transfers between devices: 27.8 us -> 29.9 us  [butterfly_gather(): got = lax.ppermute(buf, axis, pairs)]
    ppermute x8, waiting for transfers between devices: 24.4 us -> 22.3 us  [butterfly_gather(): got = lax.ppermute(buf, axis, pairs)]
    ppermute x8, starting transfers between devices: 28.4 us -> 26.5 us  [butterfly_scatter(): buf = keep + lax.ppermute(send, axis, pairs)]
    unnamed x63 -> x67, local copies, waits for them, and re-layouts: 3.83 us -> 3.84 us
  transfers between devices with their start and end apart: 20 -> 24, of which waited for: 18 -> 16; matrix products, arithmetic and copies ran while one was open for 8% -> 12% of each run, Pallas kernels for 0% -> 0%
where the time goes in v5:
time: 173 us; the launch traced here: 172 us
  starting transfers between devices  82.1 us (47%)
  waiting for transfers between devices  44.6 us (26%)
  local copies, waits for them, and re-layouts  24.9 us (14%)
  matrix products  8.6 us (5%)
  between operations  7.46 us (4%)
  other arithmetic  4.82 us (3%)
    ppermute x8, starting transfers between devices, butterfly_gather(): got = lax.ppermute(buf, axis, pairs)  29.9 us
    ppermute x8, starting transfers between devices, butterfly_scatter(): buf = keep + lax.ppermute(send, axis, pairs)  26.5 us
    ppermute x8, starting transfers between devices, with_halo(): got = lax.ppermute(face, ('gx', 'gy'), shift_pairs(sx, sy, dx, dy))  25.7 us
    ppermute x8, waiting for transfers between devices, butterfly_gather(): got = lax.ppermute(buf, axis, pairs)  22.3 us
    ppermute x8, waiting for transfers between devices, butterfly_scatter(): buf = keep + lax.ppermute(send, axis, pairs)  20.7 us
    pad x1, local copies, waits for them, and re-layouts, with_halo(): padded = jnp.pad(value, ((0, 0), (1, 1), (1, 1), (ZPAD, ZPAD), (0, 0)))  6.56 us
    dynamic_update_slice x8, local copies, waits for them, and re-layouts, with_halo(): padded = lax.dynamic_update_slice(padded, got, (0, at_x, at_y, ZPAD, 0))  6.51 us
    unnamed x67, local copies, waits for them, and re-layouts  3.84 us
  transfers between devices with their start and end apart: 24, of which 16 were waited for; matrix products, arithmetic and copies ran while one was open for 12% of the time, Pallas kernels for 0%

profile of v5, /device:TPU:1, one launch (start us, length us, event | category | flops | bytes accessed | tf_op | source)
XLA Modules:
  0.0 172.4 jit_solution(16634207926685326530)
XLA Ops:
  1.4 0.8 broadcast_bitcast_fusion
  2.1 1.2 maximum_multiply_fusion
  3.4 2.0 %convolution_convert_fusion = bf16[2,512,128,16]{2,3,1,0:T(8,128)(2,1)S(1)} fusion(bf16[2,2,512,128]{3,2,1,0:T(8,128)(2,1)S(1)} %maximum_multiply_fusion, pred[2]{0:T(512)(128)(4,1)S(1)} %get-tuple-element.98, s32[2]{0:T(128)} %bitcast.187), kind=kOutput, calls=%fused_computation.4 | convolution fusion | flops 10485824 | bytes 4718602 | tf_op jit(solution)/shard_map/ps,tsvc->tpvc/dot_general | solution.py:76
  5.5 1.6 copy.12
  7.2 6.0 %collective-permute-start = (bf16[2,1,18,32,128]{4,3,2,1,0:T(8,128)(2,1)S(1)}, bf16[2,1,18,32,128]{4,3,2,1,0:T(8,128)(2,1)}, u32[]{:S(2)}, u32[]{:S(2)}) collective-permute-start(bf16[2,1,18,32,128]{4,3,2,1,0:T(8,128)(2,1)S(1)} %get-tuple-element.21), channel_id=1, source_target_pairs={{0,16},{1,17},{2,18},{3,19},{4,20},{5,21},{6,22},{7,23},{8,24},{9,... | collective-permute-start | bytes 884744 | tf_op jit(solution)/shard_map/ppermute | solution.py:35
  13.2 1.9 %collective-permute-start.1 = (bf16[2,1,18,32,128]{4,3,2,1,0:T(8,128)(2,1)S(1)}, bf16[2,1,18,32,128]{4,3,2,1,0:T(8,128)(2,1)S(1)}, u32[]{:S(2)}, u32[]{:S(2)}) collective-permute-start(bf16[2,1,18,32,128]{4,3,2,1,0:T(8,128)(2,1)S(1)} %get-tuple-element.20), channel_id=1, source_target_pairs={{16,0},{17,1},{18,2},{19,3},{20,4},{21,5},{22,6},{23,7},{24,8},{25... | collective-permute-start | bytes 884744 | tf_op jit(solution)/shard_map/ppermute | solution.py:35
  15.2 2.2 %collective-permute-start.2 = (bf16[2,18,1,32,128]{4,3,2,1,0:T(8,128)(2,1)S(1)}, bf16[2,18,1,32,128]{4,3,2,1,0:T(8,128)(2,1)S(1)}, u32[]{:S(2)}, u32[]{:S(2)}) collective-permute-start(bf16[2,18,1,32,128]{4,3,2,1,0:T(8,128)(2,1)S(1)} %get-tuple-element.19), channel_id=1, source_target_pairs={{0,1},{1,2},{2,3},{3,4},{4,5},{5,6},{6,7},{7,8},{8,9},{9,10},{10,1... | collective-permute-start | bytes 884744 | tf_op jit(solution)/shard_map/ppermute | solution.py:35
  17.4 1.3 collective-permute-start.3
  18.7 7.4 %collective-permute-start.4 = (bf16[2,1,1,32,128]{4,3,2,1,0:T(8,128)(2,1)S(1)}, bf16[2,1,1,32,128]{4,3,2,1,0:T(8,128)(2,1)S(1)}, u32[]{:S(2)}, u32[]{:S(2)}) collective-permute-start(bf16[2,1,1,32,128]{4,3,2,1,0:T(8,128)(2,1)S(1)} %get-tuple-element.17), channel_id=1, source_target_pairs={{0,17},{1,18},{2,19},{3,20},{4,21},{5,22},{6,23},{7,24},{8,25},{9,... | collective-permute-start | bytes 49160 | tf_op jit(solution)/shard_map/ppermute | solution.py:35
  26.1 0.6 fusion.10
  26.7 0.6 fusion.23
  32.6 6.6 %pad.8 = bf16[2,18,18,48,128]{4,3,2,1,0:T(8,128)(2,1)} pad(bf16[2,16,16,32,128]{4,3,2,1,0:T(8,128)(2,1)} %bitcast.122, bf16[]{:T(256)} %constant.88.clone.1), padding=0_0x1_1x1_1x8_8x0_0 | pad | bytes 12156930 | tf_op jit(solution)/shard_map/jit(_pad)/pad | solution.py:27
  39.2 1.3 collective-permute-start.5
  40.5 1.7 %constant_dynamic-update-slice_fusion.61 = bf16[2,18,18,48,128]{4,3,2,1,0:T(8,128)(2,1)} fusion(bf16[2,18,18,48,128]{4,3,2,1,0:T(8,128)(2,1)} %pad.8, bf16[2,1,18,32,128]{4,3,2,1,0:T(8,128)(2,1)} %collective-permute-done), kind=kLoop, calls=%fused_computation.122 | loop fusion | bytes 589824 | tf_op jit(solution)/shard_map/dynamic_update_slice | solution.py:40
  42.2 4.3 %collective-permute-start.6 = (bf16[2,1,1,32,128]{4,3,2,1,0:T(8,128)(2,1)S(1)}, bf16[2,1,1,32,128]{4,3,2,1,0:T(8,128)(2,1)S(1)}, u32[]{:S(2)}, u32[]{:S(2)}) collective-permute-start(bf16[2,1,1,32,128]{4,3,2,1,0:T(8,128)(2,1)S(1)} %get-tuple-element.15), channel_id=1, source_target_pairs={{16,1},{17,2},{18,3},{19,4},{20,5},{21,6},{22,7},{23,8},{24,9},{25... | collective-permute-start | bytes 49160 | tf_op jit(solution)/shard_map/ppermute | solution.py:35
  46.5 0.8 constant_dynamic-update-slice_fusion.60
  47.3 1.3 collective-permute-start.7
  48.5 0.8 constant_dynamic-update-slice_fusion.59
  49.3 0.8 constant_dynamic-update-slice_fusion.58
  50.1 0.6 constant_dynamic-update-slice_fusion.57
  50.7 0.6 constant_dynamic-update-slice_fusion.56
  51.4 0.6 constant_dynamic-update-slice_fusion.55
  52.0 1.6 collective-permute-done.7
  53.5 0.6 constant_dynamic-update-slice_fusion.54
  54.1 2.4 %dynamic-slice_bitcast_fusion = (bf16[2,1,10,10,10,128]{5,4,3,2,1,0:T(8,128)(2,1)S(1)}, bf16[2,1,10,10,10,128]{5,4,3,2,1,0:T(8,128)(2,1)S(1)}) fusion(bf16[2,18,18,48,128]{4,3,2,1,0:T(8,128)(2,1)} %constant_dynamic-update-slice_fusion.54, s32[]{:T(128)S(6)} %select_n.202, s32[]{:T(128)S(6)} %select_n.205, s32[]{:T(128)S(6)} %select_n.207, s32[]{:T(128)S(6)} %select_n.195, ...), kind=kLoop, calls=%fused_computation.23 | loop fusion | bytes 2048024 | tf_op jit(solution)/shard_map/stack | solution.py:94
  57.3 1.0 fusion.21
  58.3 0.5 fusion.20
  58.8 1.0 fusion.19
  61.0 1.2 convolution_multiply_fusion
  62.3 0.6 collective-permute-start.8
  63.8 1.2 collective-permute-done.8
  65.2 2.7 %collective-permute-start.9 = (f32[896,128]{1,0:T(8,128)S(1)}, f32[896,128]{1,0:T(8,128)S(1)}, u32[]{:S(2)}, u32[]{:S(2)}) collective-permute-start(f32[896,128]{1,0:T(8,128)S(1)} %constant_dynamic-slice_fusion.6), channel_id=1, source_target_pairs={{0,1},{1,0},{2,3},{3,2},{4,5},{5,4},{6,7},{7,6},{8,9},{9,8},{10,11... | collective-permute-start | bytes 1376264 | tf_op jit(solution)/shard_map/ppermute | solution.py:60
  67.9 2.7 %fusion.2 = bf16[1024,128]{1,0:T(8,128)(2,1)} fusion(bf16[27,1024,128]{2,1,0:T(8,128)(2,1)S(1)} %constant_dynamic-update-slice_fusion, bf16[27,128,128]{2,1,0:T(8,128)(2,1)S(1)} %copy-done, f32[1024]{0:T(1024)S(1)} %copy-done.5), kind=kOutput, calls=%fused_computation.15 | convolution fusion | flops 906231808 | bytes 8228864 | tf_op jit(solution)/shard_map/dvc,dce->ve/dot_general | solution.py:123
  70.6 8.0 %collective-permute-done.9 = f32[896,128]{1,0:T(8,128)S(1)} collective-permute-done((f32[896,128]{1,0:T(8,128)S(1)}, f32[896,128]{1,0:T(8,128)S(1)}, u32[]{:S(2)}, u32[]{:S(2)}) %collective-permute-start.9) | collective-permute-done | bytes 458784 | tf_op jit(solution)/shard_map/ppermute | solution.py:60
  78.7 1.9 %collective-permute-start.10 = (f32[448,128]{1,0:T(8,128)S(1)}, f32[448,128]{1,0:T(8,128)S(1)}, u32[]{:S(2)}, u32[]{:S(2)}) collective-permute-start(f32[448,128]{1,0:T(8,128)S(1)} %constant_dynamic-slice_fusion.5), channel_id=1, source_target_pairs={{0,64},{16,80},{32,96},{48,112},{64,0},{80,16},{96,32},{112,48},{1... | collective-permute-start | bytes 688136 | tf_op jit(solution)/shard_map/ppermute | solution.py:60
  80.7 5.2 %collective-permute-done.10 = f32[448,128]{1,0:T(8,128)S(1)} collective-permute-done((f32[448,128]{1,0:T(8,128)S(1)}, f32[448,128]{1,0:T(8,128)S(1)}, u32[]{:S(2)}, u32[]{:S(2)}) %collective-permute-start.10) | collective-permute-done | bytes 229408 | tf_op jit(solution)/shard_map/ppermute | solution.py:60
  86.0 2.6 %collective-permute-start.11 = (f32[224,128]{1,0:T(8,128)S(1)}, f32[224,128]{1,0:T(8,128)S(1)}, u32[]{:S(2)}, u32[]{:S(2)}) collective-permute-start(f32[224,128]{1,0:T(8,128)S(1)} %constant_dynamic-slice_fusion.4), channel_id=1, source_target_pairs={{0,2},{1,3},{2,0},{3,1},{4,6},{5,7},{6,4},{7,5},{8,10},{9,11},{10,... | collective-permute-start | bytes 344072 | tf_op jit(solution)/shard_map/ppermute | solution.py:60
  88.6 2.1 %collective-permute-done.11 = f32[224,128]{1,0:T(8,128)S(1)} collective-permute-done((f32[224,128]{1,0:T(8,128)S(1)}, f32[224,128]{1,0:T(8,128)S(1)}, u32[]{:S(2)}, u32[]{:S(2)}) %collective-permute-start.11) | collective-permute-done | bytes 114720 | tf_op jit(solution)/shard_map/ppermute | solution.py:60
  90.8 4.0 %collective-permute-start.12 = (f32[112,128]{1,0:T(8,128)S(1)}, f32[112,128]{1,0:T(8,128)S(1)}, u32[]{:S(2)}, u32[]{:S(2)}) collective-permute-start(f32[112,128]{1,0:T(8,128)S(1)} %constant_dynamic-slice_fusion.3), channel_id=1, source_target_pairs={{0,32},{16,48},{32,0},{48,16},{64,96},{80,112},{96,64},{112,80},{1... | collective-permute-start | bytes 172040 | tf_op jit(solution)/shard_map/ppermute | solution.py:60
  94.8 1.5 collective-permute-done.12
  96.4 2.7 %collective-permute-start.13 = (f32[56,128]{1,0:T(8,128)S(1)}, f32[56,128]{1,0:T(8,128)S(1)}, u32[]{:S(2)}, u32[]{:S(2)}) collective-permute-start(f32[56,128]{1,0:T(8,128)S(1)} %constant_dynamic-slice_fusion.2), channel_id=1, source_target_pairs={{0,128},{16,144},{32,160},{48,176},{64,192},{80,208},{96,224},{112... | collective-permute-start | bytes 86024 | tf_op jit(solution)/shard_map/ppermute | solution.py:60
  99.2 1.6 collective-permute-done.13
  100.7 7.9 %collective-permute-start.14 = (f32[28,128]{1,0:T(8,128)S(1)}, f32[28,128]{1,0:T(8,128)S(1)}, u32[]{:S(2)}, u32[]{:S(2)}) collective-permute-start(f32[28,128]{1,0:T(8,128)S(1)} %constant_dynamic-slice_fusion.1), channel_id=1, source_target_pairs={{0,4},{1,5},{2,6},{3,7},{4,0},{5,1},{6,2},{7,3},{8,12},{9,13},{10,... | collective-permute-start | bytes 43016 | tf_op jit(solution)/shard_map/ppermute | solution.py:60
  108.7 1.1 collective-permute-done.14
  109.8 4.0 %collective-permute-start.15 = (f32[14,128]{1,0:T(8,128)S(1)}, f32[14,128]{1,0:T(8,128)S(1)}, u32[]{:S(2)}, u32[]{:S(2)}) collective-permute-start(f32[14,128]{1,0:T(8,128)S(1)} %constant_dynamic-slice_fusion), channel_id=1, source_target_pairs={{0,8},{1,9},{2,10},{3,11},{4,12},{5,13},{6,14},{7,15},{8,0},{9,1},... | collective-permute-start | bytes 21512 | tf_op jit(solution)/shard_map/ppermute | solution.py:60
  113.8 2.7 %fusion.3 = bf16[1024,128]{1,0:T(8,128)(2,1)} fusion(bf16[27,1024,128]{2,1,0:T(8,128)(2,1)S(1)} %constant_dynamic-update-slice_fusion.27, bf16[27,128,128]{2,1,0:T(8,128)(2,1)S(1)} %copy-done, f32[1024]{0:T(1024)S(1)} %copy-done.5), kind=kOutput, calls=%fused_computation.16 | convolution fusion | flops 906231808 | bytes 8228864 | tf_op jit(solution)/shard_map/dvc,dec->ve/dot_general | solution.py:126
  116.5 3.8 %collective-permute-start.16 = (f32[14,128]{1,0:T(8,128)S(1)}, f32[14,128]{1,0:T(8,128)S(1)}, u32[]{:S(2)}, u32[]{:S(2)}) collective-permute-start(f32[14,128]{1,0:T(8,128)S(1)} %dynamic-slice_add_fusion.6), channel_id=1, source_target_pairs={{0,8},{1,9},{2,10},{3,11},{4,12},{5,13},{6,14},{7,15},{8,0},{9,1},... | collective-permute-start | bytes 21512 | tf_op jit(solution)/shard_map/ppermute | solution.py:68
  120.3 2.7 %collective-permute-done.16 = f32[14,128]{1,0:T(8,128)S(1)} collective-permute-done((f32[14,128]{1,0:T(8,128)S(1)}, f32[14,128]{1,0:T(8,128)S(1)}, u32[]{:S(2)}, u32[]{:S(2)}) %collective-permute-start.16) | collective-permute-done | bytes 7200 | tf_op jit(solution)/shard_map/ppermute | solution.py:68
  123.1 2.5 %collective-permute-start.17 = (f32[28,128]{1,0:T(8,128)S(1)}, f32[28,128]{1,0:T(8,128)S(1)}, u32[]{:S(2)}, u32[]{:S(2)}) collective-permute-start(f32[28,128]{1,0:T(8,128)S(1)} %pad_maximum_fusion.8), channel_id=1, source_target_pairs={{0,4},{1,5},{2,6},{3,7},{4,0},{5,1},{6,2},{7,3},{8,12},{9,13},{10,... | collective-permute-start | bytes 43016 | tf_op jit(solution)/shard_map/ppermute | solution.py:68
  125.6 1.1 collective-permute-done.17
  126.7 2.8 %collective-permute-start.18 = (f32[56,128]{1,0:T(8,128)S(1)}, f32[56,128]{1,0:T(8,128)S(1)}, u32[]{:S(2)}, u32[]{:S(2)}) collective-permute-start(f32[56,128]{1,0:T(8,128)S(1)} %pad_maximum_fusion.7), channel_id=1, source_target_pairs={{0,128},{16,144},{32,160},{48,176},{64,192},{80,208},{96,224},{112... | collective-permute-start | bytes 86024 | tf_op jit(solution)/shard_map/ppermute | solution.py:68
  129.6 1.5 collective-permute-done.18
  131.1 3.1 %collective-permute-start.19 = (f32[112,128]{1,0:T(8,128)S(1)}, f32[112,128]{1,0:T(8,128)S(1)}, u32[]{:S(2)}, u32[]{:S(2)}) collective-permute-start(f32[112,128]{1,0:T(8,128)S(1)} %pad_maximum_fusion.6), channel_id=1, source_target_pairs={{0,32},{16,48},{32,0},{48,16},{64,96},{80,112},{96,64},{112,80},{1... | collective-permute-start | bytes 172040 | tf_op jit(solution)/shard_map/ppermute | solution.py:68
  134.1 1.6 collective-permute-done.19
  135.7 1.5 collective-permute-start.20
  137.3 2.5 %collective-permute-done.20 = f32[224,128]{1,0:T(8,128)S(1)} collective-permute-done((f32[224,128]{1,0:T(8,128)S(1)}, f32[224,128]{1,0:T(8,128)S(1)}, u32[]{:S(2)}, u32[]{:S(2)}) %collective-permute-start.20) | collective-permute-done | bytes 114720 | tf_op jit(solution)/shard_map/ppermute | solution.py:68
  139.8 1.1 collective-permute-start.21
  140.9 3.9 %collective-permute-done.21 = f32[448,128]{1,0:T(8,128)S(1)} collective-permute-done((f32[448,128]{1,0:T(8,128)S(1)}, f32[448,128]{1,0:T(8,128)S(1)}, u32[]{:S(2)}, u32[]{:S(2)}) %collective-permute-start.21) | collective-permute-done | bytes 229408 | tf_op jit(solution)/shard_map/ppermute | solution.py:68
  144.8 0.6 collective-permute-start.22
  145.4 6.8 %collective-permute-done.22 = f32[896,128]{1,0:T(8,128)S(1)} collective-permute-done((f32[896,128]{1,0:T(8,128)S(1)}, f32[896,128]{1,0:T(8,128)S(1)}, u32[]{:S(2)}, u32[]{:S(2)}) %collective-permute-start.22) | collective-permute-done | bytes 458784 | tf_op jit(solution)/shard_map/ppermute | solution.py:68
  152.4 14.5 %collective-permute-start.23 = (f32[1792,128]{1,0:T(8,128)S(1)}, f32[1792,128]{1,0:T(8,128)}, u32[]{:S(2)}, u32[]{:S(2)}) collective-permute-start(f32[1792,128]{1,0:T(8,128)S(1)} %pad_maximum_fusion.1), channel_id=1, source_target_pairs={{0,16},{16,0},{32,48},{48,32},{64,80},{80,64},{96,112},{112,96},{1... | collective-permute-start | bytes 2752520 | tf_op jit(solution)/shard_map/ppermute | solution.py:68
  166.8 2.2 %collective-permute-done.23 = f32[1792,128]{1,0:T(8,128)} collective-permute-done((f32[1792,128]{1,0:T(8,128)S(1)}, f32[1792,128]{1,0:T(8,128)}, u32[]{:S(2)}, u32[]{:S(2)}) %collective-permute-start.23) | collective-permute-done | bytes 917536 | tf_op jit(solution)/shard_map/ppermute | solution.py:68
  169.1 1.3 broadcast_select_fusion.1
  170.5 1.9 %copy.14 = f32[27,128,128]{2,1,0:T(8,128)} copy(f32[27,128,128]{1,2,0:T(8,128)S(1)} %bitcast.126) | data formatting | bytes 3538944
  (115 shorter events, 3.7 us)
Async XLA Ops:
  0.6 67.3 %copy-start = (bf16[27,128,128]{2,1,0:T(8,128)(2,1)S(1)}, bf16[27,128,128]{2,1,0:T(8,128)(2,1)}, u32[]{:S(2)}) copy-start(bf16[27,128,128]{2,1,0:T(8,128)(2,1)} %param.10) | copy-start | bytes 2654212
  3.4 24.0 %copy-start.2 = (bf16[2,2,512,128]{3,2,1,0:T(8,128)(2,1)}, bf16[2,2,512,128]{3,2,1,0:T(8,128)(2,1)S(1)}, u32[]{:S(2)}) copy-start(bf16[2,2,512,128]{3,2,1,0:T(8,128)(2,1)S(1)} %maximum_multiply_fusion) | copy-start | bytes 1572868
  5.4 20.7 %copy-start.3 = (s32[1,1,2,512]{3,2,1,0:T(2,128)S(1)}, s32[1,1,2,512]{3,2,1,0:T(2,128)}, u32[]{:S(2)}) copy-start(s32[1,1,2,512]{3,2,1,0:T(2,128)} %param.7) | copy-start | bytes 12292
  5.5 21.3 %copy-start.4 = (s32[1,1,2]{2,1,0:T(1,128)S(1)}, s32[1,1,2]{2,1,0:T(1,128)}, u32[]{:S(2)}) copy-start(s32[1,1,2]{2,1,0:T(1,128)} %param.8) | copy-start | bytes 28
  7.1 11.6 %copy-start.1 = (bf16[2,2,2,4,8,8,8,128]{7,6,3,5,2,4,1,0:T(8,128)(2,1)}, bf16[2,2,2,4,8,8,8,128]{7,6,3,5,2,4,1,0:T(8,128)(2,1)S(1)}, u32[]{:S(2)}) copy-start(bf16[2,2,2,4,8,8,8,128]{7,6,3,5,2,4,1,0:T(8,128)(2,1)S(1)} %copy.12) | copy-start | bytes 12582916
  7.2 32.0 %collective-permute-start = (bf16[2,1,18,32,128]{4,3,2,1,0:T(8,128)(2,1)S(1)}, bf16[2,1,18,32,128]{4,3,2,1,0:T(8,128)(2,1)}, u32[]{:S(2)}, u32[]{:S(2)}) collective-permute-start(bf16[2,1,18,32,128]{4,3,2,1,0:T(8,128)(2,1)S(1)} %get-tuple-element.21), channel_id=1, source_target_pairs={{0,16},{1,17},{2,18},{3,19},{4,20},{5,21},{6,22},{7,23},{8,24},{9,... | collective-permute-start | bytes 884744 | tf_op jit(solution)/shard_map/ppermute | solution.py:35
  13.2 29.0 %collective-permute-start.1 = (bf16[2,1,18,32,128]{4,3,2,1,0:T(8,128)(2,1)S(1)}, bf16[2,1,18,32,128]{4,3,2,1,0:T(8,128)(2,1)S(1)}, u32[]{:S(2)}, u32[]{:S(2)}) collective-permute-start(bf16[2,1,18,32,128]{4,3,2,1,0:T(8,128)(2,1)S(1)} %get-tuple-element.20), channel_id=1, source_target_pairs={{16,0},{17,1},{18,2},{19,3},{20,4},{21,5},{22,6},{23,7},{24,8},{25... | collective-permute-start | bytes 884744 | tf_op jit(solution)/shard_map/ppermute | solution.py:35
  15.2 32.1 %collective-permute-start.2 = (bf16[2,18,1,32,128]{4,3,2,1,0:T(8,128)(2,1)S(1)}, bf16[2,18,1,32,128]{4,3,2,1,0:T(8,128)(2,1)S(1)}, u32[]{:S(2)}, u32[]{:S(2)}) collective-permute-start(bf16[2,18,1,32,128]{4,3,2,1,0:T(8,128)(2,1)S(1)} %get-tuple-element.19), channel_id=1, source_target_pairs={{0,1},{1,2},{2,3},{3,4},{4,5},{5,6},{6,7},{7,8},{8,9},{9,10},{10,1... | collective-permute-start | bytes 884744 | tf_op jit(solution)/shard_map/ppermute | solution.py:35
  17.4 31.9 %collective-permute-start.3 = (bf16[2,18,1,32,128]{4,3,2,1,0:T(8,128)(2,1)S(1)}, bf16[2,18,1,32,128]{4,3,2,1,0:T(8,128)(2,1)S(1)}, u32[]{:S(2)}, u32[]{:S(2)}) collective-permute-start(bf16[2,18,1,32,128]{4,3,2,1,0:T(8,128)(2,1)S(1)} %get-tuple-element.18), channel_id=1, source_target_pairs={{1,0},{2,1},{3,2},{4,3},{5,4},{6,5},{7,6},{8,7},{9,8},{10,9},{11,1... | collective-permute-start | bytes 884744 | tf_op jit(solution)/shard_map/ppermute | solution.py:35
  18.7 31.4 %collective-permute-start.4 = (bf16[2,1,1,32,128]{4,3,2,1,0:T(8,128)(2,1)S(1)}, bf16[2,1,1,32,128]{4,3,2,1,0:T(8,128)(2,1)S(1)}, u32[]{:S(2)}, u32[]{:S(2)}) collective-permute-start(bf16[2,1,1,32,128]{4,3,2,1,0:T(8,128)(2,1)S(1)} %get-tuple-element.17), channel_id=1, source_target_pairs={{0,17},{1,18},{2,19},{3,20},{4,21},{5,22},{6,23},{7,24},{8,25},{9,... | collective-permute-start | bytes 49160 | tf_op jit(solution)/shard_map/ppermute | solution.py:35
  39.2 11.6 %collective-permute-start.5 = (bf16[2,1,1,32,128]{4,3,2,1,0:T(8,128)(2,1)S(1)}, bf16[2,1,1,32,128]{4,3,2,1,0:T(8,128)(2,1)S(1)}, u32[]{:S(2)}, u32[]{:S(2)}) collective-permute-start(bf16[2,1,1,32,128]{4,3,2,1,0:T(8,128)(2,1)S(1)} %get-tuple-element.16), channel_id=1, source_target_pairs={{1,16},{2,17},{3,18},{4,19},{5,20},{6,21},{7,22},{8,23},{9,24},{10... | collective-permute-start | bytes 49160 | tf_op jit(solution)/shard_map/ppermute | solution.py:35
  42.2 9.1 %collective-permute-start.6 = (bf16[2,1,1,32,128]{4,3,2,1,0:T(8,128)(2,1)S(1)}, bf16[2,1,1,32,128]{4,3,2,1,0:T(8,128)(2,1)S(1)}, u32[]{:S(2)}, u32[]{:S(2)}) collective-permute-start(bf16[2,1,1,32,128]{4,3,2,1,0:T(8,128)(2,1)S(1)} %get-tuple-element.15), channel_id=1, source_target_pairs={{16,1},{17,2},{18,3},{19,4},{20,5},{21,6},{22,7},{23,8},{24,9},{25... | collective-permute-start | bytes 49160 | tf_op jit(solution)/shard_map/ppermute | solution.py:35
  47.3 6.3 %collective-permute-start.7 = (bf16[2,1,1,32,128]{4,3,2,1,0:T(8,128)(2,1)S(1)}, bf16[2,1,1,32,128]{4,3,2,1,0:T(8,128)(2,1)S(1)}, u32[]{:S(2)}, u32[]{:S(2)}) collective-permute-start(bf16[2,1,1,32,128]{4,3,2,1,0:T(8,128)(2,1)S(1)} %get-tuple-element.14), channel_id=1, source_target_pairs={{17,0},{18,1},{19,2},{20,3},{21,4},{22,5},{23,6},{24,7},{25,8},{26... | collective-permute-start | bytes 49160 | tf_op jit(solution)/shard_map/ppermute | solution.py:35
  59.8 1.2 slice-start
  62.3 2.7 %collective-permute-start.8 = (f32[1792,128]{1,0:T(8,128)S(1)}, f32[1792,128]{1,0:T(8,128)S(1)}, u32[]{:S(2)}, u32[]{:S(2)}) collective-permute-start(f32[1792,128]{1,0:T(8,128)S(1)} %pad_dynamic-slice_fusion), channel_id=1, source_target_pairs={{0,16},{16,0},{32,48},{48,32},{64,80},{80,64},{96,112},{112,96},{1... | collective-permute-start | bytes 2752520 | tf_op jit(solution)/shard_map/ppermute | solution.py:60
  63.0 4.9 %copy-start.5 = (f32[1024]{0:T(1024)S(1)}, f32[1024]{0:T(1024)}, u32[]{:S(2)}) copy-start(f32[1024]{0:T(1024)} %fusion.10) | copy-start | bytes 12292
  65.2 13.5 %collective-permute-start.9 = (f32[896,128]{1,0:T(8,128)S(1)}, f32[896,128]{1,0:T(8,128)S(1)}, u32[]{:S(2)}, u32[]{:S(2)}) collective-permute-start(f32[896,128]{1,0:T(8,128)S(1)} %constant_dynamic-slice_fusion.6), channel_id=1, source_target_pairs={{0,1},{1,0},{2,3},{3,2},{4,5},{5,4},{6,7},{7,6},{8,9},{9,8},{10,11... | collective-permute-start | bytes 1376264 | tf_op jit(solution)/shard_map/ppermute | solution.py:60
  78.7 7.2 %collective-permute-start.10 = (f32[448,128]{1,0:T(8,128)S(1)}, f32[448,128]{1,0:T(8,128)S(1)}, u32[]{:S(2)}, u32[]{:S(2)}) collective-permute-start(f32[448,128]{1,0:T(8,128)S(1)} %constant_dynamic-slice_fusion.5), channel_id=1, source_target_pairs={{0,64},{16,80},{32,96},{48,112},{64,0},{80,16},{96,32},{112,48},{1... | collective-permute-start | bytes 688136 | tf_op jit(solution)/shard_map/ppermute | solution.py:60
  86.0 4.8 %collective-permute-start.11 = (f32[224,128]{1,0:T(8,128)S(1)}, f32[224,128]{1,0:T(8,128)S(1)}, u32[]{:S(2)}, u32[]{:S(2)}) collective-permute-start(f32[224,128]{1,0:T(8,128)S(1)} %constant_dynamic-slice_fusion.4), channel_id=1, source_target_pairs={{0,2},{1,3},{2,0},{3,1},{4,6},{5,7},{6,4},{7,5},{8,10},{9,11},{10,... | collective-permute-start | bytes 344072 | tf_op jit(solution)/shard_map/ppermute | solution.py:60
  90.8 5.6 %collective-permute-start.12 = (f32[112,128]{1,0:T(8,128)S(1)}, f32[112,128]{1,0:T(8,128)S(1)}, u32[]{:S(2)}, u32[]{:S(2)}) collective-permute-start(f32[112,128]{1,0:T(8,128)S(1)} %constant_dynamic-slice_fusion.3), channel_id=1, source_target_pairs={{0,32},{16,48},{32,0},{48,16},{64,96},{80,112},{96,64},{112,80},{1... | collective-permute-start | bytes 172040 | tf_op jit(solution)/shard_map/ppermute | solution.py:60
  96.4 4.3 %collective-permute-start.13 = (f32[56,128]{1,0:T(8,128)S(1)}, f32[56,128]{1,0:T(8,128)S(1)}, u32[]{:S(2)}, u32[]{:S(2)}) collective-permute-start(f32[56,128]{1,0:T(8,128)S(1)} %constant_dynamic-slice_fusion.2), channel_id=1, source_target_pairs={{0,128},{16,144},{32,160},{48,176},{64,192},{80,208},{96,224},{112... | collective-permute-start | bytes 86024 | tf_op jit(solution)/shard_map/ppermute | solution.py:60
  100.7 9.0 %collective-permute-start.14 = (f32[28,128]{1,0:T(8,128)S(1)}, f32[28,128]{1,0:T(8,128)S(1)}, u32[]{:S(2)}, u32[]{:S(2)}) collective-permute-start(f32[28,128]{1,0:T(8,128)S(1)} %constant_dynamic-slice_fusion.1), channel_id=1, source_target_pairs={{0,4},{1,5},{2,6},{3,7},{4,0},{5,1},{6,2},{7,3},{8,12},{9,13},{10,... | collective-permute-start | bytes 43016 | tf_op jit(solution)/shard_map/ppermute | solution.py:60
  109.8 6.7 %collective-permute-start.15 = (f32[14,128]{1,0:T(8,128)S(1)}, f32[14,128]{1,0:T(8,128)S(1)}, u32[]{:S(2)}, u32[]{:S(2)}) collective-permute-start(f32[14,128]{1,0:T(8,128)S(1)} %constant_dynamic-slice_fusion), channel_id=1, source_target_pairs={{0,8},{1,9},{2,10},{3,11},{4,12},{5,13},{6,14},{7,15},{8,0},{9,1},... | collective-permute-start | bytes 21512 | tf_op jit(solution)/shard_map/ppermute | solution.py:60
  116.5 6.5 %collective-permute-start.16 = (f32[14,128]{1,0:T(8,128)S(1)}, f32[14,128]{1,0:T(8,128)S(1)}, u32[]{:S(2)}, u32[]{:S(2)}) collective-permute-start(f32[14,128]{1,0:T(8,128)S(1)} %dynamic-slice_add_fusion.6), channel_id=1, source_target_pairs={{0,8},{1,9},{2,10},{3,11},{4,12},{5,13},{6,14},{7,15},{8,0},{9,1},... | collective-permute-start | bytes 21512 | tf_op jit(solution)/shard_map/ppermute | solution.py:68
  123.1 3.6 %collective-permute-start.17 = (f32[28,128]{1,0:T(8,128)S(1)}, f32[28,128]{1,0:T(8,128)S(1)}, u32[]{:S(2)}, u32[]{:S(2)}) collective-permute-start(f32[28,128]{1,0:T(8,128)S(1)} %pad_maximum_fusion.8), channel_id=1, source_target_pairs={{0,4},{1,5},{2,6},{3,7},{4,0},{5,1},{6,2},{7,3},{8,12},{9,13},{10,... | collective-permute-start | bytes 43016 | tf_op jit(solution)/shard_map/ppermute | solution.py:68
  126.7 4.3 %collective-permute-start.18 = (f32[56,128]{1,0:T(8,128)S(1)}, f32[56,128]{1,0:T(8,128)S(1)}, u32[]{:S(2)}, u32[]{:S(2)}) collective-permute-start(f32[56,128]{1,0:T(8,128)S(1)} %pad_maximum_fusion.7), channel_id=1, source_target_pairs={{0,128},{16,144},{32,160},{48,176},{64,192},{80,208},{96,224},{112... | collective-permute-start | bytes 86024 | tf_op jit(solution)/shard_map/ppermute | solution.py:68
  131.1 4.6 %collective-permute-start.19 = (f32[112,128]{1,0:T(8,128)S(1)}, f32[112,128]{1,0:T(8,128)S(1)}, u32[]{:S(2)}, u32[]{:S(2)}) collective-permute-start(f32[112,128]{1,0:T(8,128)S(1)} %pad_maximum_fusion.6), channel_id=1, source_target_pairs={{0,32},{16,48},{32,0},{48,16},{64,96},{80,112},{96,64},{112,80},{1... | collective-permute-start | bytes 172040 | tf_op jit(solution)/shard_map/ppermute | solution.py:68
  135.7 4.0 %collective-permute-start.20 = (f32[224,128]{1,0:T(8,128)S(1)}, f32[224,128]{1,0:T(8,128)S(1)}, u32[]{:S(2)}, u32[]{:S(2)}) collective-permute-start(f32[224,128]{1,0:T(8,128)S(1)} %pad_maximum_fusion.5), channel_id=1, source_target_pairs={{0,2},{1,3},{2,0},{3,1},{4,6},{5,7},{6,4},{7,5},{8,10},{9,11},{10,... | collective-permute-start | bytes 344072 | tf_op jit(solution)/shard_map/ppermute | solution.py:68
  139.8 5.0 %collective-permute-start.21 = (f32[448,128]{1,0:T(8,128)S(1)}, f32[448,128]{1,0:T(8,128)S(1)}, u32[]{:S(2)}, u32[]{:S(2)}) collective-permute-start(f32[448,128]{1,0:T(8,128)S(1)} %pad_maximum_fusion.4), channel_id=1, source_target_pairs={{0,64},{16,80},{32,96},{48,112},{64,0},{80,16},{96,32},{112,48},{1... | collective-permute-start | bytes 688136 | tf_op jit(solution)/shard_map/ppermute | solution.py:68
  144.8 7.4 %collective-permute-start.22 = (f32[896,128]{1,0:T(8,128)S(1)}, f32[896,128]{1,0:T(8,128)S(1)}, u32[]{:S(2)}, u32[]{:S(2)}) collective-permute-start(f32[896,128]{1,0:T(8,128)S(1)} %pad_maximum_fusion.3), channel_id=1, source_target_pairs={{0,1},{1,0},{2,3},{3,2},{4,5},{5,4},{6,7},{7,6},{8,9},{9,8},{10,11... | collective-permute-start | bytes 1376264 | tf_op jit(solution)/shard_map/ppermute | solution.py:68
  152.4 16.7 %collective-permute-start.23 = (f32[1792,128]{1,0:T(8,128)S(1)}, f32[1792,128]{1,0:T(8,128)}, u32[]{:S(2)}, u32[]{:S(2)}) collective-permute-start(f32[1792,128]{1,0:T(8,128)S(1)} %pad_maximum_fusion.1), channel_id=1, source_target_pairs={{0,16},{16,0},{32,48},{48,32},{64,80},{80,64},{96,112},{112,96},{1... | collective-permute-start | bytes 2752520 | tf_op jit(solution)/shard_map/ppermute | solution.py:68

commit v6 on v4

--- a/solution.py
+++ b/solution.py
@@ -29,32 +29,65 @@
     return padded
 
 
-STEPS = (("gx", 0), ("gy", 0), ("gx", 2), ("gy", 1), ("gx", 1), ("gx", 3), ("gy", 2), ("gy", 3))
+FIRST = ("gx", 0)
+ORDERS = (
+    (("gy", 0), ("gx", 2), ("gy", 1), ("gx", 1), ("gx", 3), ("gy", 2), ("gy", 3)),
+    (("gx", 2), ("gy", 1), ("gy", 0), ("gx", 3), ("gy", 2), ("gx", 1), ("gy", 3)),
+)
 
 
-def butterfly_scatter(value, steps=STEPS):
+def step_bit(step):
+    axis, b = step
+    return (lax.axis_index(axis) >> b) & 1
+
+
+def step_pairs(k):
+    sx, sy = lax.axis_size("gx"), lax.axis_size("gy")
+    pairs = []
+    for i in range(sx):
+        for j in range(sy):
+            axis, b = ORDERS[i & 1][k]
+            pi, pj = (i ^ (1 << b), j) if axis == "gx" else (i, j ^ (1 << b))
+            pairs.append((i * sy + j, pi * sy + pj))
+    return pairs
+
+
+def core_bit(k):
+    return jnp.where(lax.axis_index("gx") & 1 == 0, step_bit(ORDERS[0][k]), step_bit(ORDERS[1][k]))
+
+
+def butterfly_scatter(value):
     lanes = value.shape[-1]
     flat = value.reshape(-1, lanes)
     rows = flat.shape[0]
-    parts = 1 << len(steps)
+    parts = 1 << (1 + len(ORDERS[0]))
     padded_rows = -(-rows // parts) * parts
     buf = jnp.pad(flat, ((0, padded_rows - rows), (0, 0)))
-    for axis, b in steps:
+    half = buf.shape[0] // 2
+    bit = step_bit(FIRST)
+    pairs = [(i, i ^ 1) for i in range(lax.axis_size("gx"))]
+    keep = lax.dynamic_slice_in_dim(buf, bit * half, half, 0)
+    send = lax.dynamic_slice_in_dim(buf, (1 - bit) * half, half, 0)
+    buf = keep + lax.ppermute(send, "gx", pairs)
+    for k in range(len(ORDERS[0])):
         half = buf.shape[0] // 2
-        pairs = [(i, i ^ (1 << b)) for i in range(lax.axis_size(axis))]
-        bit = (lax.axis_index(axis) >> b) & 1
+        bit = core_bit(k)
         keep = lax.dynamic_slice_in_dim(buf, bit * half, half, 0)
         send = lax.dynamic_slice_in_dim(buf, (1 - bit) * half, half, 0)
-        buf = keep + lax.ppermute(send, axis, pairs)
+        buf = keep + lax.ppermute(send, ("gx", "gy"), step_pairs(k))
     return buf
 
 
-def butterfly_gather(buf, like, steps=STEPS):
-    for axis, b in reversed(steps):
-        pairs = [(i, i ^ (1 << b)) for i in range(lax.axis_size(axis))]
-        bit = (lax.axis_index(axis) >> b) & 1
-        got = lax.ppermute(buf, axis, pairs)
-        buf = jnp.concatenate([jnp.where(bit == 0, buf, got), jnp.where(bit == 0, got, buf)], 0)
+def join_halves(buf, got, bit):
+    return jnp.concatenate([jnp.where(bit == 0, buf, got), jnp.where(bit == 0, got, buf)], 0)
+
+
+def butterfly_gather(buf, like):
+    for k in reversed(range(len(ORDERS[0]))):
+        got = lax.ppermute(buf, ("gx", "gy"), step_pairs(k))
+        buf = join_halves(buf, got, core_bit(k))
+    got = lax.ppermute(buf, "gx", [(i, i ^ 1) for i in range(lax.axis_size("gx"))])
+    buf = join_halves(buf, got, step_bit(FIRST))
     return buf[: like.size // like.shape[-1]].reshape(like.shape)
 
 

time: 166 us -> 161 us (0.970)
  waiting for transfers between devices: 54.6 us -> 50.3 us
    ppermute x16, waiting for transfers between devices: 46.5 us -> 42.3 us  [the longest x7 24.4 us: butterfly_gather(): got = lax.ppermute(buf, ('gx', 'gy'), step_pairs(k))]
where the time goes in v6:
time: 161 us
  starting transfers between devices  67.7 us (42%)
  waiting for transfers between devices  50.3 us (31%)
  local copies, waits for them, and re-layouts  22.6 us (14%)
  matrix products  8.6 us (5%)
  between operations  7.54 us (5%)
  other arithmetic  4.23 us (3%)
    ppermute x7, starting transfers between devices, butterfly_scatter(): buf = keep + lax.ppermute(send, ('gx', 'gy'), step_pairs(k))  29.8 us
    ppermute x7, waiting for transfers between devices, butterfly_gather(): got = lax.ppermute(buf, ('gx', 'gy'), step_pairs(k))  24.4 us
    ppermute x7, waiting for transfers between devices, butterfly_scatter(): buf = keep + lax.ppermute(send, ('gx', 'gy'), step_pairs(k))  14.1 us
    ppermute x1, starting transfers between devices, butterfly_gather(): lax.ppermute(buf, 'gx', [(i, i ^ 1) for i in range(lax.axis_size('gx'))])  13.7 us
    ppermute x7, starting transfers between devices, butterfly_gather(): got = lax.ppermute(buf, ('gx', 'gy'), step_pairs(k))  11.7 us
    ppermute x2, starting transfers between devices, with_halo(): lax.ppermute(last, axis, up)  8.87 us
    pad x1, local copies, waits for them, and re-layouts, with_halo(): padded = jnp.pad(value, pads)  5.22 us
    ppermute x2, waiting for transfers between devices, with_halo(): lax.ppermute(last, axis, up)  4.41 us
  transfers between devices with their start and end apart: 20, of which 18 were waited for; matrix products, arithmetic and copies ran while one was open for 8% of the time, Pallas kernels for 0%

profile of v6, /device:TPU:1, one launch (start us, length us, event | category | flops | bytes accessed | tf_op | source)
XLA Modules:
  0.0 160.8 jit_solution(16106338184429334737)
XLA Ops:
  1.4 0.8 broadcast_bitcast_fusion
  2.1 1.2 maximum_multiply_fusion
  3.4 2.0 %convolution_convert_fusion = bf16[2,512,128,16]{2,3,1,0:T(8,128)(2,1)S(1)} fusion(bf16[2,2,512,128]{3,2,1,0:T(8,128)(2,1)S(1)} %maximum_multiply_fusion, pred[2]{0:T(512)(128)(4,1)S(1)} %get-tuple-element.94, s32[2]{0:T(128)} %bitcast.185), kind=kOutput, calls=%fused_computation | convolution fusion | flops 10485824 | bytes 4718602 | tf_op jit(solution)/shard_map/ps,tsvc->tpvc/dot_general | solution.py:97
  5.4 1.6 %copy.12 = bf16[2,2,2,4,8,8,8,128]{7,6,3,5,2,4,1,0:T(8,128)(2,1)S(1)} copy(bf16[2,2,2,4,8,8,8,128]{7,3,2,1,6,5,4,0:T(4,128)(2,1)S(1)} %bitcast.123) | data formatting | bytes 8388608 | tf_op jit(solution)/shard_map/reshape | solution.py:101
  7.1 0.2 pad_slice_fusion.2
  7.3 6.0 %collective-permute-start = (bf16[2,1,18,34,128]{4,3,2,1,0:T(8,128)(2,1)S(1)}, bf16[2,1,18,34,128]{4,3,2,1,0:T(8,128)(2,1)S(1)}, u32[]{:S(2)}, u32[]{:S(2)}) collective-permute-start(bf16[2,1,18,34,128]{4,3,2,1,0:T(8,128)(2,1)S(1)} %get-tuple-element.17), channel_id=1, source_target_pairs={{0,16},{16,32},{32,48},{48,64},{64,80},{80,96},{96,112},{112,128},... | collective-permute-start | bytes 940040 | tf_op jit(solution)/shard_map/ppermute | solution.py:25
  13.4 1.9 %collective-permute-start.1 = (bf16[2,1,18,34,128]{4,3,2,1,0:T(8,128)(2,1)S(1)}, bf16[2,1,18,34,128]{4,3,2,1,0:T(8,128)(2,1)S(1)}, u32[]{:S(2)}, u32[]{:S(2)}) collective-permute-start(bf16[2,1,18,34,128]{4,3,2,1,0:T(8,128)(2,1)S(1)} %get-tuple-element.16), channel_id=1, source_target_pairs={{16,0},{32,16},{48,32},{64,48},{80,64},{96,80},{112,96},{128,112},... | collective-permute-start | bytes 940040 | tf_op jit(solution)/shard_map/ppermute | solution.py:27
  15.3 5.2 %pad.8 = bf16[2,18,18,34,128]{4,3,2,1,0:T(8,128)(2,1)} pad(bf16[2,16,16,32,128]{4,3,2,1,0:T(8,128)(2,1)S(1)} %bitcast.120, bf16[]{:T(256)} %constant.82.clone.1), padding=0_0x1_1x1_1x1_1x0_0 | pad | bytes 9834498 | tf_op jit(solution)/shard_map/jit(_pad)/pad | solution.py:18
  20.5 0.8 constant_dynamic-update-slice_fusion.57
  21.3 2.4 %collective-permute-done.1 = bf16[2,1,18,34,128]{4,3,2,1,0:T(8,128)(2,1)S(1)} collective-permute-done((bf16[2,1,18,34,128]{4,3,2,1,0:T(8,128)(2,1)S(1)}, bf16[2,1,18,34,128]{4,3,2,1,0:T(8,128)(2,1)S(1)}, u32[]{:S(2)}, u32[]{:S(2)}) %collective-permute-start.1) | collective-permute-done | bytes 313376 | tf_op jit(solution)/shard_map/ppermute | solution.py:27
  23.7 0.8 constant_dynamic-update-slice_fusion.56
  24.5 1.0 slice.259
  25.5 2.8 %collective-permute-start.2 = (bf16[2,18,1,34,128]{4,3,2,1,0:T(8,128)(2,1)S(1)}, bf16[2,18,1,34,128]{4,3,2,1,0:T(8,128)(2,1)S(1)}, u32[]{:S(2)}, u32[]{:S(2)}) collective-permute-start(bf16[2,18,1,34,128]{4,3,2,1,0:T(8,128)(2,1)S(1)} %slice.259), channel_id=1, source_target_pairs={{0,1},{1,2},{2,3},{3,4},{4,5},{5,6},{6,7},{7,8},{8,9},{9,10},{10,1... | collective-permute-start | bytes 940040 | tf_op jit(solution)/shard_map/ppermute | solution.py:25
  28.4 4.4 %collective-permute-done.2 = bf16[2,18,1,34,128]{4,3,2,1,0:T(8,128)(2,1)S(1)} collective-permute-done((bf16[2,18,1,34,128]{4,3,2,1,0:T(8,128)(2,1)S(1)}, bf16[2,18,1,34,128]{4,3,2,1,0:T(8,128)(2,1)S(1)}, u32[]{:S(2)}, u32[]{:S(2)}) %collective-permute-start.2) | collective-permute-done | bytes 313376 | tf_op jit(solution)/shard_map/ppermute | solution.py:25
  32.8 2.0 %fusion.18 = (bf16[2,18,1,34,128]{4,3,2,1,0:T(8,128)(2,1)S(1)}, bf16[2,18,18,34,128]{4,3,2,1,0:T(8,128)(2,1)}) fusion(bf16[2,18,18,34,128]{4,3,2,1,0:T(8,128)(2,1)} %constant_dynamic-update-slice_fusion.56, bf16[2,18,1,34,128]{4,3,2,1,0:T(8,128)(2,1)S(1)} %collective-permute-done.2), kind=kLoop, calls=%fused_computation.132 | loop fusion | bytes 1363968 | tf_op jit(solution)/shard_map/slice | solution.py:24
  34.8 1.5 collective-permute-start.3
  36.2 0.6 fusion.23
  42.2 1.2 collective-permute-done.3
  43.5 0.9 constant_dynamic-update-slice_fusion.54
  44.3 2.4 %dynamic-slice_bitcast_fusion = (bf16[2,1,10,10,10,128]{5,4,3,2,1,0:T(8,128)(2,1)S(1)}, bf16[2,1,10,10,10,128]{5,4,3,2,1,0:T(8,128)(2,1)S(1)}) fusion(bf16[2,18,18,34,128]{4,3,2,1,0:T(8,128)(2,1)} %constant_dynamic-update-slice_fusion.54, s32[]{:T(128)S(6)} %select_n.228, s32[]{:T(128)S(6)} %select_n.231, s32[]{:T(128)S(6)} %select_n.233, s32[]{:T(128)S(6)} %select_n.221, ...), kind=kLoop, calls=%fused_computation.21 | loop fusion | bytes 2048024 | tf_op jit(solution)/shard_map/stack | solution.py:115
  46.7 0.3 fusion.7
  47.0 0.4 fusion.22
  47.4 1.0 fusion.21
  48.5 0.5 fusion.20
  48.9 1.0 fusion.19
  51.2 1.1 convolution_multiply_fusion
  52.3 0.1 pad_dynamic-slice_fusion
  52.4 0.1 collective-permute-start.4
  53.4 1.5 collective-permute-done.4
  55.0 0.1 fusion.4
  55.2 9.6 %collective-permute-start.5 = (f32[896,128]{1,0:T(8,128)S(1)}, f32[896,128]{1,0:T(8,128)S(1)}, u32[]{:S(2)}, u32[]{:S(2)}) collective-permute-start(f32[896,128]{1,0:T(8,128)S(1)} %constant_dynamic-slice_fusion.6), channel_id=1, source_target_pairs={{0,1},{1,0},{2,3},{3,2},{4,5},{5,4},{6,7},{7,6},{8,9},{9,8},{10,11... | collective-permute-start | bytes 1376264 | tf_op jit(solution)/shard_map/ppermute | solution.py:77
  64.7 2.7 %fusion.2 = bf16[1024,128]{1,0:T(8,128)(2,1)} fusion(bf16[27,1024,128]{2,1,0:T(8,128)(2,1)S(1)} %constant_dynamic-update-slice_fusion, bf16[27,128,128]{2,1,0:T(8,128)(2,1)S(1)} %copy-done, f32[1024]{0:T(1024)S(1)} %fusion.10), kind=kOutput, calls=%fused_computation.11 | convolution fusion | flops 906231808 | bytes 8228864 | tf_op jit(solution)/shard_map/dvc,dce->ve/dot_general | solution.py:144
  67.4 3.2 %collective-permute-done.5 = f32[896,128]{1,0:T(8,128)S(1)} collective-permute-done((f32[896,128]{1,0:T(8,128)S(1)}, f32[896,128]{1,0:T(8,128)S(1)}, u32[]{:S(2)}, u32[]{:S(2)}) %collective-permute-start.5) | collective-permute-done | bytes 458784 | tf_op jit(solution)/shard_map/ppermute | solution.py:77
  70.7 2.7 %collective-permute-start.6 = (f32[448,128]{1,0:T(8,128)S(1)}, f32[448,128]{1,0:T(8,128)S(1)}, u32[]{:S(2)}, u32[]{:S(2)}) collective-permute-start(f32[448,128]{1,0:T(8,128)S(1)} %constant_dynamic-slice_fusion.5), channel_id=1, source_target_pairs={{0,64},{1,65},{2,66},{3,67},{4,68},{5,69},{6,70},{7,71},{8,72},{9,... | collective-permute-start | bytes 688136 | tf_op jit(solution)/shard_map/ppermute | solution.py:77
  73.4 3.6 %collective-permute-done.6 = f32[448,128]{1,0:T(8,128)S(1)} collective-permute-done((f32[448,128]{1,0:T(8,128)S(1)}, f32[448,128]{1,0:T(8,128)S(1)}, u32[]{:S(2)}, u32[]{:S(2)}) %collective-permute-start.6) | collective-permute-done | bytes 229408 | tf_op jit(solution)/shard_map/ppermute | solution.py:77
  77.1 1.5 collective-permute-start.7
  78.6 2.2 %collective-permute-done.7 = f32[224,128]{1,0:T(8,128)S(1)} collective-permute-done((f32[224,128]{1,0:T(8,128)S(1)}, f32[224,128]{1,0:T(8,128)S(1)}, u32[]{:S(2)}, u32[]{:S(2)}) %collective-permute-start.7) | collective-permute-done | bytes 114720 | tf_op jit(solution)/shard_map/ppermute | solution.py:77
  80.9 3.6 %collective-permute-start.8 = (f32[112,128]{1,0:T(8,128)S(1)}, f32[112,128]{1,0:T(8,128)S(1)}, u32[]{:S(2)}, u32[]{:S(2)}) collective-permute-start(f32[112,128]{1,0:T(8,128)S(1)} %constant_dynamic-slice_fusion.3), channel_id=1, source_target_pairs={{0,32},{1,33},{2,34},{3,35},{4,36},{5,37},{6,38},{7,39},{8,40},{9,... | collective-permute-start | bytes 172040 | tf_op jit(solution)/shard_map/ppermute | solution.py:77
  84.5 1.5 collective-permute-done.8
  86.1 5.1 %collective-permute-start.9 = (f32[56,128]{1,0:T(8,128)S(1)}, f32[56,128]{1,0:T(8,128)S(1)}, u32[]{:S(2)}, u32[]{:S(2)}) collective-permute-start(f32[56,128]{1,0:T(8,128)S(1)} %constant_dynamic-slice_fusion.2), channel_id=1, source_target_pairs={{0,128},{1,129},{2,130},{3,131},{4,132},{5,133},{6,134},{7,135},{8... | collective-permute-start | bytes 86024 | tf_op jit(solution)/shard_map/ppermute | solution.py:77
  91.2 1.2 collective-permute-done.9
  92.4 2.0 %collective-permute-start.10 = (f32[28,128]{1,0:T(8,128)S(1)}, f32[28,128]{1,0:T(8,128)S(1)}, u32[]{:S(2)}, u32[]{:S(2)}) collective-permute-start(f32[28,128]{1,0:T(8,128)S(1)} %constant_dynamic-slice_fusion.1), channel_id=1, source_target_pairs={{0,4},{1,5},{2,6},{3,7},{4,0},{5,1},{6,2},{7,3},{8,12},{9,13},{10,... | collective-permute-start | bytes 43016 | tf_op jit(solution)/shard_map/ppermute | solution.py:77
  94.5 2.3 %collective-permute-done.10 = f32[28,128]{1,0:T(8,128)S(1)} collective-permute-done((f32[28,128]{1,0:T(8,128)S(1)}, f32[28,128]{1,0:T(8,128)S(1)}, u32[]{:S(2)}, u32[]{:S(2)}) %collective-permute-start.10) | collective-permute-done | bytes 14368 | tf_op jit(solution)/shard_map/ppermute | solution.py:77
  96.9 5.4 %collective-permute-start.11 = (f32[14,128]{1,0:T(8,128)S(1)}, f32[14,128]{1,0:T(8,128)S(1)}, u32[]{:S(2)}, u32[]{:S(2)}) collective-permute-start(f32[14,128]{1,0:T(8,128)S(1)} %constant_dynamic-slice_fusion), channel_id=1, source_target_pairs={{0,8},{1,9},{2,10},{3,11},{4,12},{5,13},{6,14},{7,15},{8,0},{9,1},... | collective-permute-start | bytes 21512 | tf_op jit(solution)/shard_map/ppermute | solution.py:77
  102.3 2.7 %fusion.3 = bf16[1024,128]{1,0:T(8,128)(2,1)} fusion(bf16[27,1024,128]{2,1,0:T(8,128)(2,1)S(1)} %constant_dynamic-update-slice_fusion.27, bf16[27,128,128]{2,1,0:T(8,128)(2,1)S(1)} %copy-done, f32[1024]{0:T(1024)S(1)} %fusion.10), kind=kOutput, calls=%fused_computation.12 | convolution fusion | flops 906231808 | bytes 8228864 | tf_op jit(solution)/shard_map/dvc,dec->ve/dot_general | solution.py:147
  105.0 3.8 %collective-permute-start.12 = (f32[14,128]{1,0:T(8,128)S(1)}, f32[14,128]{1,0:T(8,128)S(1)}, u32[]{:S(2)}, u32[]{:S(2)}) collective-permute-start(f32[14,128]{1,0:T(8,128)S(1)} %dynamic-slice_add_fusion.6), channel_id=1, source_target_pairs={{0,8},{1,9},{2,10},{3,11},{4,12},{5,13},{6,14},{7,15},{8,0},{9,1},... | collective-permute-start | bytes 21512 | tf_op jit(solution)/shard_map/ppermute | solution.py:87
  108.8 2.7 %collective-permute-done.12 = f32[14,128]{1,0:T(8,128)S(1)} collective-permute-done((f32[14,128]{1,0:T(8,128)S(1)}, f32[14,128]{1,0:T(8,128)S(1)}, u32[]{:S(2)}, u32[]{:S(2)}) %collective-permute-start.12) | collective-permute-done | bytes 7200 | tf_op jit(solution)/shard_map/ppermute | solution.py:87
  111.5 2.2 %collective-permute-start.13 = (f32[28,128]{1,0:T(8,128)S(1)}, f32[28,128]{1,0:T(8,128)S(1)}, u32[]{:S(2)}, u32[]{:S(2)}) collective-permute-start(f32[28,128]{1,0:T(8,128)S(1)} %pad_maximum_fusion.8), channel_id=1, source_target_pairs={{0,4},{1,5},{2,6},{3,7},{4,0},{5,1},{6,2},{7,3},{8,12},{9,13},{10,... | collective-permute-start | bytes 43016 | tf_op jit(solution)/shard_map/ppermute | solution.py:87
  113.7 2.0 %collective-permute-done.13 = f32[28,128]{1,0:T(8,128)S(1)} collective-permute-done((f32[28,128]{1,0:T(8,128)S(1)}, f32[28,128]{1,0:T(8,128)S(1)}, u32[]{:S(2)}, u32[]{:S(2)}) %collective-permute-start.13) | collective-permute-done | bytes 14368 | tf_op jit(solution)/shard_map/ppermute | solution.py:87
  115.7 1.2 collective-permute-start.14
  116.9 2.5 %collective-permute-done.14 = f32[56,128]{1,0:T(8,128)S(1)} collective-permute-done((f32[56,128]{1,0:T(8,128)S(1)}, f32[56,128]{1,0:T(8,128)S(1)}, u32[]{:S(2)}, u32[]{:S(2)}) %collective-permute-start.14) | collective-permute-done | bytes 28704 | tf_op jit(solution)/shard_map/ppermute | solution.py:87
  119.4 3.5 %collective-permute-start.15 = (f32[112,128]{1,0:T(8,128)S(1)}, f32[112,128]{1,0:T(8,128)S(1)}, u32[]{:S(2)}, u32[]{:S(2)}) collective-permute-start(f32[112,128]{1,0:T(8,128)S(1)} %pad_maximum_fusion.6), channel_id=1, source_target_pairs={{0,32},{1,33},{2,34},{3,35},{4,36},{5,37},{6,38},{7,39},{8,40},{9,... | collective-permute-start | bytes 172040 | tf_op jit(solution)/shard_map/ppermute | solution.py:87
  123.0 1.6 collective-permute-done.15
  124.6 0.1 collective-permute-start.16
  124.7 3.9 %collective-permute-done.16 = f32[224,128]{1,0:T(8,128)S(1)} collective-permute-done((f32[224,128]{1,0:T(8,128)S(1)}, f32[224,128]{1,0:T(8,128)S(1)}, u32[]{:S(2)}, u32[]{:S(2)}) %collective-permute-start.16) | collective-permute-done | bytes 114720 | tf_op jit(solution)/shard_map/ppermute | solution.py:87
  128.6 0.2 collective-permute-start.17
  128.9 5.0 %collective-permute-done.17 = f32[448,128]{1,0:T(8,128)S(1)} collective-permute-done((f32[448,128]{1,0:T(8,128)S(1)}, f32[448,128]{1,0:T(8,128)S(1)}, u32[]{:S(2)}, u32[]{:S(2)}) %collective-permute-start.17) | collective-permute-done | bytes 229408 | tf_op jit(solution)/shard_map/ppermute | solution.py:87
  134.0 0.7 collective-permute-start.18
  134.7 6.7 %collective-permute-done.18 = f32[896,128]{1,0:T(8,128)S(1)} collective-permute-done((f32[896,128]{1,0:T(8,128)S(1)}, f32[896,128]{1,0:T(8,128)S(1)}, u32[]{:S(2)}, u32[]{:S(2)}) %collective-permute-start.18) | collective-permute-done | bytes 458784 | tf_op jit(solution)/shard_map/ppermute | solution.py:87
  141.5 13.7 %collective-permute-start.19 = (f32[1792,128]{1,0:T(8,128)S(1)}, f32[1792,128]{1,0:T(8,128)}, u32[]{:S(2)}, u32[]{:S(2)}) collective-permute-start(f32[1792,128]{1,0:T(8,128)S(1)} %pad_maximum_fusion.1), channel_id=1, source_target_pairs={{0,16},{16,0},{32,48},{48,32},{64,80},{80,64},{96,112},{112,96},{1... | collective-permute-start | bytes 2752520 | tf_op jit(solution)/shard_map/ppermute | solution.py:89
  155.3 2.2 %collective-permute-done.19 = f32[1792,128]{1,0:T(8,128)} collective-permute-done((f32[1792,128]{1,0:T(8,128)S(1)}, f32[1792,128]{1,0:T(8,128)}, u32[]{:S(2)}, u32[]{:S(2)}) %collective-permute-start.19) | collective-permute-done | bytes 917536 | tf_op jit(solution)/shard_map/ppermute | solution.py:89
  157.5 1.3 broadcast_select_fusion.1
  158.8 0.1 pad_maximum_fusion
  158.9 1.9 %copy.14 = f32[27,128,128]{2,1,0:T(8,128)} copy(f32[27,128,128]{1,2,0:T(8,128)S(1)} %bitcast.124) | data formatting | bytes 3538944
  (98 shorter events, 2.5 us)
Async XLA Ops:
  0.6 64.1 %copy-start = (bf16[27,128,128]{2,1,0:T(8,128)(2,1)S(1)}, bf16[27,128,128]{2,1,0:T(8,128)(2,1)}, u32[]{:S(2)}) copy-start(bf16[27,128,128]{2,1,0:T(8,128)(2,1)} %param.10) | copy-start | bytes 2654212
  3.4 25.0 %copy-start.1 = (bf16[2,2,512,128]{3,2,1,0:T(8,128)(2,1)}, bf16[2,2,512,128]{3,2,1,0:T(8,128)(2,1)S(1)}, u32[]{:S(2)}) copy-start(bf16[2,2,512,128]{3,2,1,0:T(8,128)(2,1)S(1)} %maximum_multiply_fusion) | copy-start | bytes 1572868
  7.3 13.2 %collective-permute-start = (bf16[2,1,18,34,128]{4,3,2,1,0:T(8,128)(2,1)S(1)}, bf16[2,1,18,34,128]{4,3,2,1,0:T(8,128)(2,1)S(1)}, u32[]{:S(2)}, u32[]{:S(2)}) collective-permute-start(bf16[2,1,18,34,128]{4,3,2,1,0:T(8,128)(2,1)S(1)} %get-tuple-element.17), channel_id=1, source_target_pairs={{0,16},{16,32},{32,48},{48,64},{64,80},{80,96},{96,112},{112,128},... | collective-permute-start | bytes 940040 | tf_op jit(solution)/shard_map/ppermute | solution.py:25
  13.3 22.9 %copy-start.3 = (s32[1,1,2]{2,1,0:T(1,128)S(1)}, s32[1,1,2]{2,1,0:T(1,128)}, u32[]{:S(2)}) copy-start(s32[1,1,2]{2,1,0:T(1,128)} %param.8) | copy-start | bytes 28
  13.3 28.8 %copy-start.2 = (s32[1,1,2,512]{3,2,1,0:T(2,128)S(1)}, s32[1,1,2,512]{3,2,1,0:T(2,128)}, u32[]{:S(2)}) copy-start(s32[1,1,2,512]{3,2,1,0:T(2,128)} %param.7) | copy-start | bytes 12292
  13.4 10.3 %collective-permute-start.1 = (bf16[2,1,18,34,128]{4,3,2,1,0:T(8,128)(2,1)S(1)}, bf16[2,1,18,34,128]{4,3,2,1,0:T(8,128)(2,1)S(1)}, u32[]{:S(2)}, u32[]{:S(2)}) collective-permute-start(bf16[2,1,18,34,128]{4,3,2,1,0:T(8,128)(2,1)S(1)} %get-tuple-element.16), channel_id=1, source_target_pairs={{16,0},{32,16},{48,32},{64,48},{80,64},{96,80},{112,96},{128,112},... | collective-permute-start | bytes 940040 | tf_op jit(solution)/shard_map/ppermute | solution.py:27
  25.5 7.3 %collective-permute-start.2 = (bf16[2,18,1,34,128]{4,3,2,1,0:T(8,128)(2,1)S(1)}, bf16[2,18,1,34,128]{4,3,2,1,0:T(8,128)(2,1)S(1)}, u32[]{:S(2)}, u32[]{:S(2)}) collective-permute-start(bf16[2,18,1,34,128]{4,3,2,1,0:T(8,128)(2,1)S(1)} %slice.259), channel_id=1, source_target_pairs={{0,1},{1,2},{2,3},{3,4},{4,5},{5,6},{6,7},{7,8},{8,9},{9,10},{10,1... | collective-permute-start | bytes 940040 | tf_op jit(solution)/shard_map/ppermute | solution.py:25
  34.8 8.7 %collective-permute-start.3 = (bf16[2,18,1,34,128]{4,3,2,1,0:T(8,128)(2,1)S(1)}, bf16[2,18,1,34,128]{4,3,2,1,0:T(8,128)(2,1)S(1)}, u32[]{:S(2)}, u32[]{:S(2)}) collective-permute-start(bf16[2,18,1,34,128]{4,3,2,1,0:T(8,128)(2,1)S(1)} %get-tuple-element.14), channel_id=1, source_target_pairs={{1,0},{2,1},{3,2},{4,3},{5,4},{6,5},{7,6},{8,7},{9,8},{10,9},{11,1... | collective-permute-start | bytes 940040 | tf_op jit(solution)/shard_map/ppermute | solution.py:27
  50.0 1.2 slice-start
  52.4 2.6 %collective-permute-start.4 = (f32[1792,128]{1,0:T(8,128)S(1)}, f32[1792,128]{1,0:T(8,128)S(1)}, u32[]{:S(2)}, u32[]{:S(2)}) collective-permute-start(f32[1792,128]{1,0:T(8,128)S(1)} %pad_dynamic-slice_fusion), channel_id=1, source_target_pairs={{0,16},{16,0},{32,48},{48,32},{64,80},{80,64},{96,112},{112,96},{1... | collective-permute-start | bytes 2752520 | tf_op jit(solution)/shard_map/ppermute | solution.py:71
  55.2 15.4 %collective-permute-start.5 = (f32[896,128]{1,0:T(8,128)S(1)}, f32[896,128]{1,0:T(8,128)S(1)}, u32[]{:S(2)}, u32[]{:S(2)}) collective-permute-start(f32[896,128]{1,0:T(8,128)S(1)} %constant_dynamic-slice_fusion.6), channel_id=1, source_target_pairs={{0,1},{1,0},{2,3},{3,2},{4,5},{5,4},{6,7},{7,6},{8,9},{9,8},{10,11... | collective-permute-start | bytes 1376264 | tf_op jit(solution)/shard_map/ppermute | solution.py:77
  70.7 6.4 %collective-permute-start.6 = (f32[448,128]{1,0:T(8,128)S(1)}, f32[448,128]{1,0:T(8,128)S(1)}, u32[]{:S(2)}, u32[]{:S(2)}) collective-permute-start(f32[448,128]{1,0:T(8,128)S(1)} %constant_dynamic-slice_fusion.5), channel_id=1, source_target_pairs={{0,64},{1,65},{2,66},{3,67},{4,68},{5,69},{6,70},{7,71},{8,72},{9,... | collective-permute-start | bytes 688136 | tf_op jit(solution)/shard_map/ppermute | solution.py:77
  77.1 3.7 %collective-permute-start.7 = (f32[224,128]{1,0:T(8,128)S(1)}, f32[224,128]{1,0:T(8,128)S(1)}, u32[]{:S(2)}, u32[]{:S(2)}) collective-permute-start(f32[224,128]{1,0:T(8,128)S(1)} %constant_dynamic-slice_fusion.4), channel_id=1, source_target_pairs={{0,2},{1,3},{2,0},{3,1},{4,6},{5,7},{6,4},{7,5},{8,10},{9,11},{10,... | collective-permute-start | bytes 344072 | tf_op jit(solution)/shard_map/ppermute | solution.py:77
  80.9 5.1 %collective-permute-start.8 = (f32[112,128]{1,0:T(8,128)S(1)}, f32[112,128]{1,0:T(8,128)S(1)}, u32[]{:S(2)}, u32[]{:S(2)}) collective-permute-start(f32[112,128]{1,0:T(8,128)S(1)} %constant_dynamic-slice_fusion.3), channel_id=1, source_target_pairs={{0,32},{1,33},{2,34},{3,35},{4,36},{5,37},{6,38},{7,39},{8,40},{9,... | collective-permute-start | bytes 172040 | tf_op jit(solution)/shard_map/ppermute | solution.py:77
  86.1 6.4 %collective-permute-start.9 = (f32[56,128]{1,0:T(8,128)S(1)}, f32[56,128]{1,0:T(8,128)S(1)}, u32[]{:S(2)}, u32[]{:S(2)}) collective-permute-start(f32[56,128]{1,0:T(8,128)S(1)} %constant_dynamic-slice_fusion.2), channel_id=1, source_target_pairs={{0,128},{1,129},{2,130},{3,131},{4,132},{5,133},{6,134},{7,135},{8... | collective-permute-start | bytes 86024 | tf_op jit(solution)/shard_map/ppermute | solution.py:77
  92.4 4.4 %collective-permute-start.10 = (f32[28,128]{1,0:T(8,128)S(1)}, f32[28,128]{1,0:T(8,128)S(1)}, u32[]{:S(2)}, u32[]{:S(2)}) collective-permute-start(f32[28,128]{1,0:T(8,128)S(1)} %constant_dynamic-slice_fusion.1), channel_id=1, source_target_pairs={{0,4},{1,5},{2,6},{3,7},{4,0},{5,1},{6,2},{7,3},{8,12},{9,13},{10,... | collective-permute-start | bytes 43016 | tf_op jit(solution)/shard_map/ppermute | solution.py:77
  96.9 8.1 %collective-permute-start.11 = (f32[14,128]{1,0:T(8,128)S(1)}, f32[14,128]{1,0:T(8,128)S(1)}, u32[]{:S(2)}, u32[]{:S(2)}) collective-permute-start(f32[14,128]{1,0:T(8,128)S(1)} %constant_dynamic-slice_fusion), channel_id=1, source_target_pairs={{0,8},{1,9},{2,10},{3,11},{4,12},{5,13},{6,14},{7,15},{8,0},{9,1},... | collective-permute-start | bytes 21512 | tf_op jit(solution)/shard_map/ppermute | solution.py:77
  105.0 6.5 %collective-permute-start.12 = (f32[14,128]{1,0:T(8,128)S(1)}, f32[14,128]{1,0:T(8,128)S(1)}, u32[]{:S(2)}, u32[]{:S(2)}) collective-permute-start(f32[14,128]{1,0:T(8,128)S(1)} %dynamic-slice_add_fusion.6), channel_id=1, source_target_pairs={{0,8},{1,9},{2,10},{3,11},{4,12},{5,13},{6,14},{7,15},{8,0},{9,1},... | collective-permute-start | bytes 21512 | tf_op jit(solution)/shard_map/ppermute | solution.py:87
  111.5 4.2 %collective-permute-start.13 = (f32[28,128]{1,0:T(8,128)S(1)}, f32[28,128]{1,0:T(8,128)S(1)}, u32[]{:S(2)}, u32[]{:S(2)}) collective-permute-start(f32[28,128]{1,0:T(8,128)S(1)} %pad_maximum_fusion.8), channel_id=1, source_target_pairs={{0,4},{1,5},{2,6},{3,7},{4,0},{5,1},{6,2},{7,3},{8,12},{9,13},{10,... | collective-permute-start | bytes 43016 | tf_op jit(solution)/shard_map/ppermute | solution.py:87
  115.7 3.7 %collective-permute-start.14 = (f32[56,128]{1,0:T(8,128)S(1)}, f32[56,128]{1,0:T(8,128)S(1)}, u32[]{:S(2)}, u32[]{:S(2)}) collective-permute-start(f32[56,128]{1,0:T(8,128)S(1)} %pad_maximum_fusion.7), channel_id=1, source_target_pairs={{0,128},{1,129},{2,130},{3,131},{4,132},{5,133},{6,134},{7,135},{8... | collective-permute-start | bytes 86024 | tf_op jit(solution)/shard_map/ppermute | solution.py:87
  119.4 5.1 %collective-permute-start.15 = (f32[112,128]{1,0:T(8,128)S(1)}, f32[112,128]{1,0:T(8,128)S(1)}, u32[]{:S(2)}, u32[]{:S(2)}) collective-permute-start(f32[112,128]{1,0:T(8,128)S(1)} %pad_maximum_fusion.6), channel_id=1, source_target_pairs={{0,32},{1,33},{2,34},{3,35},{4,36},{5,37},{6,38},{7,39},{8,40},{9,... | collective-permute-start | bytes 172040 | tf_op jit(solution)/shard_map/ppermute | solution.py:87
  124.6 4.0 %collective-permute-start.16 = (f32[224,128]{1,0:T(8,128)S(1)}, f32[224,128]{1,0:T(8,128)S(1)}, u32[]{:S(2)}, u32[]{:S(2)}) collective-permute-start(f32[224,128]{1,0:T(8,128)S(1)} %pad_maximum_fusion.5), channel_id=1, source_target_pairs={{0,2},{1,3},{2,0},{3,1},{4,6},{5,7},{6,4},{7,5},{8,10},{9,11},{10,... | collective-permute-start | bytes 344072 | tf_op jit(solution)/shard_map/ppermute | solution.py:87
  128.6 5.3 %collective-permute-start.17 = (f32[448,128]{1,0:T(8,128)S(1)}, f32[448,128]{1,0:T(8,128)S(1)}, u32[]{:S(2)}, u32[]{:S(2)}) collective-permute-start(f32[448,128]{1,0:T(8,128)S(1)} %pad_maximum_fusion.4), channel_id=1, source_target_pairs={{0,64},{1,65},{2,66},{3,67},{4,68},{5,69},{6,70},{7,71},{8,72},{9,... | collective-permute-start | bytes 688136 | tf_op jit(solution)/shard_map/ppermute | solution.py:87
  134.0 7.4 %collective-permute-start.18 = (f32[896,128]{1,0:T(8,128)S(1)}, f32[896,128]{1,0:T(8,128)S(1)}, u32[]{:S(2)}, u32[]{:S(2)}) collective-permute-start(f32[896,128]{1,0:T(8,128)S(1)} %pad_maximum_fusion.3), channel_id=1, source_target_pairs={{0,1},{1,0},{2,3},{3,2},{4,5},{5,4},{6,7},{7,6},{8,9},{9,8},{10,11... | collective-permute-start | bytes 1376264 | tf_op jit(solution)/shard_map/ppermute | solution.py:87
  141.5 16.0 %collective-permute-start.19 = (f32[1792,128]{1,0:T(8,128)S(1)}, f32[1792,128]{1,0:T(8,128)}, u32[]{:S(2)}, u32[]{:S(2)}) collective-permute-start(f32[1792,128]{1,0:T(8,128)S(1)} %pad_maximum_fusion.1), channel_id=1, source_target_pairs={{0,16},{16,0},{32,48},{48,32},{64,80},{80,64},{96,112},{112,96},{1... | collective-permute-start | bytes 2752520 | tf_op jit(solution)/shard_map/ppermute | solution.py:89

commit v7 on v6

--- a/solution.py
+++ b/solution.py
@@ -10,22 +10,26 @@
 OFFS = 27
 
 
-def with_halo(value, sides):
-    pads = [(0, 0)] * value.ndim
-    for _, dim in sides:
-        pads[dim] = (1, 1)
-    pads[-2] = (1, 1)
-    padded = jnp.pad(value, pads)
-    for axis, dim in sides:
-        size, length = lax.axis_size(axis), padded.shape[dim]
-        up = [(i, (i + 1) % size) for i in range(size - 1)]
-        down = [(j, i) for i, j in up]
-        last = lax.slice_in_dim(padded, length - 2, length - 1, axis=dim)
-        leading = lax.slice_in_dim(padded, 1, 2, axis=dim)
-        padded = lax.dynamic_update_slice_in_dim(padded, lax.ppermute(last, axis, up), 0, axis=dim)
-        padded = lax.dynamic_update_slice_in_dim(
-            padded, lax.ppermute(leading, axis, down), length - 1, axis=dim
-        )
+def with_halo(value):
+    nx, ny = value.shape[1], value.shape[2]
+    size_x, size_y = lax.axis_size("gx"), lax.axis_size("gy")
+    up_x = [(i, i + 1) for i in range(size_x - 1)]
+    up_y = [(i, i + 1) for i in range(size_y - 1)]
+    down_x = [(j, i) for i, j in up_x]
+    down_y = [(j, i) for i, j in up_y]
+    from_left = lax.ppermute(value[:, nx - 1 : nx], "gx", up_x)
+    from_right = lax.ppermute(value[:, 0:1], "gx", down_x)
+    padded = jnp.pad(value, ((0, 0), (1, 1), (1, 1), (1, 1), (0, 0)))
+
+    def row(at):
+        return jnp.concatenate([from_left[:, :, at], value[:, :, at], from_right[:, :, at]], 1)
+
+    from_below = lax.ppermute(row(slice(ny - 1, ny)), "gy", up_y)
+    from_above = lax.ppermute(row(slice(0, 1)), "gy", down_y)
+    padded = lax.dynamic_update_slice(padded, from_left, (0, 0, 1, 1, 0))
+    padded = lax.dynamic_update_slice(padded, from_right, (0, nx + 1, 1, 1, 0))
+    padded = lax.dynamic_update_slice(padded, from_below, (0, 0, 0, 1, 0))
+    padded = lax.dynamic_update_slice(padded, from_above, (0, 0, ny + 1, 1, 0))
     return padded
 
 
@@ -134,7 +138,7 @@
     both = jnp.stack([features[0, 0], cotangent[0, 0]]) * keeper[None, :, :, None]
     grad_rows = both[1].reshape(-1, chans)
     dense = place_bricks(both, places, alive)
-    padded = with_halo(dense, (("gx", 1), ("gy", 2)))
+    padded = with_halo(dense)
     windows = cut_windows(padded, places)
     feat_stack = stack_offsets(windows[0])
     tiles = lax.axis_size("gx") * lax.axis_size("gy")

time: 161 us -> 169 us (1.050)
  local copies, waits for them, and re-layouts: 22.6 us -> 36.7 us
  starting transfers between devices: 67.7 us -> 62.4 us
  waiting for transfers between devices: 50.3 us -> 48.4 us
    dynamic_update_slice x3 -> x4, local copies, waits for them, and re-layouts: 2.48 us -> 17.6 us  [the longest x1 5.41 us: with_halo(): padded = lax.dynamic_update_slice(padded, from_below, (0, 0, 0, 1, 0))]
    ppermute x4, waiting for transfers between devices: 7.99 us -> 3.23 us  [the longest x1 2.04 us: with_halo(): from_right = lax.ppermute(value[:, 0:1], 'gx', down_x)]
    ppermute x7, starting transfers between devices: 29.8 us -> 26.2 us  [butterfly_scatter(): buf = keep + lax.ppermute(send, ('gx', 'gy'), step_pairs(k))]
    slice x3 -> x4, local copies, waits for them, and re-layouts: 3.19 us -> 0.08 us  [the longest x1 0.04 us: with_halo(): from_right = lax.ppermute(value[:, 0:1], 'gx', down_x)]
    ppermute x7, starting transfers between devices: 11.7 us -> 9.17 us  [butterfly_gather(): got = lax.ppermute(buf, ('gx', 'gy'), step_pairs(k))]
    pad x1, local copies, waits for them, and re-layouts: 5.22 us -> 7.38 us  [with_halo(): padded = jnp.pad(value, ((0, 0), (1, 1), (1, 1), (1, 1), (0, 0)))]
    ppermute x7, waiting for transfers between devices: 24.4 us -> 26.4 us  [butterfly_gather(): got = lax.ppermute(buf, ('gx', 'gy'), step_pairs(k))]
    unnamed x63 -> x65, local copies, waits for them, and re-layouts: 3.83 us -> 3.83 us
  transfers between devices with their start and end apart: 20 -> 20, of which waited for: 18 -> 17; matrix products, arithmetic and copies ran while one was open for 8% -> 16% of each run, Pallas kernels for 0% -> 0%
where the time goes in v7:
time: 169 us; the launch traced here: 168 us
  starting transfers between devices  62.4 us (37%)
  waiting for transfers between devices  48.4 us (29%)
  local copies, waits for them, and re-layouts  36.7 us (22%)
  matrix products  8.6 us (5%)
  between operations  7.52 us (4%)
  other arithmetic  4.31 us (3%)
    ppermute x7, waiting for transfers between devices, butterfly_gather(): got = lax.ppermute(buf, ('gx', 'gy'), step_pairs(k))  26.4 us
    ppermute x7, starting transfers between devices, butterfly_scatter(): buf = keep + lax.ppermute(send, ('gx', 'gy'), step_pairs(k))  26.2 us
    ppermute x7, waiting for transfers between devices, butterfly_scatter(): buf = keep + lax.ppermute(send, ('gx', 'gy'), step_pairs(k))  15 us
    ppermute x1, starting transfers between devices, butterfly_gather(): lax.ppermute(buf, 'gx', [(i, i ^ 1) for i in range(lax.axis_size('gx'))])  14.3 us
    ppermute x7, starting transfers between devices, butterfly_gather(): got = lax.ppermute(buf, ('gx', 'gy'), step_pairs(k))  9.17 us
    pad x1, local copies, waits for them, and re-layouts, with_halo(): padded = jnp.pad(value, ((0, 0), (1, 1), (1, 1), (1, 1), (0, 0)))  7.38 us
    dynamic_update_slice x1, local copies, waits for them, and re-layouts, with_halo(): padded = lax.dynamic_update_slice(padded, from_below, (0, 0, 0, 1, 0))  5.41 us
    dynamic_update_slice x1, local copies, waits for them, and re-layouts, with_halo(): padded = lax.dynamic_update_slice(padded, from_above, (0, 0, ny + 1, 1, 0))  5.38 us
  transfers between devices with their start and end apart: 20, of which 17 were waited for; matrix products, arithmetic and copies ran while one was open for 16% of the time, Pallas kernels for 0%

profile of v7, /device:TPU:1, one launch (start us, length us, event | category | flops | bytes accessed | tf_op | source)
XLA Modules:
  0.0 167.9 jit_solution(14959073706969102897)
XLA Ops:
  0.6 0.0 copy-start
  1.4 0.8 broadcast_bitcast_fusion
  2.1 1.2 maximum_multiply_fusion
  3.4 2.0 %convolution_convert_fusion = bf16[2,512,128,16]{2,3,1,0:T(8,128)(2,1)S(1)} fusion(bf16[2,2,512,128]{3,2,1,0:T(8,128)(2,1)S(1)} %maximum_multiply_fusion, pred[2]{0:T(512)(128)(4,1)S(1)} %get-tuple-element.98, s32[2]{0:T(128)} %bitcast.186), kind=kOutput, calls=%fused_computation | convolution fusion | flops 10485824 | bytes 4718602 | tf_op jit(solution)/shard_map/ps,tsvc->tpvc/dot_general | solution.py:101
  5.5 1.6 copy.12
  7.1 5.2 %collective-permute-start.1 = (bf16[2,1,16,32,128]{4,3,2,1,0:T(8,128)(2,1)S(1)}, bf16[2,1,16,32,128]{4,3,2,1,0:T(8,128)(2,1)S(1)}, u32[]{:S(2)}, u32[]{:S(2)}) collective-permute-start(bf16[2,1,16,32,128]{4,3,2,1,0:T(8,128)(2,1)S(1)} %get-tuple-element.16), channel_id=1, source_target_pairs={{16,0},{32,16},{48,32},{64,48},{80,64},{96,80},{112,96},{128,112},... | collective-permute-start | bytes 786440 | tf_op jit(solution)/shard_map/ppermute | solution.py:21
  12.4 2.8 %collective-permute-start = (bf16[2,1,16,32,128]{4,3,2,1,0:T(8,128)(2,1)S(1)}, bf16[2,1,16,32,128]{4,3,2,1,0:T(8,128)(2,1)S(1)}, u32[]{:S(2)}, u32[]{:S(2)}) collective-permute-start(bf16[2,1,16,32,128]{4,3,2,1,0:T(8,128)(2,1)S(1)} %get-tuple-element.17), channel_id=1, source_target_pairs={{0,16},{16,32},{32,48},{48,64},{64,80},{80,96},{96,112},{112,128},... | collective-permute-start | bytes 786440 | tf_op jit(solution)/shard_map/ppermute | solution.py:20
  15.3 2.0 %collective-permute-done.1 = bf16[2,1,16,32,128]{4,3,2,1,0:T(8,128)(2,1)S(1)} collective-permute-done((bf16[2,1,16,32,128]{4,3,2,1,0:T(8,128)(2,1)S(1)}, bf16[2,1,16,32,128]{4,3,2,1,0:T(8,128)(2,1)S(1)}, u32[]{:S(2)}, u32[]{:S(2)}) %collective-permute-start.1) | collective-permute-done | bytes 262176 | tf_op jit(solution)/shard_map/ppermute | solution.py:21
  17.4 1.2 collective-permute-done
  18.6 3.1 %collective-permute-start.2 = (bf16[2,18,1,32,128]{4,3,2,1,0:T(8,128)(2,1)S(1)}, bf16[2,18,1,32,128]{4,3,2,1,0:T(8,128)(2,1)S(1)}, u32[]{:S(2)}, u32[]{:S(2)}) collective-permute-start(bf16[2,18,1,32,128]{4,3,2,1,0:T(8,128)(2,1)S(1)} %pad_maximum_fusion.4), channel_id=1, source_target_pairs={{0,1},{1,2},{2,3},{3,4},{4,5},{5,6},{6,7},{7,8},{8,9},{9,10},{10,1... | collective-permute-start | bytes 884744 | tf_op jit(solution)/shard_map/ppermute | solution.py:27
  21.7 1.5 collective-permute-start.3
  23.2 0.6 fusion.26
  29.1 7.4 %pad.8 = bf16[2,18,18,34,128]{4,3,2,1,0:T(8,128)(2,1)} pad(bf16[2,16,16,32,128]{4,3,2,1,0:T(8,128)(2,1)} %bitcast.123, bf16[]{:T(256)} %constant.82.clone.1), padding=0_0x1_1x1_1x1_1x0_0 | pad | bytes 9834498 | tf_op jit(solution)/shard_map/jit(_pad)/pad | solution.py:22
  36.5 3.4 %dynamic_update_slice.12 = bf16[2,18,18,34,128]{4,3,2,1,0:T(8,128)(2,1)} dynamic-update-slice(bf16[2,18,18,34,128]{4,3,2,1,0:T(8,128)(2,1)} %pad.8, bf16[2,1,16,32,128]{4,3,2,1,0:T(8,128)(2,1)S(1)} %collective-permute-done, s32[]{:T(128)} %constant.83.clone.1, s32[]{:T(128)} %constant.83.clone.1, s32[]{:T(128)} %constant.84.clone.1, s32[]{:T(128)} %constant.84.clone.1, s32[]{:T(128)} %constant.83.clone.1) | dynamic-update-slice | bytes 524292 | tf_op jit(solution)/shard_map/dynamic_update_slice | solution.py:29
  40.0 3.4 %dynamic_update_slice.13 = bf16[2,18,18,34,128]{4,3,2,1,0:T(8,128)(2,1)} dynamic-update-slice(bf16[2,18,18,34,128]{4,3,2,1,0:T(8,128)(2,1)} %dynamic_update_slice.12, bf16[2,1,16,32,128]{4,3,2,1,0:T(8,128)(2,1)S(1)} %collective-permute-done.1, s32[]{:T(128)} %constant.83.clone.1, s32[]{:T(128)} %constant.85.clone.1, s32[]{:T(128)} %constant.84.clone.1, s32[]{:T(128)} %constant.84.clone.1, ...) | dynamic-update-slice | bytes 524292 | tf_op jit(solution)/shard_map/dynamic_update_slice | solution.py:30
  43.4 5.4 %dynamic_update_slice.14 = bf16[2,18,18,34,128]{4,3,2,1,0:T(8,128)(2,1)} dynamic-update-slice(bf16[2,18,18,34,128]{4,3,2,1,0:T(8,128)(2,1)} %dynamic_update_slice.13, bf16[2,18,1,32,128]{4,3,2,1,0:T(8,128)(2,1)S(1)} %collective-permute-done.2, s32[]{:T(128)} %constant.83.clone.1, s32[]{:T(128)} %constant.83.clone.1, s32[]{:T(128)} %constant.83.clone.1, s32[]{:T(128)} %constant.84.clone.1, ...) | dynamic-update-slice | bytes 589828 | tf_op jit(solution)/shard_map/dynamic_update_slice | solution.py:31
  48.8 5.4 %dynamic_update_slice.15 = bf16[2,18,18,34,128]{4,3,2,1,0:T(8,128)(2,1)} dynamic-update-slice(bf16[2,18,18,34,128]{4,3,2,1,0:T(8,128)(2,1)} %dynamic_update_slice.14, bf16[2,18,1,32,128]{4,3,2,1,0:T(8,128)(2,1)S(1)} %collective-permute-done.3, s32[]{:T(128)} %constant.83.clone.1, s32[]{:T(128)} %constant.83.clone.1, s32[]{:T(128)} %constant.85.clone.1, s32[]{:T(128)} %constant.84.clone.1, ...) | dynamic-update-slice | bytes 589828 | tf_op jit(solution)/shard_map/dynamic_update_slice | solution.py:32
  54.2 2.4 %dynamic-slice_bitcast_fusion = (bf16[2,1,10,10,10,128]{5,4,3,2,1,0:T(8,128)(2,1)S(1)}, bf16[2,1,10,10,10,128]{5,4,3,2,1,0:T(8,128)(2,1)S(1)}) fusion(bf16[2,18,18,34,128]{4,3,2,1,0:T(8,128)(2,1)} %dynamic_update_slice.15, s32[]{:T(128)S(6)} %select_n.228, s32[]{:T(128)S(6)} %select_n.231, s32[]{:T(128)S(6)} %select_n.233, s32[]{:T(128)S(6)} %select_n.221, ...), kind=kLoop, calls=%fused_computation.19 | loop fusion | bytes 2048024 | tf_op jit(solution)/shard_map/stack | solution.py:119
  56.5 0.3 fusion.7
  56.8 0.4 fusion.23
  57.3 1.0 fusion.22
  58.3 0.5 fusion.21
  58.8 1.0 fusion.20
  61.0 1.1 convolution_multiply_fusion
  62.2 0.1 pad_dynamic-slice_fusion
  62.3 0.1 collective-permute-start.4
  63.3 1.5 collective-permute-done.4
  64.8 0.1 fusion.4
  65.0 5.3 %collective-permute-start.5 = (f32[896,128]{1,0:T(8,128)S(1)}, f32[896,128]{1,0:T(8,128)S(1)}, u32[]{:S(2)}, u32[]{:S(2)}) collective-permute-start(f32[896,128]{1,0:T(8,128)S(1)} %constant_dynamic-slice_fusion.6), channel_id=1, source_target_pairs={{0,1},{1,0},{2,3},{3,2},{4,5},{5,4},{6,7},{7,6},{8,9},{9,8},{10,11... | collective-permute-start | bytes 1376264 | tf_op jit(solution)/shard_map/ppermute | solution.py:81
  70.3 2.7 %fusion.2 = bf16[1024,128]{1,0:T(8,128)(2,1)} fusion(bf16[27,1024,128]{2,1,0:T(8,128)(2,1)S(1)} %constant_dynamic-update-slice_fusion, bf16[27,128,128]{2,1,0:T(8,128)(2,1)S(1)} %copy-done, f32[1024]{0:T(1024)S(1)} %fusion.10), kind=kOutput, calls=%fused_computation.11 | convolution fusion | flops 906231808 | bytes 8228864 | tf_op jit(solution)/shard_map/dvc,dce->ve/dot_general | solution.py:148
  73.0 3.2 %collective-permute-done.5 = f32[896,128]{1,0:T(8,128)S(1)} collective-permute-done((f32[896,128]{1,0:T(8,128)S(1)}, f32[896,128]{1,0:T(8,128)S(1)}, u32[]{:S(2)}, u32[]{:S(2)}) %collective-permute-start.5) | collective-permute-done | bytes 458784 | tf_op jit(solution)/shard_map/ppermute | solution.py:81
  76.2 4.7 %collective-permute-start.6 = (f32[448,128]{1,0:T(8,128)S(1)}, f32[448,128]{1,0:T(8,128)S(1)}, u32[]{:S(2)}, u32[]{:S(2)}) collective-permute-start(f32[448,128]{1,0:T(8,128)S(1)} %constant_dynamic-slice_fusion.5), channel_id=1, source_target_pairs={{0,64},{1,65},{2,66},{3,67},{4,68},{5,69},{6,70},{7,71},{8,72},{9,... | collective-permute-start | bytes 688136 | tf_op jit(solution)/shard_map/ppermute | solution.py:81
  81.0 3.6 %collective-permute-done.6 = f32[448,128]{1,0:T(8,128)S(1)} collective-permute-done((f32[448,128]{1,0:T(8,128)S(1)}, f32[448,128]{1,0:T(8,128)S(1)}, u32[]{:S(2)}, u32[]{:S(2)}) %collective-permute-start.6) | collective-permute-done | bytes 229408 | tf_op jit(solution)/shard_map/ppermute | solution.py:81
  84.6 0.3 collective-permute-start.7
  85.0 3.4 %collective-permute-done.7 = f32[224,128]{1,0:T(8,128)S(1)} collective-permute-done((f32[224,128]{1,0:T(8,128)S(1)}, f32[224,128]{1,0:T(8,128)S(1)}, u32[]{:S(2)}, u32[]{:S(2)}) %collective-permute-start.7) | collective-permute-done | bytes 114720 | tf_op jit(solution)/shard_map/ppermute | solution.py:81
  88.4 3.3 %collective-permute-start.8 = (f32[112,128]{1,0:T(8,128)S(1)}, f32[112,128]{1,0:T(8,128)S(1)}, u32[]{:S(2)}, u32[]{:S(2)}) collective-permute-start(f32[112,128]{1,0:T(8,128)S(1)} %constant_dynamic-slice_fusion.3), channel_id=1, source_target_pairs={{0,32},{1,33},{2,34},{3,35},{4,36},{5,37},{6,38},{7,39},{8,40},{9,... | collective-permute-start | bytes 172040 | tf_op jit(solution)/shard_map/ppermute | solution.py:81
  91.7 1.5 collective-permute-done.8
  93.3 3.3 %collective-permute-start.9 = (f32[56,128]{1,0:T(8,128)S(1)}, f32[56,128]{1,0:T(8,128)S(1)}, u32[]{:S(2)}, u32[]{:S(2)}) collective-permute-start(f32[56,128]{1,0:T(8,128)S(1)} %constant_dynamic-slice_fusion.2), channel_id=1, source_target_pairs={{0,128},{1,129},{2,130},{3,131},{4,132},{5,133},{6,134},{7,135},{8... | collective-permute-start | bytes 86024 | tf_op jit(solution)/shard_map/ppermute | solution.py:81
  96.7 1.2 collective-permute-done.9
  97.9 2.2 %collective-permute-start.10 = (f32[28,128]{1,0:T(8,128)S(1)}, f32[28,128]{1,0:T(8,128)S(1)}, u32[]{:S(2)}, u32[]{:S(2)}) collective-permute-start(f32[28,128]{1,0:T(8,128)S(1)} %constant_dynamic-slice_fusion.1), channel_id=1, source_target_pairs={{0,4},{1,5},{2,6},{3,7},{4,0},{5,1},{6,2},{7,3},{8,12},{9,13},{10,... | collective-permute-start | bytes 43016 | tf_op jit(solution)/shard_map/ppermute | solution.py:81
  100.2 2.1 %collective-permute-done.10 = f32[28,128]{1,0:T(8,128)S(1)} collective-permute-done((f32[28,128]{1,0:T(8,128)S(1)}, f32[28,128]{1,0:T(8,128)S(1)}, u32[]{:S(2)}, u32[]{:S(2)}) %collective-permute-start.10) | collective-permute-done | bytes 14368 | tf_op jit(solution)/shard_map/ppermute | solution.py:81
  102.3 7.1 %collective-permute-start.11 = (f32[14,128]{1,0:T(8,128)S(1)}, f32[14,128]{1,0:T(8,128)S(1)}, u32[]{:S(2)}, u32[]{:S(2)}) collective-permute-start(f32[14,128]{1,0:T(8,128)S(1)} %constant_dynamic-slice_fusion), channel_id=1, source_target_pairs={{0,8},{1,9},{2,10},{3,11},{4,12},{5,13},{6,14},{7,15},{8,0},{9,1},... | collective-permute-start | bytes 21512 | tf_op jit(solution)/shard_map/ppermute | solution.py:81
  109.4 2.7 %fusion.3 = bf16[1024,128]{1,0:T(8,128)(2,1)} fusion(bf16[27,1024,128]{2,1,0:T(8,128)(2,1)S(1)} %constant_dynamic-update-slice_fusion.27, bf16[27,128,128]{2,1,0:T(8,128)(2,1)S(1)} %copy-done, f32[1024]{0:T(1024)S(1)} %fusion.10), kind=kOutput, calls=%fused_computation.12 | convolution fusion | flops 906231808 | bytes 8228864 | tf_op jit(solution)/shard_map/dvc,dec->ve/dot_general | solution.py:151
  112.1 3.8 %collective-permute-start.12 = (f32[14,128]{1,0:T(8,128)S(1)}, f32[14,128]{1,0:T(8,128)S(1)}, u32[]{:S(2)}, u32[]{:S(2)}) collective-permute-start(f32[14,128]{1,0:T(8,128)S(1)} %dynamic-slice_add_fusion.6), channel_id=1, source_target_pairs={{0,8},{1,9},{2,10},{3,11},{4,12},{5,13},{6,14},{7,15},{8,0},{9,1},... | collective-permute-start | bytes 21512 | tf_op jit(solution)/shard_map/ppermute | solution.py:91
  115.9 2.7 %collective-permute-done.12 = f32[14,128]{1,0:T(8,128)S(1)} collective-permute-done((f32[14,128]{1,0:T(8,128)S(1)}, f32[14,128]{1,0:T(8,128)S(1)}, u32[]{:S(2)}, u32[]{:S(2)}) %collective-permute-start.12) | collective-permute-done | bytes 7200 | tf_op jit(solution)/shard_map/ppermute | solution.py:91
  118.6 0.5 collective-permute-start.13
  119.1 3.7 %collective-permute-done.13 = f32[28,128]{1,0:T(8,128)S(1)} collective-permute-done((f32[28,128]{1,0:T(8,128)S(1)}, f32[28,128]{1,0:T(8,128)S(1)}, u32[]{:S(2)}, u32[]{:S(2)}) %collective-permute-start.13) | collective-permute-done | bytes 14368 | tf_op jit(solution)/shard_map/ppermute | solution.py:91
  122.8 0.1 collective-permute-start.14
  122.9 3.6 %collective-permute-done.14 = f32[56,128]{1,0:T(8,128)S(1)} collective-permute-done((f32[56,128]{1,0:T(8,128)S(1)}, f32[56,128]{1,0:T(8,128)S(1)}, u32[]{:S(2)}, u32[]{:S(2)}) %collective-permute-start.14) | collective-permute-done | bytes 28704 | tf_op jit(solution)/shard_map/ppermute | solution.py:91
  126.5 3.3 %collective-permute-start.15 = (f32[112,128]{1,0:T(8,128)S(1)}, f32[112,128]{1,0:T(8,128)S(1)}, u32[]{:S(2)}, u32[]{:S(2)}) collective-permute-start(f32[112,128]{1,0:T(8,128)S(1)} %pad_maximum_fusion.8), channel_id=1, source_target_pairs={{0,32},{1,33},{2,34},{3,35},{4,36},{5,37},{6,38},{7,39},{8,40},{9,... | collective-permute-start | bytes 172040 | tf_op jit(solution)/shard_map/ppermute | solution.py:91
  129.8 1.6 collective-permute-done.15
  131.4 0.2 collective-permute-start.16
  131.6 3.9 %collective-permute-done.16 = f32[224,128]{1,0:T(8,128)S(1)} collective-permute-done((f32[224,128]{1,0:T(8,128)S(1)}, f32[224,128]{1,0:T(8,128)S(1)}, u32[]{:S(2)}, u32[]{:S(2)}) %collective-permute-start.16) | collective-permute-done | bytes 114720 | tf_op jit(solution)/shard_map/ppermute | solution.py:91
  135.5 0.1 collective-permute-start.17
  135.6 4.9 %collective-permute-done.17 = f32[448,128]{1,0:T(8,128)S(1)} collective-permute-done((f32[448,128]{1,0:T(8,128)S(1)}, f32[448,128]{1,0:T(8,128)S(1)}, u32[]{:S(2)}, u32[]{:S(2)}) %collective-permute-start.17) | collective-permute-done | bytes 229408 | tf_op jit(solution)/shard_map/ppermute | solution.py:91
  140.5 1.3 collective-permute-start.18
  141.8 6.1 %collective-permute-done.18 = f32[896,128]{1,0:T(8,128)S(1)} collective-permute-done((f32[896,128]{1,0:T(8,128)S(1)}, f32[896,128]{1,0:T(8,128)S(1)}, u32[]{:S(2)}, u32[]{:S(2)}) %collective-permute-start.18) | collective-permute-done | bytes 458784 | tf_op jit(solution)/shard_map/ppermute | solution.py:91
  147.9 0.1 broadcast_select_fusion.3
  148.0 0.1 pad_maximum_fusion.1
  148.1 14.3 %collective-permute-start.19 = (f32[1792,128]{1,0:T(8,128)S(1)}, f32[1792,128]{1,0:T(8,128)}, u32[]{:S(2)}, u32[]{:S(2)}) collective-permute-start(f32[1792,128]{1,0:T(8,128)S(1)} %pad_maximum_fusion.1), channel_id=1, source_target_pairs={{0,16},{16,0},{32,48},{48,32},{64,80},{80,64},{96,112},{112,96},{1... | collective-permute-start | bytes 2752520 | tf_op jit(solution)/shard_map/ppermute | solution.py:93
  162.4 2.2 %collective-permute-done.19 = f32[1792,128]{1,0:T(8,128)} collective-permute-done((f32[1792,128]{1,0:T(8,128)S(1)}, f32[1792,128]{1,0:T(8,128)}, u32[]{:S(2)}, u32[]{:S(2)}) %collective-permute-start.19) | collective-permute-done | bytes 917536 | tf_op jit(solution)/shard_map/ppermute | solution.py:93
  164.6 1.3 broadcast_select_fusion.1
  165.9 0.1 pad_maximum_fusion
  166.0 1.9 %copy.14 = f32[27,128,128]{2,1,0:T(8,128)} copy(f32[27,128,128]{1,2,0:T(8,128)S(1)} %bitcast.125) | data formatting | bytes 3538944
  (104 shorter events, 2.6 us)
Async XLA Ops:
  0.6 69.6 %copy-start = (bf16[27,128,128]{2,1,0:T(8,128)(2,1)S(1)}, bf16[27,128,128]{2,1,0:T(8,128)(2,1)}, u32[]{:S(2)}) copy-start(bf16[27,128,128]{2,1,0:T(8,128)(2,1)} %param.10) | copy-start | bytes 2654212
  3.4 11.9 %copy-start.2 = (bf16[2,2,512,128]{3,2,1,0:T(8,128)(2,1)}, bf16[2,2,512,128]{3,2,1,0:T(8,128)(2,1)S(1)}, u32[]{:S(2)}) copy-start(bf16[2,2,512,128]{3,2,1,0:T(8,128)(2,1)S(1)} %maximum_multiply_fusion) | copy-start | bytes 1572868
  5.4 17.8 %copy-start.4 = (s32[1,1,2]{2,1,0:T(1,128)S(1)}, s32[1,1,2]{2,1,0:T(1,128)}, u32[]{:S(2)}) copy-start(s32[1,1,2]{2,1,0:T(1,128)} %param.8) | copy-start | bytes 28
  7.1 8.2 %copy-start.1 = (bf16[2,2,2,4,8,8,8,128]{7,6,3,5,2,4,1,0:T(8,128)(2,1)}, bf16[2,2,2,4,8,8,8,128]{7,6,3,5,2,4,1,0:T(8,128)(2,1)S(1)}, u32[]{:S(2)}) copy-start(bf16[2,2,2,4,8,8,8,128]{7,6,3,5,2,4,1,0:T(8,128)(2,1)S(1)} %copy.12) | copy-start | bytes 12582916
  7.1 29.4 %copy-start.3 = (s32[1,1,2,512]{3,2,1,0:T(2,128)S(1)}, s32[1,1,2,512]{3,2,1,0:T(2,128)}, u32[]{:S(2)}) copy-start(s32[1,1,2,512]{3,2,1,0:T(2,128)} %param.7) | copy-start | bytes 12292
  7.1 10.2 %collective-permute-start.1 = (bf16[2,1,16,32,128]{4,3,2,1,0:T(8,128)(2,1)S(1)}, bf16[2,1,16,32,128]{4,3,2,1,0:T(8,128)(2,1)S(1)}, u32[]{:S(2)}, u32[]{:S(2)}) collective-permute-start(bf16[2,1,16,32,128]{4,3,2,1,0:T(8,128)(2,1)S(1)} %get-tuple-element.16), channel_id=1, source_target_pairs={{16,0},{32,16},{48,32},{64,48},{80,64},{96,80},{112,96},{128,112},... | collective-permute-start | bytes 786440 | tf_op jit(solution)/shard_map/ppermute | solution.py:21
  12.4 6.1 %collective-permute-start = (bf16[2,1,16,32,128]{4,3,2,1,0:T(8,128)(2,1)S(1)}, bf16[2,1,16,32,128]{4,3,2,1,0:T(8,128)(2,1)S(1)}, u32[]{:S(2)}, u32[]{:S(2)}) collective-permute-start(bf16[2,1,16,32,128]{4,3,2,1,0:T(8,128)(2,1)S(1)} %get-tuple-element.17), channel_id=1, source_target_pairs={{0,16},{16,32},{32,48},{48,64},{64,80},{80,96},{96,112},{112,128},... | collective-permute-start | bytes 786440 | tf_op jit(solution)/shard_map/ppermute | solution.py:20
  18.6 24.8 %collective-permute-start.2 = (bf16[2,18,1,32,128]{4,3,2,1,0:T(8,128)(2,1)S(1)}, bf16[2,18,1,32,128]{4,3,2,1,0:T(8,128)(2,1)S(1)}, u32[]{:S(2)}, u32[]{:S(2)}) collective-permute-start(bf16[2,18,1,32,128]{4,3,2,1,0:T(8,128)(2,1)S(1)} %pad_maximum_fusion.4), channel_id=1, source_target_pairs={{0,1},{1,2},{2,3},{3,4},{4,5},{5,6},{6,7},{7,8},{8,9},{9,10},{10,1... | collective-permute-start | bytes 884744 | tf_op jit(solution)/shard_map/ppermute | solution.py:27
  21.7 27.1 %collective-permute-start.3 = (bf16[2,18,1,32,128]{4,3,2,1,0:T(8,128)(2,1)S(1)}, bf16[2,18,1,32,128]{4,3,2,1,0:T(8,128)(2,1)S(1)}, u32[]{:S(2)}, u32[]{:S(2)}) collective-permute-start(bf16[2,18,1,32,128]{4,3,2,1,0:T(8,128)(2,1)S(1)} %pad_maximum_fusion.5), channel_id=1, source_target_pairs={{1,0},{2,1},{3,2},{4,3},{5,4},{6,5},{7,6},{8,7},{9,8},{10,9},{11,1... | collective-permute-start | bytes 884744 | tf_op jit(solution)/shard_map/ppermute | solution.py:28
  59.8 1.2 slice-start
  62.3 2.6 %collective-permute-start.4 = (f32[1792,128]{1,0:T(8,128)S(1)}, f32[1792,128]{1,0:T(8,128)S(1)}, u32[]{:S(2)}, u32[]{:S(2)}) collective-permute-start(f32[1792,128]{1,0:T(8,128)S(1)} %pad_dynamic-slice_fusion), channel_id=1, source_target_pairs={{0,16},{16,0},{32,48},{48,32},{64,80},{80,64},{96,112},{112,96},{1... | collective-permute-start | bytes 2752520 | tf_op jit(solution)/shard_map/ppermute | solution.py:75
  65.0 11.1 %collective-permute-start.5 = (f32[896,128]{1,0:T(8,128)S(1)}, f32[896,128]{1,0:T(8,128)S(1)}, u32[]{:S(2)}, u32[]{:S(2)}) collective-permute-start(f32[896,128]{1,0:T(8,128)S(1)} %constant_dynamic-slice_fusion.6), channel_id=1, source_target_pairs={{0,1},{1,0},{2,3},{3,2},{4,5},{5,4},{6,7},{7,6},{8,9},{9,8},{10,11... | collective-permute-start | bytes 1376264 | tf_op jit(solution)/shard_map/ppermute | solution.py:81
  76.2 8.3 %collective-permute-start.6 = (f32[448,128]{1,0:T(8,128)S(1)}, f32[448,128]{1,0:T(8,128)S(1)}, u32[]{:S(2)}, u32[]{:S(2)}) collective-permute-start(f32[448,128]{1,0:T(8,128)S(1)} %constant_dynamic-slice_fusion.5), channel_id=1, source_target_pairs={{0,64},{1,65},{2,66},{3,67},{4,68},{5,69},{6,70},{7,71},{8,72},{9,... | collective-permute-start | bytes 688136 | tf_op jit(solution)/shard_map/ppermute | solution.py:81
  84.6 3.7 %collective-permute-start.7 = (f32[224,128]{1,0:T(8,128)S(1)}, f32[224,128]{1,0:T(8,128)S(1)}, u32[]{:S(2)}, u32[]{:S(2)}) collective-permute-start(f32[224,128]{1,0:T(8,128)S(1)} %constant_dynamic-slice_fusion.4), channel_id=1, source_target_pairs={{0,2},{1,3},{2,0},{3,1},{4,6},{5,7},{6,4},{7,5},{8,10},{9,11},{10,... | collective-permute-start | bytes 344072 | tf_op jit(solution)/shard_map/ppermute | solution.py:81
  88.4 4.9 %collective-permute-start.8 = (f32[112,128]{1,0:T(8,128)S(1)}, f32[112,128]{1,0:T(8,128)S(1)}, u32[]{:S(2)}, u32[]{:S(2)}) collective-permute-start(f32[112,128]{1,0:T(8,128)S(1)} %constant_dynamic-slice_fusion.3), channel_id=1, source_target_pairs={{0,32},{1,33},{2,34},{3,35},{4,36},{5,37},{6,38},{7,39},{8,40},{9,... | collective-permute-start | bytes 172040 | tf_op jit(solution)/shard_map/ppermute | solution.py:81
  93.3 4.6 %collective-permute-start.9 = (f32[56,128]{1,0:T(8,128)S(1)}, f32[56,128]{1,0:T(8,128)S(1)}, u32[]{:S(2)}, u32[]{:S(2)}) collective-permute-start(f32[56,128]{1,0:T(8,128)S(1)} %constant_dynamic-slice_fusion.2), channel_id=1, source_target_pairs={{0,128},{1,129},{2,130},{3,131},{4,132},{5,133},{6,134},{7,135},{8... | collective-permute-start | bytes 86024 | tf_op jit(solution)/shard_map/ppermute | solution.py:81
  97.9 4.4 %collective-permute-start.10 = (f32[28,128]{1,0:T(8,128)S(1)}, f32[28,128]{1,0:T(8,128)S(1)}, u32[]{:S(2)}, u32[]{:S(2)}) collective-permute-start(f32[28,128]{1,0:T(8,128)S(1)} %constant_dynamic-slice_fusion.1), channel_id=1, source_target_pairs={{0,4},{1,5},{2,6},{3,7},{4,0},{5,1},{6,2},{7,3},{8,12},{9,13},{10,... | collective-permute-start | bytes 43016 | tf_op jit(solution)/shard_map/ppermute | solution.py:81
  102.3 9.8 %collective-permute-start.11 = (f32[14,128]{1,0:T(8,128)S(1)}, f32[14,128]{1,0:T(8,128)S(1)}, u32[]{:S(2)}, u32[]{:S(2)}) collective-permute-start(f32[14,128]{1,0:T(8,128)S(1)} %constant_dynamic-slice_fusion), channel_id=1, source_target_pairs={{0,8},{1,9},{2,10},{3,11},{4,12},{5,13},{6,14},{7,15},{8,0},{9,1},... | collective-permute-start | bytes 21512 | tf_op jit(solution)/shard_map/ppermute | solution.py:81
  112.1 6.5 %collective-permute-start.12 = (f32[14,128]{1,0:T(8,128)S(1)}, f32[14,128]{1,0:T(8,128)S(1)}, u32[]{:S(2)}, u32[]{:S(2)}) collective-permute-start(f32[14,128]{1,0:T(8,128)S(1)} %dynamic-slice_add_fusion.6), channel_id=1, source_target_pairs={{0,8},{1,9},{2,10},{3,11},{4,12},{5,13},{6,14},{7,15},{8,0},{9,1},... | collective-permute-start | bytes 21512 | tf_op jit(solution)/shard_map/ppermute | solution.py:91
  118.6 4.2 %collective-permute-start.13 = (f32[28,128]{1,0:T(8,128)S(1)}, f32[28,128]{1,0:T(8,128)S(1)}, u32[]{:S(2)}, u32[]{:S(2)}) collective-permute-start(f32[28,128]{1,0:T(8,128)S(1)} %pad_maximum_fusion.10), channel_id=1, source_target_pairs={{0,4},{1,5},{2,6},{3,7},{4,0},{5,1},{6,2},{7,3},{8,12},{9,13},{10,... | collective-permute-start | bytes 43016 | tf_op jit(solution)/shard_map/ppermute | solution.py:91
  122.8 3.7 %collective-permute-start.14 = (f32[56,128]{1,0:T(8,128)S(1)}, f32[56,128]{1,0:T(8,128)S(1)}, u32[]{:S(2)}, u32[]{:S(2)}) collective-permute-start(f32[56,128]{1,0:T(8,128)S(1)} %pad_maximum_fusion.9), channel_id=1, source_target_pairs={{0,128},{1,129},{2,130},{3,131},{4,132},{5,133},{6,134},{7,135},{8... | collective-permute-start | bytes 86024 | tf_op jit(solution)/shard_map/ppermute | solution.py:91
  126.5 4.8 %collective-permute-start.15 = (f32[112,128]{1,0:T(8,128)S(1)}, f32[112,128]{1,0:T(8,128)S(1)}, u32[]{:S(2)}, u32[]{:S(2)}) collective-permute-start(f32[112,128]{1,0:T(8,128)S(1)} %pad_maximum_fusion.8), channel_id=1, source_target_pairs={{0,32},{1,33},{2,34},{3,35},{4,36},{5,37},{6,38},{7,39},{8,40},{9,... | collective-permute-start | bytes 172040 | tf_op jit(solution)/shard_map/ppermute | solution.py:91
  131.4 4.0 %collective-permute-start.16 = (f32[224,128]{1,0:T(8,128)S(1)}, f32[224,128]{1,0:T(8,128)S(1)}, u32[]{:S(2)}, u32[]{:S(2)}) collective-permute-start(f32[224,128]{1,0:T(8,128)S(1)} %pad_maximum_fusion.7), channel_id=1, source_target_pairs={{0,2},{1,3},{2,0},{3,1},{4,6},{5,7},{6,4},{7,5},{8,10},{9,11},{10,... | collective-permute-start | bytes 344072 | tf_op jit(solution)/shard_map/ppermute | solution.py:91
  135.5 5.0 %collective-permute-start.17 = (f32[448,128]{1,0:T(8,128)S(1)}, f32[448,128]{1,0:T(8,128)S(1)}, u32[]{:S(2)}, u32[]{:S(2)}) collective-permute-start(f32[448,128]{1,0:T(8,128)S(1)} %pad_maximum_fusion.6), channel_id=1, source_target_pairs={{0,64},{1,65},{2,66},{3,67},{4,68},{5,69},{6,70},{7,71},{8,72},{9,... | collective-permute-start | bytes 688136 | tf_op jit(solution)/shard_map/ppermute | solution.py:91
  140.5 7.4 %collective-permute-start.18 = (f32[896,128]{1,0:T(8,128)S(1)}, f32[896,128]{1,0:T(8,128)S(1)}, u32[]{:S(2)}, u32[]{:S(2)}) collective-permute-start(f32[896,128]{1,0:T(8,128)S(1)} %pad_maximum_fusion.3), channel_id=1, source_target_pairs={{0,1},{1,0},{2,3},{3,2},{4,5},{5,4},{6,7},{7,6},{8,9},{9,8},{10,11... | collective-permute-start | bytes 1376264 | tf_op jit(solution)/shard_map/ppermute | solution.py:91
  148.1 16.5 %collective-permute-start.19 = (f32[1792,128]{1,0:T(8,128)S(1)}, f32[1792,128]{1,0:T(8,128)}, u32[]{:S(2)}, u32[]{:S(2)}) collective-permute-start(f32[1792,128]{1,0:T(8,128)S(1)} %pad_maximum_fusion.1), channel_id=1, source_target_pairs={{0,16},{16,0},{32,48},{48,32},{64,80},{80,64},{96,112},{112,96},{1... | collective-permute-start | bytes 2752520 | tf_op jit(solution)/shard_map/ppermute | solution.py:93

commit v8 on v7

--- a/solution.py
+++ b/solution.py
@@ -19,18 +19,15 @@
     down_y = [(j, i) for i, j in up_y]
     from_left = lax.ppermute(value[:, nx - 1 : nx], "gx", up_x)
     from_right = lax.ppermute(value[:, 0:1], "gx", down_x)
-    padded = jnp.pad(value, ((0, 0), (1, 1), (1, 1), (1, 1), (0, 0)))
 
     def row(at):
         return jnp.concatenate([from_left[:, :, at], value[:, :, at], from_right[:, :, at]], 1)
 
     from_below = lax.ppermute(row(slice(ny - 1, ny)), "gy", up_y)
     from_above = lax.ppermute(row(slice(0, 1)), "gy", down_y)
-    padded = lax.dynamic_update_slice(padded, from_left, (0, 0, 1, 1, 0))
-    padded = lax.dynamic_update_slice(padded, from_right, (0, nx + 1, 1, 1, 0))
-    padded = lax.dynamic_update_slice(padded, from_below, (0, 0, 0, 1, 0))
-    padded = lax.dynamic_update_slice(padded, from_above, (0, 0, ny + 1, 1, 0))
-    return padded
+    wide = jnp.concatenate([from_left, value, from_right], 1)
+    full = jnp.concatenate([from_below, wide, from_above], 2)
+    return jnp.pad(full, ((0, 0), (0, 0), (0, 0), (1, 1), (0, 0)))
 
 
 FIRST = ("gx", 0)

time: 169 us -> 150 us (0.89)
  local copies, waits for them, and re-layouts: 36.7 us -> 10.2 us
  other arithmetic: 4.31 us -> 11.9 us
  starting transfers between devices: 62.4 us -> 64.8 us
  waiting for transfers between devices: 48.4 us -> 46.7 us
    dynamic_update_slice x4 -> x0, local copies, waits for them, and re-layouts: 17.6 us -> none  [the longest x1 5.41 us: with_halo(): padded = lax.dynamic_update_slice(padded, from_below, (0, 0, 0, 1, 0))]
    concatenate x0 -> x1, other arithmetic: none -> 7.54 us  [with_halo(): full = jnp.concatenate([from_below, wide, from_above], 2)]
    pad x1 -> x0, local copies, waits for them, and re-layouts: 7.38 us -> none  [with_halo(): padded = jnp.pad(value, ((0, 0), (1, 1), (1, 1), (1, 1), (0, 0)))]
    ppermute x1, waiting for transfers between devices: 0.01 us -> 2.09 us  [with_halo(): from_below = lax.ppermute(row(slice(ny - 1, ny)), 'gy', up_y)]
    ppermute x7, waiting for transfers between devices: 15 us -> 12.9 us  [butterfly_scatter(): buf = keep + lax.ppermute(send, ('gx', 'gy'), step_pairs(k))]
    ppermute x7, starting transfers between devices: 9.17 us -> 10.9 us  [butterfly_gather(): got = lax.ppermute(buf, ('gx', 'gy'), step_pairs(k))]
    ppermute x7, waiting for transfers between devices: 26.4 us -> 24.7 us  [butterfly_gather(): got = lax.ppermute(buf, ('gx', 'gy'), step_pairs(k))]
  transfers between devices with their start and end apart: 20 -> 20, of which waited for: 17 -> 18; matrix products, arithmetic and copies ran while one was open for 16% -> 5% of each run, Pallas kernels for 0% -> 0%
where the time goes in v8:
time: 150 us
  starting transfers between devices  64.8 us (43%)
  waiting for transfers between devices  46.7 us (31%)
  other arithmetic  11.9 us (8%)
  local copies, waits for them, and re-layouts  10.2 us (7%)
  matrix products  8.6 us (6%)
  between operations  7.59 us (5%)
    ppermute x7, starting transfers between devices, butterfly_scatter(): buf = keep + lax.ppermute(send, ('gx', 'gy'), step_pairs(k))  26.1 us
    ppermute x7, waiting for transfers between devices, butterfly_gather(): got = lax.ppermute(buf, ('gx', 'gy'), step_pairs(k))  24.7 us
    ppermute x1, starting transfers between devices, butterfly_gather(): lax.ppermute(buf, 'gx', [(i, i ^ 1) for i in range(lax.axis_size('gx'))])  14.2 us
    ppermute x7, waiting for transfers between devices, butterfly_scatter(): buf = keep + lax.ppermute(send, ('gx', 'gy'), step_pairs(k))  12.9 us
    ppermute x7, starting transfers between devices, butterfly_gather(): got = lax.ppermute(buf, ('gx', 'gy'), step_pairs(k))  10.9 us
    concatenate x1, other arithmetic, with_halo(): full = jnp.concatenate([from_below, wide, from_above], 2)  7.54 us
    ppermute x1, starting transfers between devices, with_halo(): from_right = lax.ppermute(value[:, 0:1], 'gx', down_x)  5.11 us
    ppermute x1, starting transfers between devices, with_halo(): from_below = lax.ppermute(row(slice(ny - 1, ny)), 'gy', up_y)  4 us
  transfers between devices with their start and end apart: 20, of which 18 were waited for; matrix products, arithmetic and copies ran while one was open for 5% of the time, Pallas kernels for 0%

profile of v8, /device:TPU:1, one launch (start us, length us, event | category | flops | bytes accessed | tf_op | source)
XLA Modules:
  0.0 149.7 jit_solution(15921404783628503624)
XLA Ops:
  0.6 0.0 copy-start
  1.4 0.8 broadcast_bitcast_fusion
  2.1 1.2 maximum_multiply_fusion
  3.4 0.0 copy-start.2
  3.4 2.0 %convolution_convert_fusion = bf16[2,512,128,16]{2,3,1,0:T(8,128)(2,1)S(1)} fusion(bf16[2,2,512,128]{3,2,1,0:T(8,128)(2,1)S(1)} %maximum_multiply_fusion, pred[2]{0:T(512)(128)(4,1)S(1)} %get-tuple-element.98, s32[2]{0:T(128)} %bitcast.186), kind=kOutput, calls=%fused_computation.10 | convolution fusion | flops 10485824 | bytes 4718602 | tf_op jit(solution)/shard_map/ps,tsvc->tpvc/dot_general | solution.py:98
  5.5 0.0 copy-start.3
  5.5 1.6 %copy.12 = bf16[2,2,2,4,8,8,8,128]{7,6,3,5,2,4,1,0:T(8,128)(2,1)S(1)} copy(bf16[2,2,2,4,8,8,8,128]{7,3,2,1,6,5,4,0:T(4,128)(2,1)S(1)} %bitcast.124) | data formatting | bytes 8388608 | tf_op jit(solution)/shard_map/reshape | solution.py:102
  7.1 5.1 %collective-permute-start.1 = (bf16[2,1,16,32,128]{4,3,2,1,0:T(8,128)(2,1)S(1)}, bf16[2,1,16,32,128]{4,3,2,1,0:T(8,128)(2,1)S(1)}, u32[]{:S(2)}, u32[]{:S(2)}) collective-permute-start(bf16[2,1,16,32,128]{4,3,2,1,0:T(8,128)(2,1)S(1)} %get-tuple-element.17), channel_id=1, source_target_pairs={{16,0},{32,16},{48,32},{64,48},{80,64},{96,80},{112,96},{128,112},... | collective-permute-start | bytes 786440 | tf_op jit(solution)/shard_map/ppermute | solution.py:21
  12.3 2.8 %collective-permute-start = (bf16[2,1,16,32,128]{4,3,2,1,0:T(8,128)(2,1)S(1)}, bf16[2,1,16,32,128]{4,3,2,1,0:T(8,128)(2,1)S(1)}, u32[]{:S(2)}, u32[]{:S(2)}) collective-permute-start(bf16[2,1,16,32,128]{4,3,2,1,0:T(8,128)(2,1)S(1)} %get-tuple-element.16), channel_id=1, source_target_pairs={{0,16},{16,32},{32,48},{48,64},{64,80},{80,96},{96,112},{112,128},... | collective-permute-start | bytes 786440 | tf_op jit(solution)/shard_map/ppermute | solution.py:20
  15.2 2.0 %collective-permute-done.1 = bf16[2,1,16,32,128]{4,3,2,1,0:T(8,128)(2,1)S(1)} collective-permute-done((bf16[2,1,16,32,128]{4,3,2,1,0:T(8,128)(2,1)S(1)}, bf16[2,1,16,32,128]{4,3,2,1,0:T(8,128)(2,1)S(1)}, u32[]{:S(2)}, u32[]{:S(2)}) %collective-permute-start.1) | collective-permute-done | bytes 262176 | tf_op jit(solution)/shard_map/ppermute | solution.py:21
  17.2 1.2 collective-permute-done
  18.5 1.3 collective-permute-start.3
  19.8 4.0 %collective-permute-start.2 = (bf16[2,18,1,32,128]{4,3,2,1,0:T(8,128)(2,1)S(1)}, bf16[2,18,1,32,128]{4,3,2,1,0:T(8,128)(2,1)S(1)}, u32[]{:S(2)}, u32[]{:S(2)}) collective-permute-start(bf16[2,18,1,32,128]{4,3,2,1,0:T(8,128)(2,1)S(1)} %pad_maximum_fusion.4), channel_id=1, source_target_pairs={{0,1},{1,2},{2,3},{3,4},{4,5},{5,6},{6,7},{7,8},{8,9},{9,10},{10,1... | collective-permute-start | bytes 884744 | tf_op jit(solution)/shard_map/ppermute | solution.py:26
  23.8 0.6 fusion.32
  29.8 2.1 %collective-permute-done.2 = bf16[2,18,1,32,128]{4,3,2,1,0:T(8,128)(2,1)S(1)} collective-permute-done((bf16[2,18,1,32,128]{4,3,2,1,0:T(8,128)(2,1)S(1)}, bf16[2,18,1,32,128]{4,3,2,1,0:T(8,128)(2,1)S(1)}, u32[]{:S(2)}, u32[]{:S(2)}) %collective-permute-start.2) | collective-permute-done | bytes 294944 | tf_op jit(solution)/shard_map/ppermute | solution.py:26
  31.9 7.5 %select_maximum_fusion = bf16[2,18,18,34,128]{4,3,2,1,0:T(8,128)(2,1)S(1)} fusion(bf16[2,18,1,32,128]{4,3,2,1,0:T(8,128)(2,1)S(1)} %collective-permute-done.3, bf16[2,18,1,32,128]{4,3,2,1,0:T(8,128)(2,1)S(1)} %collective-permute-done.2, bf16[2,1,16,32,128]{4,3,2,1,0:T(8,128)(2,1)S(1)} %collective-permute-done.1, bf16[2,16,16,32,128]{4,3,2,1,0:T(8,128)(2,1)} %bitcast.123, ...), kind=kLoop, calls=%fused_computation.3 | loop fusion | flops 50761728 | bytes 10948608 | tf_op jit(solution)/shard_map/concatenate | solution.py:29
  39.5 0.8 dynamic-slice_bitcast_fusion
  40.3 0.3 fusion.13
  40.6 0.4 fusion.29
  41.0 1.0 fusion.28
  42.1 0.5 fusion.27
  42.5 1.0 fusion.26
  43.6 0.0 slice-start
  44.8 1.1 convolution_multiply_fusion
  45.9 0.1 pad_dynamic-slice_fusion
  46.0 0.3 collective-permute-start.4
  47.2 1.5 %collective-permute-done.4 = f32[1792,128]{1,0:T(8,128)S(1)} collective-permute-done((f32[1792,128]{1,0:T(8,128)S(1)}, f32[1792,128]{1,0:T(8,128)S(1)}, u32[]{:S(2)}, u32[]{:S(2)}) %collective-permute-start.4) | collective-permute-done | bytes 917536 | tf_op jit(solution)/shard_map/ppermute | solution.py:72
  48.8 0.1 fusion.10
  48.9 5.1 %collective-permute-start.5 = (f32[896,128]{1,0:T(8,128)S(1)}, f32[896,128]{1,0:T(8,128)S(1)}, u32[]{:S(2)}, u32[]{:S(2)}) collective-permute-start(f32[896,128]{1,0:T(8,128)S(1)} %constant_dynamic-slice_fusion.6), channel_id=1, source_target_pairs={{0,1},{1,0},{2,3},{3,2},{4,5},{5,4},{6,7},{7,6},{8,9},{9,8},{10,11... | collective-permute-start | bytes 1376264 | tf_op jit(solution)/shard_map/ppermute | solution.py:78
  54.0 2.7 %fusion.8 = bf16[1024,128]{1,0:T(8,128)(2,1)} fusion(bf16[27,1024,128]{2,1,0:T(8,128)(2,1)S(1)} %constant_dynamic-update-slice_fusion, bf16[27,128,128]{2,1,0:T(8,128)(2,1)S(1)} %copy-done, f32[1024]{0:T(1024)S(1)} %fusion.16), kind=kOutput, calls=%fused_computation.21 | convolution fusion | flops 906231808 | bytes 8228864 | tf_op jit(solution)/shard_map/dvc,dce->ve/dot_general | solution.py:145
  56.8 3.2 %collective-permute-done.5 = f32[896,128]{1,0:T(8,128)S(1)} collective-permute-done((f32[896,128]{1,0:T(8,128)S(1)}, f32[896,128]{1,0:T(8,128)S(1)}, u32[]{:S(2)}, u32[]{:S(2)}) %collective-permute-start.5) | collective-permute-done | bytes 458784 | tf_op jit(solution)/shard_map/ppermute | solution.py:78
  60.0 2.6 %collective-permute-start.6 = (f32[448,128]{1,0:T(8,128)S(1)}, f32[448,128]{1,0:T(8,128)S(1)}, u32[]{:S(2)}, u32[]{:S(2)}) collective-permute-start(f32[448,128]{1,0:T(8,128)S(1)} %constant_dynamic-slice_fusion.5), channel_id=1, source_target_pairs={{0,64},{1,65},{2,66},{3,67},{4,68},{5,69},{6,70},{7,71},{8,72},{9,... | collective-permute-start | bytes 688136 | tf_op jit(solution)/shard_map/ppermute | solution.py:78
  62.6 3.6 %collective-permute-done.6 = f32[448,128]{1,0:T(8,128)S(1)} collective-permute-done((f32[448,128]{1,0:T(8,128)S(1)}, f32[448,128]{1,0:T(8,128)S(1)}, u32[]{:S(2)}, u32[]{:S(2)}) %collective-permute-start.6) | collective-permute-done | bytes 229408 | tf_op jit(solution)/shard_map/ppermute | solution.py:78
  66.3 1.4 collective-permute-start.7
  67.8 2.3 %collective-permute-done.7 = f32[224,128]{1,0:T(8,128)S(1)} collective-permute-done((f32[224,128]{1,0:T(8,128)S(1)}, f32[224,128]{1,0:T(8,128)S(1)}, u32[]{:S(2)}, u32[]{:S(2)}) %collective-permute-start.7) | collective-permute-done | bytes 114720 | tf_op jit(solution)/shard_map/ppermute | solution.py:78
  70.1 3.5 %collective-permute-start.8 = (f32[112,128]{1,0:T(8,128)S(1)}, f32[112,128]{1,0:T(8,128)S(1)}, u32[]{:S(2)}, u32[]{:S(2)}) collective-permute-start(f32[112,128]{1,0:T(8,128)S(1)} %constant_dynamic-slice_fusion.3), channel_id=1, source_target_pairs={{0,32},{1,33},{2,34},{3,35},{4,36},{5,37},{6,38},{7,39},{8,40},{9,... | collective-permute-start | bytes 172040 | tf_op jit(solution)/shard_map/ppermute | solution.py:78
  73.6 1.5 %collective-permute-done.8 = f32[112,128]{1,0:T(8,128)S(1)} collective-permute-done((f32[112,128]{1,0:T(8,128)S(1)}, f32[112,128]{1,0:T(8,128)S(1)}, u32[]{:S(2)}, u32[]{:S(2)}) %collective-permute-start.8) | collective-permute-done | bytes 57376 | tf_op jit(solution)/shard_map/ppermute | solution.py:78
  75.2 4.2 %collective-permute-start.9 = (f32[56,128]{1,0:T(8,128)S(1)}, f32[56,128]{1,0:T(8,128)S(1)}, u32[]{:S(2)}, u32[]{:S(2)}) collective-permute-start(f32[56,128]{1,0:T(8,128)S(1)} %constant_dynamic-slice_fusion.2), channel_id=1, source_target_pairs={{0,128},{1,129},{2,130},{3,131},{4,132},{5,133},{6,134},{7,135},{8... | collective-permute-start | bytes 86024 | tf_op jit(solution)/shard_map/ppermute | solution.py:78
  79.4 1.2 collective-permute-done.9
  80.6 3.4 %collective-permute-start.10 = (f32[28,128]{1,0:T(8,128)S(1)}, f32[28,128]{1,0:T(8,128)S(1)}, u32[]{:S(2)}, u32[]{:S(2)}) collective-permute-start(f32[28,128]{1,0:T(8,128)S(1)} %constant_dynamic-slice_fusion.1), channel_id=1, source_target_pairs={{0,4},{1,5},{2,6},{3,7},{4,0},{5,1},{6,2},{7,3},{8,12},{9,13},{10,... | collective-permute-start | bytes 43016 | tf_op jit(solution)/shard_map/ppermute | solution.py:78
  84.0 1.1 collective-permute-done.10
  85.2 6.0 %collective-permute-start.11 = (f32[14,128]{1,0:T(8,128)S(1)}, f32[14,128]{1,0:T(8,128)S(1)}, u32[]{:S(2)}, u32[]{:S(2)}) collective-permute-start(f32[14,128]{1,0:T(8,128)S(1)} %constant_dynamic-slice_fusion), channel_id=1, source_target_pairs={{0,8},{1,9},{2,10},{3,11},{4,12},{5,13},{6,14},{7,15},{8,0},{9,1},... | collective-permute-start | bytes 21512 | tf_op jit(solution)/shard_map/ppermute | solution.py:78
  91.2 2.7 %fusion.9 = bf16[1024,128]{1,0:T(8,128)(2,1)} fusion(bf16[27,1024,128]{2,1,0:T(8,128)(2,1)S(1)} %constant_dynamic-update-slice_fusion.27, bf16[27,128,128]{2,1,0:T(8,128)(2,1)S(1)} %copy-done, f32[1024]{0:T(1024)S(1)} %fusion.16), kind=kOutput, calls=%fused_computation.22 | convolution fusion | flops 906231808 | bytes 8228864 | tf_op jit(solution)/shard_map/dvc,dec->ve/dot_general | solution.py:148
  93.9 3.8 %collective-permute-start.12 = (f32[14,128]{1,0:T(8,128)S(1)}, f32[14,128]{1,0:T(8,128)S(1)}, u32[]{:S(2)}, u32[]{:S(2)}) collective-permute-start(f32[14,128]{1,0:T(8,128)S(1)} %dynamic-slice_add_fusion.6), channel_id=1, source_target_pairs={{0,8},{1,9},{2,10},{3,11},{4,12},{5,13},{6,14},{7,15},{8,0},{9,1},... | collective-permute-start | bytes 21512 | tf_op jit(solution)/shard_map/ppermute | solution.py:88
  97.7 2.7 %collective-permute-done.12 = f32[14,128]{1,0:T(8,128)S(1)} collective-permute-done((f32[14,128]{1,0:T(8,128)S(1)}, f32[14,128]{1,0:T(8,128)S(1)}, u32[]{:S(2)}, u32[]{:S(2)}) %collective-permute-start.12) | collective-permute-done | bytes 7200 | tf_op jit(solution)/shard_map/ppermute | solution.py:88
  100.4 2.0 %collective-permute-start.13 = (f32[28,128]{1,0:T(8,128)S(1)}, f32[28,128]{1,0:T(8,128)S(1)}, u32[]{:S(2)}, u32[]{:S(2)}) collective-permute-start(f32[28,128]{1,0:T(8,128)S(1)} %pad_maximum_fusion.10), channel_id=1, source_target_pairs={{0,4},{1,5},{2,6},{3,7},{4,0},{5,1},{6,2},{7,3},{8,12},{9,13},{10,... | collective-permute-start | bytes 43016 | tf_op jit(solution)/shard_map/ppermute | solution.py:88
  102.4 2.2 %collective-permute-done.13 = f32[28,128]{1,0:T(8,128)S(1)} collective-permute-done((f32[28,128]{1,0:T(8,128)S(1)}, f32[28,128]{1,0:T(8,128)S(1)}, u32[]{:S(2)}, u32[]{:S(2)}) %collective-permute-start.13) | collective-permute-done | bytes 14368 | tf_op jit(solution)/shard_map/ppermute | solution.py:88
  104.6 0.6 collective-permute-start.14
  105.2 3.2 %collective-permute-done.14 = f32[56,128]{1,0:T(8,128)S(1)} collective-permute-done((f32[56,128]{1,0:T(8,128)S(1)}, f32[56,128]{1,0:T(8,128)S(1)}, u32[]{:S(2)}, u32[]{:S(2)}) %collective-permute-start.14) | collective-permute-done | bytes 28704 | tf_op jit(solution)/shard_map/ppermute | solution.py:88
  108.5 3.2 %collective-permute-start.15 = (f32[112,128]{1,0:T(8,128)S(1)}, f32[112,128]{1,0:T(8,128)S(1)}, u32[]{:S(2)}, u32[]{:S(2)}) collective-permute-start(f32[112,128]{1,0:T(8,128)S(1)} %pad_maximum_fusion.8), channel_id=1, source_target_pairs={{0,32},{1,33},{2,34},{3,35},{4,36},{5,37},{6,38},{7,39},{8,40},{9,... | collective-permute-start | bytes 172040 | tf_op jit(solution)/shard_map/ppermute | solution.py:88
  111.7 1.6 %collective-permute-done.15 = f32[112,128]{1,0:T(8,128)S(1)} collective-permute-done((f32[112,128]{1,0:T(8,128)S(1)}, f32[112,128]{1,0:T(8,128)S(1)}, u32[]{:S(2)}, u32[]{:S(2)}) %collective-permute-start.15) | collective-permute-done | bytes 57376 | tf_op jit(solution)/shard_map/ppermute | solution.py:88
  113.3 0.1 collective-permute-start.16
  113.4 3.9 %collective-permute-done.16 = f32[224,128]{1,0:T(8,128)S(1)} collective-permute-done((f32[224,128]{1,0:T(8,128)S(1)}, f32[224,128]{1,0:T(8,128)S(1)}, u32[]{:S(2)}, u32[]{:S(2)}) %collective-permute-start.16) | collective-permute-done | bytes 114720 | tf_op jit(solution)/shard_map/ppermute | solution.py:88
  117.3 0.1 collective-permute-start.17
  117.4 4.9 %collective-permute-done.17 = f32[448,128]{1,0:T(8,128)S(1)} collective-permute-done((f32[448,128]{1,0:T(8,128)S(1)}, f32[448,128]{1,0:T(8,128)S(1)}, u32[]{:S(2)}, u32[]{:S(2)}) %collective-permute-start.17) | collective-permute-done | bytes 229408 | tf_op jit(solution)/shard_map/ppermute | solution.py:88
  122.4 1.1 collective-permute-start.18
  123.5 6.3 %collective-permute-done.18 = f32[896,128]{1,0:T(8,128)S(1)} collective-permute-done((f32[896,128]{1,0:T(8,128)S(1)}, f32[896,128]{1,0:T(8,128)S(1)}, u32[]{:S(2)}, u32[]{:S(2)}) %collective-permute-start.18) | collective-permute-done | bytes 458784 | tf_op jit(solution)/shard_map/ppermute | solution.py:88
  129.8 0.1 broadcast_select_fusion.3
  129.8 0.1 pad_maximum_fusion.1
  129.9 14.2 %collective-permute-start.19 = (f32[1792,128]{1,0:T(8,128)S(1)}, f32[1792,128]{1,0:T(8,128)}, u32[]{:S(2)}, u32[]{:S(2)}) collective-permute-start(f32[1792,128]{1,0:T(8,128)S(1)} %pad_maximum_fusion.1), channel_id=1, source_target_pairs={{0,16},{16,0},{32,48},{48,32},{64,80},{80,64},{96,112},{112,96},{1... | collective-permute-start | bytes 2752520 | tf_op jit(solution)/shard_map/ppermute | solution.py:90
  144.2 2.2 %collective-permute-done.19 = f32[1792,128]{1,0:T(8,128)} collective-permute-done((f32[1792,128]{1,0:T(8,128)S(1)}, f32[1792,128]{1,0:T(8,128)}, u32[]{:S(2)}, u32[]{:S(2)}) %collective-permute-start.19) | collective-permute-done | bytes 917536 | tf_op jit(solution)/shard_map/ppermute | solution.py:90
  146.4 1.3 broadcast_select_fusion.1
  147.7 0.1 pad_maximum_fusion
  147.8 1.9 %copy.14 = f32[27,128,128]{2,1,0:T(8,128)} copy(f32[27,128,128]{1,2,0:T(8,128)S(1)} %bitcast.125) | data formatting | bytes 3538944
  (100 shorter events, 2.6 us)
Async XLA Ops:
  0.6 53.4 %copy-start = (bf16[27,128,128]{2,1,0:T(8,128)(2,1)S(1)}, bf16[27,128,128]{2,1,0:T(8,128)(2,1)}, u32[]{:S(2)}) copy-start(bf16[27,128,128]{2,1,0:T(8,128)(2,1)} %param.10) | copy-start | bytes 2654212
  3.4 11.8 %copy-start.2 = (bf16[2,2,512,128]{3,2,1,0:T(8,128)(2,1)}, bf16[2,2,512,128]{3,2,1,0:T(8,128)(2,1)S(1)}, u32[]{:S(2)}) copy-start(bf16[2,2,512,128]{3,2,1,0:T(8,128)(2,1)S(1)} %maximum_multiply_fusion) | copy-start | bytes 1572868
  5.4 18.4 %copy-start.4 = (s32[1,1,2]{2,1,0:T(1,128)S(1)}, s32[1,1,2]{2,1,0:T(1,128)}, u32[]{:S(2)}) copy-start(s32[1,1,2]{2,1,0:T(1,128)} %param.8) | copy-start | bytes 28
  5.5 24.3 %copy-start.3 = (s32[1,1,2,512]{3,2,1,0:T(2,128)S(1)}, s32[1,1,2,512]{3,2,1,0:T(2,128)}, u32[]{:S(2)}) copy-start(s32[1,1,2,512]{3,2,1,0:T(2,128)} %param.7) | copy-start | bytes 12292
  7.1 8.0 %copy-start.1 = (bf16[2,2,2,4,8,8,8,128]{7,6,3,5,2,4,1,0:T(8,128)(2,1)}, bf16[2,2,2,4,8,8,8,128]{7,6,3,5,2,4,1,0:T(8,128)(2,1)S(1)}, u32[]{:S(2)}) copy-start(bf16[2,2,2,4,8,8,8,128]{7,6,3,5,2,4,1,0:T(8,128)(2,1)S(1)} %copy.12) | copy-start | bytes 12582916
  7.1 10.1 %collective-permute-start.1 = (bf16[2,1,16,32,128]{4,3,2,1,0:T(8,128)(2,1)S(1)}, bf16[2,1,16,32,128]{4,3,2,1,0:T(8,128)(2,1)S(1)}, u32[]{:S(2)}, u32[]{:S(2)}) collective-permute-start(bf16[2,1,16,32,128]{4,3,2,1,0:T(8,128)(2,1)S(1)} %get-tuple-element.17), channel_id=1, source_target_pairs={{16,0},{32,16},{48,32},{64,48},{80,64},{96,80},{112,96},{128,112},... | collective-permute-start | bytes 786440 | tf_op jit(solution)/shard_map/ppermute | solution.py:21
  12.3 6.1 %collective-permute-start = (bf16[2,1,16,32,128]{4,3,2,1,0:T(8,128)(2,1)S(1)}, bf16[2,1,16,32,128]{4,3,2,1,0:T(8,128)(2,1)S(1)}, u32[]{:S(2)}, u32[]{:S(2)}) collective-permute-start(bf16[2,1,16,32,128]{4,3,2,1,0:T(8,128)(2,1)S(1)} %get-tuple-element.16), channel_id=1, source_target_pairs={{0,16},{16,32},{32,48},{48,64},{64,80},{80,96},{96,112},{112,128},... | collective-permute-start | bytes 786440 | tf_op jit(solution)/shard_map/ppermute | solution.py:20
  18.5 11.4 %collective-permute-start.3 = (bf16[2,18,1,32,128]{4,3,2,1,0:T(8,128)(2,1)S(1)}, bf16[2,18,1,32,128]{4,3,2,1,0:T(8,128)(2,1)S(1)}, u32[]{:S(2)}, u32[]{:S(2)}) collective-permute-start(bf16[2,18,1,32,128]{4,3,2,1,0:T(8,128)(2,1)S(1)} %pad_maximum_fusion.5), channel_id=1, source_target_pairs={{1,0},{2,1},{3,2},{4,3},{5,4},{6,5},{7,6},{8,7},{9,8},{10,9},{11,1... | collective-permute-start | bytes 884744 | tf_op jit(solution)/shard_map/ppermute | solution.py:27
  19.8 12.1 %collective-permute-start.2 = (bf16[2,18,1,32,128]{4,3,2,1,0:T(8,128)(2,1)S(1)}, bf16[2,18,1,32,128]{4,3,2,1,0:T(8,128)(2,1)S(1)}, u32[]{:S(2)}, u32[]{:S(2)}) collective-permute-start(bf16[2,18,1,32,128]{4,3,2,1,0:T(8,128)(2,1)S(1)} %pad_maximum_fusion.4), channel_id=1, source_target_pairs={{0,1},{1,2},{2,3},{3,4},{4,5},{5,6},{6,7},{7,8},{8,9},{9,10},{10,1... | collective-permute-start | bytes 884744 | tf_op jit(solution)/shard_map/ppermute | solution.py:26
  43.6 1.2 slice-start
  46.0 2.7 %collective-permute-start.4 = (f32[1792,128]{1,0:T(8,128)S(1)}, f32[1792,128]{1,0:T(8,128)S(1)}, u32[]{:S(2)}, u32[]{:S(2)}) collective-permute-start(f32[1792,128]{1,0:T(8,128)S(1)} %pad_dynamic-slice_fusion), channel_id=1, source_target_pairs={{0,16},{16,0},{32,48},{48,32},{64,80},{80,64},{96,112},{112,96},{1... | collective-permute-start | bytes 2752520 | tf_op jit(solution)/shard_map/ppermute | solution.py:72
  48.9 11.0 %collective-permute-start.5 = (f32[896,128]{1,0:T(8,128)S(1)}, f32[896,128]{1,0:T(8,128)S(1)}, u32[]{:S(2)}, u32[]{:S(2)}) collective-permute-start(f32[896,128]{1,0:T(8,128)S(1)} %constant_dynamic-slice_fusion.6), channel_id=1, source_target_pairs={{0,1},{1,0},{2,3},{3,2},{4,5},{5,4},{6,7},{7,6},{8,9},{9,8},{10,11... | collective-permute-start | bytes 1376264 | tf_op jit(solution)/shard_map/ppermute | solution.py:78
  60.0 6.3 %collective-permute-start.6 = (f32[448,128]{1,0:T(8,128)S(1)}, f32[448,128]{1,0:T(8,128)S(1)}, u32[]{:S(2)}, u32[]{:S(2)}) collective-permute-start(f32[448,128]{1,0:T(8,128)S(1)} %constant_dynamic-slice_fusion.5), channel_id=1, source_target_pairs={{0,64},{1,65},{2,66},{3,67},{4,68},{5,69},{6,70},{7,71},{8,72},{9,... | collective-permute-start | bytes 688136 | tf_op jit(solution)/shard_map/ppermute | solution.py:78
  66.3 3.7 %collective-permute-start.7 = (f32[224,128]{1,0:T(8,128)S(1)}, f32[224,128]{1,0:T(8,128)S(1)}, u32[]{:S(2)}, u32[]{:S(2)}) collective-permute-start(f32[224,128]{1,0:T(8,128)S(1)} %constant_dynamic-slice_fusion.4), channel_id=1, source_target_pairs={{0,2},{1,3},{2,0},{3,1},{4,6},{5,7},{6,4},{7,5},{8,10},{9,11},{10,... | collective-permute-start | bytes 344072 | tf_op jit(solution)/shard_map/ppermute | solution.py:78
  70.1 5.0 %collective-permute-start.8 = (f32[112,128]{1,0:T(8,128)S(1)}, f32[112,128]{1,0:T(8,128)S(1)}, u32[]{:S(2)}, u32[]{:S(2)}) collective-permute-start(f32[112,128]{1,0:T(8,128)S(1)} %constant_dynamic-slice_fusion.3), channel_id=1, source_target_pairs={{0,32},{1,33},{2,34},{3,35},{4,36},{5,37},{6,38},{7,39},{8,40},{9,... | collective-permute-start | bytes 172040 | tf_op jit(solution)/shard_map/ppermute | solution.py:78
  75.2 5.5 %collective-permute-start.9 = (f32[56,128]{1,0:T(8,128)S(1)}, f32[56,128]{1,0:T(8,128)S(1)}, u32[]{:S(2)}, u32[]{:S(2)}) collective-permute-start(f32[56,128]{1,0:T(8,128)S(1)} %constant_dynamic-slice_fusion.2), channel_id=1, source_target_pairs={{0,128},{1,129},{2,130},{3,131},{4,132},{5,133},{6,134},{7,135},{8... | collective-permute-start | bytes 86024 | tf_op jit(solution)/shard_map/ppermute | solution.py:78
  80.6 4.5 %collective-permute-start.10 = (f32[28,128]{1,0:T(8,128)S(1)}, f32[28,128]{1,0:T(8,128)S(1)}, u32[]{:S(2)}, u32[]{:S(2)}) collective-permute-start(f32[28,128]{1,0:T(8,128)S(1)} %constant_dynamic-slice_fusion.1), channel_id=1, source_target_pairs={{0,4},{1,5},{2,6},{3,7},{4,0},{5,1},{6,2},{7,3},{8,12},{9,13},{10,... | collective-permute-start | bytes 43016 | tf_op jit(solution)/shard_map/ppermute | solution.py:78
  85.2 8.7 %collective-permute-start.11 = (f32[14,128]{1,0:T(8,128)S(1)}, f32[14,128]{1,0:T(8,128)S(1)}, u32[]{:S(2)}, u32[]{:S(2)}) collective-permute-start(f32[14,128]{1,0:T(8,128)S(1)} %constant_dynamic-slice_fusion), channel_id=1, source_target_pairs={{0,8},{1,9},{2,10},{3,11},{4,12},{5,13},{6,14},{7,15},{8,0},{9,1},... | collective-permute-start | bytes 21512 | tf_op jit(solution)/shard_map/ppermute | solution.py:78
  93.9 6.5 %collective-permute-start.12 = (f32[14,128]{1,0:T(8,128)S(1)}, f32[14,128]{1,0:T(8,128)S(1)}, u32[]{:S(2)}, u32[]{:S(2)}) collective-permute-start(f32[14,128]{1,0:T(8,128)S(1)} %dynamic-slice_add_fusion.6), channel_id=1, source_target_pairs={{0,8},{1,9},{2,10},{3,11},{4,12},{5,13},{6,14},{7,15},{8,0},{9,1},... | collective-permute-start | bytes 21512 | tf_op jit(solution)/shard_map/ppermute | solution.py:88
  100.4 4.2 %collective-permute-start.13 = (f32[28,128]{1,0:T(8,128)S(1)}, f32[28,128]{1,0:T(8,128)S(1)}, u32[]{:S(2)}, u32[]{:S(2)}) collective-permute-start(f32[28,128]{1,0:T(8,128)S(1)} %pad_maximum_fusion.10), channel_id=1, source_target_pairs={{0,4},{1,5},{2,6},{3,7},{4,0},{5,1},{6,2},{7,3},{8,12},{9,13},{10,... | collective-permute-start | bytes 43016 | tf_op jit(solution)/shard_map/ppermute | solution.py:88
  104.6 3.8 %collective-permute-start.14 = (f32[56,128]{1,0:T(8,128)S(1)}, f32[56,128]{1,0:T(8,128)S(1)}, u32[]{:S(2)}, u32[]{:S(2)}) collective-permute-start(f32[56,128]{1,0:T(8,128)S(1)} %pad_maximum_fusion.9), channel_id=1, source_target_pairs={{0,128},{1,129},{2,130},{3,131},{4,132},{5,133},{6,134},{7,135},{8... | collective-permute-start | bytes 86024 | tf_op jit(solution)/shard_map/ppermute | solution.py:88
  108.5 4.8 %collective-permute-start.15 = (f32[112,128]{1,0:T(8,128)S(1)}, f32[112,128]{1,0:T(8,128)S(1)}, u32[]{:S(2)}, u32[]{:S(2)}) collective-permute-start(f32[112,128]{1,0:T(8,128)S(1)} %pad_maximum_fusion.8), channel_id=1, source_target_pairs={{0,32},{1,33},{2,34},{3,35},{4,36},{5,37},{6,38},{7,39},{8,40},{9,... | collective-permute-start | bytes 172040 | tf_op jit(solution)/shard_map/ppermute | solution.py:88
  113.3 4.0 %collective-permute-start.16 = (f32[224,128]{1,0:T(8,128)S(1)}, f32[224,128]{1,0:T(8,128)S(1)}, u32[]{:S(2)}, u32[]{:S(2)}) collective-permute-start(f32[224,128]{1,0:T(8,128)S(1)} %pad_maximum_fusion.7), channel_id=1, source_target_pairs={{0,2},{1,3},{2,0},{3,1},{4,6},{5,7},{6,4},{7,5},{8,10},{9,11},{10,... | collective-permute-start | bytes 344072 | tf_op jit(solution)/shard_map/ppermute | solution.py:88
  117.3 5.0 %collective-permute-start.17 = (f32[448,128]{1,0:T(8,128)S(1)}, f32[448,128]{1,0:T(8,128)S(1)}, u32[]{:S(2)}, u32[]{:S(2)}) collective-permute-start(f32[448,128]{1,0:T(8,128)S(1)} %pad_maximum_fusion.6), channel_id=1, source_target_pairs={{0,64},{1,65},{2,66},{3,67},{4,68},{5,69},{6,70},{7,71},{8,72},{9,... | collective-permute-start | bytes 688136 | tf_op jit(solution)/shard_map/ppermute | solution.py:88
  122.4 7.4 %collective-permute-start.18 = (f32[896,128]{1,0:T(8,128)S(1)}, f32[896,128]{1,0:T(8,128)S(1)}, u32[]{:S(2)}, u32[]{:S(2)}) collective-permute-start(f32[896,128]{1,0:T(8,128)S(1)} %pad_maximum_fusion.3), channel_id=1, source_target_pairs={{0,1},{1,0},{2,3},{3,2},{4,5},{5,4},{6,7},{7,6},{8,9},{9,8},{10,11... | collective-permute-start | bytes 1376264 | tf_op jit(solution)/shard_map/ppermute | solution.py:88
  129.9 16.5 %collective-permute-start.19 = (f32[1792,128]{1,0:T(8,128)S(1)}, f32[1792,128]{1,0:T(8,128)}, u32[]{:S(2)}, u32[]{:S(2)}) collective-permute-start(f32[1792,128]{1,0:T(8,128)S(1)} %pad_maximum_fusion.1), channel_id=1, source_target_pairs={{0,16},{16,0},{32,48},{48,32},{64,80},{80,64},{96,112},{112,96},{1... | collective-permute-start | bytes 2752520 | tf_op jit(solution)/shard_map/ppermute | solution.py:90

commit v9 on v8

--- a/solution.py
+++ b/solution.py
@@ -25,6 +25,12 @@
 
     from_below = lax.ppermute(row(slice(ny - 1, ny)), "gy", up_y)
     from_above = lax.ppermute(row(slice(0, 1)), "gy", down_y)
+    return [tuple(part[kind : kind + 1] for part in (from_left, value, from_right, from_below, from_above))
+            for kind in range(value.shape[0])]
+
+
+def assemble(pieces):
+    from_left, value, from_right, from_below, from_above = pieces
     wide = jnp.concatenate([from_left, value, from_right], 1)
     full = jnp.concatenate([from_below, wide, from_above], 2)
     return jnp.pad(full, ((0, 0), (0, 0), (0, 0), (1, 1), (0, 0)))
@@ -57,7 +63,7 @@
     return jnp.where(lax.axis_index("gx") & 1 == 0, step_bit(ORDERS[0][k]), step_bit(ORDERS[1][k]))
 
 
-def butterfly_scatter(value):
+def butterfly_scatter(value, extra):
     lanes = value.shape[-1]
     flat = value.reshape(-1, lanes)
     rows = flat.shape[0]
@@ -70,13 +76,14 @@
     keep = lax.dynamic_slice_in_dim(buf, bit * half, half, 0)
     send = lax.dynamic_slice_in_dim(buf, (1 - bit) * half, half, 0)
     buf = keep + lax.ppermute(send, "gx", pairs)
+    buf, extra = lax.optimization_barrier((buf, extra))
     for k in range(len(ORDERS[0])):
         half = buf.shape[0] // 2
         bit = core_bit(k)
         keep = lax.dynamic_slice_in_dim(buf, bit * half, half, 0)
         send = lax.dynamic_slice_in_dim(buf, (1 - bit) * half, half, 0)
         buf = keep + lax.ppermute(send, ("gx", "gy"), step_pairs(k))
-    return buf
+    return buf, extra
 
 
 def join_halves(buf, got, bit):
@@ -135,16 +142,15 @@
     both = jnp.stack([features[0, 0], cotangent[0, 0]]) * keeper[None, :, :, None]
     grad_rows = both[1].reshape(-1, chans)
     dense = place_bricks(both, places, alive)
-    padded = with_halo(dense)
-    windows = cut_windows(padded, places)
-    feat_stack = stack_offsets(windows[0])
+    feat_pieces, grad_pieces = with_halo(dense)
+    feat_stack = stack_offsets(cut_windows(assemble(feat_pieces), places)[0])
     tiles = lax.axis_size("gx") * lax.axis_size("gy")
     weight_local = jnp.einsum("ve,dvc->dec", grad_rows, feat_stack, preferred_element_type=jnp.float32)
     weight_local = weight_local * jnp.float32(1.0 / tiles)
-    half_done = butterfly_scatter(weight_local)
+    half_done, grad_pieces = butterfly_scatter(weight_local, grad_pieces)
     output_sum = jnp.einsum("dvc,dce->ve", feat_stack, weight, preferred_element_type=jnp.float32)
     output_rows = (output_sum * keeper_rows).astype(jnp.bfloat16)
-    grad_stack = stack_offsets(windows[1])
+    grad_stack = stack_offsets(cut_windows(assemble(grad_pieces), places)[0])
     input_sum = jnp.einsum("dvc,dec->ve", grad_stack, weight[::-1], preferred_element_type=jnp.float32)
     input_rows = (input_sum * keeper_rows).astype(jnp.bfloat16)
     half_done, output_rows, input_rows = lax.optimization_barrier((half_done, output_rows, input_rows))

time: 150 us -> 163 us (1.087)
  local copies, waits for them, and re-layouts: 10.2 us -> 20.1 us
  starting transfers between devices: 64.8 us -> 61.4 us
  matrix products: 8.6 us -> 11.7 us
    ppermute x7, starting transfers between devices: 26.1 us -> 20 us  [butterfly_scatter(): buf = keep + lax.ppermute(send, ('gx', 'gy'), step_pairs(k))]
    slice x0 -> x5, local copies, waits for them, and re-layouts: none -> 4.31 us  [with_halo(): part[kind:kind + 1]]
    ppermute x1, waiting for transfers between devices: 2.09 us -> 5.84 us  [with_halo(): from_below = lax.ppermute(row(slice(ny - 1, ny)), 'gy', up_y)]
    ppermute x7, waiting for transfers between devices: 12.9 us -> 16.2 us  [butterfly_scatter(): buf = keep + lax.ppermute(send, ('gx', 'gy'), step_pairs(k))]
    dot_general x1, matrix products: 2.71 us -> 5.84 us  [local(): jnp.einsum('dvc,dce->ve', feat_stack, weight, preferred_element_type=jnp....]
    ppermute x7, starting transfers between devices: 10.9 us -> 13.6 us  [butterfly_gather(): got = lax.ppermute(buf, ('gx', 'gy'), step_pairs(k))]
    ppermute x7, waiting for transfers between devices: 24.7 us -> 22.1 us  [butterfly_gather(): got = lax.ppermute(buf, ('gx', 'gy'), step_pairs(k))]
    ppermute x1, waiting for transfers between devices: 2.04 us -> 0.01 us  [with_halo(): from_right = lax.ppermute(value[:, 0:1], 'gx', down_x)]
  transfers between devices with their start and end apart: 20 -> 20, of which waited for: 18 -> 16; matrix products, arithmetic and copies ran while one was open for 5% -> 11% of each run, Pallas kernels for 0% -> 0%
where the time goes in v9:
time: 163 us; the launch traced here: 162 us
  starting transfers between devices  61.4 us (38%)
  waiting for transfers between devices  48.3 us (30%)
  local copies, waits for them, and re-layouts  20.1 us (12%)
  other arithmetic  13.4 us (8%)
  matrix products  11.7 us (7%)
  between operations  7.3 us (4%)
    ppermute x7, waiting for transfers between devices, butterfly_gather(): got = lax.ppermute(buf, ('gx', 'gy'), step_pairs(k))  22.1 us
    ppermute x7, starting transfers between devices, butterfly_scatter(): buf = keep + lax.ppermute(send, ('gx', 'gy'), step_pairs(k))  20 us
    ppermute x7, waiting for transfers between devices, butterfly_scatter(): buf = keep + lax.ppermute(send, ('gx', 'gy'), step_pairs(k))  16.2 us
    ppermute x1, starting transfers between devices, butterfly_gather(): lax.ppermute(buf, 'gx', [(i, i ^ 1) for i in range(lax.axis_size('gx'))])  14.1 us
    ppermute x7, starting transfers between devices, butterfly_gather(): got = lax.ppermute(buf, ('gx', 'gy'), step_pairs(k))  13.6 us
    concatenate x2, other arithmetic, assemble(): full = jnp.concatenate([from_below, wide, from_above], 2)  5.98 us
    dot_general x1, matrix products, local(): jnp.einsum('dvc,dce->ve', feat_stack, weight, preferred_element_type=jnp....  5.84 us
    ppermute x1, waiting for transfers between devices, with_halo(): from_below = lax.ppermute(row(slice(ny - 1, ny)), 'gy', up_y)  5.84 us
  transfers between devices with their start and end apart: 20, of which 16 were waited for; matrix products, arithmetic and copies ran while one was open for 11% of the time, Pallas kernels for 0%

profile of v9, /device:TPU:1, one launch (start us, length us, event | category | flops | bytes accessed | tf_op | source)
XLA Modules:
  0.0 162.2 jit_solution(8927211017106405647)
XLA Ops:
  1.4 0.8 broadcast_bitcast_fusion
  2.1 1.2 maximum_multiply_fusion
  3.4 2.0 %convolution_convert_fusion = bf16[2,512,128,16]{2,3,1,0:T(8,128)(2,1)S(1)} fusion(bf16[2,2,512,128]{3,2,1,0:T(8,128)(2,1)S(1)} %maximum_multiply_fusion, pred[2]{0:T(512)(128)(4,1)S(1)} %get-tuple-element.122, s32[2]{0:T(128)} %bitcast.196), kind=kOutput, calls=%fused_computation.14 | convolution fusion | flops 10485824 | bytes 4718602 | tf_op jit(solution)/shard_map/ps,tsvc->tpvc/dot_general | solution.py:105
  5.4 1.6 copy.23
  7.1 0.8 fusion.23
  7.9 5.1 %collective-permute-start.1 = (bf16[2,1,16,32,128]{4,3,2,1,0:T(8,128)(2,1)}, bf16[2,1,16,32,128]{4,3,2,1,0:T(8,128)(2,1)}, u32[]{:S(2)}, u32[]{:S(2)}) collective-permute-start(bf16[2,1,16,32,128]{4,3,2,1,0:T(8,128)(2,1)} %get-tuple-element.31), channel_id=1, source_target_pairs={{16,0},{32,16},{48,32},{64,48},{80,64},{96,80},{112,96},{128,112},... | collective-permute-start | bytes 786440 | tf_op jit(solution)/shard_map/ppermute | solution.py:21
  13.0 2.8 %collective-permute-start = (bf16[2,1,16,32,128]{4,3,2,1,0:T(8,128)(2,1)}, bf16[2,1,16,32,128]{4,3,2,1,0:T(8,128)(2,1)}, u32[]{:S(2)}, u32[]{:S(2)}) collective-permute-start(bf16[2,1,16,32,128]{4,3,2,1,0:T(8,128)(2,1)} %get-tuple-element.30), channel_id=1, source_target_pairs={{0,16},{16,32},{32,48},{48,64},{64,80},{80,96},{96,112},{112,128},... | collective-permute-start | bytes 786440 | tf_op jit(solution)/shard_map/ppermute | solution.py:20
  15.9 2.3 %fusion.21 = (bf16[1,2,8,2,8,4,8,128]{7,6,5,4,3,2,1,0:T(8,128)(2,1)}, bf16[1,2,8,2,8,4,8,128]{7,6,5,4,3,2,1,0:T(8,128)(2,1)S(1)}) fusion(bf16[2,2,8,2,8,4,8,128]{7,6,5,4,3,2,1,0:T(8,128)(2,1)S(1)} %bitcast.130), kind=kLoop, calls=%fused_computation.141 | loop fusion | bytes 8388608 | tf_op jit(solution)/shard_map/slice | solution.py:28
  18.2 0.8 fusion.22
  19.0 0.7 fusion.34
  24.8 0.7 fusion.33
  25.6 0.7 fusion.32
  26.3 1.0 pad_maximum_fusion.4
  27.3 1.3 collective-permute-start.3
  28.6 1.0 pad_maximum_fusion.3
  29.6 4.0 %collective-permute-start.2 = (bf16[2,18,1,32,128]{4,3,2,1,0:T(8,128)(2,1)S(1)}, bf16[2,18,1,32,128]{4,3,2,1,0:T(8,128)(2,1)S(1)}, u32[]{:S(2)}, u32[]{:S(2)}) collective-permute-start(bf16[2,18,1,32,128]{4,3,2,1,0:T(8,128)(2,1)S(1)} %pad_maximum_fusion.3), channel_id=1, source_target_pairs={{0,1},{1,2},{2,3},{3,4},{4,5},{5,6},{6,7},{7,8},{8,9},{9,10},{10,1... | collective-permute-start | bytes 884744 | tf_op jit(solution)/shard_map/ppermute | solution.py:26
  33.6 1.0 fusion.30
  34.6 1.0 fusion.31
  35.6 1.9 %collective-permute-done.3 = bf16[2,18,1,32,128]{4,3,2,1,0:T(8,128)(2,1)S(1)} collective-permute-done((bf16[2,18,1,32,128]{4,3,2,1,0:T(8,128)(2,1)S(1)}, bf16[2,18,1,32,128]{4,3,2,1,0:T(8,128)(2,1)S(1)}, u32[]{:S(2)}, u32[]{:S(2)}) %collective-permute-start.3) | collective-permute-done | bytes 294944 | tf_op jit(solution)/shard_map/ppermute | solution.py:27
  37.5 5.8 %collective-permute-done.2 = bf16[2,18,1,32,128]{4,3,2,1,0:T(8,128)(2,1)S(1)} collective-permute-done((bf16[2,18,1,32,128]{4,3,2,1,0:T(8,128)(2,1)S(1)}, bf16[2,18,1,32,128]{4,3,2,1,0:T(8,128)(2,1)S(1)}, u32[]{:S(2)}, u32[]{:S(2)}) %collective-permute-start.2) | collective-permute-done | bytes 294944 | tf_op jit(solution)/shard_map/ppermute | solution.py:26
  43.4 3.0 %select_maximum_fusion.4 = bf16[1,18,18,34,128]{4,3,2,1,0:T(8,128)(2,1)S(1)} fusion(bf16[1,18,1,32,128]{4,3,2,1,0:T(8,128)(2,1)S(1)} %get-tuple-element.97, bf16[1,18,1,32,128]{4,3,2,1,0:T(8,128)(2,1)S(1)} %get-tuple-element.99, bf16[1,1,16,32,128]{4,3,2,1,0:T(8,128)(2,1)S(1)} %get-tuple-element.101, bf16[1,16,16,32,128]{4,3,2,1,0:T(8,128)(2,1)S(1)} %bitcast.134, ...), kind=kLoop, calls=%fused_computation.7 | loop fusion | flops 25380864 | bytes 5474304 | tf_op jit(solution)/shard_map/concatenate | solution.py:35
  46.9 0.4 fusion.27
  47.4 1.0 fusion.26
  49.7 1.2 convolution_multiply_fusion
  50.8 1.6 %copy-done.1 = bf16[27,1024,128]{2,1,0:T(8,128)(2,1)} copy-done((bf16[27,1024,128]{2,1,0:T(8,128)(2,1)}, bf16[27,1024,128]{2,1,0:T(8,128)(2,1)S(1)}, u32[]{:S(2)}) %copy-start.1) | copy-done | bytes 7077912
  52.5 1.0 pad_dynamic-slice_fusion
  53.4 0.5 collective-permute-start.4
  54.0 5.8 %fusion.8 = bf16[1024,128]{1,0:T(8,128)(2,1)} fusion(bf16[27,1024,128]{2,1,0:T(8,128)(2,1)} %copy-done.1, bf16[27,128,128]{2,1,0:T(8,128)(2,1)S(1)} %copy-done, f32[1024]{0:T(1024)S(1)} %fusion.13), kind=kOutput, calls=%fused_computation.23 | convolution fusion | flops 906231808 | bytes 8228864 | tf_op jit(solution)/shard_map/dvc,dce->ve/dot_general | solution.py:151
  59.8 1.3 fusion.10
  61.1 3.0 %select_maximum_fusion = bf16[1,18,18,34,128]{4,3,2,1,0:T(8,128)(2,1)S(1)} fusion(bf16[1,18,1,32,128]{4,3,2,1,0:T(8,128)(2,1)S(1)} %get-tuple-element.17, bf16[1,18,1,32,128]{4,3,2,1,0:T(8,128)(2,1)S(1)} %get-tuple-element.13, bf16[1,1,16,32,128]{4,3,2,1,0:T(8,128)(2,1)S(1)} %get-tuple-element.16, bf16[1,16,16,32,128]{4,3,2,1,0:T(8,128)(2,1)S(1)} %bitcast.133, ...), kind=kLoop, calls=%fused_computation.3 | loop fusion | flops 25380864 | bytes 5474304 | tf_op jit(solution)/shard_map/concatenate | solution.py:35
  64.7 0.4 fusion.25
  65.1 1.0 fusion.24
  66.2 1.7 %collective-permute-start.5 = (f32[896,128]{1,0:T(8,128)S(1)}, f32[896,128]{1,0:T(8,128)S(1)}, u32[]{:S(2)}, u32[]{:S(2)}) collective-permute-start(f32[896,128]{1,0:T(8,128)S(1)} %constant_dynamic-slice_fusion.6), channel_id=1, source_target_pairs={{0,1},{1,0},{2,3},{3,2},{4,5},{5,4},{6,7},{7,6},{8,9},{9,8},{10,11... | collective-permute-start | bytes 1376264 | tf_op jit(solution)/shard_map/ppermute | solution.py:85
  68.8 5.3 %collective-permute-done.5 = f32[896,128]{1,0:T(8,128)S(1)} collective-permute-done((f32[896,128]{1,0:T(8,128)S(1)}, f32[896,128]{1,0:T(8,128)S(1)}, u32[]{:S(2)}, u32[]{:S(2)}) %collective-permute-start.5) | collective-permute-done | bytes 458784 | tf_op jit(solution)/shard_map/ppermute | solution.py:85
  74.1 2.6 %collective-permute-start.6 = (f32[448,128]{1,0:T(8,128)S(1)}, f32[448,128]{1,0:T(8,128)S(1)}, u32[]{:S(2)}, u32[]{:S(2)}) collective-permute-start(f32[448,128]{1,0:T(8,128)S(1)} %constant_dynamic-slice_fusion.5), channel_id=1, source_target_pairs={{0,64},{1,65},{2,66},{3,67},{4,68},{5,69},{6,70},{7,71},{8,72},{9,... | collective-permute-start | bytes 688136 | tf_op jit(solution)/shard_map/ppermute | solution.py:85
  76.8 3.6 %collective-permute-done.6 = f32[448,128]{1,0:T(8,128)S(1)} collective-permute-done((f32[448,128]{1,0:T(8,128)S(1)}, f32[448,128]{1,0:T(8,128)S(1)}, u32[]{:S(2)}, u32[]{:S(2)}) %collective-permute-start.6) | collective-permute-done | bytes 229408 | tf_op jit(solution)/shard_map/ppermute | solution.py:85
  80.5 1.4 collective-permute-start.7
  81.9 2.3 %collective-permute-done.7 = f32[224,128]{1,0:T(8,128)S(1)} collective-permute-done((f32[224,128]{1,0:T(8,128)S(1)}, f32[224,128]{1,0:T(8,128)S(1)}, u32[]{:S(2)}, u32[]{:S(2)}) %collective-permute-start.7) | collective-permute-done | bytes 114720 | tf_op jit(solution)/shard_map/ppermute | solution.py:85
  84.2 3.2 %collective-permute-start.8 = (f32[112,128]{1,0:T(8,128)S(1)}, f32[112,128]{1,0:T(8,128)S(1)}, u32[]{:S(2)}, u32[]{:S(2)}) collective-permute-start(f32[112,128]{1,0:T(8,128)S(1)} %constant_dynamic-slice_fusion.3), channel_id=1, source_target_pairs={{0,32},{1,33},{2,34},{3,35},{4,36},{5,37},{6,38},{7,39},{8,40},{9,... | collective-permute-start | bytes 172040 | tf_op jit(solution)/shard_map/ppermute | solution.py:85
  87.4 1.5 collective-permute-done.8
  89.0 4.2 %collective-permute-start.9 = (f32[56,128]{1,0:T(8,128)S(1)}, f32[56,128]{1,0:T(8,128)S(1)}, u32[]{:S(2)}, u32[]{:S(2)}) collective-permute-start(f32[56,128]{1,0:T(8,128)S(1)} %constant_dynamic-slice_fusion.2), channel_id=1, source_target_pairs={{0,128},{1,129},{2,130},{3,131},{4,132},{5,133},{6,134},{7,135},{8... | collective-permute-start | bytes 86024 | tf_op jit(solution)/shard_map/ppermute | solution.py:85
  93.2 1.2 collective-permute-done.9
  94.4 1.9 %collective-permute-start.10 = (f32[28,128]{1,0:T(8,128)S(1)}, f32[28,128]{1,0:T(8,128)S(1)}, u32[]{:S(2)}, u32[]{:S(2)}) collective-permute-start(f32[28,128]{1,0:T(8,128)S(1)} %constant_dynamic-slice_fusion.1), channel_id=1, source_target_pairs={{0,4},{1,5},{2,6},{3,7},{4,0},{5,1},{6,2},{7,3},{8,12},{9,13},{10,... | collective-permute-start | bytes 43016 | tf_op jit(solution)/shard_map/ppermute | solution.py:85
  96.3 2.3 %collective-permute-done.10 = f32[28,128]{1,0:T(8,128)S(1)} collective-permute-done((f32[28,128]{1,0:T(8,128)S(1)}, f32[28,128]{1,0:T(8,128)S(1)}, u32[]{:S(2)}, u32[]{:S(2)}) %collective-permute-start.10) | collective-permute-done | bytes 14368 | tf_op jit(solution)/shard_map/ppermute | solution.py:85
  98.7 5.1 %collective-permute-start.11 = (f32[14,128]{1,0:T(8,128)S(1)}, f32[14,128]{1,0:T(8,128)S(1)}, u32[]{:S(2)}, u32[]{:S(2)}) collective-permute-start(f32[14,128]{1,0:T(8,128)S(1)} %constant_dynamic-slice_fusion), channel_id=1, source_target_pairs={{0,8},{1,9},{2,10},{3,11},{4,12},{5,13},{6,14},{7,15},{8,0},{9,1},... | collective-permute-start | bytes 21512 | tf_op jit(solution)/shard_map/ppermute | solution.py:85
  103.8 2.7 %fusion.9 = bf16[1024,128]{1,0:T(8,128)(2,1)} fusion(bf16[27,1024,128]{2,1,0:T(8,128)(2,1)S(1)} %constant_dynamic-update-slice_fusion.27, bf16[27,128,128]{2,1,0:T(8,128)(2,1)S(1)} %copy-done, f32[1024]{0:T(1024)S(1)} %fusion.13), kind=kOutput, calls=%fused_computation.24 | convolution fusion | flops 906231808 | bytes 8228864 | tf_op jit(solution)/shard_map/dvc,dec->ve/dot_general | solution.py:154
  106.5 3.8 %collective-permute-start.12 = (f32[14,128]{1,0:T(8,128)S(1)}, f32[14,128]{1,0:T(8,128)S(1)}, u32[]{:S(2)}, u32[]{:S(2)}) collective-permute-start(f32[14,128]{1,0:T(8,128)S(1)} %dynamic-slice_add_fusion.6), channel_id=1, source_target_pairs={{0,8},{1,9},{2,10},{3,11},{4,12},{5,13},{6,14},{7,15},{8,0},{9,1},... | collective-permute-start | bytes 21512 | tf_op jit(solution)/shard_map/ppermute | solution.py:95
  110.3 2.7 %collective-permute-done.12 = f32[14,128]{1,0:T(8,128)S(1)} collective-permute-done((f32[14,128]{1,0:T(8,128)S(1)}, f32[14,128]{1,0:T(8,128)S(1)}, u32[]{:S(2)}, u32[]{:S(2)}) %collective-permute-start.12) | collective-permute-done | bytes 7200 | tf_op jit(solution)/shard_map/ppermute | solution.py:95
  113.0 1.8 %collective-permute-start.13 = (f32[28,128]{1,0:T(8,128)S(1)}, f32[28,128]{1,0:T(8,128)S(1)}, u32[]{:S(2)}, u32[]{:S(2)}) collective-permute-start(f32[28,128]{1,0:T(8,128)S(1)} %pad_maximum_fusion.9), channel_id=1, source_target_pairs={{0,4},{1,5},{2,6},{3,7},{4,0},{5,1},{6,2},{7,3},{8,12},{9,13},{10,... | collective-permute-start | bytes 43016 | tf_op jit(solution)/shard_map/ppermute | solution.py:95
  114.7 2.4 %collective-permute-done.13 = f32[28,128]{1,0:T(8,128)S(1)} collective-permute-done((f32[28,128]{1,0:T(8,128)S(1)}, f32[28,128]{1,0:T(8,128)S(1)}, u32[]{:S(2)}, u32[]{:S(2)}) %collective-permute-start.13) | collective-permute-done | bytes 14368 | tf_op jit(solution)/shard_map/ppermute | solution.py:95
  117.2 1.6 %collective-permute-start.14 = (f32[56,128]{1,0:T(8,128)S(1)}, f32[56,128]{1,0:T(8,128)S(1)}, u32[]{:S(2)}, u32[]{:S(2)}) collective-permute-start(f32[56,128]{1,0:T(8,128)S(1)} %pad_maximum_fusion.8), channel_id=1, source_target_pairs={{0,128},{1,129},{2,130},{3,131},{4,132},{5,133},{6,134},{7,135},{8... | collective-permute-start | bytes 86024 | tf_op jit(solution)/shard_map/ppermute | solution.py:95
  118.8 2.3 %collective-permute-done.14 = f32[56,128]{1,0:T(8,128)S(1)} collective-permute-done((f32[56,128]{1,0:T(8,128)S(1)}, f32[56,128]{1,0:T(8,128)S(1)}, u32[]{:S(2)}, u32[]{:S(2)}) %collective-permute-start.14) | collective-permute-done | bytes 28704 | tf_op jit(solution)/shard_map/ppermute | solution.py:95
  121.1 3.1 %collective-permute-start.15 = (f32[112,128]{1,0:T(8,128)S(1)}, f32[112,128]{1,0:T(8,128)S(1)}, u32[]{:S(2)}, u32[]{:S(2)}) collective-permute-start(f32[112,128]{1,0:T(8,128)S(1)} %pad_maximum_fusion.7), channel_id=1, source_target_pairs={{0,32},{1,33},{2,34},{3,35},{4,36},{5,37},{6,38},{7,39},{8,40},{9,... | collective-permute-start | bytes 172040 | tf_op jit(solution)/shard_map/ppermute | solution.py:95
  124.3 1.6 collective-permute-done.15
  125.9 1.4 collective-permute-start.16
  127.2 2.6 %collective-permute-done.16 = f32[224,128]{1,0:T(8,128)S(1)} collective-permute-done((f32[224,128]{1,0:T(8,128)S(1)}, f32[224,128]{1,0:T(8,128)S(1)}, u32[]{:S(2)}, u32[]{:S(2)}) %collective-permute-start.16) | collective-permute-done | bytes 114720 | tf_op jit(solution)/shard_map/ppermute | solution.py:95
  129.9 0.8 collective-permute-start.17
  130.7 4.2 %collective-permute-done.17 = f32[448,128]{1,0:T(8,128)S(1)} collective-permute-done((f32[448,128]{1,0:T(8,128)S(1)}, f32[448,128]{1,0:T(8,128)S(1)}, u32[]{:S(2)}, u32[]{:S(2)}) %collective-permute-start.17) | collective-permute-done | bytes 229408 | tf_op jit(solution)/shard_map/ppermute | solution.py:95
  135.0 1.1 collective-permute-start.18
  136.1 6.3 %collective-permute-done.18 = f32[896,128]{1,0:T(8,128)S(1)} collective-permute-done((f32[896,128]{1,0:T(8,128)S(1)}, f32[896,128]{1,0:T(8,128)S(1)}, u32[]{:S(2)}, u32[]{:S(2)}) %collective-permute-start.18) | collective-permute-done | bytes 458784 | tf_op jit(solution)/shard_map/ppermute | solution.py:95
  142.5 14.1 %collective-permute-start.19 = (f32[1792,128]{1,0:T(8,128)S(1)}, f32[1792,128]{1,0:T(8,128)}, u32[]{:S(2)}, u32[]{:S(2)}) collective-permute-start(f32[1792,128]{1,0:T(8,128)S(1)} %pad_maximum_fusion.1), channel_id=1, source_target_pairs={{0,16},{16,0},{32,48},{48,32},{64,80},{80,64},{96,112},{112,96},{1... | collective-permute-start | bytes 2752520 | tf_op jit(solution)/shard_map/ppermute | solution.py:97
  156.6 2.2 %collective-permute-done.19 = f32[1792,128]{1,0:T(8,128)} collective-permute-done((f32[1792,128]{1,0:T(8,128)S(1)}, f32[1792,128]{1,0:T(8,128)}, u32[]{:S(2)}, u32[]{:S(2)}) %collective-permute-start.19) | collective-permute-done | bytes 917536 | tf_op jit(solution)/shard_map/ppermute | solution.py:97
  158.8 1.3 broadcast_select_fusion.1
  160.3 1.9 %copy.14 = f32[27,128,128]{2,1,0:T(8,128)} copy(f32[27,128,128]{1,2,0:T(8,128)S(1)} %bitcast.135) | data formatting | bytes 3538944
  (110 shorter events, 3.8 us)
Async XLA Ops:
  0.6 53.4 %copy-start = (bf16[27,128,128]{2,1,0:T(8,128)(2,1)S(1)}, bf16[27,128,128]{2,1,0:T(8,128)(2,1)}, u32[]{:S(2)}) copy-start(bf16[27,128,128]{2,1,0:T(8,128)(2,1)} %param.10) | copy-start | bytes 2654212
  3.4 16.3 %copy-start.3 = (bf16[2,2,512,128]{3,2,1,0:T(8,128)(2,1)}, bf16[2,2,512,128]{3,2,1,0:T(8,128)(2,1)S(1)}, u32[]{:S(2)}) copy-start(bf16[2,2,512,128]{3,2,1,0:T(8,128)(2,1)S(1)} %maximum_multiply_fusion) | copy-start | bytes 1572868
  7.1 11.9 %copy-start.5 = (s32[1,1,2]{2,1,0:T(1,128)S(1)}, s32[1,1,2]{2,1,0:T(1,128)}, u32[]{:S(2)}) copy-start(s32[1,1,2]{2,1,0:T(1,128)} %param.8) | copy-start | bytes 28
  7.9 16.9 %collective-permute-start.1 = (bf16[2,1,16,32,128]{4,3,2,1,0:T(8,128)(2,1)}, bf16[2,1,16,32,128]{4,3,2,1,0:T(8,128)(2,1)}, u32[]{:S(2)}, u32[]{:S(2)}) collective-permute-start(bf16[2,1,16,32,128]{4,3,2,1,0:T(8,128)(2,1)} %get-tuple-element.31), channel_id=1, source_target_pairs={{16,0},{32,16},{48,32},{64,48},{80,64},{96,80},{112,96},{128,112},... | collective-permute-start | bytes 786440 | tf_op jit(solution)/shard_map/ppermute | solution.py:21
  13.0 12.5 %collective-permute-start = (bf16[2,1,16,32,128]{4,3,2,1,0:T(8,128)(2,1)}, bf16[2,1,16,32,128]{4,3,2,1,0:T(8,128)(2,1)}, u32[]{:S(2)}, u32[]{:S(2)}) collective-permute-start(bf16[2,1,16,32,128]{4,3,2,1,0:T(8,128)(2,1)} %get-tuple-element.30), channel_id=1, source_target_pairs={{0,16},{16,32},{32,48},{48,64},{64,80},{80,96},{96,112},{112,128},... | collective-permute-start | bytes 786440 | tf_op jit(solution)/shard_map/ppermute | solution.py:20
  27.3 10.2 %collective-permute-start.3 = (bf16[2,18,1,32,128]{4,3,2,1,0:T(8,128)(2,1)S(1)}, bf16[2,18,1,32,128]{4,3,2,1,0:T(8,128)(2,1)S(1)}, u32[]{:S(2)}, u32[]{:S(2)}) collective-permute-start(bf16[2,18,1,32,128]{4,3,2,1,0:T(8,128)(2,1)S(1)} %pad_maximum_fusion.4), channel_id=1, source_target_pairs={{1,0},{2,1},{3,2},{4,3},{5,4},{6,5},{7,6},{8,7},{9,8},{10,9},{11,1... | collective-permute-start | bytes 884744 | tf_op jit(solution)/shard_map/ppermute | solution.py:27
  29.6 13.8 %collective-permute-start.2 = (bf16[2,18,1,32,128]{4,3,2,1,0:T(8,128)(2,1)S(1)}, bf16[2,18,1,32,128]{4,3,2,1,0:T(8,128)(2,1)S(1)}, u32[]{:S(2)}, u32[]{:S(2)}) collective-permute-start(bf16[2,18,1,32,128]{4,3,2,1,0:T(8,128)(2,1)S(1)} %pad_maximum_fusion.3), channel_id=1, source_target_pairs={{0,1},{1,2},{2,3},{3,4},{4,5},{5,6},{6,7},{7,8},{8,9},{9,10},{10,1... | collective-permute-start | bytes 884744 | tf_op jit(solution)/shard_map/ppermute | solution.py:26
  48.4 1.2 slice-start
  49.6 2.8 %copy-start.1 = (bf16[27,1024,128]{2,1,0:T(8,128)(2,1)}, bf16[27,1024,128]{2,1,0:T(8,128)(2,1)S(1)}, u32[]{:S(2)}) copy-start(bf16[27,1024,128]{2,1,0:T(8,128)(2,1)S(1)} %constant_dynamic-update-slice_fusion) | copy-start | bytes 21233668
  49.6 4.3 %copy-start.4 = (s32[1,1,2,512]{3,2,1,0:T(2,128)S(1)}, s32[1,1,2,512]{3,2,1,0:T(2,128)}, u32[]{:S(2)}) copy-start(s32[1,1,2,512]{3,2,1,0:T(2,128)} %param.7) | copy-start | bytes 12292
  53.4 6.4 %collective-permute-start.4 = (f32[1792,128]{1,0:T(8,128)}, f32[1792,128]{1,0:T(8,128)}, u32[]{:S(2)}, u32[]{:S(2)}) collective-permute-start(f32[1792,128]{1,0:T(8,128)} %pad_dynamic-slice_fusion), channel_id=1, source_target_pairs={{0,16},{16,0},{32,48},{48,32},{64,80},{80,64},{96,112},{112,96},{1... | collective-permute-start | bytes 2752520 | tf_op jit(solution)/shard_map/ppermute | solution.py:78
  54.0 7.2 %copy-start.2 = (bf16[1,2,8,2,8,4,8,128]{7,6,5,4,3,2,1,0:T(8,128)(2,1)S(1)}, bf16[1,2,8,2,8,4,8,128]{7,6,5,4,3,2,1,0:T(8,128)(2,1)}, u32[]{:S(2)}) copy-start(bf16[1,2,8,2,8,4,8,128]{7,6,5,4,3,2,1,0:T(8,128)(2,1)} %get-tuple-element.24) | copy-start | bytes 6291460
  66.2 7.8 %collective-permute-start.5 = (f32[896,128]{1,0:T(8,128)S(1)}, f32[896,128]{1,0:T(8,128)S(1)}, u32[]{:S(2)}, u32[]{:S(2)}) collective-permute-start(f32[896,128]{1,0:T(8,128)S(1)} %constant_dynamic-slice_fusion.6), channel_id=1, source_target_pairs={{0,1},{1,0},{2,3},{3,2},{4,5},{5,4},{6,7},{7,6},{8,9},{9,8},{10,11... | collective-permute-start | bytes 1376264 | tf_op jit(solution)/shard_map/ppermute | solution.py:85
  74.1 6.3 %collective-permute-start.6 = (f32[448,128]{1,0:T(8,128)S(1)}, f32[448,128]{1,0:T(8,128)S(1)}, u32[]{:S(2)}, u32[]{:S(2)}) collective-permute-start(f32[448,128]{1,0:T(8,128)S(1)} %constant_dynamic-slice_fusion.5), channel_id=1, source_target_pairs={{0,64},{1,65},{2,66},{3,67},{4,68},{5,69},{6,70},{7,71},{8,72},{9,... | collective-permute-start | bytes 688136 | tf_op jit(solution)/shard_map/ppermute | solution.py:85
  80.5 3.7 %collective-permute-start.7 = (f32[224,128]{1,0:T(8,128)S(1)}, f32[224,128]{1,0:T(8,128)S(1)}, u32[]{:S(2)}, u32[]{:S(2)}) collective-permute-start(f32[224,128]{1,0:T(8,128)S(1)} %constant_dynamic-slice_fusion.4), channel_id=1, source_target_pairs={{0,2},{1,3},{2,0},{3,1},{4,6},{5,7},{6,4},{7,5},{8,10},{9,11},{10,... | collective-permute-start | bytes 344072 | tf_op jit(solution)/shard_map/ppermute | solution.py:85
  84.2 4.7 %collective-permute-start.8 = (f32[112,128]{1,0:T(8,128)S(1)}, f32[112,128]{1,0:T(8,128)S(1)}, u32[]{:S(2)}, u32[]{:S(2)}) collective-permute-start(f32[112,128]{1,0:T(8,128)S(1)} %constant_dynamic-slice_fusion.3), channel_id=1, source_target_pairs={{0,32},{1,33},{2,34},{3,35},{4,36},{5,37},{6,38},{7,39},{8,40},{9,... | collective-permute-start | bytes 172040 | tf_op jit(solution)/shard_map/ppermute | solution.py:85
  89.0 5.4 %collective-permute-start.9 = (f32[56,128]{1,0:T(8,128)S(1)}, f32[56,128]{1,0:T(8,128)S(1)}, u32[]{:S(2)}, u32[]{:S(2)}) collective-permute-start(f32[56,128]{1,0:T(8,128)S(1)} %constant_dynamic-slice_fusion.2), channel_id=1, source_target_pairs={{0,128},{1,129},{2,130},{3,131},{4,132},{5,133},{6,134},{7,135},{8... | collective-permute-start | bytes 86024 | tf_op jit(solution)/shard_map/ppermute | solution.py:85
  94.4 4.2 %collective-permute-start.10 = (f32[28,128]{1,0:T(8,128)S(1)}, f32[28,128]{1,0:T(8,128)S(1)}, u32[]{:S(2)}, u32[]{:S(2)}) collective-permute-start(f32[28,128]{1,0:T(8,128)S(1)} %constant_dynamic-slice_fusion.1), channel_id=1, source_target_pairs={{0,4},{1,5},{2,6},{3,7},{4,0},{5,1},{6,2},{7,3},{8,12},{9,13},{10,... | collective-permute-start | bytes 43016 | tf_op jit(solution)/shard_map/ppermute | solution.py:85
  98.7 7.8 %collective-permute-start.11 = (f32[14,128]{1,0:T(8,128)S(1)}, f32[14,128]{1,0:T(8,128)S(1)}, u32[]{:S(2)}, u32[]{:S(2)}) collective-permute-start(f32[14,128]{1,0:T(8,128)S(1)} %constant_dynamic-slice_fusion), channel_id=1, source_target_pairs={{0,8},{1,9},{2,10},{3,11},{4,12},{5,13},{6,14},{7,15},{8,0},{9,1},... | collective-permute-start | bytes 21512 | tf_op jit(solution)/shard_map/ppermute | solution.py:85
  106.5 6.5 %collective-permute-start.12 = (f32[14,128]{1,0:T(8,128)S(1)}, f32[14,128]{1,0:T(8,128)S(1)}, u32[]{:S(2)}, u32[]{:S(2)}) collective-permute-start(f32[14,128]{1,0:T(8,128)S(1)} %dynamic-slice_add_fusion.6), channel_id=1, source_target_pairs={{0,8},{1,9},{2,10},{3,11},{4,12},{5,13},{6,14},{7,15},{8,0},{9,1},... | collective-permute-start | bytes 21512 | tf_op jit(solution)/shard_map/ppermute | solution.py:95
  113.0 4.2 %collective-permute-start.13 = (f32[28,128]{1,0:T(8,128)S(1)}, f32[28,128]{1,0:T(8,128)S(1)}, u32[]{:S(2)}, u32[]{:S(2)}) collective-permute-start(f32[28,128]{1,0:T(8,128)S(1)} %pad_maximum_fusion.9), channel_id=1, source_target_pairs={{0,4},{1,5},{2,6},{3,7},{4,0},{5,1},{6,2},{7,3},{8,12},{9,13},{10,... | collective-permute-start | bytes 43016 | tf_op jit(solution)/shard_map/ppermute | solution.py:95
  117.2 3.9 %collective-permute-start.14 = (f32[56,128]{1,0:T(8,128)S(1)}, f32[56,128]{1,0:T(8,128)S(1)}, u32[]{:S(2)}, u32[]{:S(2)}) collective-permute-start(f32[56,128]{1,0:T(8,128)S(1)} %pad_maximum_fusion.8), channel_id=1, source_target_pairs={{0,128},{1,129},{2,130},{3,131},{4,132},{5,133},{6,134},{7,135},{8... | collective-permute-start | bytes 86024 | tf_op jit(solution)/shard_map/ppermute | solution.py:95
  121.1 4.7 %collective-permute-start.15 = (f32[112,128]{1,0:T(8,128)S(1)}, f32[112,128]{1,0:T(8,128)S(1)}, u32[]{:S(2)}, u32[]{:S(2)}) collective-permute-start(f32[112,128]{1,0:T(8,128)S(1)} %pad_maximum_fusion.7), channel_id=1, source_target_pairs={{0,32},{1,33},{2,34},{3,35},{4,36},{5,37},{6,38},{7,39},{8,40},{9,... | collective-permute-start | bytes 172040 | tf_op jit(solution)/shard_map/ppermute | solution.py:95
  125.9 4.0 %collective-permute-start.16 = (f32[224,128]{1,0:T(8,128)S(1)}, f32[224,128]{1,0:T(8,128)S(1)}, u32[]{:S(2)}, u32[]{:S(2)}) collective-permute-start(f32[224,128]{1,0:T(8,128)S(1)} %pad_maximum_fusion.6), channel_id=1, source_target_pairs={{0,2},{1,3},{2,0},{3,1},{4,6},{5,7},{6,4},{7,5},{8,10},{9,11},{10,... | collective-permute-start | bytes 344072 | tf_op jit(solution)/shard_map/ppermute | solution.py:95
  129.9 5.0 %collective-permute-start.17 = (f32[448,128]{1,0:T(8,128)S(1)}, f32[448,128]{1,0:T(8,128)S(1)}, u32[]{:S(2)}, u32[]{:S(2)}) collective-permute-start(f32[448,128]{1,0:T(8,128)S(1)} %pad_maximum_fusion.5), channel_id=1, source_target_pairs={{0,64},{1,65},{2,66},{3,67},{4,68},{5,69},{6,70},{7,71},{8,72},{9,... | collective-permute-start | bytes 688136 | tf_op jit(solution)/shard_map/ppermute | solution.py:95
  135.0 7.4 %collective-permute-start.18 = (f32[896,128]{1,0:T(8,128)S(1)}, f32[896,128]{1,0:T(8,128)S(1)}, u32[]{:S(2)}, u32[]{:S(2)}) collective-permute-start(f32[896,128]{1,0:T(8,128)S(1)} %pad_maximum_fusion.2), channel_id=1, source_target_pairs={{0,1},{1,0},{2,3},{3,2},{4,5},{5,4},{6,7},{7,6},{8,9},{9,8},{10,11... | collective-permute-start | bytes 1376264 | tf_op jit(solution)/shard_map/ppermute | solution.py:95
  142.5 16.3 %collective-permute-start.19 = (f32[1792,128]{1,0:T(8,128)S(1)}, f32[1792,128]{1,0:T(8,128)}, u32[]{:S(2)}, u32[]{:S(2)}) collective-permute-start(f32[1792,128]{1,0:T(8,128)S(1)} %pad_maximum_fusion.1), channel_id=1, source_target_pairs={{0,16},{16,0},{32,48},{48,32},{64,80},{80,64},{96,112},{112,96},{1... | collective-permute-start | bytes 2752520 | tf_op jit(solution)/shard_map/ppermute | solution.py:97

commit v10 on v8

--- a/solution.py
+++ b/solution.py
@@ -27,7 +27,7 @@
     from_above = lax.ppermute(row(slice(0, 1)), "gy", down_y)
     wide = jnp.concatenate([from_left, value, from_right], 1)
     full = jnp.concatenate([from_below, wide, from_above], 2)
-    return jnp.pad(full, ((0, 0), (0, 0), (0, 0), (1, 1), (0, 0)))
+    return full
 
 
 FIRST = ("gx", 0)
@@ -105,14 +105,18 @@
 
 
 def cut_windows(padded, places):
-    kinds, chans = padded.shape[0], padded.shape[-1]
+    kinds, chans, depth = padded.shape[0], padded.shape[-1], padded.shape[3]
     windows = []
     for slot in range(places.shape[0]):
         place = places[slot]
-        starts = (0, place // (TBY * ZL) * BRICK, place // ZL % TBY * BRICK, place % ZL * BRICK, 0)
-        windows.append(
-            lax.dynamic_slice(padded, starts, (kinds, BRICK + 2, BRICK + 2, BRICK + 2, chans))
-        )
+        x0, y0, z0 = place // (TBY * ZL) * BRICK, place // ZL % TBY * BRICK, place % ZL * BRICK
+        side = (kinds, BRICK + 2, BRICK + 2, 1, chans)
+        main = lax.dynamic_slice(padded, (0, x0, y0, z0, 0), (kinds, BRICK + 2, BRICK + 2, BRICK, chans))
+        below = lax.dynamic_slice(padded, (0, x0, y0, jnp.maximum(z0 - 1, 0), 0), side)
+        above = lax.dynamic_slice(padded, (0, x0, y0, jnp.minimum(z0 + BRICK, depth - 1), 0), side)
+        below = jnp.where(z0 > 0, below, jnp.zeros_like(below))
+        above = jnp.where(z0 + BRICK < depth, above, jnp.zeros_like(above))
+        windows.append(jnp.concatenate([below, main, above], 3))
     return jnp.stack(windows, 1)
 
 

time: 150 us -> 147 us (0.980)
  other arithmetic: 11.9 us -> 9.59 us
    concatenate x1, other arithmetic: 7.54 us -> 3.76 us  [with_halo(): full = jnp.concatenate([from_below, wide, from_above], 2)]
where the time goes in v10:
time: 147 us
  starting transfers between devices  64.9 us (44%)
  waiting for transfers between devices  46.6 us (32%)
  other arithmetic  9.59 us (7%)
  local copies, waits for them, and re-layouts  9.53 us (6%)
  matrix products  8.6 us (6%)
  between operations  7.65 us (5%)
    ppermute x7, starting transfers between devices, butterfly_scatter(): buf = keep + lax.ppermute(send, ('gx', 'gy'), step_pairs(k))  26.1 us
    ppermute x7, waiting for transfers between devices, butterfly_gather(): got = lax.ppermute(buf, ('gx', 'gy'), step_pairs(k))  24.7 us
    ppermute x1, starting transfers between devices, butterfly_gather(): lax.ppermute(buf, 'gx', [(i, i ^ 1) for i in range(lax.axis_size('gx'))])  14.2 us
    ppermute x7, waiting for transfers between devices, butterfly_scatter(): buf = keep + lax.ppermute(send, ('gx', 'gy'), step_pairs(k))  12.9 us
    ppermute x7, starting transfers between devices, butterfly_gather(): got = lax.ppermute(buf, ('gx', 'gy'), step_pairs(k))  11 us
    ppermute x1, starting transfers between devices, with_halo(): from_right = lax.ppermute(value[:, 0:1], 'gx', down_x)  5.11 us
    ppermute x1, starting transfers between devices, with_halo(): from_below = lax.ppermute(row(slice(ny - 1, ny)), 'gy', up_y)  4 us
    unnamed x65, local copies, waits for them, and re-layouts  3.84 us
  transfers between devices with their start and end apart: 20, of which 18 were waited for; matrix products, arithmetic and copies ran while one was open for 5% of the time, Pallas kernels for 0%

profile of v10, /device:TPU:1, one launch (start us, length us, event | category | flops | bytes accessed | tf_op | source)
XLA Modules:
  0.0 146.9 jit_solution(9299951238529781720)
XLA Ops:
  0.6 0.0 copy-start
  1.4 0.8 broadcast_bitcast_fusion
  2.1 1.2 maximum_multiply_fusion
  3.4 2.0 %convolution_convert_fusion = bf16[2,512,128,16]{2,3,1,0:T(8,128)(2,1)S(1)} fusion(bf16[2,2,512,128]{3,2,1,0:T(8,128)(2,1)S(1)} %maximum_multiply_fusion, pred[2]{0:T(512)(128)(4,1)S(1)} %get-tuple-element.102, s32[2]{0:T(128)} %bitcast.186), kind=kOutput, calls=%fused_computation.1 | convolution fusion | flops 10485824 | bytes 4718602 | tf_op jit(solution)/shard_map/ps,tsvc->tpvc/dot_general | solution.py:98
  5.5 1.6 %copy.13 = bf16[2,2,2,4,8,8,8,128]{7,6,3,5,2,4,1,0:T(8,128)(2,1)S(1)} copy(bf16[2,2,2,4,8,8,8,128]{7,3,2,1,6,5,4,0:T(4,128)(2,1)S(1)} %bitcast.124) | data formatting | bytes 8388608 | tf_op jit(solution)/shard_map/reshape | solution.py:102
  7.1 5.1 %collective-permute-start.1 = (bf16[2,1,16,32,128]{4,3,2,1,0:T(8,128)(2,1)S(1)}, bf16[2,1,16,32,128]{4,3,2,1,0:T(8,128)(2,1)S(1)}, u32[]{:S(2)}, u32[]{:S(2)}) collective-permute-start(bf16[2,1,16,32,128]{4,3,2,1,0:T(8,128)(2,1)S(1)} %get-tuple-element.21), channel_id=1, source_target_pairs={{16,0},{32,16},{48,32},{64,48},{80,64},{96,80},{112,96},{128,112},... | collective-permute-start | bytes 786440 | tf_op jit(solution)/shard_map/ppermute | solution.py:21
  12.3 2.8 %collective-permute-start = (bf16[2,1,16,32,128]{4,3,2,1,0:T(8,128)(2,1)S(1)}, bf16[2,1,16,32,128]{4,3,2,1,0:T(8,128)(2,1)S(1)}, u32[]{:S(2)}, u32[]{:S(2)}) collective-permute-start(bf16[2,1,16,32,128]{4,3,2,1,0:T(8,128)(2,1)S(1)} %get-tuple-element.20), channel_id=1, source_target_pairs={{0,16},{16,32},{32,48},{48,64},{64,80},{80,96},{96,112},{112,128},... | collective-permute-start | bytes 786440 | tf_op jit(solution)/shard_map/ppermute | solution.py:20
  15.2 2.0 %collective-permute-done.1 = bf16[2,1,16,32,128]{4,3,2,1,0:T(8,128)(2,1)S(1)} collective-permute-done((bf16[2,1,16,32,128]{4,3,2,1,0:T(8,128)(2,1)S(1)}, bf16[2,1,16,32,128]{4,3,2,1,0:T(8,128)(2,1)S(1)}, u32[]{:S(2)}, u32[]{:S(2)}) %collective-permute-start.1) | collective-permute-done | bytes 262176 | tf_op jit(solution)/shard_map/ppermute | solution.py:21
  17.2 1.2 collective-permute-done
  18.5 1.3 collective-permute-start.3
  19.8 4.0 %collective-permute-start.2 = (bf16[2,18,1,32,128]{4,3,2,1,0:T(8,128)(2,1)S(1)}, bf16[2,18,1,32,128]{4,3,2,1,0:T(8,128)(2,1)S(1)}, u32[]{:S(2)}, u32[]{:S(2)}) collective-permute-start(bf16[2,18,1,32,128]{4,3,2,1,0:T(8,128)(2,1)S(1)} %pad_maximum_fusion.5), channel_id=1, source_target_pairs={{0,1},{1,2},{2,3},{3,4},{4,5},{5,6},{6,7},{7,8},{8,9},{9,10},{10,1... | collective-permute-start | bytes 884744 | tf_op jit(solution)/shard_map/ppermute | solution.py:26
  23.8 0.6 fusion.26
  29.9 2.0 %collective-permute-done.2 = bf16[2,18,1,32,128]{4,3,2,1,0:T(8,128)(2,1)S(1)} collective-permute-done((bf16[2,18,1,32,128]{4,3,2,1,0:T(8,128)(2,1)S(1)}, bf16[2,18,1,32,128]{4,3,2,1,0:T(8,128)(2,1)S(1)}, u32[]{:S(2)}, u32[]{:S(2)}) %collective-permute-start.2) | collective-permute-done | bytes 294944 | tf_op jit(solution)/shard_map/ppermute | solution.py:26
  31.9 3.8 %pad_maximum_fusion = bf16[2,18,18,32,128]{4,3,2,1,0:T(8,128)(2,1)S(1)} fusion(bf16[2,18,1,32,128]{4,3,2,1,0:T(8,128)(2,1)S(1)} %collective-permute-done.3, bf16[2,1,16,32,128]{4,3,2,1,0:T(8,128)(2,1)S(1)} %collective-permute-done.1, bf16[2,16,16,32,128]{4,3,2,1,0:T(8,128)(2,1)} %bitcast.123, bf16[2,1,16,32,128]{4,3,2,1,0:T(8,128)(2,1)S(1)} %collective-permute-done, ...), kind=kLoop, calls=%fused_computation | loop fusion | flops 10616832 | bytes 10616832 | tf_op jit(solution)/shard_map/concatenate | solution.py:29
  35.7 0.2 constant_dynamic-slice_fusion.7
  35.9 0.6 broadcast_select_fusion.5
  36.4 0.5 maximum_bitcast_fusion.1
  36.9 0.5 maximum_bitcast_fusion
  37.4 0.3 fusion.7
  37.7 0.4 fusion.23
  38.2 1.0 fusion.22
  39.2 0.5 fusion.21
  39.7 1.0 fusion.20
  41.9 1.1 convolution_multiply_fusion
  43.1 0.1 pad_dynamic-slice_fusion
  43.1 0.3 collective-permute-start.4
  44.3 1.5 %collective-permute-done.4 = f32[1792,128]{1,0:T(8,128)S(1)} collective-permute-done((f32[1792,128]{1,0:T(8,128)S(1)}, f32[1792,128]{1,0:T(8,128)S(1)}, u32[]{:S(2)}, u32[]{:S(2)}) %collective-permute-start.4) | collective-permute-done | bytes 917536 | tf_op jit(solution)/shard_map/ppermute | solution.py:72
  45.9 0.1 fusion.4
  46.0 5.1 %collective-permute-start.5 = (f32[896,128]{1,0:T(8,128)S(1)}, f32[896,128]{1,0:T(8,128)S(1)}, u32[]{:S(2)}, u32[]{:S(2)}) collective-permute-start(f32[896,128]{1,0:T(8,128)S(1)} %constant_dynamic-slice_fusion.6), channel_id=1, source_target_pairs={{0,1},{1,0},{2,3},{3,2},{4,5},{5,4},{6,7},{7,6},{8,9},{9,8},{10,11... | collective-permute-start | bytes 1376264 | tf_op jit(solution)/shard_map/ppermute | solution.py:78
  51.2 2.7 %fusion.2 = bf16[1024,128]{1,0:T(8,128)(2,1)} fusion(bf16[27,1024,128]{2,1,0:T(8,128)(2,1)S(1)} %constant_dynamic-update-slice_fusion, bf16[27,128,128]{2,1,0:T(8,128)(2,1)S(1)} %copy-done, f32[1024]{0:T(1024)S(1)} %fusion.10), kind=kOutput, calls=%fused_computation.12 | convolution fusion | flops 906231808 | bytes 8228864 | tf_op jit(solution)/shard_map/dvc,dce->ve/dot_general | solution.py:149
  53.9 3.2 %collective-permute-done.5 = f32[896,128]{1,0:T(8,128)S(1)} collective-permute-done((f32[896,128]{1,0:T(8,128)S(1)}, f32[896,128]{1,0:T(8,128)S(1)}, u32[]{:S(2)}, u32[]{:S(2)}) %collective-permute-start.5) | collective-permute-done | bytes 458784 | tf_op jit(solution)/shard_map/ppermute | solution.py:78
  57.1 2.6 %collective-permute-start.6 = (f32[448,128]{1,0:T(8,128)S(1)}, f32[448,128]{1,0:T(8,128)S(1)}, u32[]{:S(2)}, u32[]{:S(2)}) collective-permute-start(f32[448,128]{1,0:T(8,128)S(1)} %constant_dynamic-slice_fusion.5), channel_id=1, source_target_pairs={{0,64},{1,65},{2,66},{3,67},{4,68},{5,69},{6,70},{7,71},{8,72},{9,... | collective-permute-start | bytes 688136 | tf_op jit(solution)/shard_map/ppermute | solution.py:78
  59.8 3.6 %collective-permute-done.6 = f32[448,128]{1,0:T(8,128)S(1)} collective-permute-done((f32[448,128]{1,0:T(8,128)S(1)}, f32[448,128]{1,0:T(8,128)S(1)}, u32[]{:S(2)}, u32[]{:S(2)}) %collective-permute-start.6) | collective-permute-done | bytes 229408 | tf_op jit(solution)/shard_map/ppermute | solution.py:78
  63.4 1.4 collective-permute-start.7
  64.9 2.2 %collective-permute-done.7 = f32[224,128]{1,0:T(8,128)S(1)} collective-permute-done((f32[224,128]{1,0:T(8,128)S(1)}, f32[224,128]{1,0:T(8,128)S(1)}, u32[]{:S(2)}, u32[]{:S(2)}) %collective-permute-start.7) | collective-permute-done | bytes 114720 | tf_op jit(solution)/shard_map/ppermute | solution.py:78
  67.2 3.5 %collective-permute-start.8 = (f32[112,128]{1,0:T(8,128)S(1)}, f32[112,128]{1,0:T(8,128)S(1)}, u32[]{:S(2)}, u32[]{:S(2)}) collective-permute-start(f32[112,128]{1,0:T(8,128)S(1)} %constant_dynamic-slice_fusion.3), channel_id=1, source_target_pairs={{0,32},{1,33},{2,34},{3,35},{4,36},{5,37},{6,38},{7,39},{8,40},{9,... | collective-permute-start | bytes 172040 | tf_op jit(solution)/shard_map/ppermute | solution.py:78
  70.7 1.5 %collective-permute-done.8 = f32[112,128]{1,0:T(8,128)S(1)} collective-permute-done((f32[112,128]{1,0:T(8,128)S(1)}, f32[112,128]{1,0:T(8,128)S(1)}, u32[]{:S(2)}, u32[]{:S(2)}) %collective-permute-start.8) | collective-permute-done | bytes 57376 | tf_op jit(solution)/shard_map/ppermute | solution.py:78
  72.3 4.2 %collective-permute-start.9 = (f32[56,128]{1,0:T(8,128)S(1)}, f32[56,128]{1,0:T(8,128)S(1)}, u32[]{:S(2)}, u32[]{:S(2)}) collective-permute-start(f32[56,128]{1,0:T(8,128)S(1)} %constant_dynamic-slice_fusion.2), channel_id=1, source_target_pairs={{0,128},{1,129},{2,130},{3,131},{4,132},{5,133},{6,134},{7,135},{8... | collective-permute-start | bytes 86024 | tf_op jit(solution)/shard_map/ppermute | solution.py:78
  76.5 1.2 collective-permute-done.9
  77.7 3.4 %collective-permute-start.10 = (f32[28,128]{1,0:T(8,128)S(1)}, f32[28,128]{1,0:T(8,128)S(1)}, u32[]{:S(2)}, u32[]{:S(2)}) collective-permute-start(f32[28,128]{1,0:T(8,128)S(1)} %constant_dynamic-slice_fusion.1), channel_id=1, source_target_pairs={{0,4},{1,5},{2,6},{3,7},{4,0},{5,1},{6,2},{7,3},{8,12},{9,13},{10,... | collective-permute-start | bytes 43016 | tf_op jit(solution)/shard_map/ppermute | solution.py:78
  81.2 1.1 collective-permute-done.10
  82.3 6.0 %collective-permute-start.11 = (f32[14,128]{1,0:T(8,128)S(1)}, f32[14,128]{1,0:T(8,128)S(1)}, u32[]{:S(2)}, u32[]{:S(2)}) collective-permute-start(f32[14,128]{1,0:T(8,128)S(1)} %constant_dynamic-slice_fusion), channel_id=1, source_target_pairs={{0,8},{1,9},{2,10},{3,11},{4,12},{5,13},{6,14},{7,15},{8,0},{9,1},... | collective-permute-start | bytes 21512 | tf_op jit(solution)/shard_map/ppermute | solution.py:78
  88.3 2.7 %fusion.3 = bf16[1024,128]{1,0:T(8,128)(2,1)} fusion(bf16[27,1024,128]{2,1,0:T(8,128)(2,1)S(1)} %constant_dynamic-update-slice_fusion.27, bf16[27,128,128]{2,1,0:T(8,128)(2,1)S(1)} %copy-done, f32[1024]{0:T(1024)S(1)} %fusion.10), kind=kOutput, calls=%fused_computation.13 | convolution fusion | flops 906231808 | bytes 8228864 | tf_op jit(solution)/shard_map/dvc,dec->ve/dot_general | solution.py:152
  91.0 3.8 %collective-permute-start.12 = (f32[14,128]{1,0:T(8,128)S(1)}, f32[14,128]{1,0:T(8,128)S(1)}, u32[]{:S(2)}, u32[]{:S(2)}) collective-permute-start(f32[14,128]{1,0:T(8,128)S(1)} %dynamic-slice_add_fusion.6), channel_id=1, source_target_pairs={{0,8},{1,9},{2,10},{3,11},{4,12},{5,13},{6,14},{7,15},{8,0},{9,1},... | collective-permute-start | bytes 21512 | tf_op jit(solution)/shard_map/ppermute | solution.py:88
  94.8 2.7 %collective-permute-done.12 = f32[14,128]{1,0:T(8,128)S(1)} collective-permute-done((f32[14,128]{1,0:T(8,128)S(1)}, f32[14,128]{1,0:T(8,128)S(1)}, u32[]{:S(2)}, u32[]{:S(2)}) %collective-permute-start.12) | collective-permute-done | bytes 7200 | tf_op jit(solution)/shard_map/ppermute | solution.py:88
  97.5 2.0 %collective-permute-start.13 = (f32[28,128]{1,0:T(8,128)S(1)}, f32[28,128]{1,0:T(8,128)S(1)}, u32[]{:S(2)}, u32[]{:S(2)}) collective-permute-start(f32[28,128]{1,0:T(8,128)S(1)} %pad_maximum_fusion.11), channel_id=1, source_target_pairs={{0,4},{1,5},{2,6},{3,7},{4,0},{5,1},{6,2},{7,3},{8,12},{9,13},{10,... | collective-permute-start | bytes 43016 | tf_op jit(solution)/shard_map/ppermute | solution.py:88
  99.5 2.1 %collective-permute-done.13 = f32[28,128]{1,0:T(8,128)S(1)} collective-permute-done((f32[28,128]{1,0:T(8,128)S(1)}, f32[28,128]{1,0:T(8,128)S(1)}, u32[]{:S(2)}, u32[]{:S(2)}) %collective-permute-start.13) | collective-permute-done | bytes 14368 | tf_op jit(solution)/shard_map/ppermute | solution.py:88
  101.7 0.6 collective-permute-start.14
  102.3 3.2 %collective-permute-done.14 = f32[56,128]{1,0:T(8,128)S(1)} collective-permute-done((f32[56,128]{1,0:T(8,128)S(1)}, f32[56,128]{1,0:T(8,128)S(1)}, u32[]{:S(2)}, u32[]{:S(2)}) %collective-permute-start.14) | collective-permute-done | bytes 28704 | tf_op jit(solution)/shard_map/ppermute | solution.py:88
  105.6 3.2 %collective-permute-start.15 = (f32[112,128]{1,0:T(8,128)S(1)}, f32[112,128]{1,0:T(8,128)S(1)}, u32[]{:S(2)}, u32[]{:S(2)}) collective-permute-start(f32[112,128]{1,0:T(8,128)S(1)} %pad_maximum_fusion.9), channel_id=1, source_target_pairs={{0,32},{1,33},{2,34},{3,35},{4,36},{5,37},{6,38},{7,39},{8,40},{9,... | collective-permute-start | bytes 172040 | tf_op jit(solution)/shard_map/ppermute | solution.py:88
  108.8 1.6 %collective-permute-done.15 = f32[112,128]{1,0:T(8,128)S(1)} collective-permute-done((f32[112,128]{1,0:T(8,128)S(1)}, f32[112,128]{1,0:T(8,128)S(1)}, u32[]{:S(2)}, u32[]{:S(2)}) %collective-permute-start.15) | collective-permute-done | bytes 57376 | tf_op jit(solution)/shard_map/ppermute | solution.py:88
  110.4 0.1 collective-permute-start.16
  110.5 3.9 %collective-permute-done.16 = f32[224,128]{1,0:T(8,128)S(1)} collective-permute-done((f32[224,128]{1,0:T(8,128)S(1)}, f32[224,128]{1,0:T(8,128)S(1)}, u32[]{:S(2)}, u32[]{:S(2)}) %collective-permute-start.16) | collective-permute-done | bytes 114720 | tf_op jit(solution)/shard_map/ppermute | solution.py:88
  114.4 0.1 collective-permute-start.17
  114.5 4.9 %collective-permute-done.17 = f32[448,128]{1,0:T(8,128)S(1)} collective-permute-done((f32[448,128]{1,0:T(8,128)S(1)}, f32[448,128]{1,0:T(8,128)S(1)}, u32[]{:S(2)}, u32[]{:S(2)}) %collective-permute-start.17) | collective-permute-done | bytes 229408 | tf_op jit(solution)/shard_map/ppermute | solution.py:88
  119.5 1.1 collective-permute-start.18
  120.6 6.3 %collective-permute-done.18 = f32[896,128]{1,0:T(8,128)S(1)} collective-permute-done((f32[896,128]{1,0:T(8,128)S(1)}, f32[896,128]{1,0:T(8,128)S(1)}, u32[]{:S(2)}, u32[]{:S(2)}) %collective-permute-start.18) | collective-permute-done | bytes 458784 | tf_op jit(solution)/shard_map/ppermute | solution.py:88
  126.9 0.1 broadcast_select_fusion.3
  127.0 0.1 pad_maximum_fusion.2
  127.0 14.2 %collective-permute-start.19 = (f32[1792,128]{1,0:T(8,128)S(1)}, f32[1792,128]{1,0:T(8,128)}, u32[]{:S(2)}, u32[]{:S(2)}) collective-permute-start(f32[1792,128]{1,0:T(8,128)S(1)} %pad_maximum_fusion.2), channel_id=1, source_target_pairs={{0,16},{16,0},{32,48},{48,32},{64,80},{80,64},{96,112},{112,96},{1... | collective-permute-start | bytes 2752520 | tf_op jit(solution)/shard_map/ppermute | solution.py:90
  141.3 2.2 %collective-permute-done.19 = f32[1792,128]{1,0:T(8,128)} collective-permute-done((f32[1792,128]{1,0:T(8,128)S(1)}, f32[1792,128]{1,0:T(8,128)}, u32[]{:S(2)}, u32[]{:S(2)}) %collective-permute-start.19) | collective-permute-done | bytes 917536 | tf_op jit(solution)/shard_map/ppermute | solution.py:90
  143.5 1.3 broadcast_select_fusion.1
  144.8 0.1 pad_maximum_fusion.1
  144.9 1.9 %copy.15 = f32[27,128,128]{2,1,0:T(8,128)} copy(f32[27,128,128]{1,2,0:T(8,128)S(1)} %bitcast.125) | data formatting | bytes 3538944
  (103 shorter events, 2.6 us)
Async XLA Ops:
  0.6 50.5 %copy-start = (bf16[27,128,128]{2,1,0:T(8,128)(2,1)S(1)}, bf16[27,128,128]{2,1,0:T(8,128)(2,1)}, u32[]{:S(2)}) copy-start(bf16[27,128,128]{2,1,0:T(8,128)(2,1)} %param.10) | copy-start | bytes 2654212
  3.4 11.8 %copy-start.2 = (bf16[2,2,512,128]{3,2,1,0:T(8,128)(2,1)}, bf16[2,2,512,128]{3,2,1,0:T(8,128)(2,1)S(1)}, u32[]{:S(2)}) copy-start(bf16[2,2,512,128]{3,2,1,0:T(8,128)(2,1)S(1)} %maximum_multiply_fusion) | copy-start | bytes 1572868
  5.4 18.4 %copy-start.4 = (s32[1,1,2]{2,1,0:T(1,128)S(1)}, s32[1,1,2]{2,1,0:T(1,128)}, u32[]{:S(2)}) copy-start(s32[1,1,2]{2,1,0:T(1,128)} %param.8) | copy-start | bytes 28
  5.5 24.3 %copy-start.3 = (s32[1,1,2,512]{3,2,1,0:T(2,128)S(1)}, s32[1,1,2,512]{3,2,1,0:T(2,128)}, u32[]{:S(2)}) copy-start(s32[1,1,2,512]{3,2,1,0:T(2,128)} %param.7) | copy-start | bytes 12292
  7.1 8.0 %copy-start.1 = (bf16[2,2,2,4,8,8,8,128]{7,6,3,5,2,4,1,0:T(8,128)(2,1)}, bf16[2,2,2,4,8,8,8,128]{7,6,3,5,2,4,1,0:T(8,128)(2,1)S(1)}, u32[]{:S(2)}) copy-start(bf16[2,2,2,4,8,8,8,128]{7,6,3,5,2,4,1,0:T(8,128)(2,1)S(1)} %copy.13) | copy-start | bytes 12582916
  7.1 10.1 %collective-permute-start.1 = (bf16[2,1,16,32,128]{4,3,2,1,0:T(8,128)(2,1)S(1)}, bf16[2,1,16,32,128]{4,3,2,1,0:T(8,128)(2,1)S(1)}, u32[]{:S(2)}, u32[]{:S(2)}) collective-permute-start(bf16[2,1,16,32,128]{4,3,2,1,0:T(8,128)(2,1)S(1)} %get-tuple-element.21), channel_id=1, source_target_pairs={{16,0},{32,16},{48,32},{64,48},{80,64},{96,80},{112,96},{128,112},... | collective-permute-start | bytes 786440 | tf_op jit(solution)/shard_map/ppermute | solution.py:21
  12.3 6.1 %collective-permute-start = (bf16[2,1,16,32,128]{4,3,2,1,0:T(8,128)(2,1)S(1)}, bf16[2,1,16,32,128]{4,3,2,1,0:T(8,128)(2,1)S(1)}, u32[]{:S(2)}, u32[]{:S(2)}) collective-permute-start(bf16[2,1,16,32,128]{4,3,2,1,0:T(8,128)(2,1)S(1)} %get-tuple-element.20), channel_id=1, source_target_pairs={{0,16},{16,32},{32,48},{48,64},{64,80},{80,96},{96,112},{112,128},... | collective-permute-start | bytes 786440 | tf_op jit(solution)/shard_map/ppermute | solution.py:20
  18.5 11.4 %collective-permute-start.3 = (bf16[2,18,1,32,128]{4,3,2,1,0:T(8,128)(2,1)S(1)}, bf16[2,18,1,32,128]{4,3,2,1,0:T(8,128)(2,1)S(1)}, u32[]{:S(2)}, u32[]{:S(2)}) collective-permute-start(bf16[2,18,1,32,128]{4,3,2,1,0:T(8,128)(2,1)S(1)} %pad_maximum_fusion.6), channel_id=1, source_target_pairs={{1,0},{2,1},{3,2},{4,3},{5,4},{6,5},{7,6},{8,7},{9,8},{10,9},{11,1... | collective-permute-start | bytes 884744 | tf_op jit(solution)/shard_map/ppermute | solution.py:27
  19.8 12.1 %collective-permute-start.2 = (bf16[2,18,1,32,128]{4,3,2,1,0:T(8,128)(2,1)S(1)}, bf16[2,18,1,32,128]{4,3,2,1,0:T(8,128)(2,1)S(1)}, u32[]{:S(2)}, u32[]{:S(2)}) collective-permute-start(bf16[2,18,1,32,128]{4,3,2,1,0:T(8,128)(2,1)S(1)} %pad_maximum_fusion.5), channel_id=1, source_target_pairs={{0,1},{1,2},{2,3},{3,4},{4,5},{5,6},{6,7},{7,8},{8,9},{9,10},{10,1... | collective-permute-start | bytes 884744 | tf_op jit(solution)/shard_map/ppermute | solution.py:26
  40.7 1.2 slice-start
  43.1 2.7 %collective-permute-start.4 = (f32[1792,128]{1,0:T(8,128)S(1)}, f32[1792,128]{1,0:T(8,128)S(1)}, u32[]{:S(2)}, u32[]{:S(2)}) collective-permute-start(f32[1792,128]{1,0:T(8,128)S(1)} %pad_dynamic-slice_fusion), channel_id=1, source_target_pairs={{0,16},{16,0},{32,48},{48,32},{64,80},{80,64},{96,112},{112,96},{1... | collective-permute-start | bytes 2752520 | tf_op jit(solution)/shard_map/ppermute | solution.py:72
  46.0 11.0 %collective-permute-start.5 = (f32[896,128]{1,0:T(8,128)S(1)}, f32[896,128]{1,0:T(8,128)S(1)}, u32[]{:S(2)}, u32[]{:S(2)}) collective-permute-start(f32[896,128]{1,0:T(8,128)S(1)} %constant_dynamic-slice_fusion.6), channel_id=1, source_target_pairs={{0,1},{1,0},{2,3},{3,2},{4,5},{5,4},{6,7},{7,6},{8,9},{9,8},{10,11... | collective-permute-start | bytes 1376264 | tf_op jit(solution)/shard_map/ppermute | solution.py:78
  57.1 6.3 %collective-permute-start.6 = (f32[448,128]{1,0:T(8,128)S(1)}, f32[448,128]{1,0:T(8,128)S(1)}, u32[]{:S(2)}, u32[]{:S(2)}) collective-permute-start(f32[448,128]{1,0:T(8,128)S(1)} %constant_dynamic-slice_fusion.5), channel_id=1, source_target_pairs={{0,64},{1,65},{2,66},{3,67},{4,68},{5,69},{6,70},{7,71},{8,72},{9,... | collective-permute-start | bytes 688136 | tf_op jit(solution)/shard_map/ppermute | solution.py:78
  63.4 3.7 %collective-permute-start.7 = (f32[224,128]{1,0:T(8,128)S(1)}, f32[224,128]{1,0:T(8,128)S(1)}, u32[]{:S(2)}, u32[]{:S(2)}) collective-permute-start(f32[224,128]{1,0:T(8,128)S(1)} %constant_dynamic-slice_fusion.4), channel_id=1, source_target_pairs={{0,2},{1,3},{2,0},{3,1},{4,6},{5,7},{6,4},{7,5},{8,10},{9,11},{10,... | collective-permute-start | bytes 344072 | tf_op jit(solution)/shard_map/ppermute | solution.py:78
  67.2 5.0 %collective-permute-start.8 = (f32[112,128]{1,0:T(8,128)S(1)}, f32[112,128]{1,0:T(8,128)S(1)}, u32[]{:S(2)}, u32[]{:S(2)}) collective-permute-start(f32[112,128]{1,0:T(8,128)S(1)} %constant_dynamic-slice_fusion.3), channel_id=1, source_target_pairs={{0,32},{1,33},{2,34},{3,35},{4,36},{5,37},{6,38},{7,39},{8,40},{9,... | collective-permute-start | bytes 172040 | tf_op jit(solution)/shard_map/ppermute | solution.py:78
  72.3 5.4 %collective-permute-start.9 = (f32[56,128]{1,0:T(8,128)S(1)}, f32[56,128]{1,0:T(8,128)S(1)}, u32[]{:S(2)}, u32[]{:S(2)}) collective-permute-start(f32[56,128]{1,0:T(8,128)S(1)} %constant_dynamic-slice_fusion.2), channel_id=1, source_target_pairs={{0,128},{1,129},{2,130},{3,131},{4,132},{5,133},{6,134},{7,135},{8... | collective-permute-start | bytes 86024 | tf_op jit(solution)/shard_map/ppermute | solution.py:78
  77.7 4.5 %collective-permute-start.10 = (f32[28,128]{1,0:T(8,128)S(1)}, f32[28,128]{1,0:T(8,128)S(1)}, u32[]{:S(2)}, u32[]{:S(2)}) collective-permute-start(f32[28,128]{1,0:T(8,128)S(1)} %constant_dynamic-slice_fusion.1), channel_id=1, source_target_pairs={{0,4},{1,5},{2,6},{3,7},{4,0},{5,1},{6,2},{7,3},{8,12},{9,13},{10,... | collective-permute-start | bytes 43016 | tf_op jit(solution)/shard_map/ppermute | solution.py:78
  82.3 8.7 %collective-permute-start.11 = (f32[14,128]{1,0:T(8,128)S(1)}, f32[14,128]{1,0:T(8,128)S(1)}, u32[]{:S(2)}, u32[]{:S(2)}) collective-permute-start(f32[14,128]{1,0:T(8,128)S(1)} %constant_dynamic-slice_fusion), channel_id=1, source_target_pairs={{0,8},{1,9},{2,10},{3,11},{4,12},{5,13},{6,14},{7,15},{8,0},{9,1},... | collective-permute-start | bytes 21512 | tf_op jit(solution)/shard_map/ppermute | solution.py:78
  91.0 6.5 %collective-permute-start.12 = (f32[14,128]{1,0:T(8,128)S(1)}, f32[14,128]{1,0:T(8,128)S(1)}, u32[]{:S(2)}, u32[]{:S(2)}) collective-permute-start(f32[14,128]{1,0:T(8,128)S(1)} %dynamic-slice_add_fusion.6), channel_id=1, source_target_pairs={{0,8},{1,9},{2,10},{3,11},{4,12},{5,13},{6,14},{7,15},{8,0},{9,1},... | collective-permute-start | bytes 21512 | tf_op jit(solution)/shard_map/ppermute | solution.py:88
  97.5 4.2 %collective-permute-start.13 = (f32[28,128]{1,0:T(8,128)S(1)}, f32[28,128]{1,0:T(8,128)S(1)}, u32[]{:S(2)}, u32[]{:S(2)}) collective-permute-start(f32[28,128]{1,0:T(8,128)S(1)} %pad_maximum_fusion.11), channel_id=1, source_target_pairs={{0,4},{1,5},{2,6},{3,7},{4,0},{5,1},{6,2},{7,3},{8,12},{9,13},{10,... | collective-permute-start | bytes 43016 | tf_op jit(solution)/shard_map/ppermute | solution.py:88
  101.7 3.8 %collective-permute-start.14 = (f32[56,128]{1,0:T(8,128)S(1)}, f32[56,128]{1,0:T(8,128)S(1)}, u32[]{:S(2)}, u32[]{:S(2)}) collective-permute-start(f32[56,128]{1,0:T(8,128)S(1)} %pad_maximum_fusion.10), channel_id=1, source_target_pairs={{0,128},{1,129},{2,130},{3,131},{4,132},{5,133},{6,134},{7,135},{8... | collective-permute-start | bytes 86024 | tf_op jit(solution)/shard_map/ppermute | solution.py:88
  105.6 4.8 %collective-permute-start.15 = (f32[112,128]{1,0:T(8,128)S(1)}, f32[112,128]{1,0:T(8,128)S(1)}, u32[]{:S(2)}, u32[]{:S(2)}) collective-permute-start(f32[112,128]{1,0:T(8,128)S(1)} %pad_maximum_fusion.9), channel_id=1, source_target_pairs={{0,32},{1,33},{2,34},{3,35},{4,36},{5,37},{6,38},{7,39},{8,40},{9,... | collective-permute-start | bytes 172040 | tf_op jit(solution)/shard_map/ppermute | solution.py:88
  110.4 4.0 %collective-permute-start.16 = (f32[224,128]{1,0:T(8,128)S(1)}, f32[224,128]{1,0:T(8,128)S(1)}, u32[]{:S(2)}, u32[]{:S(2)}) collective-permute-start(f32[224,128]{1,0:T(8,128)S(1)} %pad_maximum_fusion.8), channel_id=1, source_target_pairs={{0,2},{1,3},{2,0},{3,1},{4,6},{5,7},{6,4},{7,5},{8,10},{9,11},{10,... | collective-permute-start | bytes 344072 | tf_op jit(solution)/shard_map/ppermute | solution.py:88
  114.4 5.0 %collective-permute-start.17 = (f32[448,128]{1,0:T(8,128)S(1)}, f32[448,128]{1,0:T(8,128)S(1)}, u32[]{:S(2)}, u32[]{:S(2)}) collective-permute-start(f32[448,128]{1,0:T(8,128)S(1)} %pad_maximum_fusion.7), channel_id=1, source_target_pairs={{0,64},{1,65},{2,66},{3,67},{4,68},{5,69},{6,70},{7,71},{8,72},{9,... | collective-permute-start | bytes 688136 | tf_op jit(solution)/shard_map/ppermute | solution.py:88
  119.5 7.4 %collective-permute-start.18 = (f32[896,128]{1,0:T(8,128)S(1)}, f32[896,128]{1,0:T(8,128)S(1)}, u32[]{:S(2)}, u32[]{:S(2)}) collective-permute-start(f32[896,128]{1,0:T(8,128)S(1)} %pad_maximum_fusion.4), channel_id=1, source_target_pairs={{0,1},{1,0},{2,3},{3,2},{4,5},{5,4},{6,7},{7,6},{8,9},{9,8},{10,11... | collective-permute-start | bytes 1376264 | tf_op jit(solution)/shard_map/ppermute | solution.py:88
  127.0 16.5 %collective-permute-start.19 = (f32[1792,128]{1,0:T(8,128)S(1)}, f32[1792,128]{1,0:T(8,128)}, u32[]{:S(2)}, u32[]{:S(2)}) collective-permute-start(f32[1792,128]{1,0:T(8,128)S(1)} %pad_maximum_fusion.2), channel_id=1, source_target_pairs={{0,16},{16,0},{32,48},{48,32},{64,80},{80,64},{96,112},{112,96},{1... | collective-permute-start | bytes 2752520 | tf_op jit(solution)/shard_map/ppermute | solution.py:90

commit v11 on v10

--- a/solution.py
+++ b/solution.py
@@ -88,8 +88,10 @@
         got = lax.ppermute(buf, ("gx", "gy"), step_pairs(k))
         buf = join_halves(buf, got, core_bit(k))
     got = lax.ppermute(buf, "gx", [(i, i ^ 1) for i in range(lax.axis_size("gx"))])
-    buf = join_halves(buf, got, step_bit(FIRST))
-    return buf[: like.size // like.shape[-1]].reshape(like.shape)
+    flip = (-1,) + like.shape[1:]
+    mine = buf.reshape(flip).transpose(0, 2, 1)
+    theirs = got.reshape(flip).transpose(0, 2, 1)
+    return join_halves(mine, theirs, step_bit(FIRST))[: like.shape[0]]
 
 
 def place_bricks(bricks, places, alive):
@@ -153,7 +155,7 @@
     input_rows = (input_sum * keeper_rows).astype(jnp.bfloat16)
     half_done, output_rows, input_rows = lax.optimization_barrier((half_done, output_rows, input_rows))
     weight_total = butterfly_gather(half_done, weight_local)
-    weight_grad = weight_total.transpose(0, 2, 1)
+    weight_grad = weight_total
     output = output_rows.reshape(1, 1, slots, -1, chans)
     input_grad = input_rows.reshape(1, 1, slots, -1, chans)
     return (output, input_grad, weight_grad)

time: 147 us -> 147 us (level)
  no operation moved by 1% of the time
where the time goes in v11:
time: 147 us
  starting transfers between devices  64.9 us (44%)
  waiting for transfers between devices  46.6 us (32%)
  other arithmetic  9.65 us (7%)
  local copies, waits for them, and re-layouts  9.53 us (6%)
  matrix products  8.6 us (6%)
  between operations  7.65 us (5%)
    ppermute x7, starting transfers between devices, butterfly_scatter(): buf = keep + lax.ppermute(send, ('gx', 'gy'), step_pairs(k))  26.1 us
    ppermute x7, waiting for transfers between devices, butterfly_gather(): got = lax.ppermute(buf, ('gx', 'gy'), step_pairs(k))  24.7 us
    ppermute x1, starting transfers between devices, butterfly_gather(): lax.ppermute(buf, 'gx', [(i, i ^ 1) for i in range(lax.axis_size('gx'))])  14.2 us
    ppermute x7, waiting for transfers between devices, butterfly_scatter(): buf = keep + lax.ppermute(send, ('gx', 'gy'), step_pairs(k))  12.9 us
    ppermute x7, starting transfers between devices, butterfly_gather(): got = lax.ppermute(buf, ('gx', 'gy'), step_pairs(k))  11 us
    ppermute x1, starting transfers between devices, with_halo(): from_right = lax.ppermute(value[:, 0:1], 'gx', down_x)  5.11 us
    ppermute x1, starting transfers between devices, with_halo(): from_below = lax.ppermute(row(slice(ny - 1, ny)), 'gy', up_y)  4 us
    unnamed x65, local copies, waits for them, and re-layouts  3.84 us
  transfers between devices with their start and end apart: 20, of which 18 were waited for; matrix products, arithmetic and copies ran while one was open for 5% of the time, Pallas kernels for 0%

profile of v11, /device:TPU:1, one launch (start us, length us, event | category | flops | bytes accessed | tf_op | source)
XLA Modules:
  0.0 146.9 jit_solution(881903814719120558)
XLA Ops:
  0.6 0.0 copy-start
  1.4 0.8 broadcast_bitcast_fusion
  2.1 1.2 maximum_multiply_fusion
  3.4 2.0 %convolution_convert_fusion = bf16[2,512,128,16]{2,3,1,0:T(8,128)(2,1)S(1)} fusion(bf16[2,2,512,128]{3,2,1,0:T(8,128)(2,1)S(1)} %maximum_multiply_fusion, pred[2]{0:T(512)(128)(4,1)S(1)} %get-tuple-element.102, s32[2]{0:T(128)} %bitcast.190), kind=kOutput, calls=%fused_computation.1 | convolution fusion | flops 10485824 | bytes 4718602 | tf_op jit(solution)/shard_map/ps,tsvc->tpvc/dot_general | solution.py:100
  5.5 1.6 %copy.13 = bf16[2,2,2,4,8,8,8,128]{7,6,3,5,2,4,1,0:T(8,128)(2,1)S(1)} copy(bf16[2,2,2,4,8,8,8,128]{7,3,2,1,6,5,4,0:T(4,128)(2,1)S(1)} %bitcast.127) | data formatting | bytes 8388608 | tf_op jit(solution)/shard_map/reshape | solution.py:104
  7.1 5.1 %collective-permute-start.1 = (bf16[2,1,16,32,128]{4,3,2,1,0:T(8,128)(2,1)S(1)}, bf16[2,1,16,32,128]{4,3,2,1,0:T(8,128)(2,1)S(1)}, u32[]{:S(2)}, u32[]{:S(2)}) collective-permute-start(bf16[2,1,16,32,128]{4,3,2,1,0:T(8,128)(2,1)S(1)} %get-tuple-element.21), channel_id=1, source_target_pairs={{16,0},{32,16},{48,32},{64,48},{80,64},{96,80},{112,96},{128,112},... | collective-permute-start | bytes 786440 | tf_op jit(solution)/shard_map/ppermute | solution.py:21
  12.3 2.8 %collective-permute-start = (bf16[2,1,16,32,128]{4,3,2,1,0:T(8,128)(2,1)S(1)}, bf16[2,1,16,32,128]{4,3,2,1,0:T(8,128)(2,1)S(1)}, u32[]{:S(2)}, u32[]{:S(2)}) collective-permute-start(bf16[2,1,16,32,128]{4,3,2,1,0:T(8,128)(2,1)S(1)} %get-tuple-element.20), channel_id=1, source_target_pairs={{0,16},{16,32},{32,48},{48,64},{64,80},{80,96},{96,112},{112,128},... | collective-permute-start | bytes 786440 | tf_op jit(solution)/shard_map/ppermute | solution.py:20
  15.2 2.0 %collective-permute-done.1 = bf16[2,1,16,32,128]{4,3,2,1,0:T(8,128)(2,1)S(1)} collective-permute-done((bf16[2,1,16,32,128]{4,3,2,1,0:T(8,128)(2,1)S(1)}, bf16[2,1,16,32,128]{4,3,2,1,0:T(8,128)(2,1)S(1)}, u32[]{:S(2)}, u32[]{:S(2)}) %collective-permute-start.1) | collective-permute-done | bytes 262176 | tf_op jit(solution)/shard_map/ppermute | solution.py:21
  17.2 1.2 collective-permute-done
  18.5 1.3 collective-permute-start.3
  19.8 4.0 %collective-permute-start.2 = (bf16[2,18,1,32,128]{4,3,2,1,0:T(8,128)(2,1)S(1)}, bf16[2,18,1,32,128]{4,3,2,1,0:T(8,128)(2,1)S(1)}, u32[]{:S(2)}, u32[]{:S(2)}) collective-permute-start(bf16[2,18,1,32,128]{4,3,2,1,0:T(8,128)(2,1)S(1)} %pad_maximum_fusion.5), channel_id=1, source_target_pairs={{0,1},{1,2},{2,3},{3,4},{4,5},{5,6},{6,7},{7,8},{8,9},{9,10},{10,1... | collective-permute-start | bytes 884744 | tf_op jit(solution)/shard_map/ppermute | solution.py:26
  23.8 0.6 fusion.26
  29.9 2.0 %collective-permute-done.2 = bf16[2,18,1,32,128]{4,3,2,1,0:T(8,128)(2,1)S(1)} collective-permute-done((bf16[2,18,1,32,128]{4,3,2,1,0:T(8,128)(2,1)S(1)}, bf16[2,18,1,32,128]{4,3,2,1,0:T(8,128)(2,1)S(1)}, u32[]{:S(2)}, u32[]{:S(2)}) %collective-permute-start.2) | collective-permute-done | bytes 294944 | tf_op jit(solution)/shard_map/ppermute | solution.py:26
  31.9 3.8 %pad_maximum_fusion = bf16[2,18,18,32,128]{4,3,2,1,0:T(8,128)(2,1)S(1)} fusion(bf16[2,18,1,32,128]{4,3,2,1,0:T(8,128)(2,1)S(1)} %collective-permute-done.3, bf16[2,1,16,32,128]{4,3,2,1,0:T(8,128)(2,1)S(1)} %collective-permute-done.1, bf16[2,16,16,32,128]{4,3,2,1,0:T(8,128)(2,1)} %bitcast.126, bf16[2,1,16,32,128]{4,3,2,1,0:T(8,128)(2,1)S(1)} %collective-permute-done, ...), kind=kLoop, calls=%fused_computation | loop fusion | flops 10616832 | bytes 10616832 | tf_op jit(solution)/shard_map/concatenate | solution.py:29
  35.7 0.2 constant_dynamic-slice_fusion.7
  35.9 0.6 broadcast_select_fusion.5
  36.4 0.5 maximum_bitcast_fusion.1
  36.9 0.5 maximum_bitcast_fusion
  37.4 0.3 fusion.7
  37.7 0.4 fusion.23
  38.2 1.0 fusion.22
  39.2 0.5 fusion.21
  39.7 1.0 fusion.20
  41.9 1.1 convolution_multiply_fusion
  43.1 0.1 pad_dynamic-slice_fusion
  43.1 0.3 collective-permute-start.4
  44.3 1.5 %collective-permute-done.4 = f32[1792,128]{1,0:T(8,128)S(1)} collective-permute-done((f32[1792,128]{1,0:T(8,128)S(1)}, f32[1792,128]{1,0:T(8,128)S(1)}, u32[]{:S(2)}, u32[]{:S(2)}) %collective-permute-start.4) | collective-permute-done | bytes 917536 | tf_op jit(solution)/shard_map/ppermute | solution.py:72
  45.9 0.1 fusion.4
  46.0 5.1 %collective-permute-start.5 = (f32[896,128]{1,0:T(8,128)S(1)}, f32[896,128]{1,0:T(8,128)S(1)}, u32[]{:S(2)}, u32[]{:S(2)}) collective-permute-start(f32[896,128]{1,0:T(8,128)S(1)} %constant_dynamic-slice_fusion.6), channel_id=1, source_target_pairs={{0,1},{1,0},{2,3},{3,2},{4,5},{5,4},{6,7},{7,6},{8,9},{9,8},{10,11... | collective-permute-start | bytes 1376264 | tf_op jit(solution)/shard_map/ppermute | solution.py:78
  51.2 2.7 %fusion.2 = bf16[1024,128]{1,0:T(8,128)(2,1)} fusion(bf16[27,1024,128]{2,1,0:T(8,128)(2,1)S(1)} %constant_dynamic-update-slice_fusion, bf16[27,128,128]{2,1,0:T(8,128)(2,1)S(1)} %copy-done, f32[1024]{0:T(1024)S(1)} %fusion.10), kind=kOutput, calls=%fused_computation.12 | convolution fusion | flops 906231808 | bytes 8228864 | tf_op jit(solution)/shard_map/dvc,dce->ve/dot_general | solution.py:151
  53.9 3.2 %collective-permute-done.5 = f32[896,128]{1,0:T(8,128)S(1)} collective-permute-done((f32[896,128]{1,0:T(8,128)S(1)}, f32[896,128]{1,0:T(8,128)S(1)}, u32[]{:S(2)}, u32[]{:S(2)}) %collective-permute-start.5) | collective-permute-done | bytes 458784 | tf_op jit(solution)/shard_map/ppermute | solution.py:78
  57.1 2.6 %collective-permute-start.6 = (f32[448,128]{1,0:T(8,128)S(1)}, f32[448,128]{1,0:T(8,128)S(1)}, u32[]{:S(2)}, u32[]{:S(2)}) collective-permute-start(f32[448,128]{1,0:T(8,128)S(1)} %constant_dynamic-slice_fusion.5), channel_id=1, source_target_pairs={{0,64},{1,65},{2,66},{3,67},{4,68},{5,69},{6,70},{7,71},{8,72},{9,... | collective-permute-start | bytes 688136 | tf_op jit(solution)/shard_map/ppermute | solution.py:78
  59.8 3.6 %collective-permute-done.6 = f32[448,128]{1,0:T(8,128)S(1)} collective-permute-done((f32[448,128]{1,0:T(8,128)S(1)}, f32[448,128]{1,0:T(8,128)S(1)}, u32[]{:S(2)}, u32[]{:S(2)}) %collective-permute-start.6) | collective-permute-done | bytes 229408 | tf_op jit(solution)/shard_map/ppermute | solution.py:78
  63.4 1.4 collective-permute-start.7
  64.9 2.2 %collective-permute-done.7 = f32[224,128]{1,0:T(8,128)S(1)} collective-permute-done((f32[224,128]{1,0:T(8,128)S(1)}, f32[224,128]{1,0:T(8,128)S(1)}, u32[]{:S(2)}, u32[]{:S(2)}) %collective-permute-start.7) | collective-permute-done | bytes 114720 | tf_op jit(solution)/shard_map/ppermute | solution.py:78
  67.2 3.5 %collective-permute-start.8 = (f32[112,128]{1,0:T(8,128)S(1)}, f32[112,128]{1,0:T(8,128)S(1)}, u32[]{:S(2)}, u32[]{:S(2)}) collective-permute-start(f32[112,128]{1,0:T(8,128)S(1)} %constant_dynamic-slice_fusion.3), channel_id=1, source_target_pairs={{0,32},{1,33},{2,34},{3,35},{4,36},{5,37},{6,38},{7,39},{8,40},{9,... | collective-permute-start | bytes 172040 | tf_op jit(solution)/shard_map/ppermute | solution.py:78
  70.7 1.5 %collective-permute-done.8 = f32[112,128]{1,0:T(8,128)S(1)} collective-permute-done((f32[112,128]{1,0:T(8,128)S(1)}, f32[112,128]{1,0:T(8,128)S(1)}, u32[]{:S(2)}, u32[]{:S(2)}) %collective-permute-start.8) | collective-permute-done | bytes 57376 | tf_op jit(solution)/shard_map/ppermute | solution.py:78
  72.3 4.2 %collective-permute-start.9 = (f32[56,128]{1,0:T(8,128)S(1)}, f32[56,128]{1,0:T(8,128)S(1)}, u32[]{:S(2)}, u32[]{:S(2)}) collective-permute-start(f32[56,128]{1,0:T(8,128)S(1)} %constant_dynamic-slice_fusion.2), channel_id=1, source_target_pairs={{0,128},{1,129},{2,130},{3,131},{4,132},{5,133},{6,134},{7,135},{8... | collective-permute-start | bytes 86024 | tf_op jit(solution)/shard_map/ppermute | solution.py:78
  76.5 1.2 collective-permute-done.9
  77.7 3.4 %collective-permute-start.10 = (f32[28,128]{1,0:T(8,128)S(1)}, f32[28,128]{1,0:T(8,128)S(1)}, u32[]{:S(2)}, u32[]{:S(2)}) collective-permute-start(f32[28,128]{1,0:T(8,128)S(1)} %constant_dynamic-slice_fusion.1), channel_id=1, source_target_pairs={{0,4},{1,5},{2,6},{3,7},{4,0},{5,1},{6,2},{7,3},{8,12},{9,13},{10,... | collective-permute-start | bytes 43016 | tf_op jit(solution)/shard_map/ppermute | solution.py:78
  81.2 1.1 collective-permute-done.10
  82.3 6.0 %collective-permute-start.11 = (f32[14,128]{1,0:T(8,128)S(1)}, f32[14,128]{1,0:T(8,128)S(1)}, u32[]{:S(2)}, u32[]{:S(2)}) collective-permute-start(f32[14,128]{1,0:T(8,128)S(1)} %constant_dynamic-slice_fusion), channel_id=1, source_target_pairs={{0,8},{1,9},{2,10},{3,11},{4,12},{5,13},{6,14},{7,15},{8,0},{9,1},... | collective-permute-start | bytes 21512 | tf_op jit(solution)/shard_map/ppermute | solution.py:78
  88.3 2.7 %fusion.3 = bf16[1024,128]{1,0:T(8,128)(2,1)} fusion(bf16[27,1024,128]{2,1,0:T(8,128)(2,1)S(1)} %constant_dynamic-update-slice_fusion.27, bf16[27,128,128]{2,1,0:T(8,128)(2,1)S(1)} %copy-done, f32[1024]{0:T(1024)S(1)} %fusion.10), kind=kOutput, calls=%fused_computation.13 | convolution fusion | flops 906231808 | bytes 8228864 | tf_op jit(solution)/shard_map/dvc,dec->ve/dot_general | solution.py:154
  91.0 3.8 %collective-permute-start.12 = (f32[14,128]{1,0:T(8,128)S(1)}, f32[14,128]{1,0:T(8,128)S(1)}, u32[]{:S(2)}, u32[]{:S(2)}) collective-permute-start(f32[14,128]{1,0:T(8,128)S(1)} %dynamic-slice_add_fusion.6), channel_id=1, source_target_pairs={{0,8},{1,9},{2,10},{3,11},{4,12},{5,13},{6,14},{7,15},{8,0},{9,1},... | collective-permute-start | bytes 21512 | tf_op jit(solution)/shard_map/ppermute | solution.py:88
  94.8 2.7 %collective-permute-done.12 = f32[14,128]{1,0:T(8,128)S(1)} collective-permute-done((f32[14,128]{1,0:T(8,128)S(1)}, f32[14,128]{1,0:T(8,128)S(1)}, u32[]{:S(2)}, u32[]{:S(2)}) %collective-permute-start.12) | collective-permute-done | bytes 7200 | tf_op jit(solution)/shard_map/ppermute | solution.py:88
  97.5 2.0 %collective-permute-start.13 = (f32[28,128]{1,0:T(8,128)S(1)}, f32[28,128]{1,0:T(8,128)S(1)}, u32[]{:S(2)}, u32[]{:S(2)}) collective-permute-start(f32[28,128]{1,0:T(8,128)S(1)} %pad_maximum_fusion.11), channel_id=1, source_target_pairs={{0,4},{1,5},{2,6},{3,7},{4,0},{5,1},{6,2},{7,3},{8,12},{9,13},{10,... | collective-permute-start | bytes 43016 | tf_op jit(solution)/shard_map/ppermute | solution.py:88
  99.5 2.1 %collective-permute-done.13 = f32[28,128]{1,0:T(8,128)S(1)} collective-permute-done((f32[28,128]{1,0:T(8,128)S(1)}, f32[28,128]{1,0:T(8,128)S(1)}, u32[]{:S(2)}, u32[]{:S(2)}) %collective-permute-start.13) | collective-permute-done | bytes 14368 | tf_op jit(solution)/shard_map/ppermute | solution.py:88
  101.7 0.6 collective-permute-start.14
  102.3 3.2 %collective-permute-done.14 = f32[56,128]{1,0:T(8,128)S(1)} collective-permute-done((f32[56,128]{1,0:T(8,128)S(1)}, f32[56,128]{1,0:T(8,128)S(1)}, u32[]{:S(2)}, u32[]{:S(2)}) %collective-permute-start.14) | collective-permute-done | bytes 28704 | tf_op jit(solution)/shard_map/ppermute | solution.py:88
  105.6 3.2 %collective-permute-start.15 = (f32[112,128]{1,0:T(8,128)S(1)}, f32[112,128]{1,0:T(8,128)S(1)}, u32[]{:S(2)}, u32[]{:S(2)}) collective-permute-start(f32[112,128]{1,0:T(8,128)S(1)} %pad_maximum_fusion.9), channel_id=1, source_target_pairs={{0,32},{1,33},{2,34},{3,35},{4,36},{5,37},{6,38},{7,39},{8,40},{9,... | collective-permute-start | bytes 172040 | tf_op jit(solution)/shard_map/ppermute | solution.py:88
  108.8 1.6 %collective-permute-done.15 = f32[112,128]{1,0:T(8,128)S(1)} collective-permute-done((f32[112,128]{1,0:T(8,128)S(1)}, f32[112,128]{1,0:T(8,128)S(1)}, u32[]{:S(2)}, u32[]{:S(2)}) %collective-permute-start.15) | collective-permute-done | bytes 57376 | tf_op jit(solution)/shard_map/ppermute | solution.py:88
  110.4 0.1 collective-permute-start.16
  110.5 3.9 %collective-permute-done.16 = f32[224,128]{1,0:T(8,128)S(1)} collective-permute-done((f32[224,128]{1,0:T(8,128)S(1)}, f32[224,128]{1,0:T(8,128)S(1)}, u32[]{:S(2)}, u32[]{:S(2)}) %collective-permute-start.16) | collective-permute-done | bytes 114720 | tf_op jit(solution)/shard_map/ppermute | solution.py:88
  114.4 0.1 collective-permute-start.17
  114.5 4.9 %collective-permute-done.17 = f32[448,128]{1,0:T(8,128)S(1)} collective-permute-done((f32[448,128]{1,0:T(8,128)S(1)}, f32[448,128]{1,0:T(8,128)S(1)}, u32[]{:S(2)}, u32[]{:S(2)}) %collective-permute-start.17) | collective-permute-done | bytes 229408 | tf_op jit(solution)/shard_map/ppermute | solution.py:88
  119.5 1.1 collective-permute-start.18
  120.6 6.3 %collective-permute-done.18 = f32[896,128]{1,0:T(8,128)S(1)} collective-permute-done((f32[896,128]{1,0:T(8,128)S(1)}, f32[896,128]{1,0:T(8,128)S(1)}, u32[]{:S(2)}, u32[]{:S(2)}) %collective-permute-start.18) | collective-permute-done | bytes 458784 | tf_op jit(solution)/shard_map/ppermute | solution.py:88
  126.9 0.1 broadcast_select_fusion.3
  127.0 0.1 pad_maximum_fusion.2
  127.0 14.2 %collective-permute-start.19 = (f32[1792,128]{1,0:T(8,128)S(1)}, f32[1792,128]{1,0:T(8,128)}, u32[]{:S(2)}, u32[]{:S(2)}) collective-permute-start(f32[1792,128]{1,0:T(8,128)S(1)} %pad_maximum_fusion.2), channel_id=1, source_target_pairs={{0,16},{16,0},{32,48},{48,32},{64,80},{80,64},{96,112},{112,96},{1... | collective-permute-start | bytes 2752520 | tf_op jit(solution)/shard_map/ppermute | solution.py:90
  141.3 2.2 %collective-permute-done.19 = f32[1792,128]{1,0:T(8,128)} collective-permute-done((f32[1792,128]{1,0:T(8,128)S(1)}, f32[1792,128]{1,0:T(8,128)}, u32[]{:S(2)}, u32[]{:S(2)}) %collective-permute-start.19) | collective-permute-done | bytes 917536 | tf_op jit(solution)/shard_map/ppermute | solution.py:90
  143.5 1.3 broadcast_select_fusion.1
  144.8 0.2 pad_maximum_fusion.1
  145.0 1.9 %copy.15 = f32[27,128,128]{2,1,0:T(8,128)} copy(f32[27,128,128]{1,2,0:T(8,128)S(1)} %pad_maximum_fusion.1) | data formatting | bytes 3538944
  (103 shorter events, 2.6 us)
Async XLA Ops:
  0.6 50.5 %copy-start = (bf16[27,128,128]{2,1,0:T(8,128)(2,1)S(1)}, bf16[27,128,128]{2,1,0:T(8,128)(2,1)}, u32[]{:S(2)}) copy-start(bf16[27,128,128]{2,1,0:T(8,128)(2,1)} %param.10) | copy-start | bytes 2654212
  3.4 11.8 %copy-start.2 = (bf16[2,2,512,128]{3,2,1,0:T(8,128)(2,1)}, bf16[2,2,512,128]{3,2,1,0:T(8,128)(2,1)S(1)}, u32[]{:S(2)}) copy-start(bf16[2,2,512,128]{3,2,1,0:T(8,128)(2,1)S(1)} %maximum_multiply_fusion) | copy-start | bytes 1572868
  5.4 18.4 %copy-start.4 = (s32[1,1,2]{2,1,0:T(1,128)S(1)}, s32[1,1,2]{2,1,0:T(1,128)}, u32[]{:S(2)}) copy-start(s32[1,1,2]{2,1,0:T(1,128)} %param.8) | copy-start | bytes 28
  5.5 24.3 %copy-start.3 = (s32[1,1,2,512]{3,2,1,0:T(2,128)S(1)}, s32[1,1,2,512]{3,2,1,0:T(2,128)}, u32[]{:S(2)}) copy-start(s32[1,1,2,512]{3,2,1,0:T(2,128)} %param.7) | copy-start | bytes 12292
  7.1 8.0 %copy-start.1 = (bf16[2,2,2,4,8,8,8,128]{7,6,3,5,2,4,1,0:T(8,128)(2,1)}, bf16[2,2,2,4,8,8,8,128]{7,6,3,5,2,4,1,0:T(8,128)(2,1)S(1)}, u32[]{:S(2)}) copy-start(bf16[2,2,2,4,8,8,8,128]{7,6,3,5,2,4,1,0:T(8,128)(2,1)S(1)} %copy.13) | copy-start | bytes 12582916
  7.1 10.1 %collective-permute-start.1 = (bf16[2,1,16,32,128]{4,3,2,1,0:T(8,128)(2,1)S(1)}, bf16[2,1,16,32,128]{4,3,2,1,0:T(8,128)(2,1)S(1)}, u32[]{:S(2)}, u32[]{:S(2)}) collective-permute-start(bf16[2,1,16,32,128]{4,3,2,1,0:T(8,128)(2,1)S(1)} %get-tuple-element.21), channel_id=1, source_target_pairs={{16,0},{32,16},{48,32},{64,48},{80,64},{96,80},{112,96},{128,112},... | collective-permute-start | bytes 786440 | tf_op jit(solution)/shard_map/ppermute | solution.py:21
  12.3 6.1 %collective-permute-start = (bf16[2,1,16,32,128]{4,3,2,1,0:T(8,128)(2,1)S(1)}, bf16[2,1,16,32,128]{4,3,2,1,0:T(8,128)(2,1)S(1)}, u32[]{:S(2)}, u32[]{:S(2)}) collective-permute-start(bf16[2,1,16,32,128]{4,3,2,1,0:T(8,128)(2,1)S(1)} %get-tuple-element.20), channel_id=1, source_target_pairs={{0,16},{16,32},{32,48},{48,64},{64,80},{80,96},{96,112},{112,128},... | collective-permute-start | bytes 786440 | tf_op jit(solution)/shard_map/ppermute | solution.py:20
  18.5 11.4 %collective-permute-start.3 = (bf16[2,18,1,32,128]{4,3,2,1,0:T(8,128)(2,1)S(1)}, bf16[2,18,1,32,128]{4,3,2,1,0:T(8,128)(2,1)S(1)}, u32[]{:S(2)}, u32[]{:S(2)}) collective-permute-start(bf16[2,18,1,32,128]{4,3,2,1,0:T(8,128)(2,1)S(1)} %pad_maximum_fusion.6), channel_id=1, source_target_pairs={{1,0},{2,1},{3,2},{4,3},{5,4},{6,5},{7,6},{8,7},{9,8},{10,9},{11,1... | collective-permute-start | bytes 884744 | tf_op jit(solution)/shard_map/ppermute | solution.py:27
  19.8 12.1 %collective-permute-start.2 = (bf16[2,18,1,32,128]{4,3,2,1,0:T(8,128)(2,1)S(1)}, bf16[2,18,1,32,128]{4,3,2,1,0:T(8,128)(2,1)S(1)}, u32[]{:S(2)}, u32[]{:S(2)}) collective-permute-start(bf16[2,18,1,32,128]{4,3,2,1,0:T(8,128)(2,1)S(1)} %pad_maximum_fusion.5), channel_id=1, source_target_pairs={{0,1},{1,2},{2,3},{3,4},{4,5},{5,6},{6,7},{7,8},{8,9},{9,10},{10,1... | collective-permute-start | bytes 884744 | tf_op jit(solution)/shard_map/ppermute | solution.py:26
  40.7 1.2 slice-start
  43.1 2.7 %collective-permute-start.4 = (f32[1792,128]{1,0:T(8,128)S(1)}, f32[1792,128]{1,0:T(8,128)S(1)}, u32[]{:S(2)}, u32[]{:S(2)}) collective-permute-start(f32[1792,128]{1,0:T(8,128)S(1)} %pad_dynamic-slice_fusion), channel_id=1, source_target_pairs={{0,16},{16,0},{32,48},{48,32},{64,80},{80,64},{96,112},{112,96},{1... | collective-permute-start | bytes 2752520 | tf_op jit(solution)/shard_map/ppermute | solution.py:72
  46.0 11.0 %collective-permute-start.5 = (f32[896,128]{1,0:T(8,128)S(1)}, f32[896,128]{1,0:T(8,128)S(1)}, u32[]{:S(2)}, u32[]{:S(2)}) collective-permute-start(f32[896,128]{1,0:T(8,128)S(1)} %constant_dynamic-slice_fusion.6), channel_id=1, source_target_pairs={{0,1},{1,0},{2,3},{3,2},{4,5},{5,4},{6,7},{7,6},{8,9},{9,8},{10,11... | collective-permute-start | bytes 1376264 | tf_op jit(solution)/shard_map/ppermute | solution.py:78
  57.1 6.3 %collective-permute-start.6 = (f32[448,128]{1,0:T(8,128)S(1)}, f32[448,128]{1,0:T(8,128)S(1)}, u32[]{:S(2)}, u32[]{:S(2)}) collective-permute-start(f32[448,128]{1,0:T(8,128)S(1)} %constant_dynamic-slice_fusion.5), channel_id=1, source_target_pairs={{0,64},{1,65},{2,66},{3,67},{4,68},{5,69},{6,70},{7,71},{8,72},{9,... | collective-permute-start | bytes 688136 | tf_op jit(solution)/shard_map/ppermute | solution.py:78
  63.4 3.7 %collective-permute-start.7 = (f32[224,128]{1,0:T(8,128)S(1)}, f32[224,128]{1,0:T(8,128)S(1)}, u32[]{:S(2)}, u32[]{:S(2)}) collective-permute-start(f32[224,128]{1,0:T(8,128)S(1)} %constant_dynamic-slice_fusion.4), channel_id=1, source_target_pairs={{0,2},{1,3},{2,0},{3,1},{4,6},{5,7},{6,4},{7,5},{8,10},{9,11},{10,... | collective-permute-start | bytes 344072 | tf_op jit(solution)/shard_map/ppermute | solution.py:78
  67.2 5.0 %collective-permute-start.8 = (f32[112,128]{1,0:T(8,128)S(1)}, f32[112,128]{1,0:T(8,128)S(1)}, u32[]{:S(2)}, u32[]{:S(2)}) collective-permute-start(f32[112,128]{1,0:T(8,128)S(1)} %constant_dynamic-slice_fusion.3), channel_id=1, source_target_pairs={{0,32},{1,33},{2,34},{3,35},{4,36},{5,37},{6,38},{7,39},{8,40},{9,... | collective-permute-start | bytes 172040 | tf_op jit(solution)/shard_map/ppermute | solution.py:78
  72.3 5.4 %collective-permute-start.9 = (f32[56,128]{1,0:T(8,128)S(1)}, f32[56,128]{1,0:T(8,128)S(1)}, u32[]{:S(2)}, u32[]{:S(2)}) collective-permute-start(f32[56,128]{1,0:T(8,128)S(1)} %constant_dynamic-slice_fusion.2), channel_id=1, source_target_pairs={{0,128},{1,129},{2,130},{3,131},{4,132},{5,133},{6,134},{7,135},{8... | collective-permute-start | bytes 86024 | tf_op jit(solution)/shard_map/ppermute | solution.py:78
  77.7 4.5 %collective-permute-start.10 = (f32[28,128]{1,0:T(8,128)S(1)}, f32[28,128]{1,0:T(8,128)S(1)}, u32[]{:S(2)}, u32[]{:S(2)}) collective-permute-start(f32[28,128]{1,0:T(8,128)S(1)} %constant_dynamic-slice_fusion.1), channel_id=1, source_target_pairs={{0,4},{1,5},{2,6},{3,7},{4,0},{5,1},{6,2},{7,3},{8,12},{9,13},{10,... | collective-permute-start | bytes 43016 | tf_op jit(solution)/shard_map/ppermute | solution.py:78
  82.3 8.7 %collective-permute-start.11 = (f32[14,128]{1,0:T(8,128)S(1)}, f32[14,128]{1,0:T(8,128)S(1)}, u32[]{:S(2)}, u32[]{:S(2)}) collective-permute-start(f32[14,128]{1,0:T(8,128)S(1)} %constant_dynamic-slice_fusion), channel_id=1, source_target_pairs={{0,8},{1,9},{2,10},{3,11},{4,12},{5,13},{6,14},{7,15},{8,0},{9,1},... | collective-permute-start | bytes 21512 | tf_op jit(solution)/shard_map/ppermute | solution.py:78
  91.0 6.5 %collective-permute-start.12 = (f32[14,128]{1,0:T(8,128)S(1)}, f32[14,128]{1,0:T(8,128)S(1)}, u32[]{:S(2)}, u32[]{:S(2)}) collective-permute-start(f32[14,128]{1,0:T(8,128)S(1)} %dynamic-slice_add_fusion.6), channel_id=1, source_target_pairs={{0,8},{1,9},{2,10},{3,11},{4,12},{5,13},{6,14},{7,15},{8,0},{9,1},... | collective-permute-start | bytes 21512 | tf_op jit(solution)/shard_map/ppermute | solution.py:88
  97.5 4.2 %collective-permute-start.13 = (f32[28,128]{1,0:T(8,128)S(1)}, f32[28,128]{1,0:T(8,128)S(1)}, u32[]{:S(2)}, u32[]{:S(2)}) collective-permute-start(f32[28,128]{1,0:T(8,128)S(1)} %pad_maximum_fusion.11), channel_id=1, source_target_pairs={{0,4},{1,5},{2,6},{3,7},{4,0},{5,1},{6,2},{7,3},{8,12},{9,13},{10,... | collective-permute-start | bytes 43016 | tf_op jit(solution)/shard_map/ppermute | solution.py:88
  101.7 3.8 %collective-permute-start.14 = (f32[56,128]{1,0:T(8,128)S(1)}, f32[56,128]{1,0:T(8,128)S(1)}, u32[]{:S(2)}, u32[]{:S(2)}) collective-permute-start(f32[56,128]{1,0:T(8,128)S(1)} %pad_maximum_fusion.10), channel_id=1, source_target_pairs={{0,128},{1,129},{2,130},{3,131},{4,132},{5,133},{6,134},{7,135},{8... | collective-permute-start | bytes 86024 | tf_op jit(solution)/shard_map/ppermute | solution.py:88
  105.6 4.8 %collective-permute-start.15 = (f32[112,128]{1,0:T(8,128)S(1)}, f32[112,128]{1,0:T(8,128)S(1)}, u32[]{:S(2)}, u32[]{:S(2)}) collective-permute-start(f32[112,128]{1,0:T(8,128)S(1)} %pad_maximum_fusion.9), channel_id=1, source_target_pairs={{0,32},{1,33},{2,34},{3,35},{4,36},{5,37},{6,38},{7,39},{8,40},{9,... | collective-permute-start | bytes 172040 | tf_op jit(solution)/shard_map/ppermute | solution.py:88
  110.4 4.0 %collective-permute-start.16 = (f32[224,128]{1,0:T(8,128)S(1)}, f32[224,128]{1,0:T(8,128)S(1)}, u32[]{:S(2)}, u32[]{:S(2)}) collective-permute-start(f32[224,128]{1,0:T(8,128)S(1)} %pad_maximum_fusion.8), channel_id=1, source_target_pairs={{0,2},{1,3},{2,0},{3,1},{4,6},{5,7},{6,4},{7,5},{8,10},{9,11},{10,... | collective-permute-start | bytes 344072 | tf_op jit(solution)/shard_map/ppermute | solution.py:88
  114.4 5.0 %collective-permute-start.17 = (f32[448,128]{1,0:T(8,128)S(1)}, f32[448,128]{1,0:T(8,128)S(1)}, u32[]{:S(2)}, u32[]{:S(2)}) collective-permute-start(f32[448,128]{1,0:T(8,128)S(1)} %pad_maximum_fusion.7), channel_id=1, source_target_pairs={{0,64},{1,65},{2,66},{3,67},{4,68},{5,69},{6,70},{7,71},{8,72},{9,... | collective-permute-start | bytes 688136 | tf_op jit(solution)/shard_map/ppermute | solution.py:88
  119.5 7.4 %collective-permute-start.18 = (f32[896,128]{1,0:T(8,128)S(1)}, f32[896,128]{1,0:T(8,128)S(1)}, u32[]{:S(2)}, u32[]{:S(2)}) collective-permute-start(f32[896,128]{1,0:T(8,128)S(1)} %pad_maximum_fusion.4), channel_id=1, source_target_pairs={{0,1},{1,0},{2,3},{3,2},{4,5},{5,4},{6,7},{7,6},{8,9},{9,8},{10,11... | collective-permute-start | bytes 1376264 | tf_op jit(solution)/shard_map/ppermute | solution.py:88
  127.0 16.5 %collective-permute-start.19 = (f32[1792,128]{1,0:T(8,128)S(1)}, f32[1792,128]{1,0:T(8,128)}, u32[]{:S(2)}, u32[]{:S(2)}) collective-permute-start(f32[1792,128]{1,0:T(8,128)S(1)} %pad_maximum_fusion.2), channel_id=1, source_target_pairs={{0,16},{16,0},{32,48},{48,32},{64,80},{80,64},{96,112},{112,96},{1... | collective-permute-start | bytes 2752520 | tf_op jit(solution)/shard_map/ppermute | solution.py:90
